TPU v7x, 32 devices: a whole 2x2x4 slice. The times are simulated.
32 devices in a mesh: xy: 16 (over z, y, core), gz: 2 (over x).
Axes of the slice: x: 2, y: 2, z: 4, core: 2. Of those that a mesh axis runs over, the one named last changes fastest.
Arguments:
- volume: float32 [32, 262144], P('gz', 'xy'), may hold values from -4 to 4
- measured: float32 [2, 32, 4096], P(None, 'gz', 'xy'), may hold values from -12 to 12
- band_start: int32 [2, 16], P(None, 'xy'), may hold values from 0 to 3584
- column_offset: int32 [2, 262144], P(None, 'xy'), may hold values from 0 to 509
- column_width: int32 [2, 262144], P(None, 'xy'), may hold values from 1 to 3
- amplitude: float32 [2, 262144], P(None, 'xy'), may hold values from 0.01 to 0.1
- axial_weight: float32 [3, 2, 32], P(None, None, 'gz'), may hold values from 0.2 to 1
Outputs:
- volume_next: float32 [32, 262144], P('gz', 'xy')
- residual: float32 [2, 32, 4096], P(None, 'gz', 'xy')
All inputs are finite; a program needn't handle non-finite values.
Results may differ from a plain program's by a relative error of at most 0.0003.
Values sent between devices are 32-bit elements; how exact they have to be, the bound alone decides.
No kernel may reach another device: no remote copies, remote signals or barrier semaphores. Data moves between devices by JAX's collectives and lax.ppermute only.
A program may use at most 64 MiB of HBM per device.

v0:
```python
import math

import jax
import jax.numpy as jnp
from jax import lax
from jax.sharding import PartitionSpec as P

U = 4096
B = 512


RELAX = 0.9


def extended(cells, sides, width):
    for axis, dim in sides:
        count = lax.axis_size(axis)
        ends = count - 1
        head = lax.slice_in_dim(cells, 0, width, axis=dim)
        tail = lax.slice_in_dim(cells, cells.shape[dim] - width, cells.shape[dim], axis=dim)
        cells = jnp.concatenate(
            [
                lax.ppermute(tail, axis, [(i, (i + 1) % count) for i in range(ends)]),
                cells,
                lax.ppermute(head, axis, [((i + 1) % count, i) for i in range(ends)]),
            ],
            axis=dim,
        )
    return cells


def footprint(amp_block, off_block, wid_block, band_width):
    positions = jnp.arange(band_width, dtype=jnp.int32)[None, :]
    inside = (positions >= off_block[:, None]) & (positions < (off_block + wid_block)[:, None])
    return jnp.where(inside, amp_block[:, None], jnp.zeros((), jnp.float32))


def column_block(columns):
    return math.gcd(columns, 2048)


def joint_weights(amplitude, column_offset, column_width, first_column, block_size):
    pieces = []
    for view_index in range(amplitude.shape[0]):
        pieces.append(
            footprint(
                lax.dynamic_slice_in_dim(amplitude[view_index], first_column, block_size, 0),
                lax.dynamic_slice_in_dim(column_offset[view_index], first_column, block_size, 0),
                lax.dynamic_slice_in_dim(column_width[view_index], first_column, block_size, 0),
                B,
            )
        )
    return jnp.concatenate(pieces, axis=1)


def forward_band(volume, amplitude, column_offset, column_width):
    view_count = amplitude.shape[0]
    slab_rows = volume.shape[0]
    block_size = column_block(volume.shape[1])

    def block_step(running, block_index):
        first_column = block_index * block_size
        slab_cells = lax.dynamic_slice_in_dim(volume, first_column, block_size, 1)
        proj_rows, cover_rows = running
        weights = joint_weights(amplitude, column_offset, column_width, first_column, block_size)
        proj_rows = proj_rows + jnp.dot(slab_cells, weights, precision=lax.Precision.HIGHEST)
        cover_rows = cover_rows + jnp.sum(weights, axis=0)
        return ((proj_rows, cover_rows), None)

    starting = (
        jnp.zeros((slab_rows, view_count * B), jnp.float32),
        jnp.zeros((view_count * B,), jnp.float32),
    )
    outcome = lax.scan(
        block_step, starting, jnp.arange(volume.shape[1] // block_size, dtype=jnp.int32)
    )
    proj_rows, cover_rows = outcome[0]
    band_proj = jnp.transpose(proj_rows.reshape(slab_rows, view_count, B), (1, 0, 2))
    band_cover = cover_rows.reshape(view_count, B)
    return (band_proj, band_cover)


def backward_band(back_band, amplitude, column_offset, column_width, columns):
    block_size = column_block(columns)
    view_count = back_band.shape[0]
    slab_rows = back_band.shape[1]
    joined_rows = jnp.transpose(back_band, (1, 0, 2)).reshape(slab_rows, view_count * B)

    def block_values(block_index):
        first_column = block_index * block_size
        weights = joint_weights(amplitude, column_offset, column_width, first_column, block_size)
        return jnp.einsum("sj,cj->sc", joined_rows, weights, precision=lax.Precision.HIGHEST)

    blocks = lax.map(block_values, jnp.arange(columns // block_size, dtype=jnp.int32))
    return jnp.moveaxis(blocks, 0, 1).reshape(slab_rows, columns)


def place_band(band_rows, band_start):
    placed = []
    for view_index in range(band_rows.shape[0]):
        blank_rows = jnp.zeros((band_rows.shape[1], U), jnp.float32)
        placed.append(
            lax.dynamic_update_slice(
                blank_rows, band_rows[view_index], (jnp.int32(0), band_start[view_index, 0])
            )
        )
    return jnp.stack(placed)


def take_band(full_rows, band_start):
    picked = []
    for view_index in range(full_rows.shape[0]):
        picked.append(
            lax.dynamic_slice(
                full_rows[view_index],
                (jnp.int32(0), band_start[view_index, 0]),
                (full_rows.shape[1], B),
            )
        )
    return jnp.stack(picked)


def axial_forward(padded, lower_index, centre_field, middle_weight):
    return (
        middle_weight * centre_field + padded[lower_index][:, 2:] + padded[lower_index + 1][:, :-2]
    )


def axial_backward(field, padded_rows, low_weight, mid_weight, high_weight):
    return low_weight * padded_rows[:, :-2] + mid_weight * field + high_weight * padded_rows[:, 2:]


def local(volume, measured, band_start, column_offset, column_width, amplitude, axial_weight):
    slab_rows = volume.shape[0]
    view_count = amplitude.shape[0]
    low_weight = axial_weight[0][:, :, None]
    mid_weight = axial_weight[1][:, :, None]
    high_weight = axial_weight[2][:, :, None]
    band_proj, band_cover = forward_band(volume, amplitude, column_offset, column_width)
    measured_full = lax.all_gather(measured, "xy", axis=2, tiled=True)
    cover_rows = jnp.broadcast_to(band_cover[:, None, :], band_proj.shape)
    stacked = jnp.stack(
        [
            low_weight * band_proj,
            high_weight * band_proj,
            low_weight * cover_rows,
            high_weight * cover_rows,
        ]
    )
    padded = extended(stacked, (("gz", 2),), 1)
    projection_band = axial_forward(padded, 0, band_proj, mid_weight)
    coverage_band = axial_forward(padded, 2, cover_rows, mid_weight)
    projection, coverage = lax.psum(
        (place_band(projection_band, band_start), place_band(coverage_band, band_start)), "xy"
    )
    residual_full = (measured_full - projection) / jnp.maximum(coverage, 1.0)
    shard_width = measured.shape[2]
    residual_shard = lax.dynamic_slice_in_dim(
        residual_full, lax.axis_index("xy") * shard_width, shard_width, 2
    )
    residual_band = take_band(residual_full, band_start)
    padded_rows = extended(residual_band, (("gz", 1),), 1)
    back_band = axial_backward(residual_band, padded_rows, low_weight, mid_weight, high_weight)
    correction = backward_band(back_band, amplitude, column_offset, column_width, volume.shape[1])
    global_rows = lax.axis_index("gz") * slab_rows + jnp.arange(slab_rows, dtype=jnp.int32)
    total_rows = slab_rows * lax.axis_size("gz")
    row_weight = (
        jnp.where(global_rows[None, :] > 0, axial_weight[0], 0.0)
        + axial_weight[1]
        + jnp.where(global_rows[None, :] < total_rows - 1, axial_weight[2], 0.0)
    )
    column_mass = amplitude * column_width.astype(jnp.float32)
    normalizer = jnp.zeros_like(volume)
    for view_index in range(view_count):
        normalizer = normalizer + row_weight[view_index][:, None] * column_mass[view_index][None, :]
    volume_next = volume + RELAX * correction / normalizer
    return (volume_next, residual_shard)


def solution(mesh):
    return jax.shard_map(
        local,
        mesh=mesh,
        in_specs=(
            P("gz", "xy"),
            P(None, "gz", "xy"),
            P(None, "xy"),
            P(None, "xy"),
            P(None, "xy"),
            P(None, "xy"),
            P(None, None, "gz"),
        ),
        out_specs=(P("gz", "xy"), P(None, "gz", "xy")),
        check_vma=False,
    )
```

profile of v0, /device:TPU:0, one launch (start us, length us, event | category | flops | bytes accessed | tf_op | source)
XLA Modules:
  0.0 326.3 jit_solution(2100854280282810262)
XLA Ops:
  8.1 88.7 %while.24 = (s32[]{:T(128)}, f32[16,1024]{1,0:T(8,128)S(1)}, f32[1024]{0:T(1024)S(1)}, s32[8]{0:T(128)S(1)}, f32[16,16384]{1,0:T(8,128)}, /*index=5*/s32[2,16384...) while((s32[]{:T(128)}, f32[16,1024]{1,0:T(8,128)S(1)}, ...), condition=%wide.region_2.3_spmd.clone, body=%wide.region_0.2_spmd.clone.sunk | while | flops 417371136 | bytes 26427608 | solution.py:74
  9.4 1.1 fusion.70
  10.5 1.3 fusion.71
  14.2 5.0 %fusion.74 = f32[16,1024]{1,0:T(8,128)S(1)} fusion(f32[2048,512]{1,0:T(8,128)S(1)} %fusion.72, f32[2048,512]{1,0:T(8,128)S(1)} %fusion.73, f32[16,16384]{1,0:T(8,128)} %get-tuple-element.353, s32[]{:T(128)S(6)} %select_n.75, f32[16,1024]{1,0:T(8,128)S(1)} %get-tuple-element.338, pred[]{:T(512)S(6)} %compare.3), kind=kOutput, calls=%fused_computation.32.clone.1 | convolution fusion | flops 404783104 | bytes 8650757 | tf_op jit(solution)/shard_map/while/body/eval_jaxpr/dot_general | solution.py:66
  20.4 1.1 fusion.70
  21.6 1.3 fusion.71
  25.3 5.0 %fusion.74 = f32[16,1024]{1,0:T(8,128)S(1)} fusion(f32[2048,512]{1,0:T(8,128)S(1)} %fusion.72, f32[2048,512]{1,0:T(8,128)S(1)} %fusion.73, f32[16,16384]{1,0:T(8,128)} %get-tuple-element.353, s32[]{:T(128)S(6)} %select_n.75, f32[16,1024]{1,0:T(8,128)S(1)} %get-tuple-element.338, pred[]{:T(512)S(6)} %compare.3), kind=kOutput, calls=%fused_computation.32.clone.1 | convolution fusion | flops 404783104 | bytes 8650757 | tf_op jit(solution)/shard_map/while/body/eval_jaxpr/dot_general | solution.py:66
  31.5 1.1 fusion.70
  32.7 1.3 fusion.71
  36.4 5.0 %fusion.74 = f32[16,1024]{1,0:T(8,128)S(1)} fusion(f32[2048,512]{1,0:T(8,128)S(1)} %fusion.72, f32[2048,512]{1,0:T(8,128)S(1)} %fusion.73, f32[16,16384]{1,0:T(8,128)} %get-tuple-element.353, s32[]{:T(128)S(6)} %select_n.75, f32[16,1024]{1,0:T(8,128)S(1)} %get-tuple-element.338, pred[]{:T(512)S(6)} %compare.3), kind=kOutput, calls=%fused_computation.32.clone.1 | convolution fusion | flops 404783104 | bytes 8650757 | tf_op jit(solution)/shard_map/while/body/eval_jaxpr/dot_general | solution.py:66
  42.6 1.1 fusion.70
  43.7 1.3 fusion.71
  47.5 5.0 %fusion.74 = f32[16,1024]{1,0:T(8,128)S(1)} fusion(f32[2048,512]{1,0:T(8,128)S(1)} %fusion.72, f32[2048,512]{1,0:T(8,128)S(1)} %fusion.73, f32[16,16384]{1,0:T(8,128)} %get-tuple-element.353, s32[]{:T(128)S(6)} %select_n.75, f32[16,1024]{1,0:T(8,128)S(1)} %get-tuple-element.338, pred[]{:T(512)S(6)} %compare.3), kind=kOutput, calls=%fused_computation.32.clone.1 | convolution fusion | flops 404783104 | bytes 8650757 | tf_op jit(solution)/shard_map/while/body/eval_jaxpr/dot_general | solution.py:66
  53.7 1.1 fusion.70
  54.8 1.3 fusion.71
  58.6 5.0 %fusion.74 = f32[16,1024]{1,0:T(8,128)S(1)} fusion(f32[2048,512]{1,0:T(8,128)S(1)} %fusion.72, f32[2048,512]{1,0:T(8,128)S(1)} %fusion.73, f32[16,16384]{1,0:T(8,128)} %get-tuple-element.353, s32[]{:T(128)S(6)} %select_n.75, f32[16,1024]{1,0:T(8,128)S(1)} %get-tuple-element.338, pred[]{:T(512)S(6)} %compare.3), kind=kOutput, calls=%fused_computation.32.clone.1 | convolution fusion | flops 404783104 | bytes 8650757 | tf_op jit(solution)/shard_map/while/body/eval_jaxpr/dot_general | solution.py:66
  64.8 1.1 fusion.70
  65.9 1.3 fusion.71
  69.7 5.0 %fusion.74 = f32[16,1024]{1,0:T(8,128)S(1)} fusion(f32[2048,512]{1,0:T(8,128)S(1)} %fusion.72, f32[2048,512]{1,0:T(8,128)S(1)} %fusion.73, f32[16,16384]{1,0:T(8,128)} %get-tuple-element.353, s32[]{:T(128)S(6)} %select_n.75, f32[16,1024]{1,0:T(8,128)S(1)} %get-tuple-element.338, pred[]{:T(512)S(6)} %compare.3), kind=kOutput, calls=%fused_computation.32.clone.1 | convolution fusion | flops 404783104 | bytes 8650757 | tf_op jit(solution)/shard_map/while/body/eval_jaxpr/dot_general | solution.py:66
  75.9 1.1 fusion.70
  77.0 1.3 fusion.71
  80.8 5.0 %fusion.74 = f32[16,1024]{1,0:T(8,128)S(1)} fusion(f32[2048,512]{1,0:T(8,128)S(1)} %fusion.72, f32[2048,512]{1,0:T(8,128)S(1)} %fusion.73, f32[16,16384]{1,0:T(8,128)} %get-tuple-element.353, s32[]{:T(128)S(6)} %select_n.75, f32[16,1024]{1,0:T(8,128)S(1)} %get-tuple-element.338, pred[]{:T(512)S(6)} %compare.3), kind=kOutput, calls=%fused_computation.32.clone.1 | convolution fusion | flops 404783104 | bytes 8650757 | tf_op jit(solution)/shard_map/while/body/eval_jaxpr/dot_general | solution.py:66
  88.1 1.3 fusion.71
  91.9 5.0 %fusion.74 = f32[16,1024]{1,0:T(8,128)S(1)} fusion(f32[2048,512]{1,0:T(8,128)S(1)} %fusion.72, f32[2048,512]{1,0:T(8,128)S(1)} %fusion.73, f32[16,16384]{1,0:T(8,128)} %get-tuple-element.353, s32[]{:T(128)S(6)} %select_n.75, f32[16,1024]{1,0:T(8,128)S(1)} %get-tuple-element.338, pred[]{:T(512)S(6)} %compare.3), kind=kOutput, calls=%fused_computation.32.clone.1 | convolution fusion | flops 404783104 | bytes 8650757 | tf_op jit(solution)/shard_map/while/body/eval_jaxpr/dot_general | solution.py:66
  97.2 4.8 %collective-permute-start = (f32[4,2,1,512]{3,1,2,0:T(2,128)S(1)}, f32[4,2,1,512]{3,1,2,0:T(2,128)S(1)}, u32[]{:S(2)}, u32[]{:S(2)}) collective-permute-start(f32[4,2,1,512]{3,1,2,0:T(2,128)S(1)} %get-tuple-element.174), channel_id=1, source_target_pairs={{0,1},{2,3},{4,5},{6,7},{8,9},{10,11},{12,13},{14,15},{16,17},{18,... | collective-permute-start | bytes 49160 | tf_op jit(solution)/shard_map/ppermute | solution.py:23
  102.0 1.5 collective-permute-start.1
  109.9 2.7 dynamic_update_slice.21
  112.9 2.7 dynamic_update_slice.23
  115.8 2.7 dynamic_update_slice.22
  118.5 1.3 pad_maximum_fusion.5
  120.0 2.7 dynamic_update_slice.20
  122.7 1.3 pad_maximum_fusion.4
  124.1 23.5 %all_gather.3 = f32[2,16,4096]{2,0,1:T(2,128)S(1)} all-gather(f32[2,16,256]{2,0,1:T(2,128)S(1)} %copy.19), channel_id=1, replica_groups=mesh['xy'=16,'gz'=2] {'xy'}, dimensions={2}, use_global_device_ids=true | all-gather | bytes 557056 | tf_op jit(solution)/shard_map/all_gather | solution.py:140
  147.6 73.0 %all-reduce.3.cloned.1.call-done = (f32[2,16,4096]{2,0,1:T(2,128)}, f32[2,16,4096]{2,0,1:T(2,128)}) async-done(((f32[2,16,4096]{2,0,1:T(2,128)}, f32[2,16,4096]{2,0,1:T(2,128)}), (f32[2,16,4096]{2,0,1:T(2,128)}, f32[2,16,4096]{2,0,1:T(2,128)})) %all-reduce.3.cloned.1.call-update) | async-done | bytes 1048592 | tf_op jit(solution)/shard_map/psum | solution.py:153
  220.6 1.7 maximum_divide_fusion
  223.2 3.4 %collective-permute-start.2 = (f32[2,1,512]{2,0,1:T(2,128)S(1)}, f32[2,1,512]{2,0,1:T(2,128)S(1)}, u32[]{:S(2)}, u32[]{:S(2)}) collective-permute-start(f32[2,1,512]{2,0,1:T(2,128)S(1)} %get-tuple-element.178), channel_id=1, source_target_pairs={{0,1},{2,3},{4,5},{6,7},{8,9},{10,11},{12,13},{14,15},{16,17},{18,... | collective-permute-start | bytes 12296 | tf_op jit(solution)/shard_map/ppermute | solution.py:23
  226.5 1.5 collective-permute-start.3
  228.7 3.3 %collective-permute-done.3 = f32[2,1,512]{2,0,1:T(2,128)S(1)} collective-permute-done((f32[2,1,512]{2,0,1:T(2,128)S(1)}, f32[2,1,512]{2,0,1:T(2,128)S(1)}, u32[]{:S(2)}, u32[]{:S(2)}) %collective-permute-start.3) | collective-permute-done | bytes 4128 | tf_op jit(solution)/shard_map/ppermute | solution.py:25
  232.2 84.7 %while.23 = (s32[]{:T(128)}, f32[8,16,2048]{2,1,0:T(8,128)S(1)}, s32[2,16384]{1,0:T(2,128)S(1)}, s32[8]{0:T(128)S(1)}, s32[2,16384]{1,0:T(2,128)S(1)}, /*index=5...) while((s32[]{:T(128)}, f32[8,16,2048]{2,1,0:T(8,128)S(1)}, ...), condition=%wide.region_6.7_spmd, body=%wide.region_5.6_spmd.sunk | while | flops 413143040 | bytes 17957064 | solution.py:94
  235.7 7.1 %fusion.68 = f32[8,16,2048]{2,1,0:T(8,128)S(1)} fusion(f32[8,16,2048]{2,1,0:T(8,128)S(1)} %get-tuple-element.373, s32[]{:T(128)S(6)} %copy.46, f32[16,1024]{1,0:T(8,128)S(1)} %get-tuple-element.389, f32[2048,512]{1,0:T(8,128)S(1)} %fusion.66, f32[2048,512]{1,0:T(8,128)S(1)} %fusion.67), kind=kOutput, calls=%fused_computation.13.clone.1 | convolution fusion | flops 404750336 | bytes 8585220 | tf_op jit(solution)/shard_map/while/body/eval_jaxpr/sj,cj->sc/dot_general | solution.py:92
  246.3 7.1 %fusion.68 = f32[8,16,2048]{2,1,0:T(8,128)S(1)} fusion(f32[8,16,2048]{2,1,0:T(8,128)S(1)} %get-tuple-element.373, s32[]{:T(128)S(6)} %copy.46, f32[16,1024]{1,0:T(8,128)S(1)} %get-tuple-element.389, f32[2048,512]{1,0:T(8,128)S(1)} %fusion.66, f32[2048,512]{1,0:T(8,128)S(1)} %fusion.67), kind=kOutput, calls=%fused_computation.13.clone.1 | convolution fusion | flops 404750336 | bytes 8585220 | tf_op jit(solution)/shard_map/while/body/eval_jaxpr/sj,cj->sc/dot_general | solution.py:92
  256.9 7.1 %fusion.68 = f32[8,16,2048]{2,1,0:T(8,128)S(1)} fusion(f32[8,16,2048]{2,1,0:T(8,128)S(1)} %get-tuple-element.373, s32[]{:T(128)S(6)} %copy.46, f32[16,1024]{1,0:T(8,128)S(1)} %get-tuple-element.389, f32[2048,512]{1,0:T(8,128)S(1)} %fusion.66, f32[2048,512]{1,0:T(8,128)S(1)} %fusion.67), kind=kOutput, calls=%fused_computation.13.clone.1 | convolution fusion | flops 404750336 | bytes 8585220 | tf_op jit(solution)/shard_map/while/body/eval_jaxpr/sj,cj->sc/dot_general | solution.py:92
  267.5 7.1 %fusion.68 = f32[8,16,2048]{2,1,0:T(8,128)S(1)} fusion(f32[8,16,2048]{2,1,0:T(8,128)S(1)} %get-tuple-element.373, s32[]{:T(128)S(6)} %copy.46, f32[16,1024]{1,0:T(8,128)S(1)} %get-tuple-element.389, f32[2048,512]{1,0:T(8,128)S(1)} %fusion.66, f32[2048,512]{1,0:T(8,128)S(1)} %fusion.67), kind=kOutput, calls=%fused_computation.13.clone.1 | convolution fusion | flops 404750336 | bytes 8585220 | tf_op jit(solution)/shard_map/while/body/eval_jaxpr/sj,cj->sc/dot_general | solution.py:92
  278.1 7.1 %fusion.68 = f32[8,16,2048]{2,1,0:T(8,128)S(1)} fusion(f32[8,16,2048]{2,1,0:T(8,128)S(1)} %get-tuple-element.373, s32[]{:T(128)S(6)} %copy.46, f32[16,1024]{1,0:T(8,128)S(1)} %get-tuple-element.389, f32[2048,512]{1,0:T(8,128)S(1)} %fusion.66, f32[2048,512]{1,0:T(8,128)S(1)} %fusion.67), kind=kOutput, calls=%fused_computation.13.clone.1 | convolution fusion | flops 404750336 | bytes 8585220 | tf_op jit(solution)/shard_map/while/body/eval_jaxpr/sj,cj->sc/dot_general | solution.py:92
  288.7 7.1 %fusion.68 = f32[8,16,2048]{2,1,0:T(8,128)S(1)} fusion(f32[8,16,2048]{2,1,0:T(8,128)S(1)} %get-tuple-element.373, s32[]{:T(128)S(6)} %copy.46, f32[16,1024]{1,0:T(8,128)S(1)} %get-tuple-element.389, f32[2048,512]{1,0:T(8,128)S(1)} %fusion.66, f32[2048,512]{1,0:T(8,128)S(1)} %fusion.67), kind=kOutput, calls=%fused_computation.13.clone.1 | convolution fusion | flops 404750336 | bytes 8585220 | tf_op jit(solution)/shard_map/while/body/eval_jaxpr/sj,cj->sc/dot_general | solution.py:92
  299.3 7.1 %fusion.68 = f32[8,16,2048]{2,1,0:T(8,128)S(1)} fusion(f32[8,16,2048]{2,1,0:T(8,128)S(1)} %get-tuple-element.373, s32[]{:T(128)S(6)} %copy.46, f32[16,1024]{1,0:T(8,128)S(1)} %get-tuple-element.389, f32[2048,512]{1,0:T(8,128)S(1)} %fusion.66, f32[2048,512]{1,0:T(8,128)S(1)} %fusion.67), kind=kOutput, calls=%fused_computation.13.clone.1 | convolution fusion | flops 404750336 | bytes 8585220 | tf_op jit(solution)/shard_map/while/body/eval_jaxpr/sj,cj->sc/dot_general | solution.py:92
  309.8 7.1 %fusion.68 = f32[8,16,2048]{2,1,0:T(8,128)S(1)} fusion(f32[8,16,2048]{2,1,0:T(8,128)S(1)} %get-tuple-element.373, s32[]{:T(128)S(6)} %copy.46, f32[16,1024]{1,0:T(8,128)S(1)} %get-tuple-element.389, f32[2048,512]{1,0:T(8,128)S(1)} %fusion.66, f32[2048,512]{1,0:T(8,128)S(1)} %fusion.67), kind=kOutput, calls=%fused_computation.13.clone.1 | convolution fusion | flops 404750336 | bytes 8585220 | tf_op jit(solution)/shard_map/while/body/eval_jaxpr/sj,cj->sc/dot_general | solution.py:92
  318.2 1.3 divide_add_fusion
  (251 shorter events, 53.5 us)
Async XLA Ops:
  7.2 213.4 %all-reduce.3.cloned.1.call-start = ((), (), s32[]{:S(2)}) async-start(), calls=%async_computation | async-start | bytes 2097152 | tf_op jit(solution)/shard_map/psum | solution.py:153
  8.1 96.4 %copy-start.6 = (s32[2,1]{0,1:T(1,128)S(1)}, s32[2,1]{0,1:T(1,128)}, u32[]{:S(2)}) copy-start(s32[2,1]{0,1:T(1,128)} %param.13) | copy-start | bytes 28
  96.8 27.2 %copy-start.5 = (f32[3,2,16]{2,1,0:T(2,128)S(1)}, f32[3,2,16]{2,1,0:T(2,128)}, u32[]{:S(2)}) copy-start(f32[3,2,16]{2,1,0:T(2,128)} %param.17) | copy-start | bytes 1156
  96.8 27.2 %copy-start.4 = (f32[2,16,256]{2,1,0:T(8,128)S(1)}, f32[2,16,256]{2,1,0:T(8,128)}, u32[]{:S(2)}) copy-start(f32[2,16,256]{2,1,0:T(8,128)} %param.12) | copy-start | bytes 98308
  97.2 12.1 %collective-permute-start = (f32[4,2,1,512]{3,1,2,0:T(2,128)S(1)}, f32[4,2,1,512]{3,1,2,0:T(2,128)S(1)}, u32[]{:S(2)}, u32[]{:S(2)}) collective-permute-start(f32[4,2,1,512]{3,1,2,0:T(2,128)S(1)} %get-tuple-element.174), channel_id=1, source_target_pairs={{0,1},{2,3},{4,5},{6,7},{8,9},{10,11},{12,13},{14,15},{16,17},{18,... | collective-permute-start | bytes 49160 | tf_op jit(solution)/shard_map/ppermute | solution.py:23
  102.0 7.2 %collective-permute-start.1 = (f32[4,2,1,512]{3,1,2,0:T(2,128)S(1)}, f32[4,2,1,512]{3,1,2,0:T(2,128)S(1)}, u32[]{:S(2)}, u32[]{:S(2)}) collective-permute-start(f32[4,2,1,512]{3,1,2,0:T(2,128)S(1)} %get-tuple-element.175), channel_id=1, source_target_pairs={{1,0},{3,2},{5,4},{7,6},{9,8},{11,10},{13,12},{15,14},{17,16},{19,... | collective-permute-start | bytes 49160 | tf_op jit(solution)/shard_map/ppermute | solution.py:25
  112.8 119.4 %copy-start = (f32[2,16384]{1,0:T(2,128)S(1)}, f32[2,16384]{1,0:T(2,128)}, u32[]{:S(2)}) copy-start(f32[2,16384]{1,0:T(2,128)} %get-tuple-element.398) | copy-start | bytes 393220
  112.8 119.4 %copy-start.1 = (s32[2,16384]{1,0:T(2,128)S(1)}, s32[2,16384]{1,0:T(2,128)}, u32[]{:S(2)}) copy-start(s32[2,16384]{1,0:T(2,128)} %get-tuple-element.399) | copy-start | bytes 393220
  112.9 119.4 %copy-start.2 = (s32[2,16384]{1,0:T(2,128)S(1)}, s32[2,16384]{1,0:T(2,128)}, u32[]{:S(2)}) copy-start(s32[2,16384]{1,0:T(2,128)} %get-tuple-element.400) | copy-start | bytes 393220
  223.2 5.5 %collective-permute-start.2 = (f32[2,1,512]{2,0,1:T(2,128)S(1)}, f32[2,1,512]{2,0,1:T(2,128)S(1)}, u32[]{:S(2)}, u32[]{:S(2)}) collective-permute-start(f32[2,1,512]{2,0,1:T(2,128)S(1)} %get-tuple-element.178), channel_id=1, source_target_pairs={{0,1},{2,3},{4,5},{6,7},{8,9},{10,11},{12,13},{14,15},{16,17},{18,... | collective-permute-start | bytes 12296 | tf_op jit(solution)/shard_map/ppermute | solution.py:23
  226.5 5.5 %collective-permute-start.3 = (f32[2,1,512]{2,0,1:T(2,128)S(1)}, f32[2,1,512]{2,0,1:T(2,128)S(1)}, u32[]{:S(2)}, u32[]{:S(2)}) collective-permute-start(f32[2,1,512]{2,0,1:T(2,128)S(1)} %get-tuple-element.179), channel_id=1, source_target_pairs={{1,0},{3,2},{5,4},{7,6},{9,8},{11,10},{13,12},{15,14},{17,16},{19,... | collective-permute-start | bytes 12296 | tf_op jit(solution)/shard_map/ppermute | solution.py:25
  317.0 1.2 copy-start.3
Sparse Core Ops, SparseCore 0:
  124.2 96.4 all-reduce.2
where the time goes:
time: 327 us; the launch traced here: 326 us
  matrix products  96.7 us (30%)
  waiting for transfers between devices  76.4 us (23%)
  local copies, waits for them, and re-layouts  48.5 us (15%)
  other arithmetic  39.8 us (12%)
  blocking collectives  23.5 us (7%)
  between operations  18.3 us (6%)
  loops' own time  12 us (4%)
  starting transfers between devices  11.2 us (3%)
    psum x1, waiting for transfers between devices, local(): lax.psum((place_band(projection_band, band_start), place_band(coverage_ba...  73 us
    dot_general x8, matrix products, block_values(): jnp.einsum('sj,cj->sc', joined_rows, weights, precision=lax.Precision.HIG...  57 us
    dot_general x8, matrix products, block_step(): jnp.dot(slab_cells, weights, precision=lax.Precision.HIGHEST)  39.7 us
    select_n x32, other arithmetic, footprint(): return jnp.where(inside, amp_block[:, None], jnp.zeros((), jnp.float32))  28 us
    all_gather x1, blocking collectives, local(): measured_full = lax.all_gather(measured, 'xy', axis=2, tiled=True)  23.5 us
    slice x16, local copies, waits for them, and re-layouts, joint_weights(): column_width[view_index]  12.4 us
    dynamic_update_slice x4, local copies, waits for them, and re-layouts, place_band(): lax.dynamic_update_slice(blank_rows, band_rows[view_index], (jnp.int32(0)...  10.9 us
    slice x16, local copies, waits for them, and re-layouts, joint_weights(): amplitude[view_index]  9.59 us
  transfers between devices with their start and end apart: 5, of which 2 were waited for; matrix products, arithmetic and copies ran while one was open for 1% of the time, Pallas kernels for 0%

commit v1 on v0

v1 whole, which is shorter than its diff:
```python
import jax
import jax.numpy as jnp
from jax import lax
from jax.experimental import pallas as pl
from jax.experimental.pallas import tpu as pltpu
from jax.sharding import PartitionSpec as P

B = 512
RELAX = 0.9
CHUNK = 512
INTERPRET = False


def _band_mask(off, wid, rows, width):
    u = lax.broadcasted_iota(jnp.int32, (rows, width), 0)
    inside = (u >= off) & (u < off + wid)
    return jnp.where(inside, 1.0, 0.0).astype(jnp.bfloat16)


def _split(x):
    hi = x.astype(jnp.bfloat16)
    lo = (x - hi.astype(jnp.float32)).astype(jnp.bfloat16)
    return hi, lo


def _forward_kernel(vol_ref, amp_ref, off_ref, wid_ref, out_ref):
    slab_rows, columns = vol_ref.shape
    view_count = amp_ref.shape[0]
    band = out_ref.shape[2]
    out_ref[...] = jnp.zeros(out_ref.shape, jnp.float32)
    row = lax.broadcasted_iota(jnp.int32, (slab_rows, CHUNK), 0)

    def body(j, carry):
        c0 = pl.multiple_of(j * CHUNK, CHUNK)
        cells = vol_ref[:, pl.ds(c0, CHUNK)]
        for v in range(view_count):
            amp = amp_ref[pl.ds(v, 1), pl.ds(c0, CHUNK)]
            off = off_ref[pl.ds(v, 1), pl.ds(c0, CHUNK)]
            wid = wid_ref[pl.ds(v, 1), pl.ds(c0, CHUNK)]
            x = jnp.concatenate([cells * amp, jnp.where(row == 0, amp, 0.0)], axis=0)
            hi, lo = _split(x)
            lhs = jnp.concatenate([hi, lo], axis=0)
            mask = _band_mask(off, wid, band, CHUNK)
            out_ref[v] += lax.dot_general(
                lhs, mask, (((1,), (1,)), ((), ())), preferred_element_type=jnp.float32
            )
        return carry

    lax.fori_loop(0, columns // CHUNK, body, 0)


def forward_band(volume, amplitude, column_offset, column_width):
    slab_rows = volume.shape[0]
    view_count = amplitude.shape[0]
    acc = pl.pallas_call(
        _forward_kernel,
        out_shape=jax.ShapeDtypeStruct((view_count, 4 * slab_rows, B), jnp.float32),
        interpret=INTERPRET,
    )(volume, amplitude, column_offset, column_width)
    summed = acc[:, : 2 * slab_rows] + acc[:, 2 * slab_rows :]
    return summed[:, : slab_rows + 1]


def _backward_kernel(back_ref, vol_ref, amp_ref, off_ref, wid_ref, rw_ref, out_ref, split_ref):
    slab_rows, columns = vol_ref.shape
    view_count, _, band = back_ref.shape
    for v in range(view_count):
        hi, lo = _split(back_ref[v])
        split_ref[v] = jnp.concatenate([hi, lo], axis=0)

    def body(j, carry):
        c0 = pl.multiple_of(j * CHUNK, CHUNK)
        correction = None
        normalizer = None
        for v in range(view_count):
            amp = amp_ref[pl.ds(v, 1), pl.ds(c0, CHUNK)]
            off = off_ref[pl.ds(v, 1), pl.ds(c0, CHUNK)]
            wid = wid_ref[pl.ds(v, 1), pl.ds(c0, CHUNK)]
            mask = _band_mask(off, wid, band, CHUNK)
            r = jnp.dot(split_ref[v], mask, preferred_element_type=jnp.float32)
            part = amp * (r[:slab_rows] + r[slab_rows:])
            mass = rw_ref[v] * (amp * wid.astype(jnp.float32))
            correction = part if correction is None else correction + part
            normalizer = mass if normalizer is None else normalizer + mass
        cells = vol_ref[:, pl.ds(c0, CHUNK)]
        out_ref[:, pl.ds(c0, CHUNK)] = cells + RELAX * correction / normalizer
        return carry

    lax.fori_loop(0, columns // CHUNK, body, 0)


def backward_update(back_band, volume, amplitude, column_offset, column_width, row_weight):
    view_count, slab_rows, band = back_band.shape
    return pl.pallas_call(
        _backward_kernel,
        out_shape=jax.ShapeDtypeStruct(volume.shape, jnp.float32),
        scratch_shapes=[pltpu.VMEM((view_count, 2 * slab_rows, band), jnp.bfloat16)],
        interpret=INTERPRET,
    )(back_band, volume, amplitude, column_offset, column_width, row_weight[:, :, None])


def local(volume, measured, band_start, column_offset, column_width, amplitude, axial_weight):
    slab_rows = volume.shape[0]
    view_count = amplitude.shape[0]
    xy_count = lax.axis_size("xy")
    gz_count = lax.axis_size("gz")
    shard_width = measured.shape[2]
    detector_width = shard_width * xy_count
    total_rows = slab_rows * gz_count
    first_row = lax.axis_index("gz") * slab_rows
    up_pairs = [(i, i + 1) for i in range(gz_count - 1)]
    down_pairs = [(i + 1, i) for i in range(gz_count - 1)]

    weights_all = lax.all_gather(axial_weight, "gz", axis=2, tiled=True)
    padded_weights = jnp.pad(weights_all, ((0, 0), (0, 0), (2, 2)))
    measured_ext = jnp.concatenate(
        [
            lax.ppermute(measured[:, slab_rows - 1 :], "gz", up_pairs),
            measured,
            lax.ppermute(measured[:, :1], "gz", down_pairs),
        ],
        axis=1,
    )

    band_rows = forward_band(volume, amplitude, column_offset, column_width)
    placed = []
    for v in range(view_count):
        blank = jnp.zeros((slab_rows + 1, detector_width), jnp.float32)
        placed.append(lax.dynamic_update_slice(blank, band_rows[v], (jnp.int32(0), band_start[v, 0])))
    reduced = lax.psum_scatter(jnp.stack(placed), "xy", scatter_dimension=2, tiled=True)
    proj_cols = reduced[:, :slab_rows]
    cover = reduced[:, slab_rows : slab_rows + 1]
    proj_ext = jnp.concatenate(
        [
            lax.ppermute(proj_cols[:, slab_rows - 2 :], "gz", up_pairs),
            proj_cols,
            lax.ppermute(proj_cols[:, :2], "gz", down_pairs),
        ],
        axis=1,
    )

    ext_rows = slab_rows + 2

    def weight_rows(kind, shift):
        return lax.dynamic_slice_in_dim(padded_weights[kind], first_row + 1 + shift, ext_rows, 1)[:, :, None]

    mid_w = weight_rows(1, 0)
    next_w = weight_rows(0, 1)
    prev_w = weight_rows(2, -1)
    centre = proj_ext[:, 1 : ext_rows + 1]
    after = proj_ext[:, 2 : ext_rows + 2]
    before = proj_ext[:, 0:ext_rows]
    projection = mid_w * centre + next_w * after + prev_w * before
    coverage = mid_w * cover + next_w * cover + prev_w * cover
    residual_ext = (measured_ext - projection) / jnp.maximum(coverage, 1.0)
    global_rows = first_row - 1 + jnp.arange(ext_rows, dtype=jnp.int32)
    valid = (global_rows >= 0) & (global_rows < total_rows)
    residual_ext = jnp.where(valid[None, :, None], residual_ext, 0.0)
    residual = residual_ext[:, 1 : slab_rows + 1]

    back_rows = (
        axial_weight[0][:, :, None] * residual_ext[:, 0:slab_rows]
        + axial_weight[1][:, :, None] * residual
        + axial_weight[2][:, :, None] * residual_ext[:, 2 : slab_rows + 2]
    )
    back_full = lax.all_gather(back_rows, "xy", axis=2, tiled=True)
    back_band = jnp.stack(
        [
            lax.dynamic_slice(back_full[v], (jnp.int32(0), band_start[v, 0]), (slab_rows, B))
            for v in range(view_count)
        ]
    )

    own_rows = first_row + jnp.arange(slab_rows, dtype=jnp.int32)
    row_weight = (
        jnp.where(own_rows[None, :] > 0, axial_weight[0], 0.0)
        + axial_weight[1]
        + jnp.where(own_rows[None, :] < total_rows - 1, axial_weight[2], 0.0)
    )
    volume_next = backward_update(back_band, volume, amplitude, column_offset, column_width, row_weight)
    return (volume_next, residual)


def solution(mesh):
    return jax.shard_map(
        local,
        mesh=mesh,
        in_specs=(
            P("gz", "xy"),
            P(None, "gz", "xy"),
            P(None, "xy"),
            P(None, "xy"),
            P(None, "xy"),
            P(None, "xy"),
            P(None, None, "gz"),
        ),
        out_specs=(P("gz", "xy"), P(None, "gz", "xy")),
        check_vma=False,
    )
```

time: 327 us -> 149 us (0.46)
  matrix products: 96.7 us -> 0 us
  local copies, waits for them, and re-layouts: 48.5 us -> 6.39 us
  other arithmetic: 39.8 us -> 3.98 us
  Pallas kernels: 0 us -> 35.4 us
  waiting for transfers between devices: 76.4 us -> 47 us
  loops' own time: 12 us -> 0 us
    dot_general x16 -> x0, matrix products: 96.7 us -> none  [the longest x8 57 us: block_values(): jnp.einsum('sj,cj->sc', joined_rows, weights, precision=lax.Precision.HIG...]
    psum x1 -> x0, waiting for transfers between devices: 73 us -> none  [local(): lax.psum((place_band(projection_band, band_start), place_band(coverage_ba...]
    reduce_scatter x0 -> x1, waiting for transfers between devices: none -> 46.5 us  [local(): lax.psum_scatter(jnp.stack(placed), 'xy', scatter_dimension=2, tiled=True)]
    pallas_call x0 -> x2, Pallas kernels: none -> 35.4 us  [the longest x1 19.4 us: forward_band(): pl.pallas_call(_forward_kernel, out_shape=jax.ShapeDtypeStruct((view_coun...]
    select_n x32 -> x1, other arithmetic: 28 us -> 0.1 us  [local(): residual_ext = jnp.where(valid[None, :, None], residual_ext, 0.0)]
    slice x36 -> x9, local copies, waits for them, and re-layouts: 23.3 us -> 3.21 us  [the longest x1 1.39 us: local(): band_start[v, 0]]
    another operation x2 -> x0, loops' own time: 12 us -> none  [the longest x1 6.01 us: forward_band(): lax.scan(block_step, starting, jnp.arange(volume.shape[1] // block_size,...]
    dynamic_slice x99 -> x7, local copies, waits for them, and re-layouts: 10.6 us -> 0.47 us  [the longest x5 0.31 us: weight_rows(): lax.dynamic_slice_in_dim(padded_weights[kind], first_row + 1 + shift, ext...]
  transfers between devices with their start and end apart: 5 -> 5, of which waited for: 2 -> 2; matrix products, arithmetic and copies ran while one was open for 1% -> 2% of each run, Pallas kernels for 0% -> 0%
where the time goes in v1:
time: 149 us; the launch traced here: 148 us
  waiting for transfers between devices  47 us (32%)
  Pallas kernels  35.4 us (24%)
  blocking collectives  25.3 us (17%)
  between operations  18.2 us (12%)
  starting transfers between devices  12.1 us (8%)
  local copies, waits for them, and re-layouts  6.39 us (4%)
  other arithmetic  3.98 us (3%)
    reduce_scatter x1, waiting for transfers between devices, local(): lax.psum_scatter(jnp.stack(placed), 'xy', scatter_dimension=2, tiled=True)  46.5 us
    all_gather x1, blocking collectives, local(): back_full = lax.all_gather(back_rows, 'xy', axis=2, tiled=True)  20.9 us
    pallas_call x1, Pallas kernels, forward_band(): pl.pallas_call(_forward_kernel, out_shape=jax.ShapeDtypeStruct((view_coun...  19.4 us
    pallas_call x1, Pallas kernels, backward_update(): pl.pallas_call(_backward_kernel, out_shape=jax.ShapeDtypeStruct(volume.sh...  16 us
    ppermute x1, starting transfers between devices, local(): lax.ppermute(measured[:, slab_rows - 1:], 'gz', up_pairs)  4.84 us
    ppermute x1, starting transfers between devices, local(): lax.ppermute(proj_cols[:, slab_rows - 2:], 'gz', up_pairs)  4.54 us
    all_gather x1, blocking collectives, local(): weights_all = lax.all_gather(axial_weight, 'gz', axis=2, tiled=True)  4.4 us
  transfers between devices with their start and end apart: 5, of which 2 were waited for; matrix products, arithmetic and copies ran while one was open for 2% of the time, Pallas kernels for 0%

profile of v1, /device:TPU:0, one launch (start us, length us, event | category | flops | bytes accessed | tf_op | source)
XLA Modules:
  0.0 148.4 jit_solution(13118580444699887828)
XLA Ops:
  7.2 0.0 reduce-scatter.2.cloned.1.call-start
  7.2 1.4 fusion.14
  11.3 19.4 %shard_map.86 = f32[2,64,512]{2,1,0:T(8,128)} custom-call(f32[16,16384]{1,0:T(8,128)} %vol_ref.3, f32[2,16384]{1,0:T(2,128)} %amp_ref.3, s32[2,16384]{1,0:T(2,128)} %off_ref.3, s32[2,16384]{1,0:T(2,128)} %wid_ref.3), custom_call_target="tpu_custom_call" | custom-call | tf_op jit(solution)/shard_map/pallas_call | solution.py:55
  30.7 1.0 slice_add_fusion
  33.1 0.8 dynamic_update_slice.9
  33.9 0.8 dynamic_update_slice.8
  34.7 0.9 pad_maximum_fusion
  35.6 0.0 copy-start
  35.6 0.0 reduce-scatter.2.cloned.1.call-update
  35.6 0.7 copy-done
  36.4 0.0 copy-start.1
  36.4 1.4 collective-permute-start.1
  37.8 4.8 %collective-permute-start = (f32[2,1,256]{2,1,0:T(1,128)S(1)}, f32[2,1,256]{2,1,0:T(1,128)S(1)}, u32[]{:S(2)}, u32[]{:S(2)}) collective-permute-start(f32[2,1,256]{2,1,0:T(1,128)S(1)} %get-tuple-element.13), channel_id=1, source_target_pairs={{0,1},{2,3},{4,5},{6,7},{8,9},{10,11},{12,13},{14,15},{16,17},{18,... | collective-permute-start | bytes 6152 | tf_op jit(solution)/shard_map/ppermute | solution.py:118
  42.6 0.0 copy-done.1
  42.6 0.1 copy.12
  42.7 4.4 %all_gather.6 = f32[3,2,32]{0,1,2:T(2,128)S(1)} all-gather(f32[3,2,16]{0,1,2:T(2,128)S(1)} %copy.12), channel_id=1, replica_groups=mesh['xy'=16,'gz'=2] {'gz'}, dimensions={2}, use_global_device_ids=true | all-gather | bytes 1152 | tf_op jit(solution)/shard_map/all_gather | solution.py:114
  47.1 0.1 pad_slice_fusion.2
  47.3 0.1 copy.15
  47.4 0.1 copy.14
  47.5 0.1 copy.13
  47.6 0.1 copy.18
  47.7 0.1 copy.17
  47.8 0.1 copy.16
  47.9 0.7 select_add_fusion.rw_ref
  48.6 46.5 %reduce-scatter.2.cloned.1.call-done = f32[2,17,256]{2,1,0:T(8,128)} async-done(((f32[2,17,4096]{2,1,0:T(8,128)}), f32[2,17,256]{2,1,0:T(8,128)}) %reduce-scatter.2.cloned.1.call-update) | async-done | bytes 34832 | tf_op jit(solution)/shard_map/reduce_scatter | solution.py:130
  95.0 0.7 fusion.12
  95.8 1.3 collective-permute-start.3
  97.0 4.5 %collective-permute-start.2 = (f32[2,2,256]{2,1,0:T(2,128)S(1)}, f32[2,2,256]{2,1,0:T(2,128)S(1)}, u32[]{:S(2)}, u32[]{:S(2)}) collective-permute-start(f32[2,2,256]{2,1,0:T(2,128)S(1)} %get-tuple-element.8), channel_id=1, source_target_pairs={{0,1},{2,3},{4,5},{6,7},{8,9},{10,11},{12,13},{14,15},{16,17},{18,... | collective-permute-start | bytes 12296 | tf_op jit(solution)/shard_map/ppermute | solution.py:135
  101.6 0.7 slice.117
  102.3 0.0 slice-start
  102.3 0.0 collective-permute-done.1
  102.3 0.0 collective-permute-done
  102.4 0.0 collective-permute-done.3
  102.4 0.5 collective-permute-done.2
  102.9 0.2 slice-done
  103.1 0.1 fusion.5
  103.2 0.6 fusion.6
  103.8 20.9 %all_gather.7 = f32[2,16,4096]{2,1,0:T(8,128)S(1)} all-gather(f32[2,16,256]{2,1,0:T(8,128)S(1)} %get-tuple-element.2), channel_id=1, replica_groups=mesh['xy'=16,'gz'=2] {'xy'}, dimensions={2}, use_global_device_ids=true | all-gather | bytes 557056 | tf_op jit(solution)/shard_map/all_gather | solution.py:166
  124.7 0.1 constant_dynamic-slice_fusion
  124.8 0.1 constant_dynamic-slice_fusion.1
  124.9 0.6 pad_maximum_fusion.1.back_ref
  125.5 16.0 %shard_map.87 = f32[16,16384]{1,0:T(8,128)} custom-call(f32[2,16,512]{2,1,0:T(8,128)} %pad_maximum_fusion.1.back_ref, f32[16,16384]{1,0:T(8,128)} %vol_ref.3, f32[2,16384]{1,0:T(2,128)} %amp_ref.3, s32[2,16384]{1,0:T(2,128)} %off_ref.3, s32[2,16384]{1,0:T(2,128)} %wid_ref.3, f32[2,16,1]{2,1,0:T(8,128)} %select_add_fusion.rw_ref), custom_call_target="tpu_custom_call" | custom-call | tf_op jit(solution)/shard_map/pallas_call | solution.py:94
  (12 shorter events, 0.2 us)
Async XLA Ops:
  7.2 87.9 %reduce-scatter.2.cloned.1.call-start = ((), (), s32[]{:S(2)}) async-start(), calls=%async_computation.1 | async-start | bytes 835584 | tf_op jit(solution)/shard_map/reduce_scatter | solution.py:130
  35.6 0.8 copy-start
  36.4 6.3 %copy-start.1 = (f32[3,2,16]{2,1,0:T(2,128)S(1)}, f32[3,2,16]{2,1,0:T(2,128)}, u32[]{:S(2)}) copy-start(f32[3,2,16]{2,1,0:T(2,128)} %param.13) | copy-start | bytes 1156
  36.4 66.0 %collective-permute-start.1 = (f32[2,1,256]{2,1,0:T(1,128)S(1)}, f32[2,1,256]{2,1,0:T(1,128)S(1)}, u32[]{:S(2)}, u32[]{:S(2)}) collective-permute-start(f32[2,1,256]{2,1,0:T(1,128)S(1)} %get-tuple-element.14), channel_id=1, source_target_pairs={{1,0},{3,2},{5,4},{7,6},{9,8},{11,10},{13,12},{15,14},{17,16},{19,... | collective-permute-start | bytes 6152 | tf_op jit(solution)/shard_map/ppermute | solution.py:120
  37.8 64.6 %collective-permute-start = (f32[2,1,256]{2,1,0:T(1,128)S(1)}, f32[2,1,256]{2,1,0:T(1,128)S(1)}, u32[]{:S(2)}, u32[]{:S(2)}) collective-permute-start(f32[2,1,256]{2,1,0:T(1,128)S(1)} %get-tuple-element.13), channel_id=1, source_target_pairs={{0,1},{2,3},{4,5},{6,7},{8,9},{10,11},{12,13},{14,15},{16,17},{18,... | collective-permute-start | bytes 6152 | tf_op jit(solution)/shard_map/ppermute | solution.py:118
  95.8 6.6 %collective-permute-start.3 = (f32[2,2,256]{2,1,0:T(2,128)S(1)}, f32[2,2,256]{2,1,0:T(2,128)S(1)}, u32[]{:S(2)}, u32[]{:S(2)}) collective-permute-start(f32[2,2,256]{2,1,0:T(2,128)S(1)} %get-tuple-element.9), channel_id=1, source_target_pairs={{1,0},{3,2},{5,4},{7,6},{9,8},{11,10},{13,12},{15,14},{17,16},{19,... | collective-permute-start | bytes 12296 | tf_op jit(solution)/shard_map/ppermute | solution.py:137
  97.0 5.9 %collective-permute-start.2 = (f32[2,2,256]{2,1,0:T(2,128)S(1)}, f32[2,2,256]{2,1,0:T(2,128)S(1)}, u32[]{:S(2)}, u32[]{:S(2)}) collective-permute-start(f32[2,2,256]{2,1,0:T(2,128)S(1)} %get-tuple-element.8), channel_id=1, source_target_pairs={{0,1},{2,3},{4,5},{6,7},{8,9},{10,11},{12,13},{14,15},{16,17},{18,... | collective-permute-start | bytes 12296 | tf_op jit(solution)/shard_map/ppermute | solution.py:135
  102.3 0.8 slice-start
Sparse Core Ops, SparseCore 0:
  35.7 59.2 reduce-scatter.1

commit v2 on v1

--- a/solution.py
+++ b/solution.py
@@ -99,6 +99,41 @@
     )(back_band, volume, amplitude, column_offset, column_width, row_weight[:, :, None])
 
 
+def _bit_count(count):
+    bits = count.bit_length() - 1
+    assert 1 << bits == count
+    return bits
+
+
+def reduce_scatter_xy(x, count):
+    lead = x.shape[:-1]
+    width = x.shape[-1] // count
+    bits = _bit_count(count)
+    idx = lax.axis_index("xy")
+    y = x.reshape(lead + (2,) * bits + (width,))
+    for j in range(bits):
+        axis = len(lead) + bits - 1 - j
+        bit = (idx >> j) & 1
+        keep = lax.dynamic_index_in_dim(y, bit, axis, keepdims=False)
+        send = lax.dynamic_index_in_dim(y, 1 - bit, axis, keepdims=False)
+        y = keep + lax.ppermute(send, "xy", [(i, i ^ (1 << j)) for i in range(count)])
+    return y
+
+
+def all_gather_xy(x, count):
+    lead = x.shape[:-1]
+    bits = _bit_count(count)
+    idx = lax.axis_index("xy")
+    y = x
+    for step, j in enumerate(reversed(range(bits))):
+        bit = (idx >> j) & 1
+        other = lax.ppermute(y, "xy", [(i, i ^ (1 << j)) for i in range(count)])
+        low = jnp.where(bit == 0, y, other)
+        high = jnp.where(bit == 0, other, y)
+        y = jnp.stack([low, high], axis=len(lead) + step)
+    return y.reshape(lead + (count * x.shape[-1],))
+
+
 def local(volume, measured, band_start, column_offset, column_width, amplitude, axial_weight):
     slab_rows = volume.shape[0]
     view_count = amplitude.shape[0]
@@ -111,23 +146,30 @@
     up_pairs = [(i, i + 1) for i in range(gz_count - 1)]
     down_pairs = [(i + 1, i) for i in range(gz_count - 1)]
 
-    weights_all = lax.all_gather(axial_weight, "gz", axis=2, tiled=True)
-    padded_weights = jnp.pad(weights_all, ((0, 0), (0, 0), (2, 2)))
-    measured_ext = jnp.concatenate(
-        [
-            lax.ppermute(measured[:, slab_rows - 1 :], "gz", up_pairs),
-            measured,
-            lax.ppermute(measured[:, :1], "gz", down_pairs),
-        ],
-        axis=1,
-    )
+    def pack(meas_rows, weight_cols):
+        flat = jnp.transpose(weight_cols, (1, 0, 2)).reshape(view_count, 1, -1)
+        flat = jnp.pad(flat, ((0, 0), (0, 0), (0, shard_width - flat.shape[2])))
+        return jnp.concatenate([meas_rows, flat], axis=1)
+
+    def unpack(packed):
+        cols = packed[:, 1, : 3 * 2].reshape(view_count, 3, 2)
+        return packed[:, :1], jnp.transpose(cols, (1, 0, 2))
+
+    from_below = lax.ppermute(
+        pack(measured[:, slab_rows - 1 :], axial_weight[:, :, slab_rows - 2 :]), "gz", up_pairs
+    )
+    from_above = lax.ppermute(pack(measured[:, :1], axial_weight[:, :, :2]), "gz", down_pairs)
+    meas_below, weight_below = unpack(from_below)
+    meas_above, weight_above = unpack(from_above)
+    measured_ext = jnp.concatenate([meas_below, measured, meas_above], axis=1)
+    weight_ext = jnp.concatenate([weight_below, axial_weight, weight_above], axis=2)
 
     band_rows = forward_band(volume, amplitude, column_offset, column_width)
     placed = []
     for v in range(view_count):
         blank = jnp.zeros((slab_rows + 1, detector_width), jnp.float32)
         placed.append(lax.dynamic_update_slice(blank, band_rows[v], (jnp.int32(0), band_start[v, 0])))
-    reduced = lax.psum_scatter(jnp.stack(placed), "xy", scatter_dimension=2, tiled=True)
+    reduced = reduce_scatter_xy(jnp.stack(placed), xy_count)
     proj_cols = reduced[:, :slab_rows]
     cover = reduced[:, slab_rows : slab_rows + 1]
     proj_ext = jnp.concatenate(
@@ -140,13 +182,9 @@
     )
 
     ext_rows = slab_rows + 2
-
-    def weight_rows(kind, shift):
-        return lax.dynamic_slice_in_dim(padded_weights[kind], first_row + 1 + shift, ext_rows, 1)[:, :, None]
-
-    mid_w = weight_rows(1, 0)
-    next_w = weight_rows(0, 1)
-    prev_w = weight_rows(2, -1)
+    mid_w = weight_ext[1, :, 1 : ext_rows + 1][:, :, None]
+    next_w = weight_ext[0, :, 2 : ext_rows + 2][:, :, None]
+    prev_w = weight_ext[2, :, 0:ext_rows][:, :, None]
     centre = proj_ext[:, 1 : ext_rows + 1]
     after = proj_ext[:, 2 : ext_rows + 2]
     before = proj_ext[:, 0:ext_rows]
@@ -163,7 +201,7 @@
         + axial_weight[1][:, :, None] * residual
         + axial_weight[2][:, :, None] * residual_ext[:, 2 : slab_rows + 2]
     )
-    back_full = lax.all_gather(back_rows, "xy", axis=2, tiled=True)
+    back_full = all_gather_xy(back_rows, xy_count)
     back_band = jnp.stack(
         [
             lax.dynamic_slice(back_full[v], (jnp.int32(0), band_start[v, 0]), (slab_rows, B))

time: 149 us -> 99.3 us (0.67)
  waiting for transfers between devices: 47 us -> 18 us
  blocking collectives: 25.3 us -> 0 us
  between operations: 18.2 us -> 4.93 us
  starting transfers between devices: 12.1 us -> 22.5 us
  local copies, waits for them, and re-layouts: 6.39 us -> 13.9 us
    reduce_scatter x1 -> x0, waiting for transfers between devices: 46.5 us -> none  [local(): lax.psum_scatter(jnp.stack(placed), 'xy', scatter_dimension=2, tiled=True)]
    all_gather x2 -> x0, blocking collectives: 25.3 us -> none  [the longest x1 20.9 us: local(): back_full = lax.all_gather(back_rows, 'xy', axis=2, tiled=True)]
    ppermute x2 -> x10, waiting for transfers between devices: 0.01 us -> 14 us  [the longest x4 8.8 us: all_gather_xy(): other = lax.ppermute(y, 'xy', [(i, i ^ 1 << j) for i in range(count)])]
    ppermute x2 -> x10, starting transfers between devices: 6.25 us -> 19.6 us  [the longest x4 7.77 us: reduce_scatter_xy(): y = keep + lax.ppermute(send, 'xy', [(i, i ^ 1 << j) for i in range(count)])]
    dynamic_update_slice x2, local copies, waits for them, and re-layouts: 1.54 us -> 7.65 us  [local(): lax.dynamic_update_slice(blank, band_rows[v], (jnp.int32(0), band_start[v...]
    ppermute x1, waiting for transfers between devices: 0.01 us -> 4.05 us  [local(): lax.ppermute(proj_cols[:, :2], 'gz', down_pairs)]
    ppermute x1, starting transfers between devices: 4.54 us -> 1.63 us  [local(): lax.ppermute(proj_cols[:, slab_rows - 2:], 'gz', up_pairs)]
  transfers between devices with their start and end apart: 5 -> 12, of which waited for: 2 -> 8; matrix products, arithmetic and copies ran while one was open for 2% -> 2% of each run, Pallas kernels for 0% -> 0%
where the time goes in v2:
time: 99.3 us; the launch traced here: 98.8 us
  Pallas kernels  35.4 us (36%)
  starting transfers between devices  22.5 us (23%)
  waiting for transfers between devices  18 us (18%)
  local copies, waits for them, and re-layouts  13.9 us (14%)
  between operations  4.93 us (5%)
  other arithmetic  4.11 us (4%)
    pallas_call x1, Pallas kernels, forward_band(): pl.pallas_call(_forward_kernel, out_shape=jax.ShapeDtypeStruct((view_coun...  19.4 us
    pallas_call x1, Pallas kernels, backward_update(): pl.pallas_call(_backward_kernel, out_shape=jax.ShapeDtypeStruct(volume.sh...  16 us
    ppermute x4, waiting for transfers between devices, all_gather_xy(): other = lax.ppermute(y, 'xy', [(i, i ^ 1 << j) for i in range(count)])  8.8 us
    ppermute x4, starting transfers between devices, reduce_scatter_xy(): y = keep + lax.ppermute(send, 'xy', [(i, i ^ 1 << j) for i in range(count)])  7.77 us
    dynamic_update_slice x2, local copies, waits for them, and re-layouts, local(): lax.dynamic_update_slice(blank, band_rows[v], (jnp.int32(0), band_start[v...  7.65 us
    ppermute x4, starting transfers between devices, all_gather_xy(): other = lax.ppermute(y, 'xy', [(i, i ^ 1 << j) for i in range(count)])  6.01 us
    ppermute x4, waiting for transfers between devices, reduce_scatter_xy(): y = keep + lax.ppermute(send, 'xy', [(i, i ^ 1 << j) for i in range(count)])  5.18 us
    ppermute x1, starting transfers between devices, local(): lax.ppermute(pack(measured[:, slab_rows - 1:], axial_weight[:, :, slab_ro...  4.53 us
  transfers between devices with their start and end apart: 12, of which 8 were waited for; matrix products, arithmetic and copies ran while one was open for 2% of the time, Pallas kernels for 0%

profile of v2, /device:TPU:0, one launch (start us, length us, event | category | flops | bytes accessed | tf_op | source)
XLA Modules:
  0.0 98.8 jit_solution(1252748781815838360)
XLA Ops:
  0.6 0.6 copy-done.2
  1.3 0.6 fusion.20
  4.5 19.4 %shard_map.86 = f32[2,64,512]{2,1,0:T(8,128)} custom-call(f32[16,16384]{1,0:T(8,128)} %vol_ref.3, f32[2,16384]{1,0:T(2,128)} %amp_ref.3, s32[2,16384]{1,0:T(2,128)} %off_ref.3, s32[2,16384]{1,0:T(2,128)} %wid_ref.3), custom_call_target="tpu_custom_call" | custom-call | tf_op jit(solution)/shard_map/pallas_call | solution.py:55
  23.9 1.0 slice_add_fusion
  26.3 0.2 stack.52.clone
  26.5 3.8 %dynamic_update_slice.9 = f32[1,17,4096]{2,0,1:T(1,128)S(1)} dynamic-update-slice(f32[1,17,4096]{2,0,1:T(1,128)S(1)} %stack.52.clone, f32[1,17,512]{2,0,1:T(1,128)S(1)} %copy.69, s32[]{:T(128)} %constant.53.clone.1, s32[]{:T(128)} %constant.53.clone.1, s32[]{:T(128)S(6)} %select_n.114) | dynamic-update-slice | bytes 69636 | tf_op jit(solution)/shard_map/dynamic_update_slice | solution.py:171
  30.4 0.2 stack.52.clone.1
  30.6 3.8 %dynamic_update_slice.8 = f32[1,17,4096]{2,0,1:T(1,128)S(1)} dynamic-update-slice(f32[1,17,4096]{2,0,1:T(1,128)S(1)} %stack.52.clone.1, f32[1,17,512]{2,0,1:T(1,128)S(1)} %copy.68, s32[]{:T(128)} %constant.53.clone.1, s32[]{:T(128)} %constant.53.clone.1, s32[]{:T(128)S(6)} %select_n.113) | dynamic-update-slice | bytes 69636 | tf_op jit(solution)/shard_map/dynamic_update_slice | solution.py:171
  34.4 0.5 pad_maximum_fusion
  34.9 0.7 reshape.120
  35.6 0.6 constant_dynamic-slice_fusion.7
  36.2 0.1 copy.97
  36.4 0.5 collective-permute-start.2
  37.0 0.7 copy-done
  37.8 0.3 collective-permute-done.2
  38.1 0.2 bitcast_add_fusion
  38.3 0.2 constant_dynamic-slice_fusion.5
  38.6 3.0 %collective-permute-start.3 = (f32[2,17,2,2,256]{4,3,2,1,0:T(2,128)S(1)}, f32[2,17,2,2,256]{4,3,2,1,0:T(2,128)S(1)}, u32[]{:S(2)}, u32[]{:S(2)}) collective-permute-start(f32[2,17,2,2,256]{4,3,2,1,0:T(2,128)S(1)} %bitcast.79), channel_id=1, source_target_pairs={{0,4},{2,6},{4,0},{6,2},{8,12},{10,14},{12,8},{14,10},{16,20},{18,... | collective-permute-start | bytes 417800 | tf_op jit(solution)/shard_map/ppermute | solution.py:119
  41.6 1.3 %collective-permute-start.1 = (f32[2,2,256]{2,0,1:T(2,128)S(1)}, f32[2,2,256]{2,0,1:T(2,128)S(1)}, u32[]{:S(2)}, u32[]{:S(2)}) collective-permute-start(f32[2,2,256]{2,0,1:T(2,128)S(1)} %select_maximum_fusion), channel_id=1, source_target_pairs={{1,0},{3,2},{5,4},{7,6},{9,8},{11,10},{13,12},{15,14},{17,16},{19,... | collective-permute-start | bytes 12296 | tf_op jit(solution)/shard_map/ppermute | solution.py:161
  43.0 4.5 %collective-permute-start = (f32[2,2,256]{2,0,1:T(2,128)S(1)}, f32[2,2,256]{2,0,1:T(2,128)S(1)}, u32[]{:S(2)}, u32[]{:S(2)}) collective-permute-start(f32[2,2,256]{2,0,1:T(2,128)S(1)} %select_maximum_fusion.1), channel_id=1, source_target_pairs={{0,1},{2,3},{4,5},{6,7},{8,9},{10,11},{12,13},{14,15},{16,17},{18,... | collective-permute-start | bytes 12296 | tf_op jit(solution)/shard_map/ppermute | solution.py:158
  47.5 0.1 bitcast_add_fusion.1
  47.6 0.1 constant_dynamic-slice_fusion.3
  47.8 1.6 %collective-permute-start.4 = (f32[2,17,2,256]{3,2,1,0:T(2,128)S(1)}, f32[2,17,2,256]{3,2,1,0:T(2,128)S(1)}, u32[]{:S(2)}, u32[]{:S(2)}) collective-permute-start(f32[2,17,2,256]{3,2,1,0:T(2,128)S(1)} %bitcast.80), channel_id=1, source_target_pairs={{0,8},{2,10},{4,12},{6,14},{8,0},{10,2},{12,4},{14,6},{16,24},{18,... | collective-permute-start | bytes 208904 | tf_op jit(solution)/shard_map/ppermute | solution.py:119
  49.5 2.7 %collective-permute-done.4 = f32[2,17,2,256]{3,2,1,0:T(2,128)S(1)} collective-permute-done((f32[2,17,2,256]{3,2,1,0:T(2,128)S(1)}, f32[2,17,2,256]{3,2,1,0:T(2,128)S(1)}, u32[]{:S(2)}, u32[]{:S(2)}) %collective-permute-start.4) | collective-permute-done | bytes 69664 | tf_op jit(solution)/shard_map/ppermute | solution.py:119
  52.3 2.7 %collective-permute-start.5 = (f32[2,17,256]{2,1,0:T(8,128)S(1)}, f32[2,17,256]{2,1,0:T(8,128)S(1)}, u32[]{:S(2)}, u32[]{:S(2)}) collective-permute-start(f32[2,17,256]{2,1,0:T(8,128)S(1)} %bitcast.81), channel_id=1, source_target_pairs={{0,16},{2,18},{4,20},{6,22},{8,24},{10,26},{12,28},{14,30},{16,0},... | collective-permute-start | bytes 104456 | tf_op jit(solution)/shard_map/ppermute | solution.py:119
  55.2 2.2 %collective-permute-done.5 = f32[2,17,256]{2,1,0:T(8,128)S(1)} collective-permute-done((f32[2,17,256]{2,1,0:T(8,128)S(1)}, f32[2,17,256]{2,1,0:T(8,128)S(1)}, u32[]{:S(2)}, u32[]{:S(2)}) %collective-permute-start.5) | collective-permute-done | bytes 34848 | tf_op jit(solution)/shard_map/ppermute | solution.py:119
  57.4 1.6 %collective-permute-start.6 = (f32[2,2,256]{2,1,0:T(2,128)S(1)}, f32[2,2,256]{2,1,0:T(2,128)S(1)}, u32[]{:S(2)}, u32[]{:S(2)}) collective-permute-start(f32[2,2,256]{2,1,0:T(2,128)S(1)} %get-tuple-element.28), channel_id=1, source_target_pairs={{0,1},{2,3},{4,5},{6,7},{8,9},{10,11},{12,13},{14,15},{16,17},{18,... | collective-permute-start | bytes 12296 | tf_op jit(solution)/shard_map/ppermute | solution.py:177
  59.0 1.3 %collective-permute-start.7 = (f32[2,2,256]{2,1,0:T(2,128)S(1)}, f32[2,2,256]{2,1,0:T(2,128)S(1)}, u32[]{:S(2)}, u32[]{:S(2)}) collective-permute-start(f32[2,2,256]{2,1,0:T(2,128)S(1)} %get-tuple-element.29), channel_id=1, source_target_pairs={{1,0},{3,2},{5,4},{7,6},{9,8},{11,10},{13,12},{15,14},{17,16},{19,... | collective-permute-start | bytes 12296 | tf_op jit(solution)/shard_map/ppermute | solution.py:179
  60.5 4.0 %collective-permute-done.7 = f32[2,2,256]{2,1,0:T(2,128)S(1)} collective-permute-done((f32[2,2,256]{2,1,0:T(2,128)S(1)}, f32[2,2,256]{2,1,0:T(2,128)S(1)}, u32[]{:S(2)}, u32[]{:S(2)}) %collective-permute-start.7) | collective-permute-done | bytes 4128 | tf_op jit(solution)/shard_map/ppermute | solution.py:179
  64.5 0.1 fusion.6
  64.6 0.6 fusion.7
  65.3 2.6 %collective-permute-start.8 = (f32[2,16,256]{2,1,0:T(8,128)S(1)}, f32[2,16,256]{2,1,0:T(8,128)S(1)}, u32[]{:S(2)}, u32[]{:S(2)}) collective-permute-start(f32[2,16,256]{2,1,0:T(8,128)S(1)} %get-tuple-element.2), channel_id=1, source_target_pairs={{0,16},{2,18},{4,20},{6,22},{8,24},{10,26},{12,28},{14,30},{16,0},... | collective-permute-start | bytes 98312 | tf_op jit(solution)/shard_map/ppermute | solution.py:130
  67.9 2.2 %collective-permute-done.8 = f32[2,16,256]{2,1,0:T(8,128)S(1)} collective-permute-done((f32[2,16,256]{2,1,0:T(8,128)S(1)}, f32[2,16,256]{2,1,0:T(8,128)S(1)}, u32[]{:S(2)}, u32[]{:S(2)}) %collective-permute-start.8) | collective-permute-done | bytes 32800 | tf_op jit(solution)/shard_map/ppermute | solution.py:130
  70.1 1.7 %collective-permute-start.9 = (f32[2,16,2,256]{3,1,0,2:T(8,128)S(1)}, f32[2,16,2,256]{3,1,0,2:T(8,128)S(1)}, u32[]{:S(2)}, u32[]{:S(2)}) collective-permute-start(f32[2,16,2,256]{3,1,0,2:T(8,128)S(1)} %pad_maximum_fusion.4), channel_id=1, source_target_pairs={{0,8},{2,10},{4,12},{6,14},{8,0},{10,2},{12,4},{14,6},{16,24},{18,... | collective-permute-start | bytes 196616 | tf_op jit(solution)/shard_map/ppermute | solution.py:130
  71.8 2.6 %collective-permute-done.9 = f32[2,16,2,256]{3,1,0,2:T(8,128)S(1)} collective-permute-done((f32[2,16,2,256]{3,1,0,2:T(8,128)S(1)}, f32[2,16,2,256]{3,1,0,2:T(8,128)S(1)}, u32[]{:S(2)}, u32[]{:S(2)}) %collective-permute-start.9) | collective-permute-done | bytes 65568 | tf_op jit(solution)/shard_map/ppermute | solution.py:130
  74.5 1.6 %collective-permute-start.10 = (f32[2,16,2,2,256]{4,1,0,2,3:T(8,128)S(1)}, f32[2,16,2,2,256]{4,1,0,2,3:T(8,128)S(1)}, u32[]{:S(2)}, u32[]{:S(2)}) collective-permute-start(f32[2,16,2,2,256]{4,1,0,2,3:T(8,128)S(1)} %pad_maximum_fusion.3), channel_id=1, source_target_pairs={{0,4},{2,6},{4,0},{6,2},{8,12},{10,14},{12,8},{14,10},{16,20},{18,... | collective-permute-start | bytes 393224 | tf_op jit(solution)/shard_map/ppermute | solution.py:130
  76.1 3.4 %collective-permute-done.10 = f32[2,16,2,2,256]{4,1,0,2,3:T(8,128)S(1)} collective-permute-done((f32[2,16,2,2,256]{4,1,0,2,3:T(8,128)S(1)}, f32[2,16,2,2,256]{4,1,0,2,3:T(8,128)S(1)}, u32[]{:S(2)}, u32[]{:S(2)}) %collective-permute-start.10) | collective-permute-done | bytes 131104 | tf_op jit(solution)/shard_map/ppermute | solution.py:130
  79.7 0.1 copy.76
  79.7 0.1 copy.78
  79.9 0.7 select_add_fusion.rw_ref
  80.6 0.6 collective-permute-done.11
  81.3 0.2 copy.74
  81.5 0.2 squeeze.63
  81.7 0.2 copy.75
  81.9 0.2 squeeze.64
  82.1 0.1 dynamic-slice_bitcast_fusion
  82.2 0.6 pad_maximum_fusion.5.back_ref
  82.8 16.0 %shard_map.87 = f32[16,16384]{1,0:T(8,128)} custom-call(f32[2,16,512]{2,1,0:T(8,128)} %pad_maximum_fusion.5.back_ref, f32[16,16384]{1,0:T(8,128)} %vol_ref.3, f32[2,16384]{1,0:T(2,128)} %amp_ref.3, s32[2,16384]{1,0:T(2,128)} %off_ref.3, s32[2,16384]{1,0:T(2,128)} %wid_ref.3, f32[2,16,1]{2,1,0:T(8,128)} %select_add_fusion.rw_ref), custom_call_target="tpu_custom_call" | custom-call | tf_op jit(solution)/shard_map/pallas_call | solution.py:94
  (55 shorter events, 1.3 us)
Async XLA Ops:
  0.6 0.7 copy-start.2
  36.2 0.8 copy-start.1
  36.4 1.7 %collective-permute-start.2 = (f32[2,17,2,2,2,256]{5,4,3,2,1,0:T(2,128)S(1)}, f32[2,17,2,2,2,256]{5,4,3,2,1,0:T(2,128)S(1)}, u32[]{:S(2)}, u32[]{:S(2)}) collective-permute-start(f32[2,17,2,2,2,256]{5,4,3,2,1,0:T(2,128)S(1)} %bitcast.78), channel_id=1, source_target_pairs={{0,2},{2,0},{4,6},{6,4},{8,10},{10,8},{12,14},{14,12},{16,18},{18,... | collective-permute-start | bytes 835592 | tf_op jit(solution)/shard_map/ppermute | solution.py:119
  37.0 0.7 copy-start
  38.6 8.9 %collective-permute-start.3 = (f32[2,17,2,2,256]{4,3,2,1,0:T(2,128)S(1)}, f32[2,17,2,2,256]{4,3,2,1,0:T(2,128)S(1)}, u32[]{:S(2)}, u32[]{:S(2)}) collective-permute-start(f32[2,17,2,2,256]{4,3,2,1,0:T(2,128)S(1)} %bitcast.79), channel_id=1, source_target_pairs={{0,4},{2,6},{4,0},{6,2},{8,12},{10,14},{12,8},{14,10},{16,20},{18,... | collective-permute-start | bytes 417800 | tf_op jit(solution)/shard_map/ppermute | solution.py:119
  41.6 13.4 %collective-permute-start.1 = (f32[2,2,256]{2,0,1:T(2,128)S(1)}, f32[2,2,256]{2,0,1:T(2,128)S(1)}, u32[]{:S(2)}, u32[]{:S(2)}) collective-permute-start(f32[2,2,256]{2,0,1:T(2,128)S(1)} %select_maximum_fusion), channel_id=1, source_target_pairs={{1,0},{3,2},{5,4},{7,6},{9,8},{11,10},{13,12},{15,14},{17,16},{19,... | collective-permute-start | bytes 12296 | tf_op jit(solution)/shard_map/ppermute | solution.py:161
  43.0 12.1 %collective-permute-start = (f32[2,2,256]{2,0,1:T(2,128)S(1)}, f32[2,2,256]{2,0,1:T(2,128)S(1)}, u32[]{:S(2)}, u32[]{:S(2)}) collective-permute-start(f32[2,2,256]{2,0,1:T(2,128)S(1)} %select_maximum_fusion.1), channel_id=1, source_target_pairs={{0,1},{2,3},{4,5},{6,7},{8,9},{10,11},{12,13},{14,15},{16,17},{18,... | collective-permute-start | bytes 12296 | tf_op jit(solution)/shard_map/ppermute | solution.py:158
  47.8 4.4 %collective-permute-start.4 = (f32[2,17,2,256]{3,2,1,0:T(2,128)S(1)}, f32[2,17,2,256]{3,2,1,0:T(2,128)S(1)}, u32[]{:S(2)}, u32[]{:S(2)}) collective-permute-start(f32[2,17,2,256]{3,2,1,0:T(2,128)S(1)} %bitcast.80), channel_id=1, source_target_pairs={{0,8},{2,10},{4,12},{6,14},{8,0},{10,2},{12,4},{14,6},{16,24},{18,... | collective-permute-start | bytes 208904 | tf_op jit(solution)/shard_map/ppermute | solution.py:119
  52.3 5.1 %collective-permute-start.5 = (f32[2,17,256]{2,1,0:T(8,128)S(1)}, f32[2,17,256]{2,1,0:T(8,128)S(1)}, u32[]{:S(2)}, u32[]{:S(2)}) collective-permute-start(f32[2,17,256]{2,1,0:T(8,128)S(1)} %bitcast.81), channel_id=1, source_target_pairs={{0,16},{2,18},{4,20},{6,22},{8,24},{10,26},{12,28},{14,30},{16,0},... | collective-permute-start | bytes 104456 | tf_op jit(solution)/shard_map/ppermute | solution.py:119
  57.4 3.1 %collective-permute-start.6 = (f32[2,2,256]{2,1,0:T(2,128)S(1)}, f32[2,2,256]{2,1,0:T(2,128)S(1)}, u32[]{:S(2)}, u32[]{:S(2)}) collective-permute-start(f32[2,2,256]{2,1,0:T(2,128)S(1)} %get-tuple-element.28), channel_id=1, source_target_pairs={{0,1},{2,3},{4,5},{6,7},{8,9},{10,11},{12,13},{14,15},{16,17},{18,... | collective-permute-start | bytes 12296 | tf_op jit(solution)/shard_map/ppermute | solution.py:177
  59.0 5.5 %collective-permute-start.7 = (f32[2,2,256]{2,1,0:T(2,128)S(1)}, f32[2,2,256]{2,1,0:T(2,128)S(1)}, u32[]{:S(2)}, u32[]{:S(2)}) collective-permute-start(f32[2,2,256]{2,1,0:T(2,128)S(1)} %get-tuple-element.29), channel_id=1, source_target_pairs={{1,0},{3,2},{5,4},{7,6},{9,8},{11,10},{13,12},{15,14},{17,16},{19,... | collective-permute-start | bytes 12296 | tf_op jit(solution)/shard_map/ppermute | solution.py:179
  65.3 4.8 %collective-permute-start.8 = (f32[2,16,256]{2,1,0:T(8,128)S(1)}, f32[2,16,256]{2,1,0:T(8,128)S(1)}, u32[]{:S(2)}, u32[]{:S(2)}) collective-permute-start(f32[2,16,256]{2,1,0:T(8,128)S(1)} %get-tuple-element.2), channel_id=1, source_target_pairs={{0,16},{2,18},{4,20},{6,22},{8,24},{10,26},{12,28},{14,30},{16,0},... | collective-permute-start | bytes 98312 | tf_op jit(solution)/shard_map/ppermute | solution.py:130
  70.1 4.3 %collective-permute-start.9 = (f32[2,16,2,256]{3,1,0,2:T(8,128)S(1)}, f32[2,16,2,256]{3,1,0,2:T(8,128)S(1)}, u32[]{:S(2)}, u32[]{:S(2)}) collective-permute-start(f32[2,16,2,256]{3,1,0,2:T(8,128)S(1)} %pad_maximum_fusion.4), channel_id=1, source_target_pairs={{0,8},{2,10},{4,12},{6,14},{8,0},{10,2},{12,4},{14,6},{16,24},{18,... | collective-permute-start | bytes 196616 | tf_op jit(solution)/shard_map/ppermute | solution.py:130
  74.5 5.0 %collective-permute-start.10 = (f32[2,16,2,2,256]{4,1,0,2,3:T(8,128)S(1)}, f32[2,16,2,2,256]{4,1,0,2,3:T(8,128)S(1)}, u32[]{:S(2)}, u32[]{:S(2)}) collective-permute-start(f32[2,16,2,2,256]{4,1,0,2,3:T(8,128)S(1)} %pad_maximum_fusion.3), channel_id=1, source_target_pairs={{0,4},{2,6},{4,0},{6,2},{8,12},{10,14},{12,8},{14,10},{16,20},{18,... | collective-permute-start | bytes 393224 | tf_op jit(solution)/shard_map/ppermute | solution.py:130
  79.6 1.6 %collective-permute-start.11 = (f32[2,16,2,2,2,256]{5,1,0,2,3,4:T(8,128)S(1)}, f32[2,16,2,2,2,256]{5,1,0,2,3,4:T(8,128)S(1)}, u32[]{:S(2)}, u32[]{:S(2)}) collective-permute-start(f32[2,16,2,2,2,256]{5,1,0,2,3,4:T(8,128)S(1)} %pad_maximum_fusion.2), channel_id=1, source_target_pairs={{0,2},{2,0},{4,6},{6,4},{8,10},{10,8},{12,14},{14,12},{16,18},{18,... | collective-permute-start | bytes 786440 | tf_op jit(solution)/shard_map/ppermute | solution.py:130

commit v3 on v2

--- a/solution.py
+++ b/solution.py
@@ -106,13 +106,13 @@
 
 
 def reduce_scatter_xy(x, count):
-    lead = x.shape[:-1]
-    width = x.shape[-1] // count
+    rows = x.shape[0]
+    width = x.shape[1] // count
     bits = _bit_count(count)
     idx = lax.axis_index("xy")
-    y = x.reshape(lead + (2,) * bits + (width,))
+    y = jnp.transpose(x.reshape(rows, count, width), (1, 0, 2)).reshape((2,) * bits + (rows, width))
     for j in range(bits):
-        axis = len(lead) + bits - 1 - j
+        axis = bits - 1 - j
         bit = (idx >> j) & 1
         keep = lax.dynamic_index_in_dim(y, bit, axis, keepdims=False)
         send = lax.dynamic_index_in_dim(y, 1 - bit, axis, keepdims=False)
@@ -121,7 +121,7 @@
 
 
 def all_gather_xy(x, count):
-    lead = x.shape[:-1]
+    rows, width = x.shape
     bits = _bit_count(count)
     idx = lax.axis_index("xy")
     y = x
@@ -130,8 +130,8 @@
         other = lax.ppermute(y, "xy", [(i, i ^ (1 << j)) for i in range(count)])
         low = jnp.where(bit == 0, y, other)
         high = jnp.where(bit == 0, other, y)
-        y = jnp.stack([low, high], axis=len(lead) + step)
-    return y.reshape(lead + (count * x.shape[-1],))
+        y = jnp.stack([low, high], axis=step)
+    return jnp.transpose(y.reshape(count, rows, width), (1, 0, 2)).reshape(rows, count * width)
 
 
 def local(volume, measured, band_start, column_offset, column_width, amplitude, axial_weight):
@@ -165,11 +165,11 @@
     weight_ext = jnp.concatenate([weight_below, axial_weight, weight_above], axis=2)
 
     band_rows = forward_band(volume, amplitude, column_offset, column_width)
-    placed = []
+    band_height = slab_rows + 1
+    placed = jnp.zeros((view_count * band_height, detector_width), jnp.float32)
     for v in range(view_count):
-        blank = jnp.zeros((slab_rows + 1, detector_width), jnp.float32)
-        placed.append(lax.dynamic_update_slice(blank, band_rows[v], (jnp.int32(0), band_start[v, 0])))
-    reduced = reduce_scatter_xy(jnp.stack(placed), xy_count)
+        placed = lax.dynamic_update_slice(placed, band_rows[v], (jnp.int32(v * band_height), band_start[v, 0]))
+    reduced = reduce_scatter_xy(placed, xy_count).reshape(view_count, band_height, shard_width)
     proj_cols = reduced[:, :slab_rows]
     cover = reduced[:, slab_rows : slab_rows + 1]
     proj_ext = jnp.concatenate(
@@ -201,7 +201,8 @@
         + axial_weight[1][:, :, None] * residual
         + axial_weight[2][:, :, None] * residual_ext[:, 2 : slab_rows + 2]
     )
-    back_full = all_gather_xy(back_rows, xy_count)
+    back_full = all_gather_xy(back_rows.reshape(view_count * slab_rows, shard_width), xy_count)
+    back_full = back_full.reshape(view_count, slab_rows, detector_width)
     back_band = jnp.stack(
         [
             lax.dynamic_slice(back_full[v], (jnp.int32(0), band_start[v, 0]), (slab_rows, B))

time: 99.3 us -> 92.5 us (0.932)
  local copies, waits for them, and re-layouts: 13.9 us -> 7.26 us
  starting transfers between devices: 22.5 us -> 24.2 us
  waiting for transfers between devices: 18 us -> 16.8 us
    dynamic_update_slice x2, local copies, waits for them, and re-layouts: 7.65 us -> 3.06 us  [local(): lax.dynamic_update_slice(placed, band_rows[v], (jnp.int32(v * band_height...]
    ppermute x1, waiting for transfers between devices: 4.05 us -> 0.01 us  [local(): lax.ppermute(proj_cols[:, :2], 'gz', down_pairs)]
    ppermute x1, starting transfers between devices: 1.63 us -> 4.54 us  [local(): lax.ppermute(proj_cols[:, slab_rows - 2:], 'gz', up_pairs)]
    ppermute x4, starting transfers between devices: 6.01 us -> 4.68 us  [all_gather_xy(): other = lax.ppermute(y, 'xy', [(i, i ^ 1 << j) for i in range(count)])]
    ppermute x4, waiting for transfers between devices: 8.8 us -> 10.1 us  [all_gather_xy(): other = lax.ppermute(y, 'xy', [(i, i ^ 1 << j) for i in range(count)])]
    unnamed x12 -> x10, local copies, waits for them, and re-layouts: 1.53 us -> 0.33 us
    ppermute x1, waiting for transfers between devices: 0.01 us -> 1.16 us  [local(): lax.ppermute(proj_cols[:, slab_rows - 2:], 'gz', up_pairs)]
where the time goes in v3:
time: 92.5 us; the launch traced here: 92.1 us
  Pallas kernels  35.4 us (38%)
  starting transfers between devices  24.2 us (26%)
  waiting for transfers between devices  16.8 us (18%)
  local copies, waits for them, and re-layouts  7.26 us (8%)
  between operations  4.69 us (5%)
  other arithmetic  3.64 us (4%)
    pallas_call x1, Pallas kernels, forward_band(): pl.pallas_call(_forward_kernel, out_shape=jax.ShapeDtypeStruct((view_coun...  19.4 us
    pallas_call x1, Pallas kernels, backward_update(): pl.pallas_call(_backward_kernel, out_shape=jax.ShapeDtypeStruct(volume.sh...  16 us
    ppermute x4, waiting for transfers between devices, all_gather_xy(): other = lax.ppermute(y, 'xy', [(i, i ^ 1 << j) for i in range(count)])  10.1 us
    ppermute x4, starting transfers between devices, reduce_scatter_xy(): y = keep + lax.ppermute(send, 'xy', [(i, i ^ 1 << j) for i in range(count)])  7.88 us
    ppermute x4, waiting for transfers between devices, reduce_scatter_xy(): y = keep + lax.ppermute(send, 'xy', [(i, i ^ 1 << j) for i in range(count)])  5.55 us
    ppermute x4, starting transfers between devices, all_gather_xy(): other = lax.ppermute(y, 'xy', [(i, i ^ 1 << j) for i in range(count)])  4.68 us
    ppermute x1, starting transfers between devices, local(): lax.ppermute(proj_cols[:, slab_rows - 2:], 'gz', up_pairs)  4.54 us
    ppermute x1, starting transfers between devices, local(): lax.ppermute(pack(measured[:, slab_rows - 1:], axial_weight[:, :, slab_ro...  4.54 us
  transfers between devices with their start and end apart: 12, of which 8 were waited for; matrix products, arithmetic and copies ran while one was open for 2% of the time, Pallas kernels for 0%

profile of v3, /device:TPU:0, one launch (start us, length us, event | category | flops | bytes accessed | tf_op | source)
XLA Modules:
  0.0 92.1 jit_solution(11001836931167004252)
XLA Ops:
  0.6 1.3 %fusion.18 = (s32[1,1]{0,1:T(1,128)}, s32[1,1]{0,1:T(1,128)}) fusion(s32[2,1]{0,1:T(1,128)} %param.9), kind=kLoop, calls=%fused_computation.79 | loop fusion | bytes 16 | tf_op jit(solution)/shard_map/slice | solution.py:171
  4.4 19.4 %shard_map.86 = f32[2,64,512]{2,1,0:T(8,128)} custom-call(f32[16,16384]{1,0:T(8,128)} %vol_ref.3, f32[2,16384]{1,0:T(2,128)} %amp_ref.3, s32[2,16384]{1,0:T(2,128)} %off_ref.3, s32[2,16384]{1,0:T(2,128)} %wid_ref.3), custom_call_target="tpu_custom_call" | custom-call | tf_op jit(solution)/shard_map/pallas_call | solution.py:55
  23.8 1.0 %slice_add_fusion = f32[2,32,512]{2,1,0:T(8,128)S(1)} fusion(f32[2,64,512]{2,1,0:T(8,128)} %shard_map.86), kind=kLoop, calls=%fused_computation.11 | loop fusion | flops 32768 | bytes 393216 | tf_op jit(solution)/shard_map/add | solution.py:60
  26.1 1.7 %dynamic_update_slice.6 = f32[34,4096]{1,0:T(8,128)S(1)} dynamic-update-slice(f32[34,4096]{1,0:T(8,128)S(1)} %broadcast_in_dim.38, f32[17,512]{1,0:T(8,128)S(1)} %get-tuple-element.23, s32[]{:T(128)} %constant.52.clone.1, s32[]{:T(128)S(6)} %select_n.113) | dynamic-update-slice | bytes 69636 | tf_op jit(solution)/shard_map/dynamic_update_slice | solution.py:171
  27.8 1.3 %dynamic_update_slice.7 = f32[34,4096]{1,0:T(8,128)S(1)} dynamic-update-slice(f32[34,4096]{1,0:T(8,128)S(1)} %dynamic_update_slice.6, f32[17,512]{1,0:T(8,128)S(1)} %get-tuple-element.22, s32[]{:T(128)} %constant.61.clone.1, s32[]{:T(128)S(6)} %select_n.114) | dynamic-update-slice | bytes 69636 | tf_op jit(solution)/shard_map/dynamic_update_slice | solution.py:171
  29.2 0.2 copy.91
  29.4 0.3 reshape.126
  29.7 0.6 constant_dynamic-slice_fusion.7
  30.3 0.1 copy.101
  30.5 0.5 collective-permute-start.2
  31.0 0.1 slice_bitcast_fusion.6
  31.1 0.1 reshape.124
  31.3 0.9 %collective-permute-done.2 = f32[2,2,2,34,256]{4,2,3,1,0:T(2,128)S(1)} collective-permute-done((f32[2,2,2,34,256]{4,2,3,1,0:T(2,128)S(1)}, f32[2,2,2,34,256]{4,2,3,1,0:T(2,128)S(1)}, u32[]{:S(2)}, u32[]{:S(2)}) %collective-permute-start.2) | collective-permute-done | bytes 278560 | tf_op jit(solution)/shard_map/ppermute | solution.py:119
  32.2 0.2 bitcast_add_fusion
  32.4 0.2 constant_dynamic-slice_fusion.5
  32.7 0.1 copy.102
  32.7 2.8 %collective-permute-start.3 = (f32[2,2,34,256]{3,1,2,0:T(2,128)S(1)}, f32[2,2,34,256]{3,1,2,0:T(2,128)S(1)}, u32[]{:S(2)}, u32[]{:S(2)}) collective-permute-start(f32[2,2,34,256]{3,1,2,0:T(2,128)S(1)} %bitcast.111), channel_id=1, source_target_pairs={{0,4},{2,6},{4,0},{6,2},{8,12},{10,14},{12,8},{14,10},{16,20},{18,... | collective-permute-start | bytes 417800 | tf_op jit(solution)/shard_map/ppermute | solution.py:119
  35.6 1.3 %collective-permute-start.1 = (f32[2,2,256]{2,0,1:T(2,128)S(1)}, f32[2,2,256]{2,0,1:T(2,128)S(1)}, u32[]{:S(2)}, u32[]{:S(2)}) collective-permute-start(f32[2,2,256]{2,0,1:T(2,128)S(1)} %select_maximum_fusion), channel_id=1, source_target_pairs={{1,0},{3,2},{5,4},{7,6},{9,8},{11,10},{13,12},{15,14},{17,16},{19,... | collective-permute-start | bytes 12296 | tf_op jit(solution)/shard_map/ppermute | solution.py:161
  36.9 0.1 reshape.123
  37.0 4.5 %collective-permute-start = (f32[2,2,256]{2,0,1:T(2,128)S(1)}, f32[2,2,256]{2,0,1:T(2,128)S(1)}, u32[]{:S(2)}, u32[]{:S(2)}) collective-permute-start(f32[2,2,256]{2,0,1:T(2,128)S(1)} %select_maximum_fusion.1), channel_id=1, source_target_pairs={{0,1},{2,3},{4,5},{6,7},{8,9},{10,11},{12,13},{14,15},{16,17},{18,... | collective-permute-start | bytes 12296 | tf_op jit(solution)/shard_map/ppermute | solution.py:158
  41.5 0.1 bitcast_add_fusion.1
  41.6 0.1 constant_dynamic-slice_fusion.3
  41.8 1.8 %collective-permute-start.4 = (f32[2,34,256]{2,0,1:T(2,128)S(1)}, f32[2,34,256]{2,0,1:T(2,128)S(1)}, u32[]{:S(2)}, u32[]{:S(2)}) collective-permute-start(f32[2,34,256]{2,0,1:T(2,128)S(1)} %bitcast.113), channel_id=1, source_target_pairs={{0,8},{2,10},{4,12},{6,14},{8,0},{10,2},{12,4},{14,6},{16,24},{18,... | collective-permute-start | bytes 208904 | tf_op jit(solution)/shard_map/ppermute | solution.py:119
  43.6 2.6 %collective-permute-done.4 = f32[2,34,256]{2,0,1:T(2,128)S(1)} collective-permute-done((f32[2,34,256]{2,0,1:T(2,128)S(1)}, f32[2,34,256]{2,0,1:T(2,128)S(1)}, u32[]{:S(2)}, u32[]{:S(2)}) %collective-permute-start.4) | collective-permute-done | bytes 69664 | tf_op jit(solution)/shard_map/ppermute | solution.py:119
  46.3 2.8 %collective-permute-start.5 = (f32[34,256]{1,0:T(8,128)S(1)}, f32[34,256]{1,0:T(8,128)S(1)}, u32[]{:S(2)}, u32[]{:S(2)}) collective-permute-start(f32[34,256]{1,0:T(8,128)S(1)} %bitcast.114), channel_id=1, source_target_pairs={{0,16},{2,18},{4,20},{6,22},{8,24},{10,26},{12,28},{14,30},{16,0},... | collective-permute-start | bytes 104456 | tf_op jit(solution)/shard_map/ppermute | solution.py:119
  49.1 0.1 reshape_squeeze.7
  49.2 0.1 reshape_squeeze.6
  49.3 2.0 %collective-permute-done.5 = f32[34,256]{1,0:T(8,128)S(1)} collective-permute-done((f32[34,256]{1,0:T(8,128)S(1)}, f32[34,256]{1,0:T(8,128)S(1)}, u32[]{:S(2)}, u32[]{:S(2)}) %collective-permute-start.5) | collective-permute-done | bytes 34848 | tf_op jit(solution)/shard_map/ppermute | solution.py:119
  51.3 1.3 %collective-permute-start.7 = (f32[2,2,256]{2,1,0:T(2,128)S(1)}, f32[2,2,256]{2,1,0:T(2,128)S(1)}, u32[]{:S(2)}, u32[]{:S(2)}) collective-permute-start(f32[2,2,256]{2,1,0:T(2,128)S(1)} %get-tuple-element.29), channel_id=1, source_target_pairs={{1,0},{3,2},{5,4},{7,6},{9,8},{11,10},{13,12},{15,14},{17,16},{19,... | collective-permute-start | bytes 12296 | tf_op jit(solution)/shard_map/ppermute | solution.py:179
  52.6 4.5 %collective-permute-start.6 = (f32[2,2,256]{2,1,0:T(2,128)S(1)}, f32[2,2,256]{2,1,0:T(2,128)S(1)}, u32[]{:S(2)}, u32[]{:S(2)}) collective-permute-start(f32[2,2,256]{2,1,0:T(2,128)S(1)} %get-tuple-element.28), channel_id=1, source_target_pairs={{0,1},{2,3},{4,5},{6,7},{8,9},{10,11},{12,13},{14,15},{16,17},{18,... | collective-permute-start | bytes 12296 | tf_op jit(solution)/shard_map/ppermute | solution.py:177
  57.2 0.1 add_add_fusion
  57.3 1.2 %collective-permute-done.6 = f32[2,2,256]{2,1,0:T(2,128)S(1)} collective-permute-done((f32[2,2,256]{2,1,0:T(2,128)S(1)}, f32[2,2,256]{2,1,0:T(2,128)S(1)}, u32[]{:S(2)}, u32[]{:S(2)}) %collective-permute-start.6) | collective-permute-done | bytes 4128 | tf_op jit(solution)/shard_map/ppermute | solution.py:177
  58.5 0.1 fusion.5
  58.6 0.6 fusion.6
  59.2 2.7 %collective-permute-start.8 = (f32[32,256]{1,0:T(8,128)S(1)}, f32[32,256]{1,0:T(8,128)S(1)}, u32[]{:S(2)}, u32[]{:S(2)}) collective-permute-start(f32[32,256]{1,0:T(8,128)S(1)} %bitcast.112), channel_id=1, source_target_pairs={{0,16},{2,18},{4,20},{6,22},{8,24},{10,26},{12,28},{14,30},{16,0},... | collective-permute-start | bytes 98312 | tf_op jit(solution)/shard_map/ppermute | solution.py:130
  62.0 2.1 %collective-permute-done.8 = f32[32,256]{1,0:T(8,128)S(1)} collective-permute-done((f32[32,256]{1,0:T(8,128)S(1)}, f32[32,256]{1,0:T(8,128)S(1)}, u32[]{:S(2)}, u32[]{:S(2)}) %collective-permute-start.8) | collective-permute-done | bytes 32800 | tf_op jit(solution)/shard_map/ppermute | solution.py:130
  64.1 1.8 %collective-permute-start.9 = (f32[2,32,256]{2,1,0:T(8,128)S(1)}, f32[2,32,256]{2,1,0:T(8,128)S(1)}, u32[]{:S(2)}, u32[]{:S(2)}) collective-permute-start(f32[2,32,256]{2,1,0:T(8,128)S(1)} %pad_maximum_fusion.3), channel_id=1, source_target_pairs={{0,8},{2,10},{4,12},{6,14},{8,0},{10,2},{12,4},{14,6},{16,24},{18,... | collective-permute-start | bytes 196616 | tf_op jit(solution)/shard_map/ppermute | solution.py:130
  65.8 2.6 %collective-permute-done.9 = f32[2,32,256]{2,1,0:T(8,128)S(1)} collective-permute-done((f32[2,32,256]{2,1,0:T(8,128)S(1)}, f32[2,32,256]{2,1,0:T(8,128)S(1)}, u32[]{:S(2)}, u32[]{:S(2)}) %collective-permute-start.9) | collective-permute-done | bytes 65568 | tf_op jit(solution)/shard_map/ppermute | solution.py:130
  68.4 0.1 collective-permute-start.10
  68.5 4.9 %collective-permute-done.10 = f32[2,2,32,256]{3,2,1,0:T(8,128)S(1)} collective-permute-done((f32[2,2,32,256]{3,2,1,0:T(8,128)S(1)}, f32[2,2,32,256]{3,2,1,0:T(8,128)S(1)}, u32[]{:S(2)}, u32[]{:S(2)}) %collective-permute-start.10) | collective-permute-done | bytes 131104 | tf_op jit(solution)/shard_map/ppermute | solution.py:130
  73.6 0.1 copy.83
  73.7 0.1 copy.82
  73.8 0.1 copy.81
  73.9 0.7 select_add_fusion.rw_ref
  74.6 0.6 collective-permute-done.11
  75.3 0.1 dynamic-slice_bitcast_fusion
  75.4 0.6 pad_maximum_fusion.4.back_ref
  76.1 16.0 %shard_map.87 = f32[16,16384]{1,0:T(8,128)} custom-call(f32[2,16,512]{2,1,0:T(8,128)} %pad_maximum_fusion.4.back_ref, f32[16,16384]{1,0:T(8,128)} %vol_ref.3, f32[2,16384]{1,0:T(2,128)} %amp_ref.3, s32[2,16384]{1,0:T(2,128)} %off_ref.3, s32[2,16384]{1,0:T(2,128)} %wid_ref.3, f32[2,16,1]{2,1,0:T(8,128)} %select_add_fusion.rw_ref), custom_call_target="tpu_custom_call" | custom-call | tf_op jit(solution)/shard_map/pallas_call | solution.py:94
  (51 shorter events, 0.8 us)
Async XLA Ops:
  30.3 0.7 copy-start
  30.5 0.8 copy-start.1
  30.5 1.7 %collective-permute-start.2 = (f32[2,2,2,34,256]{4,2,3,1,0:T(2,128)S(1)}, f32[2,2,2,34,256]{4,2,3,1,0:T(2,128)S(1)}, u32[]{:S(2)}, u32[]{:S(2)}) collective-permute-start(f32[2,2,2,34,256]{4,2,3,1,0:T(2,128)S(1)} %bitcast.110), channel_id=1, source_target_pairs={{0,2},{2,0},{4,6},{6,4},{8,10},{10,8},{12,14},{14,12},{16,18},{18,... | collective-permute-start | bytes 835592 | tf_op jit(solution)/shard_map/ppermute | solution.py:119
  32.7 8.8 %collective-permute-start.3 = (f32[2,2,34,256]{3,1,2,0:T(2,128)S(1)}, f32[2,2,34,256]{3,1,2,0:T(2,128)S(1)}, u32[]{:S(2)}, u32[]{:S(2)}) collective-permute-start(f32[2,2,34,256]{3,1,2,0:T(2,128)S(1)} %bitcast.111), channel_id=1, source_target_pairs={{0,4},{2,6},{4,0},{6,2},{8,12},{10,14},{12,8},{14,10},{16,20},{18,... | collective-permute-start | bytes 417800 | tf_op jit(solution)/shard_map/ppermute | solution.py:119
  35.6 13.5 %collective-permute-start.1 = (f32[2,2,256]{2,0,1:T(2,128)S(1)}, f32[2,2,256]{2,0,1:T(2,128)S(1)}, u32[]{:S(2)}, u32[]{:S(2)}) collective-permute-start(f32[2,2,256]{2,0,1:T(2,128)S(1)} %select_maximum_fusion), channel_id=1, source_target_pairs={{1,0},{3,2},{5,4},{7,6},{9,8},{11,10},{13,12},{15,14},{17,16},{19,... | collective-permute-start | bytes 12296 | tf_op jit(solution)/shard_map/ppermute | solution.py:161
  37.0 12.2 %collective-permute-start = (f32[2,2,256]{2,0,1:T(2,128)S(1)}, f32[2,2,256]{2,0,1:T(2,128)S(1)}, u32[]{:S(2)}, u32[]{:S(2)}) collective-permute-start(f32[2,2,256]{2,0,1:T(2,128)S(1)} %select_maximum_fusion.1), channel_id=1, source_target_pairs={{0,1},{2,3},{4,5},{6,7},{8,9},{10,11},{12,13},{14,15},{16,17},{18,... | collective-permute-start | bytes 12296 | tf_op jit(solution)/shard_map/ppermute | solution.py:158
  41.8 4.4 %collective-permute-start.4 = (f32[2,34,256]{2,0,1:T(2,128)S(1)}, f32[2,34,256]{2,0,1:T(2,128)S(1)}, u32[]{:S(2)}, u32[]{:S(2)}) collective-permute-start(f32[2,34,256]{2,0,1:T(2,128)S(1)} %bitcast.113), channel_id=1, source_target_pairs={{0,8},{2,10},{4,12},{6,14},{8,0},{10,2},{12,4},{14,6},{16,24},{18,... | collective-permute-start | bytes 208904 | tf_op jit(solution)/shard_map/ppermute | solution.py:119
  46.3 5.0 %collective-permute-start.5 = (f32[34,256]{1,0:T(8,128)S(1)}, f32[34,256]{1,0:T(8,128)S(1)}, u32[]{:S(2)}, u32[]{:S(2)}) collective-permute-start(f32[34,256]{1,0:T(8,128)S(1)} %bitcast.114), channel_id=1, source_target_pairs={{0,16},{2,18},{4,20},{6,22},{8,24},{10,26},{12,28},{14,30},{16,0},... | collective-permute-start | bytes 104456 | tf_op jit(solution)/shard_map/ppermute | solution.py:119
  51.3 6.0 %collective-permute-start.7 = (f32[2,2,256]{2,1,0:T(2,128)S(1)}, f32[2,2,256]{2,1,0:T(2,128)S(1)}, u32[]{:S(2)}, u32[]{:S(2)}) collective-permute-start(f32[2,2,256]{2,1,0:T(2,128)S(1)} %get-tuple-element.29), channel_id=1, source_target_pairs={{1,0},{3,2},{5,4},{7,6},{9,8},{11,10},{13,12},{15,14},{17,16},{19,... | collective-permute-start | bytes 12296 | tf_op jit(solution)/shard_map/ppermute | solution.py:179
  52.6 5.9 %collective-permute-start.6 = (f32[2,2,256]{2,1,0:T(2,128)S(1)}, f32[2,2,256]{2,1,0:T(2,128)S(1)}, u32[]{:S(2)}, u32[]{:S(2)}) collective-permute-start(f32[2,2,256]{2,1,0:T(2,128)S(1)} %get-tuple-element.28), channel_id=1, source_target_pairs={{0,1},{2,3},{4,5},{6,7},{8,9},{10,11},{12,13},{14,15},{16,17},{18,... | collective-permute-start | bytes 12296 | tf_op jit(solution)/shard_map/ppermute | solution.py:177
  59.2 4.8 %collective-permute-start.8 = (f32[32,256]{1,0:T(8,128)S(1)}, f32[32,256]{1,0:T(8,128)S(1)}, u32[]{:S(2)}, u32[]{:S(2)}) collective-permute-start(f32[32,256]{1,0:T(8,128)S(1)} %bitcast.112), channel_id=1, source_target_pairs={{0,16},{2,18},{4,20},{6,22},{8,24},{10,26},{12,28},{14,30},{16,0},... | collective-permute-start | bytes 98312 | tf_op jit(solution)/shard_map/ppermute | solution.py:130
  64.1 4.3 %collective-permute-start.9 = (f32[2,32,256]{2,1,0:T(8,128)S(1)}, f32[2,32,256]{2,1,0:T(8,128)S(1)}, u32[]{:S(2)}, u32[]{:S(2)}) collective-permute-start(f32[2,32,256]{2,1,0:T(8,128)S(1)} %pad_maximum_fusion.3), channel_id=1, source_target_pairs={{0,8},{2,10},{4,12},{6,14},{8,0},{10,2},{12,4},{14,6},{16,24},{18,... | collective-permute-start | bytes 196616 | tf_op jit(solution)/shard_map/ppermute | solution.py:130
  68.4 5.0 %collective-permute-start.10 = (f32[2,2,32,256]{3,2,1,0:T(8,128)S(1)}, f32[2,2,32,256]{3,2,1,0:T(8,128)S(1)}, u32[]{:S(2)}, u32[]{:S(2)}) collective-permute-start(f32[2,2,32,256]{3,2,1,0:T(8,128)S(1)} %pad_maximum_fusion.2), channel_id=1, source_target_pairs={{0,4},{2,6},{4,0},{6,2},{8,12},{10,14},{12,8},{14,10},{16,20},{18,... | collective-permute-start | bytes 393224 | tf_op jit(solution)/shard_map/ppermute | solution.py:130
  73.5 1.6 %collective-permute-start.11 = (f32[2,2,2,32,256]{4,3,2,1,0:T(8,128)S(1)}, f32[2,2,2,32,256]{4,3,2,1,0:T(8,128)S(1)}, u32[]{:S(2)}, u32[]{:S(2)}) collective-permute-start(f32[2,2,2,32,256]{4,3,2,1,0:T(8,128)S(1)} %pad_maximum_fusion.1), channel_id=1, source_target_pairs={{0,2},{2,0},{4,6},{6,4},{8,10},{10,8},{12,14},{14,12},{16,18},{18,... | collective-permute-start | bytes 786440 | tf_op jit(solution)/shard_map/ppermute | solution.py:130

commit v4 on v3

--- a/solution.py
+++ b/solution.py
@@ -105,22 +105,7 @@
     return bits
 
 
-def reduce_scatter_xy(x, count):
-    rows = x.shape[0]
-    width = x.shape[1] // count
-    bits = _bit_count(count)
-    idx = lax.axis_index("xy")
-    y = jnp.transpose(x.reshape(rows, count, width), (1, 0, 2)).reshape((2,) * bits + (rows, width))
-    for j in range(bits):
-        axis = bits - 1 - j
-        bit = (idx >> j) & 1
-        keep = lax.dynamic_index_in_dim(y, bit, axis, keepdims=False)
-        send = lax.dynamic_index_in_dim(y, 1 - bit, axis, keepdims=False)
-        y = keep + lax.ppermute(send, "xy", [(i, i ^ (1 << j)) for i in range(count)])
-    return y
-
-
-def all_gather_xy(x, count):
+def all_gather_tiles(x, count):
     rows, width = x.shape
     bits = _bit_count(count)
     idx = lax.axis_index("xy")
@@ -131,7 +116,21 @@
         low = jnp.where(bit == 0, y, other)
         high = jnp.where(bit == 0, other, y)
         y = jnp.stack([low, high], axis=step)
-    return jnp.transpose(y.reshape(count, rows, width), (1, 0, 2)).reshape(rows, count * width)
+    return y.reshape(count, rows, width)
+
+
+def window_sum(bands, starts, positions, width):
+    tiles, views, rows, band = bands.shape
+    padded = jnp.pad(bands, ((0, 0), (0, 0), (0, 0), (width, width)))
+    out = []
+    for v in range(views):
+        total = None
+        for t in range(tiles):
+            shift = jnp.clip(positions[v] - starts[t, v] + width, 0, band + width)
+            piece = lax.dynamic_slice(padded[t, v], (jnp.int32(0), shift), (rows, width))
+            total = piece if total is None else total + piece
+        out.append(total)
+    return jnp.stack(out)
 
 
 def local(volume, measured, band_start, column_offset, column_width, amplitude, axial_weight):
@@ -145,6 +144,7 @@
     first_row = lax.axis_index("gz") * slab_rows
     up_pairs = [(i, i + 1) for i in range(gz_count - 1)]
     down_pairs = [(i + 1, i) for i in range(gz_count - 1)]
+    ext_rows = slab_rows + 2
 
     def pack(meas_rows, weight_cols):
         flat = jnp.transpose(weight_cols, (1, 0, 2)).reshape(view_count, 1, -1)
@@ -163,51 +163,54 @@
     meas_above, weight_above = unpack(from_above)
     measured_ext = jnp.concatenate([meas_below, measured, meas_above], axis=1)
     weight_ext = jnp.concatenate([weight_below, axial_weight, weight_above], axis=2)
+    meas_tiles = all_gather_tiles(measured_ext.reshape(view_count * ext_rows, shard_width), xy_count)
+    meas_full = jnp.transpose(meas_tiles, (1, 0, 2)).reshape(view_count, ext_rows, detector_width)
 
     band_rows = forward_band(volume, amplitude, column_offset, column_width)
     band_height = slab_rows + 1
-    placed = jnp.zeros((view_count * band_height, detector_width), jnp.float32)
-    for v in range(view_count):
-        placed = lax.dynamic_update_slice(placed, band_rows[v], (jnp.int32(v * band_height), band_start[v, 0]))
-    reduced = reduce_scatter_xy(placed, xy_count).reshape(view_count, band_height, shard_width)
-    proj_cols = reduced[:, :slab_rows]
-    cover = reduced[:, slab_rows : slab_rows + 1]
-    proj_ext = jnp.concatenate(
-        [
-            lax.ppermute(proj_cols[:, slab_rows - 2 :], "gz", up_pairs),
-            proj_cols,
-            lax.ppermute(proj_cols[:, :2], "gz", down_pairs),
-        ],
-        axis=1,
-    )
-
-    ext_rows = slab_rows + 2
+    start_row = jnp.pad(band_start[:, 0].astype(jnp.float32), (0, B - view_count))[None]
+    payload = jnp.concatenate([band_rows.reshape(view_count * band_height, B), start_row], axis=0)
+    gathered = all_gather_tiles(payload, xy_count)
+    starts = gathered[:, view_count * band_height, :view_count].astype(jnp.int32)
+    bands = gathered[:, : view_count * band_height].reshape(xy_count, view_count, band_height, B)
+    my_start = [band_start[v, 0] for v in range(view_count)]
+    shard_pos = lax.axis_index("xy") * shard_width
+    band_win = window_sum(bands, starts, my_start, B)
+    shard_win = window_sum(bands, starts, [shard_pos] * view_count, shard_width)
+
+    edge_up = jnp.concatenate([band_win[:, slab_rows - 2 : slab_rows], shard_win[:, slab_rows - 2 : slab_rows]], axis=2)
+    edge_down = jnp.concatenate([band_win[:, :2], shard_win[:, :2]], axis=2)
+    halo_below = lax.ppermute(edge_up, "gz", up_pairs)
+    halo_above = lax.ppermute(edge_down, "gz", down_pairs)
+
     mid_w = weight_ext[1, :, 1 : ext_rows + 1][:, :, None]
     next_w = weight_ext[0, :, 2 : ext_rows + 2][:, :, None]
     prev_w = weight_ext[2, :, 0:ext_rows][:, :, None]
-    centre = proj_ext[:, 1 : ext_rows + 1]
-    after = proj_ext[:, 2 : ext_rows + 2]
-    before = proj_ext[:, 0:ext_rows]
-    projection = mid_w * centre + next_w * after + prev_w * before
-    coverage = mid_w * cover + next_w * cover + prev_w * cover
-    residual_ext = (measured_ext - projection) / jnp.maximum(coverage, 1.0)
     global_rows = first_row - 1 + jnp.arange(ext_rows, dtype=jnp.int32)
     valid = (global_rows >= 0) & (global_rows < total_rows)
-    residual_ext = jnp.where(valid[None, :, None], residual_ext, 0.0)
-    residual = residual_ext[:, 1 : slab_rows + 1]
-
-    back_rows = (
-        axial_weight[0][:, :, None] * residual_ext[:, 0:slab_rows]
-        + axial_weight[1][:, :, None] * residual
-        + axial_weight[2][:, :, None] * residual_ext[:, 2 : slab_rows + 2]
-    )
-    back_full = all_gather_xy(back_rows.reshape(view_count * slab_rows, shard_width), xy_count)
-    back_full = back_full.reshape(view_count, slab_rows, detector_width)
-    back_band = jnp.stack(
-        [
-            lax.dynamic_slice(back_full[v], (jnp.int32(0), band_start[v, 0]), (slab_rows, B))
-            for v in range(view_count)
-        ]
+
+    def residual_rows(win, lo, hi, meas_ext):
+        proj_ext = jnp.concatenate(
+            [halo_below[:, :, lo:hi], win[:, :slab_rows], halo_above[:, :, lo:hi]], axis=1
+        )
+        cover = win[:, slab_rows : slab_rows + 1]
+        centre = proj_ext[:, 1 : ext_rows + 1]
+        after = proj_ext[:, 2 : ext_rows + 2]
+        before = proj_ext[:, 0:ext_rows]
+        projection = mid_w * centre + next_w * after + prev_w * before
+        coverage = mid_w * cover + next_w * cover + prev_w * cover
+        res = (meas_ext - projection) / jnp.maximum(coverage, 1.0)
+        return jnp.where(valid[None, :, None], res, 0.0)
+
+    residual = residual_rows(shard_win, B, B + shard_width, measured_ext)[:, 1 : slab_rows + 1]
+    meas_band = jnp.stack(
+        [lax.dynamic_slice(meas_full[v], (jnp.int32(0), my_start[v]), (ext_rows, B)) for v in range(view_count)]
+    )
+    res_band = residual_rows(band_win, 0, B, meas_band)
+    back_band = (
+        axial_weight[0][:, :, None] * res_band[:, 0:slab_rows]
+        + axial_weight[1][:, :, None] * res_band[:, 1 : slab_rows + 1]
+        + axial_weight[2][:, :, None] * res_band[:, 2 : slab_rows + 2]
     )
 
     own_rows = first_row + jnp.arange(slab_rows, dtype=jnp.int32)

time: 92.5 us -> 164 us (1.77)
  between operations: 4.69 us -> 65.9 us
  local copies, waits for them, and re-layouts: 7.26 us -> 17.9 us
  other arithmetic: 3.64 us -> 9.19 us
  waiting for transfers between devices: 16.8 us -> 12.7 us
  starting transfers between devices: 24.2 us -> 21.3 us
    slice x4 -> x19, local copies, waits for them, and re-layouts: 1.33 us -> 11.5 us  [the longest x4 5.08 us: window_sum(): padded[t, v]]
    add x6, other arithmetic: 1.05 us -> 6.14 us  [the longest x4 5.36 us: window_sum(): total = piece if total is None else total + piece]
    ppermute x10, waiting for transfers between devices: 16.8 us -> 12.7 us  [the longest x8 11.4 us: all_gather_tiles(): other = lax.ppermute(y, 'xy', [(i, i ^ 1 << j) for i in range(count)])]
    dynamic_update_slice x2 -> x0, local copies, waits for them, and re-layouts: 3.06 us -> none  [local(): lax.dynamic_update_slice(placed, band_rows[v], (jnp.int32(v * band_height...]
    ppermute x10, starting transfers between devices: 18.4 us -> 15.5 us  [the longest x8 9.66 us: all_gather_tiles(): other = lax.ppermute(y, 'xy', [(i, i ^ 1 << j) for i in range(count)])]
    another operation x1 -> x4, local copies, waits for them, and re-layouts: 0.09 us -> 2.53 us  [the longest x3 1.79 us: all_gather_tiles(): y = jnp.stack([low, high], axis=step)]
  transfers between devices with their start and end apart: 12 -> 12, of which waited for: 8 -> 6; matrix products, arithmetic and copies ran while one was open for 2% -> 6% of each run, Pallas kernels for 0% -> 0%
where the time goes in v4:
time: 164 us; the launch traced here: 162 us
  between operations  65.9 us (40%)
  Pallas kernels  35.4 us (22%)
  starting transfers between devices  21.3 us (13%)
  local copies, waits for them, and re-layouts  17.9 us (11%)
  waiting for transfers between devices  12.7 us (8%)
  other arithmetic  9.19 us (6%)
    pallas_call x1, Pallas kernels, forward_band(): pl.pallas_call(_forward_kernel, out_shape=jax.ShapeDtypeStruct((view_coun...  19.4 us
    pallas_call x1, Pallas kernels, backward_update(): pl.pallas_call(_backward_kernel, out_shape=jax.ShapeDtypeStruct(volume.sh...  16 us
    ppermute x8, waiting for transfers between devices, all_gather_tiles(): other = lax.ppermute(y, 'xy', [(i, i ^ 1 << j) for i in range(count)])  11.4 us
    ppermute x8, starting transfers between devices, all_gather_tiles(): other = lax.ppermute(y, 'xy', [(i, i ^ 1 << j) for i in range(count)])  9.66 us
    add x4, other arithmetic, window_sum(): total = piece if total is None else total + piece  5.36 us
    slice x4, local copies, waits for them, and re-layouts, window_sum(): padded[t, v]  5.08 us
    ppermute x1, starting transfers between devices, local(): halo_below = lax.ppermute(edge_up, 'gz', up_pairs)  4.54 us
    ppermute x1, starting transfers between devices, local(): lax.ppermute(pack(measured[:, slab_rows - 1:], axial_weight[:, :, slab_ro...  4.54 us
  transfers between devices with their start and end apart: 12, of which 6 were waited for; matrix products, arithmetic and copies ran while one was open for 6% of the time, Pallas kernels for 0%

profile of v4, /device:TPU:0, one launch (start us, length us, event | category | flops | bytes accessed | tf_op | source)
XLA Modules:
  0.0 162.4 jit_solution(13245521823873850631)
XLA Ops:
  0.7 0.7 convert_bitcast_fusion
  1.4 19.4 %shard_map.86 = f32[2,64,512]{2,1,0:T(8,128)} custom-call(f32[16,16384]{1,0:T(8,128)} %vol_ref.3, f32[2,16384]{1,0:T(2,128)} %amp_ref.3, s32[2,16384]{1,0:T(2,128)} %off_ref.3, s32[2,16384]{1,0:T(2,128)} %wid_ref.3), custom_call_target="tpu_custom_call" | custom-call | tf_op jit(solution)/shard_map/pallas_call | solution.py:55
  20.8 1.0 fusion.32
  21.8 4.1 %collective-permute-start.6 = (f32[35,512]{1,0:T(8,128)S(1)}, f32[35,512]{1,0:T(8,128)S(1)}, u32[]{:S(2)}, u32[]{:S(2)}) collective-permute-start(f32[35,512]{1,0:T(8,128)S(1)} %pad_maximum_fusion.10), channel_id=1, source_target_pairs={{0,16},{2,18},{4,20},{6,22},{8,24},{10,26},{12,28},{14,30},{16,0},... | collective-permute-start | bytes 215048 | tf_op jit(solution)/shard_map/ppermute | solution.py:115
  26.1 1.3 collective-permute-start.1
  27.5 4.5 %collective-permute-start = (f32[2,2,256]{2,1,0:T(2,128)S(1)}, f32[2,2,256]{2,1,0:T(2,128)S(1)}, u32[]{:S(2)}, u32[]{:S(2)}) collective-permute-start(f32[2,2,256]{2,1,0:T(2,128)S(1)} %select_maximum_fusion.1), channel_id=1, source_target_pairs={{0,1},{2,3},{4,5},{6,7},{8,9},{10,11},{12,13},{14,15},{16,17},{18,... | collective-permute-start | bytes 12296 | tf_op jit(solution)/shard_map/ppermute | solution.py:158
  32.1 0.6 fusion.36
  32.7 0.6 slice_bitcast_fusion.6
  33.6 0.7 select_add_fusion.rw_ref
  36.8 0.6 slice.628
  39.1 0.7 slice.626
  39.8 0.7 slice.625
  40.4 0.6 slice.622
  41.1 0.6 slice.620
  41.7 2.0 %collective-permute-done.2 = f32[36,256]{1,0:T(8,128)S(1)} collective-permute-done((f32[36,256]{1,0:T(8,128)S(1)}, f32[36,256]{1,0:T(8,128)S(1)}, u32[]{:S(2)}, u32[]{:S(2)}) %collective-permute-start.2) | collective-permute-done | bytes 36896 | tf_op jit(solution)/shard_map/ppermute | solution.py:115
  43.7 1.6 %collective-permute-start.3 = (f32[2,36,256]{2,1,0:T(8,128)S(1)}, f32[2,36,256]{2,1,0:T(8,128)S(1)}, u32[]{:S(2)}, u32[]{:S(2)}) collective-permute-start(f32[2,36,256]{2,1,0:T(8,128)S(1)} %pad_maximum_fusion.9), channel_id=1, source_target_pairs={{0,8},{2,10},{4,12},{6,14},{8,0},{10,2},{12,4},{14,6},{16,24},{18,... | collective-permute-start | bytes 221192 | tf_op jit(solution)/shard_map/ppermute | solution.py:115
  45.4 0.5 collective-permute-start.7
  45.9 2.3 %collective-permute-done.3 = f32[2,36,256]{2,1,0:T(8,128)S(1)} collective-permute-done((f32[2,36,256]{2,1,0:T(8,128)S(1)}, f32[2,36,256]{2,1,0:T(8,128)S(1)}, u32[]{:S(2)}, u32[]{:S(2)}) %collective-permute-start.3) | collective-permute-done | bytes 73760 | tf_op jit(solution)/shard_map/ppermute | solution.py:115
  48.3 1.6 collective-permute-start.4
  49.9 0.9 collective-permute-done.7
  50.9 1.6 collective-permute-start.8
  52.4 2.8 %collective-permute-done.4 = f32[2,2,36,256]{3,2,0,1:T(8,128)S(1)} collective-permute-done((f32[2,2,36,256]{3,2,0,1:T(8,128)S(1)}, f32[2,2,36,256]{3,2,0,1:T(8,128)S(1)}, u32[]{:S(2)}, u32[]{:S(2)}) %collective-permute-start.4) | collective-permute-done | bytes 147488 | tf_op jit(solution)/shard_map/ppermute | solution.py:115
  55.3 3.4 %collective-permute-done.8 = f32[2,2,35,512]{3,2,0,1:T(8,128)S(1)} collective-permute-done((f32[2,2,35,512]{3,2,0,1:T(8,128)S(1)}, f32[2,2,35,512]{3,2,0,1:T(8,128)S(1)}, u32[]{:S(2)}, u32[]{:S(2)}) %collective-permute-start.8) | collective-permute-done | bytes 286752 | tf_op jit(solution)/shard_map/ppermute | solution.py:115
  58.8 0.4 copy.64
  59.5 0.5 copy.61
  60.0 0.4 reshape.837
  60.5 0.2 copy.80
  60.7 0.2 copy.79
  61.0 0.7 dynamic-slice_bitcast_fusion
  62.0 0.9 copy.67
  62.9 0.8 reshape.839
  63.9 0.7 copy.68
  64.6 1.2 pad_slice_fusion.44
  65.7 1.4 pad_slice_fusion.63
  67.2 0.7 fusion.34
  67.9 0.7 fusion.35
  68.6 1.4 pad_slice_fusion.11
  91.9 1.1 pad_slice_fusion.15
  131.7 1.5 add_bitcast_fusion
  133.3 1.2 add_bitcast_fusion.1
  134.8 1.3 add_bitcast_fusion.2
  136.1 1.3 add_bitcast_fusion.3
  137.5 1.3 collective-permute-start.11
  138.8 4.5 %collective-permute-start.10 = (f32[2,2,768]{2,1,0:T(2,128)S(1)}, f32[2,2,768]{2,1,0:T(2,128)S(1)}, u32[]{:S(2)}, u32[]{:S(2)}) collective-permute-start(f32[2,2,768]{2,1,0:T(2,128)S(1)} %get-tuple-element.90), channel_id=1, source_target_pairs={{0,1},{2,3},{4,5},{6,7},{8,9},{10,11},{12,13},{14,15},{16,17},{18,... | collective-permute-start | bytes 36872 | tf_op jit(solution)/shard_map/ppermute | solution.py:183
  143.4 1.3 collective-permute-done.10
  144.9 0.7 fusion.9.back_ref
  145.6 16.0 %shard_map.87 = f32[16,16384]{1,0:T(8,128)} custom-call(f32[2,16,512]{2,1,0:T(8,128)} %fusion.9.back_ref, f32[16,16384]{1,0:T(8,128)} %vol_ref.3, f32[2,16384]{1,0:T(2,128)} %amp_ref.3, s32[2,16384]{1,0:T(2,128)} %off_ref.3, s32[2,16384]{1,0:T(2,128)} %wid_ref.3, f32[2,16,1]{2,1,0:T(8,128)} %select_add_fusion.rw_ref), custom_call_target="tpu_custom_call" | custom-call | tf_op jit(solution)/shard_map/pallas_call | solution.py:94
  161.7 0.7 fusion.19
  (102 shorter events, 2.4 us)
Async XLA Ops:
  0.6 31.5 %copy-start.11 = (s32[2,1]{0,1:T(1,128)S(1)}, s32[2,1]{0,1:T(1,128)}, u32[]{:S(2)}) copy-start(s32[2,1]{0,1:T(1,128)} %param.9) | copy-start | bytes 28
  0.6 25.3 %copy-start.2 = (f32[3,2,16]{2,1,0:T(2,128)S(1)}, f32[3,2,16]{2,1,0:T(2,128)}, u32[]{:S(2)}) copy-start(f32[3,2,16]{2,1,0:T(2,128)} %param.13) | copy-start | bytes 1156
  0.7 25.5 %copy-start.3 = (f32[2,16,256]{2,1,0:T(8,128)S(1)}, f32[2,16,256]{2,1,0:T(8,128)}, u32[]{:S(2)}) copy-start(f32[2,16,256]{2,1,0:T(8,128)} %param.8) | copy-start | bytes 98308
  21.8 23.5 %collective-permute-start.6 = (f32[35,512]{1,0:T(8,128)S(1)}, f32[35,512]{1,0:T(8,128)S(1)}, u32[]{:S(2)}, u32[]{:S(2)}) collective-permute-start(f32[35,512]{1,0:T(8,128)S(1)} %pad_maximum_fusion.10), channel_id=1, source_target_pairs={{0,16},{2,18},{4,20},{6,22},{8,24},{10,26},{12,28},{14,30},{16,0},... | collective-permute-start | bytes 215048 | tf_op jit(solution)/shard_map/ppermute | solution.py:115
  26.1 12.5 %collective-permute-start.1 = (f32[2,2,256]{2,1,0:T(2,128)S(1)}, f32[2,2,256]{2,1,0:T(2,128)S(1)}, u32[]{:S(2)}, u32[]{:S(2)}) collective-permute-start(f32[2,2,256]{2,1,0:T(2,128)S(1)} %select_maximum_fusion), channel_id=1, source_target_pairs={{1,0},{3,2},{5,4},{7,6},{9,8},{11,10},{13,12},{15,14},{17,16},{19,... | collective-permute-start | bytes 12296 | tf_op jit(solution)/shard_map/ppermute | solution.py:161
  27.5 11.1 %collective-permute-start = (f32[2,2,256]{2,1,0:T(2,128)S(1)}, f32[2,2,256]{2,1,0:T(2,128)S(1)}, u32[]{:S(2)}, u32[]{:S(2)}) collective-permute-start(f32[2,2,256]{2,1,0:T(2,128)S(1)} %select_maximum_fusion.1), channel_id=1, source_target_pairs={{0,1},{2,3},{4,5},{6,7},{8,9},{10,11},{12,13},{14,15},{16,17},{18,... | collective-permute-start | bytes 12296 | tf_op jit(solution)/shard_map/ppermute | solution.py:158
  34.2 4.4 %copy-start.12 = (pred[18]{0:T(512)(128)(4,1)}, pred[18]{0:T(512)(128)(4,1)S(1)}, u32[]{:S(2)}) copy-start(pred[18]{0:T(512)(128)(4,1)S(1)} %compare_and_fusion) | copy-start | bytes 58
  38.7 5.0 %collective-permute-start.2 = (f32[36,256]{1,0:T(8,128)S(1)}, f32[36,256]{1,0:T(8,128)S(1)}, u32[]{:S(2)}, u32[]{:S(2)}) collective-permute-start(f32[36,256]{1,0:T(8,128)S(1)} %reshape.836), channel_id=1, source_target_pairs={{0,16},{2,18},{4,20},{6,22},{8,24},{10,26},{12,28},{14,30},{16,0},... | collective-permute-start | bytes 110600 | tf_op jit(solution)/shard_map/ppermute | solution.py:115
  43.7 4.5 %collective-permute-start.3 = (f32[2,36,256]{2,1,0:T(8,128)S(1)}, f32[2,36,256]{2,1,0:T(8,128)S(1)}, u32[]{:S(2)}, u32[]{:S(2)}) collective-permute-start(f32[2,36,256]{2,1,0:T(8,128)S(1)} %pad_maximum_fusion.9), channel_id=1, source_target_pairs={{0,8},{2,10},{4,12},{6,14},{8,0},{10,2},{12,4},{14,6},{16,24},{18,... | collective-permute-start | bytes 221192 | tf_op jit(solution)/shard_map/ppermute | solution.py:115
  45.4 5.4 %collective-permute-start.7 = (f32[2,35,512]{2,1,0:T(8,128)S(1)}, f32[2,35,512]{2,1,0:T(8,128)S(1)}, u32[]{:S(2)}, u32[]{:S(2)}) collective-permute-start(f32[2,35,512]{2,1,0:T(8,128)S(1)} %pad_maximum_fusion.6), channel_id=1, source_target_pairs={{0,8},{2,10},{4,12},{6,14},{8,0},{10,2},{12,4},{14,6},{16,24},{18,... | collective-permute-start | bytes 430088 | tf_op jit(solution)/shard_map/ppermute | solution.py:115
  48.3 6.9 %collective-permute-start.4 = (f32[2,2,36,256]{3,2,0,1:T(8,128)S(1)}, f32[2,2,36,256]{3,2,0,1:T(8,128)S(1)}, u32[]{:S(2)}, u32[]{:S(2)}) collective-permute-start(f32[2,2,36,256]{3,2,0,1:T(8,128)S(1)} %pad_maximum_fusion.5), channel_id=1, source_target_pairs={{0,4},{2,6},{4,0},{6,2},{8,12},{10,14},{12,8},{14,10},{16,20},{18,... | collective-permute-start | bytes 442376 | tf_op jit(solution)/shard_map/ppermute | solution.py:115
  50.9 7.9 %collective-permute-start.8 = (f32[2,2,35,512]{3,2,0,1:T(8,128)S(1)}, f32[2,2,35,512]{3,2,0,1:T(8,128)S(1)}, u32[]{:S(2)}, u32[]{:S(2)}) collective-permute-start(f32[2,2,35,512]{3,2,0,1:T(8,128)S(1)} %pad_maximum_fusion.4), channel_id=1, source_target_pairs={{0,4},{2,6},{4,0},{6,2},{8,12},{10,14},{12,8},{14,10},{16,20},{18,... | collective-permute-start | bytes 860168 | tf_op jit(solution)/shard_map/ppermute | solution.py:115
  55.3 4.1 %collective-permute-start.5 = (f32[2,2,2,36,256]{4,3,0,1,2:T(8,128)S(1)}, f32[2,2,2,36,256]{4,3,0,1,2:T(8,128)S(1)}, u32[]{:S(2)}, u32[]{:S(2)}) collective-permute-start(f32[2,2,2,36,256]{4,3,0,1,2:T(8,128)S(1)} %pad_maximum_fusion.3), channel_id=1, source_target_pairs={{0,2},{2,0},{4,6},{6,4},{8,10},{10,8},{12,14},{14,12},{16,18},{18,... | collective-permute-start | bytes 884744 | tf_op jit(solution)/shard_map/ppermute | solution.py:115
  59.3 2.4 %collective-permute-start.9 = (f32[2,2,2,35,512]{4,2,3,1,0:T(2,128)S(1)}, f32[2,2,2,35,512]{4,2,3,1,0:T(2,128)S(1)}, u32[]{:S(2)}, u32[]{:S(2)}) collective-permute-start(f32[2,2,2,35,512]{4,2,3,1,0:T(2,128)S(1)} %copy.64), channel_id=1, source_target_pairs={{0,2},{2,0},{4,6},{6,4},{8,10},{10,8},{12,14},{14,12},{16,18},{18,... | collective-permute-start | bytes 1720328 | tf_op jit(solution)/shard_map/ppermute | solution.py:115
  131.7 13.0 %copy-start = (f32[1,18,512]{2,1,0:T(8,128)S(1)}, f32[1,18,512]{2,1,0:T(8,128)}, u32[]{:S(2)}) copy-start(f32[1,18,512]{2,1,0:T(8,128)} %get-tuple-element.140) | copy-start | bytes 110596
  131.7 13.0 %copy-start.1 = (f32[1,18,512]{2,1,0:T(8,128)S(1)}, f32[1,18,512]{2,1,0:T(8,128)}, u32[]{:S(2)}) copy-start(f32[1,18,512]{2,1,0:T(8,128)} %get-tuple-element.141) | copy-start | bytes 110596
  131.7 13.0 %copy-start.13 = (pred[18]{0:T(512)(128)(4,1)S(1)}, pred[18]{0:T(512)(128)(4,1)}, u32[]{:S(2)}) copy-start(pred[18]{0:T(512)(128)(4,1)} %copy-done.12) | copy-start | bytes 58
  133.3 11.6 %copy-start.4 = (f32[2,16]{1,0:T(2,128)S(1)}, f32[2,16]{1,0:T(2,128)}, u32[]{:S(2)}) copy-start(f32[2,16]{1,0:T(2,128)} %get-tuple-element.97) | copy-start | bytes 388
  133.3 11.6 %copy-start.5 = (f32[2,16]{1,0:T(2,128)S(1)}, f32[2,16]{1,0:T(2,128)}, u32[]{:S(2)}) copy-start(f32[2,16]{1,0:T(2,128)} %get-tuple-element.98) | copy-start | bytes 388
  133.3 11.6 %copy-start.6 = (f32[2,16]{1,0:T(2,128)S(1)}, f32[2,16]{1,0:T(2,128)}, u32[]{:S(2)}) copy-start(f32[2,16]{1,0:T(2,128)} %get-tuple-element.99) | copy-start | bytes 388
  137.5 5.9 %collective-permute-start.11 = (f32[2,2,768]{2,1,0:T(2,128)S(1)}, f32[2,2,768]{2,1,0:T(2,128)S(1)}, u32[]{:S(2)}, u32[]{:S(2)}) collective-permute-start(f32[2,2,768]{2,1,0:T(2,128)S(1)} %get-tuple-element.91), channel_id=1, source_target_pairs={{1,0},{3,2},{5,4},{7,6},{9,8},{11,10},{13,12},{15,14},{17,16},{19,... | collective-permute-start | bytes 36872 | tf_op jit(solution)/shard_map/ppermute | solution.py:184
  138.8 5.9 %collective-permute-start.10 = (f32[2,2,768]{2,1,0:T(2,128)S(1)}, f32[2,2,768]{2,1,0:T(2,128)S(1)}, u32[]{:S(2)}, u32[]{:S(2)}) collective-permute-start(f32[2,2,768]{2,1,0:T(2,128)S(1)} %get-tuple-element.90), channel_id=1, source_target_pairs={{0,1},{2,3},{4,5},{6,7},{8,9},{10,11},{12,13},{14,15},{16,17},{18,... | collective-permute-start | bytes 36872 | tf_op jit(solution)/shard_map/ppermute | solution.py:183
  144.7 16.9 %copy-start.7 = (f32[2,16]{1,0:T(2,128)S(1)}, f32[2,16]{1,0:T(2,128)}, u32[]{:S(2)}) copy-start(f32[2,16]{1,0:T(2,128)} %slice.626) | copy-start | bytes 388
  144.7 16.9 %copy-start.8 = (f32[2,16]{1,0:T(2,128)S(1)}, f32[2,16]{1,0:T(2,128)}, u32[]{:S(2)}) copy-start(f32[2,16]{1,0:T(2,128)} %slice.625) | copy-start | bytes 388
  144.7 16.9 %copy-start.9 = (f32[2,16]{1,0:T(2,128)S(1)}, f32[2,16]{1,0:T(2,128)}, u32[]{:S(2)}) copy-start(f32[2,16]{1,0:T(2,128)} %slice.622) | copy-start | bytes 388
  144.8 16.9 %copy-start.10 = (f32[2,16]{1,0:T(2,128)S(1)}, f32[2,16]{1,0:T(2,128)}, u32[]{:S(2)}) copy-start(f32[2,16]{1,0:T(2,128)} %slice.620) | copy-start | bytes 388
  144.8 16.9 %copy-start.14 = (pred[16]{0:T(512)(128)(4,1)S(1)}, pred[16]{0:T(512)(128)(4,1)}, u32[]{:S(2)}) copy-start(pred[16]{0:T(512)(128)(4,1)} %slice.628) | copy-start | bytes 52

commit v5 on v4

--- a/solution.py
+++ b/solution.py
@@ -55,6 +55,11 @@
     acc = pl.pallas_call(
         _forward_kernel,
         out_shape=jax.ShapeDtypeStruct((view_count, 4 * slab_rows, B), jnp.float32),
+        cost_estimate=pl.CostEstimate(
+            flops=2 * view_count * 4 * slab_rows * B * volume.shape[1],
+            transcendentals=0,
+            bytes_accessed=4 * (volume.size + 3 * amplitude.size),
+        ),
         interpret=INTERPRET,
     )(volume, amplitude, column_offset, column_width)
     summed = acc[:, : 2 * slab_rows] + acc[:, 2 * slab_rows :]
@@ -95,6 +100,11 @@
         _backward_kernel,
         out_shape=jax.ShapeDtypeStruct(volume.shape, jnp.float32),
         scratch_shapes=[pltpu.VMEM((view_count, 2 * slab_rows, band), jnp.bfloat16)],
+        cost_estimate=pl.CostEstimate(
+            flops=2 * view_count * 2 * slab_rows * band * volume.shape[1],
+            transcendentals=0,
+            bytes_accessed=4 * (2 * volume.size + 3 * amplitude.size),
+        ),
         interpret=INTERPRET,
     )(back_band, volume, amplitude, column_offset, column_width, row_weight[:, :, None])
 
@@ -119,18 +129,37 @@
     return y.reshape(count, rows, width)
 
 
-def window_sum(bands, starts, positions, width):
+def _window_kernel(starts_ref, spots_ref, bands_ref, band_out, shard_out):
+    tiles, views, rows, band = bands_ref.shape
+    for out_ref, slot in ((band_out, 0), (shard_out, 1)):
+        width = out_ref.shape[2]
+        length = band + 2 * width
+        gap = jnp.zeros((rows, width), jnp.float32)
+        for v in range(views):
+            spot = spots_ref[slot, v]
+            total = None
+            for t in range(tiles):
+                shift = jnp.clip(spot - starts_ref[t, v] + width, 0, band + width)
+                ext = jnp.concatenate([gap, bands_ref[t, v], gap], axis=1)
+                rolled = pltpu.roll(ext, (length - shift) % length, 1)
+                piece = rolled[:, :width]
+                total = piece if total is None else total + piece
+            out_ref[v] = total
+
+
+def window_sums(bands, starts, band_spots, shard_spot, shard_width):
     tiles, views, rows, band = bands.shape
-    padded = jnp.pad(bands, ((0, 0), (0, 0), (0, 0), (width, width)))
-    out = []
-    for v in range(views):
-        total = None
-        for t in range(tiles):
-            shift = jnp.clip(positions[v] - starts[t, v] + width, 0, band + width)
-            piece = lax.dynamic_slice(padded[t, v], (jnp.int32(0), shift), (rows, width))
-            total = piece if total is None else total + piece
-        out.append(total)
-    return jnp.stack(out)
+    spots = jnp.stack([jnp.stack(band_spots), jnp.stack([shard_spot] * views)]).astype(jnp.int32)
+    smem = pl.BlockSpec(memory_space=pltpu.SMEM)
+    return pl.pallas_call(
+        _window_kernel,
+        out_shape=(
+            jax.ShapeDtypeStruct((views, rows, band), jnp.float32),
+            jax.ShapeDtypeStruct((views, rows, shard_width), jnp.float32),
+        ),
+        in_specs=[smem, smem, pl.BlockSpec(memory_space=pltpu.VMEM)],
+        interpret=INTERPRET,
+    )(starts, spots, bands)
 
 
 def local(volume, measured, band_start, column_offset, column_width, amplitude, axial_weight):
@@ -175,8 +204,7 @@
     bands = gathered[:, : view_count * band_height].reshape(xy_count, view_count, band_height, B)
     my_start = [band_start[v, 0] for v in range(view_count)]
     shard_pos = lax.axis_index("xy") * shard_width
-    band_win = window_sum(bands, starts, my_start, B)
-    shard_win = window_sum(bands, starts, [shard_pos] * view_count, shard_width)
+    band_win, shard_win = window_sums(bands, starts, my_start, shard_pos, shard_width)
 
     edge_up = jnp.concatenate([band_win[:, slab_rows - 2 : slab_rows], shard_win[:, slab_rows - 2 : slab_rows]], axis=2)
     edge_down = jnp.concatenate([band_win[:, :2], shard_win[:, :2]], axis=2)

time: 164 us -> 100 us (0.61)
  between operations: 65.9 us -> 5.12 us
  other arithmetic: 9.19 us -> 5.74 us
  Pallas kernels: 35.4 us -> 38.4 us
  local copies, waits for them, and re-layouts: 17.9 us -> 15.3 us
    add x4 -> x0, other arithmetic: 5.36 us -> none  [window_sum(): total = piece if total is None else total + piece]
    pallas_call x0 -> x1, Pallas kernels: none -> 3.01 us  [window_sums(): pl.pallas_call(_window_kernel, out_shape=(jax.ShapeDtypeStruct((views, ro...]
    slice x5, local copies, waits for them, and re-layouts: 3.23 us -> 0.36 us  [local(): residual_rows(shard_win, B, B + shard_width, measured_ext)]
    ppermute x8, waiting for transfers between devices: 11.4 us -> 13.7 us  [all_gather_tiles(): other = lax.ppermute(y, 'xy', [(i, i ^ 1 << j) for i in range(count)])]
    another operation x5 -> x2, other arithmetic: 0.03 us -> 1.99 us  [window_sums(): jnp.stack([jnp.stack(band_spots), jnp.stack([shard_spot] * views)])]
    slice x6, local copies, waits for them, and re-layouts: 6.52 us -> 4.61 us  [the longest x2 1.61 us: residual_rows(): win[:, :slab_rows]]
  transfers between devices with their start and end apart: 12 -> 12, of which waited for: 6 -> 5; matrix products, arithmetic and copies ran while one was open for 6% -> 12% of each run, Pallas kernels for 0% -> 0%
where the time goes in v5:
time: 100 us; the launch traced here: 99.7 us
  Pallas kernels  38.4 us (38%)
  starting transfers between devices  21.3 us (21%)
  local copies, waits for them, and re-layouts  15.3 us (15%)
  waiting for transfers between devices  13.7 us (14%)
  other arithmetic  5.74 us (6%)
  between operations  5.12 us (5%)
    pallas_call x1, Pallas kernels, forward_band(): pl.pallas_call(_forward_kernel, out_shape=jax.ShapeDtypeStruct((view_coun...  19.4 us
    pallas_call x1, Pallas kernels, backward_update(): pl.pallas_call(_backward_kernel, out_shape=jax.ShapeDtypeStruct(volume.sh...  16 us
    ppermute x8, waiting for transfers between devices, all_gather_tiles(): other = lax.ppermute(y, 'xy', [(i, i ^ 1 << j) for i in range(count)])  13.7 us
    ppermute x8, starting transfers between devices, all_gather_tiles(): other = lax.ppermute(y, 'xy', [(i, i ^ 1 << j) for i in range(count)])  9.67 us
    ppermute x1, starting transfers between devices, local(): halo_below = lax.ppermute(edge_up, 'gz', up_pairs)  4.54 us
    ppermute x1, starting transfers between devices, local(): lax.ppermute(pack(measured[:, slab_rows - 1:], axial_weight[:, :, slab_ro...  4.54 us
    pallas_call x1, Pallas kernels, window_sums(): pl.pallas_call(_window_kernel, out_shape=(jax.ShapeDtypeStruct((views, ro...  3.01 us
  transfers between devices with their start and end apart: 12, of which 5 were waited for; matrix products, arithmetic and copies ran while one was open for 12% of the time, Pallas kernels for 0%

profile of v5, /device:TPU:0, one launch (start us, length us, event | category | flops | bytes accessed | tf_op | source)
XLA Modules:
  0.0 99.7 jit_solution(10742443057043471126)
XLA Ops:
  0.6 0.7 convert_bitcast_fusion
  1.3 19.4 %shard_map.86 = f32[2,64,512]{2,1,0:T(8,128)} custom-call(f32[16,16384]{1,0:T(8,128)} %vol_ref.3, f32[2,16384]{1,0:T(2,128)} %amp_ref.3, s32[2,16384]{1,0:T(2,128)} %off_ref.3, s32[2,16384]{1,0:T(2,128)} %wid_ref.3), custom_call_target="tpu_custom_call" | custom-call | flops 2147483648 | bytes 1441792 | tf_op jit(solution)/shard_map/pallas_call | solution.py:55
  20.7 1.0 fusion.27
  21.8 4.1 %collective-permute-start.6 = (f32[35,512]{1,0:T(8,128)S(1)}, f32[35,512]{1,0:T(8,128)S(1)}, u32[]{:S(2)}, u32[]{:S(2)}) collective-permute-start(f32[35,512]{1,0:T(8,128)S(1)} %pad_maximum_fusion.10), channel_id=1, source_target_pairs={{0,16},{2,18},{4,20},{6,22},{8,24},{10,26},{12,28},{14,30},{16,0},... | collective-permute-start | bytes 215048 | tf_op jit(solution)/shard_map/ppermute | solution.py:125
  26.1 1.3 %collective-permute-start.1 = (f32[2,2,256]{2,1,0:T(2,128)S(1)}, f32[2,2,256]{2,1,0:T(2,128)S(1)}, u32[]{:S(2)}, u32[]{:S(2)}) collective-permute-start(f32[2,2,256]{2,1,0:T(2,128)S(1)} %select_maximum_fusion), channel_id=1, source_target_pairs={{1,0},{3,2},{5,4},{7,6},{9,8},{11,10},{13,12},{15,14},{17,16},{19,... | collective-permute-start | bytes 12296 | tf_op jit(solution)/shard_map/ppermute | solution.py:190
  27.5 4.5 %collective-permute-start = (f32[2,2,256]{2,1,0:T(2,128)S(1)}, f32[2,2,256]{2,1,0:T(2,128)S(1)}, u32[]{:S(2)}, u32[]{:S(2)}) collective-permute-start(f32[2,2,256]{2,1,0:T(2,128)S(1)} %select_maximum_fusion.1), channel_id=1, source_target_pairs={{0,1},{2,3},{4,5},{6,7},{8,9},{10,11},{12,13},{14,15},{16,17},{18,... | collective-permute-start | bytes 12296 | tf_op jit(solution)/shard_map/ppermute | solution.py:187
  32.0 0.7 fusion.31
  32.7 0.1 copy.76
  32.8 0.1 copy.75
  32.9 0.1 copy.74
  33.0 1.4 %add_bitcast_fusion = (s32[1,2]{1,0:T(1,128)S(1)}, s32[1,2]{1,0:T(1,128)S(1)}) fusion(s32[1]{0:T(128)} %bitcast.33, s32[1]{0:T(128)} %bitcast.32, s32[1]{0:T(128)} %bitcast.35), kind=kLoop, calls=%fused_computation.91 | loop fusion | flops 4 | bytes 28 | tf_op jit(solution)/shard_map/stack | solution.py:152
  34.4 0.6 pad_add_fusion.spots_ref
  35.0 0.7 select_add_fusion.rw_ref
  40.5 4.3 %collective-permute-done.2 = f32[36,256]{1,0:T(8,128)S(1)} collective-permute-done((f32[36,256]{1,0:T(8,128)S(1)}, f32[36,256]{1,0:T(8,128)S(1)}, u32[]{:S(2)}, u32[]{:S(2)}) %collective-permute-start.2) | collective-permute-done | bytes 36896 | tf_op jit(solution)/shard_map/ppermute | solution.py:125
  44.9 2.1 %collective-permute-start.3 = (f32[2,36,256]{2,1,0:T(8,128)S(1)}, f32[2,36,256]{2,1,0:T(8,128)S(1)}, u32[]{:S(2)}, u32[]{:S(2)}) collective-permute-start(f32[2,36,256]{2,1,0:T(8,128)S(1)} %pad_maximum_fusion.9), channel_id=1, source_target_pairs={{0,8},{2,10},{4,12},{6,14},{8,0},{10,2},{12,4},{14,6},{16,24},{18,... | collective-permute-start | bytes 221192 | tf_op jit(solution)/shard_map/ppermute | solution.py:125
  47.0 0.1 collective-permute-start.7
  47.1 2.3 %collective-permute-done.3 = f32[2,36,256]{2,1,0:T(8,128)S(1)} collective-permute-done((f32[2,36,256]{2,1,0:T(8,128)S(1)}, f32[2,36,256]{2,1,0:T(8,128)S(1)}, u32[]{:S(2)}, u32[]{:S(2)}) %collective-permute-start.3) | collective-permute-done | bytes 73760 | tf_op jit(solution)/shard_map/ppermute | solution.py:125
  49.4 1.6 %collective-permute-start.4 = (f32[2,2,36,256]{3,2,0,1:T(8,128)S(1)}, f32[2,2,36,256]{3,2,0,1:T(8,128)S(1)}, u32[]{:S(2)}, u32[]{:S(2)}) collective-permute-start(f32[2,2,36,256]{3,2,0,1:T(8,128)S(1)} %pad_maximum_fusion.5), channel_id=1, source_target_pairs={{0,4},{2,6},{4,0},{6,2},{8,12},{10,14},{12,8},{14,10},{16,20},{18,... | collective-permute-start | bytes 442376 | tf_op jit(solution)/shard_map/ppermute | solution.py:125
  51.0 1.3 %collective-permute-done.7 = f32[2,35,512]{2,1,0:T(8,128)S(1)} collective-permute-done((f32[2,35,512]{2,1,0:T(8,128)S(1)}, f32[2,35,512]{2,1,0:T(8,128)S(1)}, u32[]{:S(2)}, u32[]{:S(2)}) %collective-permute-start.7) | collective-permute-done | bytes 143392 | tf_op jit(solution)/shard_map/ppermute | solution.py:125
  52.4 1.6 %collective-permute-start.8 = (f32[2,2,35,512]{3,2,0,1:T(8,128)S(1)}, f32[2,2,35,512]{3,2,0,1:T(8,128)S(1)}, u32[]{:S(2)}, u32[]{:S(2)}) collective-permute-start(f32[2,2,35,512]{3,2,0,1:T(8,128)S(1)} %pad_maximum_fusion.4), channel_id=1, source_target_pairs={{0,4},{2,6},{4,0},{6,2},{8,12},{10,14},{12,8},{14,10},{16,20},{18,... | collective-permute-start | bytes 860168 | tf_op jit(solution)/shard_map/ppermute | solution.py:125
  54.0 2.3 %collective-permute-done.4 = f32[2,2,36,256]{3,2,0,1:T(8,128)S(1)} collective-permute-done((f32[2,2,36,256]{3,2,0,1:T(8,128)S(1)}, f32[2,2,36,256]{3,2,0,1:T(8,128)S(1)}, u32[]{:S(2)}, u32[]{:S(2)}) %collective-permute-start.4) | collective-permute-done | bytes 147488 | tf_op jit(solution)/shard_map/ppermute | solution.py:125
  56.5 3.4 %collective-permute-done.8 = f32[2,2,35,512]{3,2,0,1:T(8,128)S(1)} collective-permute-done((f32[2,2,35,512]{3,2,0,1:T(8,128)S(1)}, f32[2,2,35,512]{3,2,0,1:T(8,128)S(1)}, u32[]{:S(2)}, u32[]{:S(2)}) %collective-permute-start.8) | collective-permute-done | bytes 286752 | tf_op jit(solution)/shard_map/ppermute | solution.py:125
  60.0 0.4 copy.65
  60.6 0.5 copy.62
  61.1 0.4 reshape.129
  61.6 0.2 copy.81
  61.9 1.0 copy.80
  62.9 0.2 fusion
  63.1 0.1 pad_maximum_fusion
  63.2 0.9 copy.68
  64.1 0.8 reshape.131
  64.9 0.1 slice.190
  65.1 0.7 copy.70.starts_ref
  65.8 1.9 %copy.71.bands_ref = f32[16,2,17,512]{3,2,1,0:T(8,128)} copy(f32[16,2,17,512]{3,0,2,1:T(8,128)S(1)} %bitcast.96) | data formatting | bytes 2228224 | tf_op jit(solution)/shard_map/reshape | solution.py:204
  67.7 3.0 %shard_map.87 = (f32[2,17,512]{2,1,0:T(8,128)}, f32[2,17,256]{2,1,0:T(8,128)}) custom-call(s32[16,2]{1,0:T(8,128)} %copy.70.starts_ref, s32[2,2]{1,0:T(2,128)} %pad_add_fusion.spots_ref, f32[16,2,17,512]{3,2,1,0:T(8,128)} %copy.71.bands_ref), custom_call_target="tpu_custom_call" | custom-call | tf_op jit(solution)/shard_map/pallas_call | solution.py:154
  70.7 0.7 fusion.29
  71.4 0.8 fusion.28
  72.2 1.3 %collective-permute-start.11 = (f32[2,2,768]{2,1,0:T(2,128)S(1)}, f32[2,2,768]{2,1,0:T(2,128)S(1)}, u32[]{:S(2)}, u32[]{:S(2)}) collective-permute-start(f32[2,2,768]{2,1,0:T(2,128)S(1)} %pad_maximum_fusion.16), channel_id=1, source_target_pairs={{1,0},{3,2},{5,4},{7,6},{9,8},{11,10},{13,12},{15,14},{17,16},{19,... | collective-permute-start | bytes 36872 | tf_op jit(solution)/shard_map/ppermute | solution.py:212
  73.5 4.5 %collective-permute-start.10 = (f32[2,2,768]{2,1,0:T(2,128)S(1)}, f32[2,2,768]{2,1,0:T(2,128)S(1)}, u32[]{:S(2)}, u32[]{:S(2)}) collective-permute-start(f32[2,2,768]{2,1,0:T(2,128)S(1)} %pad_maximum_fusion.15), channel_id=1, source_target_pairs={{0,1},{2,3},{4,5},{6,7},{8,9},{10,11},{12,13},{14,15},{16,17},{18,... | collective-permute-start | bytes 36872 | tf_op jit(solution)/shard_map/ppermute | solution.py:211
  78.1 0.9 dynamic-slice_bitcast_fusion
  79.0 0.8 slice.160
  79.8 0.8 slice.167
  80.6 0.8 slice.174
  81.3 0.7 slice.177
  82.1 0.1 fusion.7
  82.2 0.7 fusion.8.back_ref
  82.9 16.0 %shard_map.88 = f32[16,16384]{1,0:T(8,128)} custom-call(f32[2,16,512]{2,1,0:T(8,128)} %fusion.8.back_ref, f32[16,16384]{1,0:T(8,128)} %vol_ref.3, f32[2,16384]{1,0:T(2,128)} %amp_ref.3, s32[2,16384]{1,0:T(2,128)} %off_ref.3, s32[2,16384]{1,0:T(2,128)} %wid_ref.3, f32[2,16,1]{2,1,0:T(8,128)} %select_add_fusion.rw_ref), custom_call_target="tpu_custom_call" | custom-call | flops 1073741824 | bytes 2490368 | tf_op jit(solution)/shard_map/pallas_call | solution.py:99
  99.0 0.7 fusion.17
  (74 shorter events, 1.9 us)
Async XLA Ops:
  1.3 24.6 %copy-start = (f32[3,2,16]{2,1,0:T(2,128)S(1)}, f32[3,2,16]{2,1,0:T(2,128)}, u32[]{:S(2)}) copy-start(f32[3,2,16]{2,1,0:T(2,128)} %param.13) | copy-start | bytes 1156
  1.3 24.8 %copy-start.1 = (f32[2,16,256]{2,1,0:T(8,128)S(1)}, f32[2,16,256]{2,1,0:T(8,128)}, u32[]{:S(2)}) copy-start(f32[2,16,256]{2,1,0:T(8,128)} %param.8) | copy-start | bytes 98308
  1.3 30.7 %copy-start.2 = (s32[2,1]{0,1:T(1,128)S(1)}, s32[2,1]{0,1:T(1,128)}, u32[]{:S(2)}) copy-start(s32[2,1]{0,1:T(1,128)} %param.9) | copy-start | bytes 28
  21.8 25.1 %collective-permute-start.6 = (f32[35,512]{1,0:T(8,128)S(1)}, f32[35,512]{1,0:T(8,128)S(1)}, u32[]{:S(2)}, u32[]{:S(2)}) collective-permute-start(f32[35,512]{1,0:T(8,128)S(1)} %pad_maximum_fusion.10), channel_id=1, source_target_pairs={{0,16},{2,18},{4,20},{6,22},{8,24},{10,26},{12,28},{14,30},{16,0},... | collective-permute-start | bytes 215048 | tf_op jit(solution)/shard_map/ppermute | solution.py:125
  26.1 13.7 %collective-permute-start.1 = (f32[2,2,256]{2,1,0:T(2,128)S(1)}, f32[2,2,256]{2,1,0:T(2,128)S(1)}, u32[]{:S(2)}, u32[]{:S(2)}) collective-permute-start(f32[2,2,256]{2,1,0:T(2,128)S(1)} %select_maximum_fusion), channel_id=1, source_target_pairs={{1,0},{3,2},{5,4},{7,6},{9,8},{11,10},{13,12},{15,14},{17,16},{19,... | collective-permute-start | bytes 12296 | tf_op jit(solution)/shard_map/ppermute | solution.py:190
  27.5 12.3 %collective-permute-start = (f32[2,2,256]{2,1,0:T(2,128)S(1)}, f32[2,2,256]{2,1,0:T(2,128)S(1)}, u32[]{:S(2)}, u32[]{:S(2)}) collective-permute-start(f32[2,2,256]{2,1,0:T(2,128)S(1)} %select_maximum_fusion.1), channel_id=1, source_target_pairs={{0,1},{2,3},{4,5},{6,7},{8,9},{10,11},{12,13},{14,15},{16,17},{18,... | collective-permute-start | bytes 12296 | tf_op jit(solution)/shard_map/ppermute | solution.py:187
  39.9 5.0 %collective-permute-start.2 = (f32[36,256]{1,0:T(8,128)S(1)}, f32[36,256]{1,0:T(8,128)S(1)}, u32[]{:S(2)}, u32[]{:S(2)}) collective-permute-start(f32[36,256]{1,0:T(8,128)S(1)} %reshape.128), channel_id=1, source_target_pairs={{0,16},{2,18},{4,20},{6,22},{8,24},{10,26},{12,28},{14,30},{16,0},... | collective-permute-start | bytes 110600 | tf_op jit(solution)/shard_map/ppermute | solution.py:125
  44.9 4.5 %collective-permute-start.3 = (f32[2,36,256]{2,1,0:T(8,128)S(1)}, f32[2,36,256]{2,1,0:T(8,128)S(1)}, u32[]{:S(2)}, u32[]{:S(2)}) collective-permute-start(f32[2,36,256]{2,1,0:T(8,128)S(1)} %pad_maximum_fusion.9), channel_id=1, source_target_pairs={{0,8},{2,10},{4,12},{6,14},{8,0},{10,2},{12,4},{14,6},{16,24},{18,... | collective-permute-start | bytes 221192 | tf_op jit(solution)/shard_map/ppermute | solution.py:125
  47.0 5.4 %collective-permute-start.7 = (f32[2,35,512]{2,1,0:T(8,128)S(1)}, f32[2,35,512]{2,1,0:T(8,128)S(1)}, u32[]{:S(2)}, u32[]{:S(2)}) collective-permute-start(f32[2,35,512]{2,1,0:T(8,128)S(1)} %pad_maximum_fusion.6), channel_id=1, source_target_pairs={{0,8},{2,10},{4,12},{6,14},{8,0},{10,2},{12,4},{14,6},{16,24},{18,... | collective-permute-start | bytes 430088 | tf_op jit(solution)/shard_map/ppermute | solution.py:125
  49.4 6.9 %collective-permute-start.4 = (f32[2,2,36,256]{3,2,0,1:T(8,128)S(1)}, f32[2,2,36,256]{3,2,0,1:T(8,128)S(1)}, u32[]{:S(2)}, u32[]{:S(2)}) collective-permute-start(f32[2,2,36,256]{3,2,0,1:T(8,128)S(1)} %pad_maximum_fusion.5), channel_id=1, source_target_pairs={{0,4},{2,6},{4,0},{6,2},{8,12},{10,14},{12,8},{14,10},{16,20},{18,... | collective-permute-start | bytes 442376 | tf_op jit(solution)/shard_map/ppermute | solution.py:125
  52.4 7.4 %collective-permute-start.8 = (f32[2,2,35,512]{3,2,0,1:T(8,128)S(1)}, f32[2,2,35,512]{3,2,0,1:T(8,128)S(1)}, u32[]{:S(2)}, u32[]{:S(2)}) collective-permute-start(f32[2,2,35,512]{3,2,0,1:T(8,128)S(1)} %pad_maximum_fusion.4), channel_id=1, source_target_pairs={{0,4},{2,6},{4,0},{6,2},{8,12},{10,14},{12,8},{14,10},{16,20},{18,... | collective-permute-start | bytes 860168 | tf_op jit(solution)/shard_map/ppermute | solution.py:125
  56.4 4.1 %collective-permute-start.5 = (f32[2,2,2,36,256]{4,3,0,1,2:T(8,128)S(1)}, f32[2,2,2,36,256]{4,3,0,1,2:T(8,128)S(1)}, u32[]{:S(2)}, u32[]{:S(2)}) collective-permute-start(f32[2,2,2,36,256]{4,3,0,1,2:T(8,128)S(1)} %pad_maximum_fusion.3), channel_id=1, source_target_pairs={{0,2},{2,0},{4,6},{6,4},{8,10},{10,8},{12,14},{14,12},{16,18},{18,... | collective-permute-start | bytes 884744 | tf_op jit(solution)/shard_map/ppermute | solution.py:125
  60.4 2.4 %collective-permute-start.9 = (f32[2,2,2,35,512]{4,2,3,1,0:T(2,128)S(1)}, f32[2,2,2,35,512]{4,2,3,1,0:T(2,128)S(1)}, u32[]{:S(2)}, u32[]{:S(2)}) collective-permute-start(f32[2,2,2,35,512]{4,2,3,1,0:T(2,128)S(1)} %copy.65), channel_id=1, source_target_pairs={{0,2},{2,0},{4,6},{6,4},{8,10},{10,8},{12,14},{14,12},{16,18},{18,... | collective-permute-start | bytes 1720328 | tf_op jit(solution)/shard_map/ppermute | solution.py:125
  72.2 9.9 %collective-permute-start.11 = (f32[2,2,768]{2,1,0:T(2,128)S(1)}, f32[2,2,768]{2,1,0:T(2,128)S(1)}, u32[]{:S(2)}, u32[]{:S(2)}) collective-permute-start(f32[2,2,768]{2,1,0:T(2,128)S(1)} %pad_maximum_fusion.16), channel_id=1, source_target_pairs={{1,0},{3,2},{5,4},{7,6},{9,8},{11,10},{13,12},{15,14},{17,16},{19,... | collective-permute-start | bytes 36872 | tf_op jit(solution)/shard_map/ppermute | solution.py:212
  73.5 8.6 %collective-permute-start.10 = (f32[2,2,768]{2,1,0:T(2,128)S(1)}, f32[2,2,768]{2,1,0:T(2,128)S(1)}, u32[]{:S(2)}, u32[]{:S(2)}) collective-permute-start(f32[2,2,768]{2,1,0:T(2,128)S(1)} %pad_maximum_fusion.15), channel_id=1, source_target_pairs={{0,1},{2,3},{4,5},{6,7},{8,9},{10,11},{12,13},{14,15},{16,17},{18,... | collective-permute-start | bytes 36872 | tf_op jit(solution)/shard_map/ppermute | solution.py:211

commit v6 on v5

--- a/solution.py
+++ b/solution.py
@@ -174,53 +174,60 @@
     up_pairs = [(i, i + 1) for i in range(gz_count - 1)]
     down_pairs = [(i + 1, i) for i in range(gz_count - 1)]
     ext_rows = slab_rows + 2
-
-    def pack(meas_rows, weight_cols):
-        flat = jnp.transpose(weight_cols, (1, 0, 2)).reshape(view_count, 1, -1)
-        flat = jnp.pad(flat, ((0, 0), (0, 0), (0, shard_width - flat.shape[2])))
-        return jnp.concatenate([meas_rows, flat], axis=1)
-
-    def unpack(packed):
-        cols = packed[:, 1, : 3 * 2].reshape(view_count, 3, 2)
-        return packed[:, :1], jnp.transpose(cols, (1, 0, 2))
-
-    from_below = lax.ppermute(
-        pack(measured[:, slab_rows - 1 :], axial_weight[:, :, slab_rows - 2 :]), "gz", up_pairs
-    )
-    from_above = lax.ppermute(pack(measured[:, :1], axial_weight[:, :, :2]), "gz", down_pairs)
-    meas_below, weight_below = unpack(from_below)
-    meas_above, weight_above = unpack(from_above)
-    measured_ext = jnp.concatenate([meas_below, measured, meas_above], axis=1)
-    weight_ext = jnp.concatenate([weight_below, axial_weight, weight_above], axis=2)
-    meas_tiles = all_gather_tiles(measured_ext.reshape(view_count * ext_rows, shard_width), xy_count)
-    meas_full = jnp.transpose(meas_tiles, (1, 0, 2)).reshape(view_count, ext_rows, detector_width)
+    band_height = slab_rows + 1
+    band_part = view_count * band_height
+    meas_part = view_count * slab_rows * shard_width // B
 
     band_rows = forward_band(volume, amplitude, column_offset, column_width)
-    band_height = slab_rows + 1
     start_row = jnp.pad(band_start[:, 0].astype(jnp.float32), (0, B - view_count))[None]
-    payload = jnp.concatenate([band_rows.reshape(view_count * band_height, B), start_row], axis=0)
+    payload = jnp.concatenate(
+        [band_rows.reshape(band_part, B), measured.reshape(meas_part, B), start_row], axis=0
+    )
     gathered = all_gather_tiles(payload, xy_count)
-    starts = gathered[:, view_count * band_height, :view_count].astype(jnp.int32)
-    bands = gathered[:, : view_count * band_height].reshape(xy_count, view_count, band_height, B)
+    starts = gathered[:, band_part + meas_part, :view_count].astype(jnp.int32)
+    bands = gathered[:, :band_part].reshape(xy_count, view_count, band_height, B)
+    meas_tiles = gathered[:, band_part : band_part + meas_part].reshape(
+        xy_count, view_count, slab_rows, shard_width
+    )
+    meas_full = jnp.transpose(meas_tiles, (1, 2, 0, 3)).reshape(view_count, slab_rows, detector_width)
     my_start = [band_start[v, 0] for v in range(view_count)]
     shard_pos = lax.axis_index("xy") * shard_width
     band_win, shard_win = window_sums(bands, starts, my_start, shard_pos, shard_width)
-
-    edge_up = jnp.concatenate([band_win[:, slab_rows - 2 : slab_rows], shard_win[:, slab_rows - 2 : slab_rows]], axis=2)
-    edge_down = jnp.concatenate([band_win[:, :2], shard_win[:, :2]], axis=2)
-    halo_below = lax.ppermute(edge_up, "gz", up_pairs)
-    halo_above = lax.ppermute(edge_down, "gz", down_pairs)
-
+    meas_band = jnp.stack(
+        [lax.dynamic_slice(meas_full[v], (jnp.int32(0), my_start[v]), (slab_rows, B)) for v in range(view_count)]
+    )
+
+    def halo_payload(p_rows, m_row, weight_cols):
+        p = jnp.concatenate([band_win[:, p_rows], shard_win[:, p_rows]], axis=2)
+        m = jnp.concatenate([meas_band[:, m_row], measured[:, m_row]], axis=2)
+        w = jnp.transpose(weight_cols, (1, 0, 2)).reshape(view_count, 1, -1)
+        w = jnp.pad(w, ((0, 0), (0, 0), (0, B + shard_width - w.shape[2])))
+        return jnp.concatenate([p, m, w], axis=1)
+
+    halo_below = lax.ppermute(
+        halo_payload(slice(slab_rows - 2, slab_rows), slice(slab_rows - 1, slab_rows), axial_weight[:, :, slab_rows - 2 :]),
+        "gz",
+        up_pairs,
+    )
+    halo_above = lax.ppermute(
+        halo_payload(slice(0, 2), slice(0, 1), axial_weight[:, :, :2]), "gz", down_pairs
+    )
+
+    def halo_weights(halo):
+        return jnp.transpose(halo[:, 3, : 3 * 2].reshape(view_count, 3, 2), (1, 0, 2))
+
+    weight_ext = jnp.concatenate([halo_weights(halo_below), axial_weight, halo_weights(halo_above)], axis=2)
     mid_w = weight_ext[1, :, 1 : ext_rows + 1][:, :, None]
     next_w = weight_ext[0, :, 2 : ext_rows + 2][:, :, None]
     prev_w = weight_ext[2, :, 0:ext_rows][:, :, None]
     global_rows = first_row - 1 + jnp.arange(ext_rows, dtype=jnp.int32)
     valid = (global_rows >= 0) & (global_rows < total_rows)
 
-    def residual_rows(win, lo, hi, meas_ext):
+    def residual_rows(win, meas, lo, hi):
         proj_ext = jnp.concatenate(
-            [halo_below[:, :, lo:hi], win[:, :slab_rows], halo_above[:, :, lo:hi]], axis=1
+            [halo_below[:, 0:2, lo:hi], win[:, :slab_rows], halo_above[:, 0:2, lo:hi]], axis=1
         )
+        meas_ext = jnp.concatenate([halo_below[:, 2:3, lo:hi], meas, halo_above[:, 2:3, lo:hi]], axis=1)
         cover = win[:, slab_rows : slab_rows + 1]
         centre = proj_ext[:, 1 : ext_rows + 1]
         after = proj_ext[:, 2 : ext_rows + 2]
@@ -230,11 +237,8 @@
         res = (meas_ext - projection) / jnp.maximum(coverage, 1.0)
         return jnp.where(valid[None, :, None], res, 0.0)
 
-    residual = residual_rows(shard_win, B, B + shard_width, measured_ext)[:, 1 : slab_rows + 1]
-    meas_band = jnp.stack(
-        [lax.dynamic_slice(meas_full[v], (jnp.int32(0), my_start[v]), (ext_rows, B)) for v in range(view_count)]
-    )
-    res_band = residual_rows(band_win, 0, B, meas_band)
+    residual = residual_rows(shard_win, measured, B, B + shard_width)[:, 1 : slab_rows + 1]
+    res_band = residual_rows(band_win, meas_band, 0, B)
     back_band = (
         axial_weight[0][:, :, None] * res_band[:, 0:slab_rows]
         + axial_weight[1][:, :, None] * res_band[:, 1 : slab_rows + 1]

time: 100 us -> 101 us (1.010); the launches traced: 99.7 us -> 99.3 us
  starting transfers between devices: 21.3 us -> 12.1 us
  waiting for transfers between devices: 13.7 us -> 22.5 us
    ppermute x8 -> x4, waiting for transfers between devices: 13.7 us -> 21.1 us  [all_gather_tiles(): other = lax.ppermute(y, 'xy', [(i, i ^ 1 << j) for i in range(count)])]
    ppermute x4 -> x2, starting transfers between devices: 11.7 us -> 5.82 us  [the longest x1 4.53 us: local(): lax.ppermute(halo_payload(slice(slab_rows - 2, slab_rows), slice(slab_row...]
    ppermute x8 -> x4, starting transfers between devices: 9.67 us -> 6.3 us  [all_gather_tiles(): other = lax.ppermute(y, 'xy', [(i, i ^ 1 << j) for i in range(count)])]
    ppermute x4 -> x2, waiting for transfers between devices: 0.01 us -> 1.36 us  [the longest x1 1.36 us: local(): lax.ppermute(halo_payload(slice(slab_rows - 2, slab_rows), slice(slab_row...]
    reshape x5 -> x6, local copies, waits for them, and re-layouts: 2.05 us -> 2.86 us  [the longest x1 1.83 us: local(): gathered[:, :band_part].reshape(xy_count, view_count, band_height, B)]
    slice x16 -> x22, local copies, waits for them, and re-layouts: 2.04 us -> 2.7 us  [the longest x2 1.52 us: halo_payload(): p = jnp.concatenate([band_win[:, p_rows], shard_win[:, p_rows]], axis=2)]
  transfers between devices with their start and end apart: 12 -> 6, of which waited for: 5 -> 4; matrix products, arithmetic and copies ran while one was open for 12% -> 7% of each run, Pallas kernels for 0% -> 0%
where the time goes in v6:
time: 101 us; the launch traced here: 99.3 us
  Pallas kernels  38.4 us (38%)
  waiting for transfers between devices  22.5 us (22%)
  local copies, waits for them, and re-layouts  15.6 us (15%)
  starting transfers between devices  12.1 us (12%)
  other arithmetic  5.74 us (6%)
  between operations  4.9 us (5%)
    ppermute x4, waiting for transfers between devices, all_gather_tiles(): other = lax.ppermute(y, 'xy', [(i, i ^ 1 << j) for i in range(count)])  21.1 us
    pallas_call x1, Pallas kernels, forward_band(): pl.pallas_call(_forward_kernel, out_shape=jax.ShapeDtypeStruct((view_coun...  19.4 us
    pallas_call x1, Pallas kernels, backward_update(): pl.pallas_call(_backward_kernel, out_shape=jax.ShapeDtypeStruct(volume.sh...  16 us
    ppermute x4, starting transfers between devices, all_gather_tiles(): other = lax.ppermute(y, 'xy', [(i, i ^ 1 << j) for i in range(count)])  6.3 us
    ppermute x1, starting transfers between devices, local(): lax.ppermute(halo_payload(slice(slab_rows - 2, slab_rows), slice(slab_row...  4.53 us
    pallas_call x1, Pallas kernels, window_sums(): pl.pallas_call(_window_kernel, out_shape=(jax.ShapeDtypeStruct((views, ro...  3.01 us
  transfers between devices with their start and end apart: 6, of which 4 were waited for; matrix products, arithmetic and copies ran while one was open for 7% of the time, Pallas kernels for 0%

profile of v6, /device:TPU:0, one launch (start us, length us, event | category | flops | bytes accessed | tf_op | source)
XLA Modules:
  0.0 99.3 jit_solution(7168612381529763670)
XLA Ops:
  0.6 0.7 convert_bitcast_fusion
  1.3 0.8 reshape.127
  2.1 19.4 %shard_map.86 = f32[2,64,512]{2,1,0:T(8,128)} custom-call(f32[16,16384]{1,0:T(8,128)} %vol_ref.3, f32[2,16384]{1,0:T(2,128)} %amp_ref.3, s32[2,16384]{1,0:T(2,128)} %off_ref.3, s32[2,16384]{1,0:T(2,128)} %wid_ref.3), custom_call_target="tpu_custom_call" | custom-call | flops 2147483648 | bytes 1441792 | tf_op jit(solution)/shard_map/pallas_call | solution.py:55
  21.5 1.0 fusion.30
  22.6 4.1 %collective-permute-start = (f32[51,512]{1,0:T(8,128)S(1)}, f32[51,512]{1,0:T(8,128)S(1)}, u32[]{:S(2)}, u32[]{:S(2)}) collective-permute-start(f32[51,512]{1,0:T(8,128)S(1)} %pad_maximum_fusion.4), channel_id=1, source_target_pairs={{0,16},{2,18},{4,20},{6,22},{8,24},{10,26},{12,28},{14,30},{16,0},... | collective-permute-start | bytes 313352 | tf_op jit(solution)/shard_map/ppermute | solution.py:125
  26.7 5.6 %collective-permute-done = f32[51,512]{1,0:T(8,128)S(1)} collective-permute-done((f32[51,512]{1,0:T(8,128)S(1)}, f32[51,512]{1,0:T(8,128)S(1)}, u32[]{:S(2)}, u32[]{:S(2)}) %collective-permute-start) | collective-permute-done | bytes 104480 | tf_op jit(solution)/shard_map/ppermute | solution.py:125
  32.3 0.8 collective-permute-start.1
  33.1 6.1 %collective-permute-done.1 = f32[2,51,512]{2,1,0:T(8,128)S(1)} collective-permute-done((f32[2,51,512]{2,1,0:T(8,128)S(1)}, f32[2,51,512]{2,1,0:T(8,128)S(1)}, u32[]{:S(2)}, u32[]{:S(2)}) %collective-permute-start.1) | collective-permute-done | bytes 208928 | tf_op jit(solution)/shard_map/ppermute | solution.py:125
  39.3 1.3 %collective-permute-start.2 = (f32[2,2,51,512]{3,2,0,1:T(8,128)S(1)}, f32[2,2,51,512]{3,2,0,1:T(8,128)S(1)}, u32[]{:S(2)}, u32[]{:S(2)}) collective-permute-start(f32[2,2,51,512]{3,2,0,1:T(8,128)S(1)} %pad_maximum_fusion.2), channel_id=1, source_target_pairs={{0,4},{2,6},{4,0},{6,2},{8,12},{10,14},{12,8},{14,10},{16,20},{18,... | collective-permute-start | bytes 1253384 | tf_op jit(solution)/shard_map/ppermute | solution.py:125
  40.7 9.4 %collective-permute-done.2 = f32[2,2,51,512]{3,2,0,1:T(8,128)S(1)} collective-permute-done((f32[2,2,51,512]{3,2,0,1:T(8,128)S(1)}, f32[2,2,51,512]{3,2,0,1:T(8,128)S(1)}, u32[]{:S(2)}, u32[]{:S(2)}) %collective-permute-start.2) | collective-permute-done | bytes 417824 | tf_op jit(solution)/shard_map/ppermute | solution.py:125
  50.1 0.1 select_bitcast_fusion.3
  50.3 0.6 copy.95
  51.0 0.6 fusion.34
  54.2 0.1 reshape.131
  54.3 0.1 reshape.132
  54.4 0.1 copy.115
  54.5 0.1 copy.114
  54.6 0.1 copy.113
  56.0 1.4 %add_bitcast_fusion = (s32[1,2]{1,0:T(1,128)S(1)}, s32[1,2]{1,0:T(1,128)S(1)}) fusion(s32[1]{0:T(128)} %bitcast.13, s32[1]{0:T(128)} %bitcast.12, s32[1]{0:T(128)} %bitcast.15), kind=kLoop, calls=%fused_computation.86 | loop fusion | flops 4 | bytes 28 | tf_op jit(solution)/shard_map/stack | solution.py:152
  57.4 0.6 pad_add_fusion.spots_ref
  58.0 0.7 select_add_fusion.rw_ref
  58.7 0.3 select_bitcast_fusion.1
  59.0 0.2 pad_maximum_fusion
  59.1 1.3 %copy.98 = f32[2,2,2,2,51,512]{5,3,2,1,0,4:T(2,128)S(1)} copy(f32[2,2,2,2,51,512]{5,4,0,1,2,3:T(8,128)S(1)} %pad_maximum_fusion) | data formatting | bytes 3342336 | tf_op jit(solution)/shard_map/stack | solution.py:128
  60.4 1.1 %reshape.128 = f32[16,51,512]{2,0,1:T(8,128)S(1)} reshape(f32[2,2,2,2,51,512]{5,3,2,1,0,4:T(2,128)S(1)} %copy.98) | data formatting | bytes 3342336 | tf_op jit(solution)/shard_map/reshape | solution.py:129
  61.6 0.3 copy.102
  62.0 0.8 copy-done
  63.0 0.1 copy.121
  63.1 0.7 copy.100.starts_ref
  63.8 0.4 slice-done
  64.1 1.8 %copy.101.bands_ref = f32[16,2,17,512]{3,2,1,0:T(8,128)} copy(f32[16,2,17,512]{3,0,2,1:T(8,128)S(1)} %bitcast.80) | data formatting | bytes 2228224 | tf_op jit(solution)/shard_map/reshape | solution.py:188
  66.0 3.0 %shard_map.87 = (f32[2,17,512]{2,1,0:T(8,128)}, f32[2,17,256]{2,1,0:T(8,128)}) custom-call(s32[16,2]{1,0:T(8,128)} %copy.100.starts_ref, s32[2,2]{1,0:T(2,128)} %pad_add_fusion.spots_ref, f32[16,2,17,512]{3,2,1,0:T(8,128)} %copy.101.bands_ref), custom_call_target="tpu_custom_call" | custom-call | tf_op jit(solution)/shard_map/pallas_call | solution.py:154
  69.0 0.7 fusion.32
  69.7 0.8 fusion.31
  70.5 0.1 dynamic-slice_bitcast_fusion
  70.6 1.3 %collective-permute-start.5 = (f32[2,4,768]{2,1,0:T(4,128)S(1)}, f32[2,4,768]{2,1,0:T(4,128)S(1)}, u32[]{:S(2)}, u32[]{:S(2)}) collective-permute-start(f32[2,4,768]{2,1,0:T(4,128)S(1)} %get-tuple-element.25), channel_id=1, source_target_pairs={{1,0},{3,2},{5,4},{7,6},{9,8},{11,10},{13,12},{15,14},{17,16},{19,... | collective-permute-start | bytes 73736 | tf_op jit(solution)/shard_map/ppermute | solution.py:212
  72.0 0.8 slice.180
  72.9 0.8 slice.185
  73.6 0.8 slice.194
  74.4 0.7 slice.197
  75.1 4.5 %collective-permute-start.4 = (f32[2,4,768]{2,1,0:T(4,128)S(1)}, f32[2,4,768]{2,1,0:T(4,128)S(1)}, u32[]{:S(2)}, u32[]{:S(2)}) collective-permute-start(f32[2,4,768]{2,1,0:T(4,128)S(1)} %get-tuple-element.24), channel_id=1, source_target_pairs={{0,1},{2,3},{4,5},{6,7},{8,9},{10,11},{12,13},{14,15},{16,17},{18,... | collective-permute-start | bytes 73736 | tf_op jit(solution)/shard_map/ppermute | solution.py:207
  79.7 0.1 reshape_squeeze.7
  79.8 1.4 %collective-permute-done.4 = f32[2,4,768]{2,1,0:T(4,128)S(1)} collective-permute-done((f32[2,4,768]{2,1,0:T(4,128)S(1)}, f32[2,4,768]{2,1,0:T(4,128)S(1)}, u32[]{:S(2)}, u32[]{:S(2)}) %collective-permute-start.4) | collective-permute-done | bytes 24608 | tf_op jit(solution)/shard_map/ppermute | solution.py:207
  81.2 0.1 reshape_squeeze.6
  81.7 0.1 fusion.5
  81.8 0.7 fusion.6.back_ref
  82.5 16.0 %shard_map.88 = f32[16,16384]{1,0:T(8,128)} custom-call(f32[2,16,512]{2,1,0:T(8,128)} %fusion.6.back_ref, f32[16,16384]{1,0:T(8,128)} %vol_ref.3, f32[2,16384]{1,0:T(2,128)} %amp_ref.3, s32[2,16384]{1,0:T(2,128)} %off_ref.3, s32[2,16384]{1,0:T(2,128)} %wid_ref.3, f32[2,16,1]{2,1,0:T(8,128)} %select_add_fusion.rw_ref), custom_call_target="tpu_custom_call" | custom-call | flops 1073741824 | bytes 2490368 | tf_op jit(solution)/shard_map/pallas_call | solution.py:99
  98.6 0.7 fusion.15
  (55 shorter events, 1.2 us)
Async XLA Ops:
  22.5 18.1 %copy-start.2 = (f32[3,2,16]{2,1,0:T(2,128)S(1)}, f32[3,2,16]{2,1,0:T(2,128)}, u32[]{:S(2)}) copy-start(f32[3,2,16]{2,1,0:T(2,128)} %param.13) | copy-start | bytes 1156
  22.6 9.7 %collective-permute-start = (f32[51,512]{1,0:T(8,128)S(1)}, f32[51,512]{1,0:T(8,128)S(1)}, u32[]{:S(2)}, u32[]{:S(2)}) collective-permute-start(f32[51,512]{1,0:T(8,128)S(1)} %pad_maximum_fusion.4), channel_id=1, source_target_pairs={{0,16},{2,18},{4,20},{6,22},{8,24},{10,26},{12,28},{14,30},{16,0},... | collective-permute-start | bytes 313352 | tf_op jit(solution)/shard_map/ppermute | solution.py:125
  32.3 6.9 %collective-permute-start.1 = (f32[2,51,512]{2,1,0:T(8,128)S(1)}, f32[2,51,512]{2,1,0:T(8,128)S(1)}, u32[]{:S(2)}, u32[]{:S(2)}) collective-permute-start(f32[2,51,512]{2,1,0:T(8,128)S(1)} %pad_maximum_fusion.3), channel_id=1, source_target_pairs={{0,8},{2,10},{4,12},{6,14},{8,0},{10,2},{12,4},{14,6},{16,24},{18,... | collective-permute-start | bytes 626696 | tf_op jit(solution)/shard_map/ppermute | solution.py:125
  39.3 10.8 %collective-permute-start.2 = (f32[2,2,51,512]{3,2,0,1:T(8,128)S(1)}, f32[2,2,51,512]{3,2,0,1:T(8,128)S(1)}, u32[]{:S(2)}, u32[]{:S(2)}) collective-permute-start(f32[2,2,51,512]{3,2,0,1:T(8,128)S(1)} %pad_maximum_fusion.2), channel_id=1, source_target_pairs={{0,4},{2,6},{4,0},{6,2},{8,12},{10,14},{12,8},{14,10},{16,20},{18,... | collective-permute-start | bytes 1253384 | tf_op jit(solution)/shard_map/ppermute | solution.py:125
  50.2 0.8 copy-start.3
  50.2 7.8 %copy-start.1 = (f32[2,16,256]{2,1,0:T(8,128)S(1)}, f32[2,16,256]{2,1,0:T(8,128)}, u32[]{:S(2)}) copy-start(f32[2,16,256]{2,1,0:T(8,128)} %param.8) | copy-start | bytes 98308
  51.0 7.7 %collective-permute-start.3 = (f32[2,2,2,51,512]{4,2,3,1,0:T(2,128)S(1)}, f32[2,2,2,51,512]{4,2,3,1,0:T(2,128)S(1)}, u32[]{:S(2)}, u32[]{:S(2)}) collective-permute-start(f32[2,2,2,51,512]{4,2,3,1,0:T(2,128)S(1)} %copy.95), channel_id=1, source_target_pairs={{0,2},{2,0},{4,6},{6,4},{8,10},{10,8},{12,14},{14,12},{16,18},{18,... | collective-permute-start | bytes 2506760 | tf_op jit(solution)/shard_map/ppermute | solution.py:125
  61.6 1.2 %copy-start = (f32[16,51,512]{2,0,1:T(8,128)}, f32[16,51,512]{2,0,1:T(8,128)S(1)}, u32[]{:S(2)}) copy-start(f32[16,51,512]{2,0,1:T(8,128)S(1)} %reshape.128) | copy-start | bytes 5013508
  62.9 1.3 %slice-start = ((f32[16,51,512]{2,0,1:T(8,128)}), f32[16,34,512]{2,0,1:T(8,128)S(1)}, s32[]{:S(2)}) async-start(f32[16,51,512]{2,0,1:T(8,128)} %copy-done), calls=%async_computation | async-start | bytes 2228224 | tf_op jit(solution)/shard_map/slice | solution.py:188
  70.6 9.0 %collective-permute-start.5 = (f32[2,4,768]{2,1,0:T(4,128)S(1)}, f32[2,4,768]{2,1,0:T(4,128)S(1)}, u32[]{:S(2)}, u32[]{:S(2)}) collective-permute-start(f32[2,4,768]{2,1,0:T(4,128)S(1)} %get-tuple-element.25), channel_id=1, source_target_pairs={{1,0},{3,2},{5,4},{7,6},{9,8},{11,10},{13,12},{15,14},{17,16},{19,... | collective-permute-start | bytes 73736 | tf_op jit(solution)/shard_map/ppermute | solution.py:212
  75.1 6.0 %collective-permute-start.4 = (f32[2,4,768]{2,1,0:T(4,128)S(1)}, f32[2,4,768]{2,1,0:T(4,128)S(1)}, u32[]{:S(2)}, u32[]{:S(2)}) collective-permute-start(f32[2,4,768]{2,1,0:T(4,128)S(1)} %get-tuple-element.24), channel_id=1, source_target_pairs={{0,1},{2,3},{4,5},{6,7},{8,9},{10,11},{12,13},{14,15},{16,17},{18,... | collective-permute-start | bytes 73736 | tf_op jit(solution)/shard_map/ppermute | solution.py:207

commit v7 on v3

--- a/solution.py
+++ b/solution.py
@@ -7,13 +7,13 @@
 
 B = 512
 RELAX = 0.9
-CHUNK = 512
+CHUNK = 2048
 INTERPRET = False
 
 
 def _band_mask(off, wid, rows, width):
     u = lax.broadcasted_iota(jnp.int32, (rows, width), 0)
-    inside = (u >= off) & (u < off + wid)
+    inside = (u - off).astype(jnp.uint32) < wid.astype(jnp.uint32)
     return jnp.where(inside, 1.0, 0.0).astype(jnp.bfloat16)
 
 

time: 92.5 us -> 79.9 us (0.86)
  Pallas kernels: 35.4 us -> 22.9 us
  waiting for transfers between devices: 16.8 us -> 15.4 us
  starting transfers between devices: 24.2 us -> 25.2 us
    pallas_call x1, Pallas kernels: 16 us -> 9.65 us  [backward_update(): pl.pallas_call(_backward_kernel, out_shape=jax.ShapeDtypeStruct(volume.sh...]
    pallas_call x1, Pallas kernels: 19.4 us -> 13.2 us  [forward_band(): pl.pallas_call(_forward_kernel, out_shape=jax.ShapeDtypeStruct((view_coun...]
where the time goes in v7:
time: 79.9 us; the launch traced here: 79.3 us
  starting transfers between devices  25.2 us (32%)
  Pallas kernels  22.9 us (29%)
  waiting for transfers between devices  15.4 us (19%)
  local copies, waits for them, and re-layouts  7.58 us (9%)
  between operations  4.69 us (6%)
  other arithmetic  3.64 us (5%)
    pallas_call x1, Pallas kernels, forward_band(): pl.pallas_call(_forward_kernel, out_shape=jax.ShapeDtypeStruct((view_coun...  13.2 us
    pallas_call x1, Pallas kernels, backward_update(): pl.pallas_call(_backward_kernel, out_shape=jax.ShapeDtypeStruct(volume.sh...  9.65 us
    ppermute x4, waiting for transfers between devices, all_gather_xy(): other = lax.ppermute(y, 'xy', [(i, i ^ 1 << j) for i in range(count)])  9.29 us
    ppermute x4, starting transfers between devices, reduce_scatter_xy(): y = keep + lax.ppermute(send, 'xy', [(i, i ^ 1 << j) for i in range(count)])  7.97 us
    ppermute x4, starting transfers between devices, all_gather_xy(): other = lax.ppermute(y, 'xy', [(i, i ^ 1 << j) for i in range(count)])  5.54 us
    ppermute x4, waiting for transfers between devices, reduce_scatter_xy(): y = keep + lax.ppermute(send, 'xy', [(i, i ^ 1 << j) for i in range(count)])  4.93 us
    ppermute x1, starting transfers between devices, local(): lax.ppermute(proj_cols[:, slab_rows - 2:], 'gz', up_pairs)  4.54 us
    ppermute x1, starting transfers between devices, local(): lax.ppermute(pack(measured[:, slab_rows - 1:], axial_weight[:, :, slab_ro...  4.54 us
  transfers between devices with their start and end apart: 12, of which 8 were waited for; matrix products, arithmetic and copies ran while one was open for 2% of the time, Pallas kernels for 0%

profile of v7, /device:TPU:0, one launch (start us, length us, event | category | flops | bytes accessed | tf_op | source)
XLA Modules:
  0.0 79.3 jit_solution(16259538221914516741)
XLA Ops:
  0.6 1.3 %fusion.18 = (s32[1,1]{0,1:T(1,128)}, s32[1,1]{0,1:T(1,128)}) fusion(s32[2,1]{0,1:T(1,128)} %param.9), kind=kLoop, calls=%fused_computation.79 | loop fusion | bytes 16 | tf_op jit(solution)/shard_map/slice | solution.py:171
  4.4 13.2 %shard_map.86 = f32[2,64,512]{2,1,0:T(8,128)} custom-call(f32[16,16384]{1,0:T(8,128)} %vol_ref.3, f32[2,16384]{1,0:T(2,128)} %amp_ref.3, s32[2,16384]{1,0:T(2,128)} %off_ref.3, s32[2,16384]{1,0:T(2,128)} %wid_ref.3), custom_call_target="tpu_custom_call" | custom-call | tf_op jit(solution)/shard_map/pallas_call | solution.py:55
  17.6 1.0 %slice_add_fusion = f32[2,32,512]{2,1,0:T(8,128)S(1)} fusion(f32[2,64,512]{2,1,0:T(8,128)} %shard_map.86), kind=kLoop, calls=%fused_computation.11 | loop fusion | flops 32768 | bytes 393216 | tf_op jit(solution)/shard_map/add | solution.py:60
  19.9 1.7 %dynamic_update_slice.6 = f32[34,4096]{1,0:T(8,128)S(1)} dynamic-update-slice(f32[34,4096]{1,0:T(8,128)S(1)} %broadcast_in_dim.38, f32[17,512]{1,0:T(8,128)S(1)} %get-tuple-element.23, s32[]{:T(128)} %constant.52.clone.1, s32[]{:T(128)S(6)} %select_n.113) | dynamic-update-slice | bytes 69636 | tf_op jit(solution)/shard_map/dynamic_update_slice | solution.py:171
  21.6 1.3 %dynamic_update_slice.7 = f32[34,4096]{1,0:T(8,128)S(1)} dynamic-update-slice(f32[34,4096]{1,0:T(8,128)S(1)} %dynamic_update_slice.6, f32[17,512]{1,0:T(8,128)S(1)} %get-tuple-element.22, s32[]{:T(128)} %constant.61.clone.1, s32[]{:T(128)S(6)} %select_n.114) | dynamic-update-slice | bytes 69636 | tf_op jit(solution)/shard_map/dynamic_update_slice | solution.py:171
  22.9 0.2 copy.91
  23.2 0.3 reshape.126
  23.5 0.6 constant_dynamic-slice_fusion.7
  24.1 0.1 copy.101
  24.3 0.2 collective-permute-start.2
  24.5 0.3 copy-done
  24.9 0.1 reshape.124
  25.0 0.1 copy-done.1
  25.0 0.9 %collective-permute-done.2 = f32[2,2,2,34,256]{4,2,3,1,0:T(2,128)S(1)} collective-permute-done((f32[2,2,2,34,256]{4,2,3,1,0:T(2,128)S(1)}, f32[2,2,2,34,256]{4,2,3,1,0:T(2,128)S(1)}, u32[]{:S(2)}, u32[]{:S(2)}) %collective-permute-start.2) | collective-permute-done | bytes 278560 | tf_op jit(solution)/shard_map/ppermute | solution.py:119
  25.9 0.2 bitcast_add_fusion
  26.1 0.2 constant_dynamic-slice_fusion.5
  26.4 2.5 %collective-permute-start.3 = (f32[2,2,34,256]{3,1,2,0:T(2,128)S(1)}, f32[2,2,34,256]{3,1,2,0:T(2,128)S(1)}, u32[]{:S(2)}, u32[]{:S(2)}) collective-permute-start(f32[2,2,34,256]{3,1,2,0:T(2,128)S(1)} %bitcast.111), channel_id=1, source_target_pairs={{0,4},{2,6},{4,0},{6,2},{8,12},{10,14},{12,8},{14,10},{16,20},{18,... | collective-permute-start | bytes 417800 | tf_op jit(solution)/shard_map/ppermute | solution.py:119
  28.9 1.3 %collective-permute-start.1 = (f32[2,2,256]{2,0,1:T(2,128)S(1)}, f32[2,2,256]{2,0,1:T(2,128)S(1)}, u32[]{:S(2)}, u32[]{:S(2)}) collective-permute-start(f32[2,2,256]{2,0,1:T(2,128)S(1)} %select_maximum_fusion), channel_id=1, source_target_pairs={{1,0},{3,2},{5,4},{7,6},{9,8},{11,10},{13,12},{15,14},{17,16},{19,... | collective-permute-start | bytes 12296 | tf_op jit(solution)/shard_map/ppermute | solution.py:161
  30.2 0.1 reshape.123
  30.3 4.5 %collective-permute-start = (f32[2,2,256]{2,0,1:T(2,128)S(1)}, f32[2,2,256]{2,0,1:T(2,128)S(1)}, u32[]{:S(2)}, u32[]{:S(2)}) collective-permute-start(f32[2,2,256]{2,0,1:T(2,128)S(1)} %select_maximum_fusion.1), channel_id=1, source_target_pairs={{0,1},{2,3},{4,5},{6,7},{8,9},{10,11},{12,13},{14,15},{16,17},{18,... | collective-permute-start | bytes 12296 | tf_op jit(solution)/shard_map/ppermute | solution.py:158
  34.9 0.1 bitcast_add_fusion.1
  35.0 0.1 constant_dynamic-slice_fusion.3
  35.2 2.2 %collective-permute-start.4 = (f32[2,34,256]{2,0,1:T(2,128)S(1)}, f32[2,34,256]{2,0,1:T(2,128)S(1)}, u32[]{:S(2)}, u32[]{:S(2)}) collective-permute-start(f32[2,34,256]{2,0,1:T(2,128)S(1)} %bitcast.113), channel_id=1, source_target_pairs={{0,8},{2,10},{4,12},{6,14},{8,0},{10,2},{12,4},{14,6},{16,24},{18,... | collective-permute-start | bytes 208904 | tf_op jit(solution)/shard_map/ppermute | solution.py:119
  37.4 2.3 %collective-permute-done.4 = f32[2,34,256]{2,0,1:T(2,128)S(1)} collective-permute-done((f32[2,34,256]{2,0,1:T(2,128)S(1)}, f32[2,34,256]{2,0,1:T(2,128)S(1)}, u32[]{:S(2)}, u32[]{:S(2)}) %collective-permute-start.4) | collective-permute-done | bytes 69664 | tf_op jit(solution)/shard_map/ppermute | solution.py:119
  39.8 3.1 %collective-permute-start.5 = (f32[34,256]{1,0:T(8,128)S(1)}, f32[34,256]{1,0:T(8,128)S(1)}, u32[]{:S(2)}, u32[]{:S(2)}) collective-permute-start(f32[34,256]{1,0:T(8,128)S(1)} %bitcast.114), channel_id=1, source_target_pairs={{0,16},{2,18},{4,20},{6,22},{8,24},{10,26},{12,28},{14,30},{16,0},... | collective-permute-start | bytes 104456 | tf_op jit(solution)/shard_map/ppermute | solution.py:119
  42.9 0.1 reshape_squeeze.7
  43.0 0.1 reshape_squeeze.6
  43.1 1.8 %collective-permute-done.5 = f32[34,256]{1,0:T(8,128)S(1)} collective-permute-done((f32[34,256]{1,0:T(8,128)S(1)}, f32[34,256]{1,0:T(8,128)S(1)}, u32[]{:S(2)}, u32[]{:S(2)}) %collective-permute-start.5) | collective-permute-done | bytes 34848 | tf_op jit(solution)/shard_map/ppermute | solution.py:119
  44.9 1.3 %collective-permute-start.7 = (f32[2,2,256]{2,1,0:T(2,128)S(1)}, f32[2,2,256]{2,1,0:T(2,128)S(1)}, u32[]{:S(2)}, u32[]{:S(2)}) collective-permute-start(f32[2,2,256]{2,1,0:T(2,128)S(1)} %get-tuple-element.29), channel_id=1, source_target_pairs={{1,0},{3,2},{5,4},{7,6},{9,8},{11,10},{13,12},{15,14},{17,16},{19,... | collective-permute-start | bytes 12296 | tf_op jit(solution)/shard_map/ppermute | solution.py:179
  46.2 4.5 %collective-permute-start.6 = (f32[2,2,256]{2,1,0:T(2,128)S(1)}, f32[2,2,256]{2,1,0:T(2,128)S(1)}, u32[]{:S(2)}, u32[]{:S(2)}) collective-permute-start(f32[2,2,256]{2,1,0:T(2,128)S(1)} %get-tuple-element.28), channel_id=1, source_target_pairs={{0,1},{2,3},{4,5},{6,7},{8,9},{10,11},{12,13},{14,15},{16,17},{18,... | collective-permute-start | bytes 12296 | tf_op jit(solution)/shard_map/ppermute | solution.py:177
  50.8 0.1 add_add_fusion
  50.9 1.2 %collective-permute-done.6 = f32[2,2,256]{2,1,0:T(2,128)S(1)} collective-permute-done((f32[2,2,256]{2,1,0:T(2,128)S(1)}, f32[2,2,256]{2,1,0:T(2,128)S(1)}, u32[]{:S(2)}, u32[]{:S(2)}) %collective-permute-start.6) | collective-permute-done | bytes 4128 | tf_op jit(solution)/shard_map/ppermute | solution.py:177
  52.1 0.1 fusion.5
  52.2 0.6 fusion.6
  52.8 3.0 %collective-permute-start.8 = (f32[32,256]{1,0:T(8,128)S(1)}, f32[32,256]{1,0:T(8,128)S(1)}, u32[]{:S(2)}, u32[]{:S(2)}) collective-permute-start(f32[32,256]{1,0:T(8,128)S(1)} %bitcast.112), channel_id=1, source_target_pairs={{0,16},{2,18},{4,20},{6,22},{8,24},{10,26},{12,28},{14,30},{16,0},... | collective-permute-start | bytes 98312 | tf_op jit(solution)/shard_map/ppermute | solution.py:130
  55.7 1.9 %collective-permute-done.8 = f32[32,256]{1,0:T(8,128)S(1)} collective-permute-done((f32[32,256]{1,0:T(8,128)S(1)}, f32[32,256]{1,0:T(8,128)S(1)}, u32[]{:S(2)}, u32[]{:S(2)}) %collective-permute-start.8) | collective-permute-done | bytes 32800 | tf_op jit(solution)/shard_map/ppermute | solution.py:130
  57.7 1.9 %collective-permute-start.9 = (f32[2,32,256]{2,1,0:T(8,128)S(1)}, f32[2,32,256]{2,1,0:T(8,128)S(1)}, u32[]{:S(2)}, u32[]{:S(2)}) collective-permute-start(f32[2,32,256]{2,1,0:T(8,128)S(1)} %pad_maximum_fusion.3), channel_id=1, source_target_pairs={{0,8},{2,10},{4,12},{6,14},{8,0},{10,2},{12,4},{14,6},{16,24},{18,... | collective-permute-start | bytes 196616 | tf_op jit(solution)/shard_map/ppermute | solution.py:130
  59.6 2.4 %collective-permute-done.9 = f32[2,32,256]{2,1,0:T(8,128)S(1)} collective-permute-done((f32[2,32,256]{2,1,0:T(8,128)S(1)}, f32[2,32,256]{2,1,0:T(8,128)S(1)}, u32[]{:S(2)}, u32[]{:S(2)}) %collective-permute-start.9) | collective-permute-done | bytes 65568 | tf_op jit(solution)/shard_map/ppermute | solution.py:130
  62.0 0.6 collective-permute-start.10
  62.6 4.5 %collective-permute-done.10 = f32[2,2,32,256]{3,2,1,0:T(8,128)S(1)} collective-permute-done((f32[2,2,32,256]{3,2,1,0:T(8,128)S(1)}, f32[2,2,32,256]{3,2,1,0:T(8,128)S(1)}, u32[]{:S(2)}, u32[]{:S(2)}) %collective-permute-start.10) | collective-permute-done | bytes 131104 | tf_op jit(solution)/shard_map/ppermute | solution.py:130
  67.2 0.1 copy.83
  67.3 0.1 copy.82
  67.4 0.1 copy.81
  67.5 0.7 select_add_fusion.rw_ref
  68.2 0.6 collective-permute-done.11
  68.9 0.1 dynamic-slice_bitcast_fusion
  69.0 0.6 pad_maximum_fusion.4.back_ref
  69.7 9.7 %shard_map.87 = f32[16,16384]{1,0:T(8,128)} custom-call(f32[2,16,512]{2,1,0:T(8,128)} %pad_maximum_fusion.4.back_ref, f32[16,16384]{1,0:T(8,128)} %vol_ref.3, f32[2,16384]{1,0:T(2,128)} %amp_ref.3, s32[2,16384]{1,0:T(2,128)} %off_ref.3, s32[2,16384]{1,0:T(2,128)} %wid_ref.3, f32[2,16,1]{2,1,0:T(8,128)} %select_add_fusion.rw_ref), custom_call_target="tpu_custom_call" | custom-call | tf_op jit(solution)/shard_map/pallas_call | solution.py:94
  (51 shorter events, 0.8 us)
Async XLA Ops:
  24.1 0.7 copy-start
  24.3 0.8 copy-start.1
  24.3 1.6 %collective-permute-start.2 = (f32[2,2,2,34,256]{4,2,3,1,0:T(2,128)S(1)}, f32[2,2,2,34,256]{4,2,3,1,0:T(2,128)S(1)}, u32[]{:S(2)}, u32[]{:S(2)}) collective-permute-start(f32[2,2,2,34,256]{4,2,3,1,0:T(2,128)S(1)} %bitcast.110), channel_id=1, source_target_pairs={{0,2},{2,0},{4,6},{6,4},{8,10},{10,8},{12,14},{14,12},{16,18},{18,... | collective-permute-start | bytes 835592 | tf_op jit(solution)/shard_map/ppermute | solution.py:119
  26.4 8.4 %collective-permute-start.3 = (f32[2,2,34,256]{3,1,2,0:T(2,128)S(1)}, f32[2,2,34,256]{3,1,2,0:T(2,128)S(1)}, u32[]{:S(2)}, u32[]{:S(2)}) collective-permute-start(f32[2,2,34,256]{3,1,2,0:T(2,128)S(1)} %bitcast.111), channel_id=1, source_target_pairs={{0,4},{2,6},{4,0},{6,2},{8,12},{10,14},{12,8},{14,10},{16,20},{18,... | collective-permute-start | bytes 417800 | tf_op jit(solution)/shard_map/ppermute | solution.py:119
  28.9 14.0 %collective-permute-start.1 = (f32[2,2,256]{2,0,1:T(2,128)S(1)}, f32[2,2,256]{2,0,1:T(2,128)S(1)}, u32[]{:S(2)}, u32[]{:S(2)}) collective-permute-start(f32[2,2,256]{2,0,1:T(2,128)S(1)} %select_maximum_fusion), channel_id=1, source_target_pairs={{1,0},{3,2},{5,4},{7,6},{9,8},{11,10},{13,12},{15,14},{17,16},{19,... | collective-permute-start | bytes 12296 | tf_op jit(solution)/shard_map/ppermute | solution.py:161
  30.3 12.7 %collective-permute-start = (f32[2,2,256]{2,0,1:T(2,128)S(1)}, f32[2,2,256]{2,0,1:T(2,128)S(1)}, u32[]{:S(2)}, u32[]{:S(2)}) collective-permute-start(f32[2,2,256]{2,0,1:T(2,128)S(1)} %select_maximum_fusion.1), channel_id=1, source_target_pairs={{0,1},{2,3},{4,5},{6,7},{8,9},{10,11},{12,13},{14,15},{16,17},{18,... | collective-permute-start | bytes 12296 | tf_op jit(solution)/shard_map/ppermute | solution.py:158
  35.2 4.5 %collective-permute-start.4 = (f32[2,34,256]{2,0,1:T(2,128)S(1)}, f32[2,34,256]{2,0,1:T(2,128)S(1)}, u32[]{:S(2)}, u32[]{:S(2)}) collective-permute-start(f32[2,34,256]{2,0,1:T(2,128)S(1)} %bitcast.113), channel_id=1, source_target_pairs={{0,8},{2,10},{4,12},{6,14},{8,0},{10,2},{12,4},{14,6},{16,24},{18,... | collective-permute-start | bytes 208904 | tf_op jit(solution)/shard_map/ppermute | solution.py:119
  39.8 5.1 %collective-permute-start.5 = (f32[34,256]{1,0:T(8,128)S(1)}, f32[34,256]{1,0:T(8,128)S(1)}, u32[]{:S(2)}, u32[]{:S(2)}) collective-permute-start(f32[34,256]{1,0:T(8,128)S(1)} %bitcast.114), channel_id=1, source_target_pairs={{0,16},{2,18},{4,20},{6,22},{8,24},{10,26},{12,28},{14,30},{16,0},... | collective-permute-start | bytes 104456 | tf_op jit(solution)/shard_map/ppermute | solution.py:119
  44.9 6.0 %collective-permute-start.7 = (f32[2,2,256]{2,1,0:T(2,128)S(1)}, f32[2,2,256]{2,1,0:T(2,128)S(1)}, u32[]{:S(2)}, u32[]{:S(2)}) collective-permute-start(f32[2,2,256]{2,1,0:T(2,128)S(1)} %get-tuple-element.29), channel_id=1, source_target_pairs={{1,0},{3,2},{5,4},{7,6},{9,8},{11,10},{13,12},{15,14},{17,16},{19,... | collective-permute-start | bytes 12296 | tf_op jit(solution)/shard_map/ppermute | solution.py:179
  46.2 5.9 %collective-permute-start.6 = (f32[2,2,256]{2,1,0:T(2,128)S(1)}, f32[2,2,256]{2,1,0:T(2,128)S(1)}, u32[]{:S(2)}, u32[]{:S(2)}) collective-permute-start(f32[2,2,256]{2,1,0:T(2,128)S(1)} %get-tuple-element.28), channel_id=1, source_target_pairs={{0,1},{2,3},{4,5},{6,7},{8,9},{10,11},{12,13},{14,15},{16,17},{18,... | collective-permute-start | bytes 12296 | tf_op jit(solution)/shard_map/ppermute | solution.py:177
  52.8 4.8 %collective-permute-start.8 = (f32[32,256]{1,0:T(8,128)S(1)}, f32[32,256]{1,0:T(8,128)S(1)}, u32[]{:S(2)}, u32[]{:S(2)}) collective-permute-start(f32[32,256]{1,0:T(8,128)S(1)} %bitcast.112), channel_id=1, source_target_pairs={{0,16},{2,18},{4,20},{6,22},{8,24},{10,26},{12,28},{14,30},{16,0},... | collective-permute-start | bytes 98312 | tf_op jit(solution)/shard_map/ppermute | solution.py:130
  57.7 4.3 %collective-permute-start.9 = (f32[2,32,256]{2,1,0:T(8,128)S(1)}, f32[2,32,256]{2,1,0:T(8,128)S(1)}, u32[]{:S(2)}, u32[]{:S(2)}) collective-permute-start(f32[2,32,256]{2,1,0:T(8,128)S(1)} %pad_maximum_fusion.3), channel_id=1, source_target_pairs={{0,8},{2,10},{4,12},{6,14},{8,0},{10,2},{12,4},{14,6},{16,24},{18,... | collective-permute-start | bytes 196616 | tf_op jit(solution)/shard_map/ppermute | solution.py:130
  62.0 5.0 %collective-permute-start.10 = (f32[2,2,32,256]{3,2,1,0:T(8,128)S(1)}, f32[2,2,32,256]{3,2,1,0:T(8,128)S(1)}, u32[]{:S(2)}, u32[]{:S(2)}) collective-permute-start(f32[2,2,32,256]{3,2,1,0:T(8,128)S(1)} %pad_maximum_fusion.2), channel_id=1, source_target_pairs={{0,4},{2,6},{4,0},{6,2},{8,12},{10,14},{12,8},{14,10},{16,20},{18,... | collective-permute-start | bytes 393224 | tf_op jit(solution)/shard_map/ppermute | solution.py:130
  67.1 1.6 %collective-permute-start.11 = (f32[2,2,2,32,256]{4,3,2,1,0:T(8,128)S(1)}, f32[2,2,2,32,256]{4,3,2,1,0:T(8,128)S(1)}, u32[]{:S(2)}, u32[]{:S(2)}) collective-permute-start(f32[2,2,2,32,256]{4,3,2,1,0:T(8,128)S(1)} %pad_maximum_fusion.1), channel_id=1, source_target_pairs={{0,2},{2,0},{4,6},{6,4},{8,10},{10,8},{12,14},{14,12},{16,18},{18,... | collective-permute-start | bytes 786440 | tf_op jit(solution)/shard_map/ppermute | solution.py:130

commit v8 on v7

--- a/solution.py
+++ b/solution.py
@@ -155,14 +155,6 @@
         cols = packed[:, 1, : 3 * 2].reshape(view_count, 3, 2)
         return packed[:, :1], jnp.transpose(cols, (1, 0, 2))
 
-    from_below = lax.ppermute(
-        pack(measured[:, slab_rows - 1 :], axial_weight[:, :, slab_rows - 2 :]), "gz", up_pairs
-    )
-    from_above = lax.ppermute(pack(measured[:, :1], axial_weight[:, :, :2]), "gz", down_pairs)
-    meas_below, weight_below = unpack(from_below)
-    meas_above, weight_above = unpack(from_above)
-    measured_ext = jnp.concatenate([meas_below, measured, meas_above], axis=1)
-    weight_ext = jnp.concatenate([weight_below, axial_weight, weight_above], axis=2)
 
     band_rows = forward_band(volume, amplitude, column_offset, column_width)
     band_height = slab_rows + 1
@@ -172,14 +164,24 @@
     reduced = reduce_scatter_xy(placed, xy_count).reshape(view_count, band_height, shard_width)
     proj_cols = reduced[:, :slab_rows]
     cover = reduced[:, slab_rows : slab_rows + 1]
-    proj_ext = jnp.concatenate(
-        [
-            lax.ppermute(proj_cols[:, slab_rows - 2 :], "gz", up_pairs),
-            proj_cols,
-            lax.ppermute(proj_cols[:, :2], "gz", down_pairs),
-        ],
-        axis=1,
-    )
+    halo_below = lax.ppermute(
+        jnp.concatenate(
+            [proj_cols[:, slab_rows - 2 :], pack(measured[:, slab_rows - 1 :], axial_weight[:, :, slab_rows - 2 :])],
+            axis=1,
+        ),
+        "gz",
+        up_pairs,
+    )
+    halo_above = lax.ppermute(
+        jnp.concatenate([proj_cols[:, :2], pack(measured[:, :1], axial_weight[:, :, :2])], axis=1),
+        "gz",
+        down_pairs,
+    )
+    proj_ext = jnp.concatenate([halo_below[:, :2], proj_cols, halo_above[:, :2]], axis=1)
+    meas_below, weight_below = unpack(halo_below[:, 2:])
+    meas_above, weight_above = unpack(halo_above[:, 2:])
+    measured_ext = jnp.concatenate([meas_below, measured, meas_above], axis=1)
+    weight_ext = jnp.concatenate([weight_below, axial_weight, weight_above], axis=2)
 
     ext_rows = slab_rows + 2
     mid_w = weight_ext[1, :, 1 : ext_rows + 1][:, :, None]

time: 79.9 us -> 81.4 us (1.019)
  waiting for transfers between devices: 15.4 us -> 22.7 us
  starting transfers between devices: 25.2 us -> 18.9 us
    ppermute x4 -> x2, starting transfers between devices: 11.7 us -> 4.91 us  [the longest x1 3.62 us: local(): lax.ppermute(jnp.concatenate([proj_cols[:, slab_rows - 2:], pack(measured...]
    ppermute x4, waiting for transfers between devices: 4.93 us -> 9.72 us  [reduce_scatter_xy(): y = keep + lax.ppermute(send, 'xy', [(i, i ^ 1 << j) for i in range(count)])]
    ppermute x4 -> x2, waiting for transfers between devices: 1.16 us -> 4.18 us  [the longest x1 4.18 us: local(): lax.ppermute(jnp.concatenate([proj_cols[:, :2], pack(measured[:, :1], axi...]
  transfers between devices with their start and end apart: 12 -> 10, of which waited for: 8 -> 9; matrix products, arithmetic and copies ran while one was open for 2% -> 2% of each run, Pallas kernels for 0% -> 0%
where the time goes in v8:
time: 81.4 us; the launch traced here: 80.9 us
  Pallas kernels  22.9 us (28%)
  waiting for transfers between devices  22.7 us (28%)
  starting transfers between devices  18.9 us (23%)
  local copies, waits for them, and re-layouts  8.2 us (10%)
  between operations  4.64 us (6%)
  other arithmetic  3.63 us (4%)
    pallas_call x1, Pallas kernels, forward_band(): pl.pallas_call(_forward_kernel, out_shape=jax.ShapeDtypeStruct((view_coun...  13.2 us
    ppermute x4, waiting for transfers between devices, reduce_scatter_xy(): y = keep + lax.ppermute(send, 'xy', [(i, i ^ 1 << j) for i in range(count)])  9.72 us
    pallas_call x1, Pallas kernels, backward_update(): pl.pallas_call(_backward_kernel, out_shape=jax.ShapeDtypeStruct(volume.sh...  9.66 us
    ppermute x4, waiting for transfers between devices, all_gather_xy(): other = lax.ppermute(y, 'xy', [(i, i ^ 1 << j) for i in range(count)])  8.84 us
    ppermute x4, starting transfers between devices, reduce_scatter_xy(): y = keep + lax.ppermute(send, 'xy', [(i, i ^ 1 << j) for i in range(count)])  7.99 us
    ppermute x4, starting transfers between devices, all_gather_xy(): other = lax.ppermute(y, 'xy', [(i, i ^ 1 << j) for i in range(count)])  5.97 us
    ppermute x1, waiting for transfers between devices, local(): lax.ppermute(jnp.concatenate([proj_cols[:, :2], pack(measured[:, :1], axi...  4.18 us
    ppermute x1, starting transfers between devices, local(): lax.ppermute(jnp.concatenate([proj_cols[:, slab_rows - 2:], pack(measured...  3.62 us
  transfers between devices with their start and end apart: 10, of which 9 were waited for; matrix products, arithmetic and copies ran while one was open for 2% of the time, Pallas kernels for 0%

profile of v8, /device:TPU:0, one launch (start us, length us, event | category | flops | bytes accessed | tf_op | source)
XLA Modules:
  0.0 80.9 jit_solution(554309214356031980)
XLA Ops:
  0.6 0.6 copy-done.5
  1.3 0.6 fusion.18
  4.3 13.2 %shard_map.86 = f32[2,64,512]{2,1,0:T(8,128)} custom-call(f32[16,16384]{1,0:T(8,128)} %vol_ref.3, f32[2,16384]{1,0:T(2,128)} %amp_ref.3, s32[2,16384]{1,0:T(2,128)} %off_ref.3, s32[2,16384]{1,0:T(2,128)} %wid_ref.3), custom_call_target="tpu_custom_call" | custom-call | tf_op jit(solution)/shard_map/pallas_call | solution.py:55
  17.5 1.0 %slice_add_fusion = f32[2,32,512]{2,1,0:T(8,128)S(1)} fusion(f32[2,64,512]{2,1,0:T(8,128)} %shard_map.86), kind=kLoop, calls=%fused_computation.11 | loop fusion | flops 32768 | bytes 393216 | tf_op jit(solution)/shard_map/add | solution.py:60
  19.8 1.7 %dynamic_update_slice.6 = f32[34,4096]{1,0:T(8,128)S(1)} dynamic-update-slice(f32[34,4096]{1,0:T(8,128)S(1)} %broadcast_in_dim.38, f32[17,512]{1,0:T(8,128)S(1)} %get-tuple-element.23, s32[]{:T(128)} %constant.52.clone.1, s32[]{:T(128)S(6)} %select_n.113) | dynamic-update-slice | bytes 69636 | tf_op jit(solution)/shard_map/dynamic_update_slice | solution.py:163
  21.5 1.3 %dynamic_update_slice.7 = f32[34,4096]{1,0:T(8,128)S(1)} dynamic-update-slice(f32[34,4096]{1,0:T(8,128)S(1)} %dynamic_update_slice.6, f32[17,512]{1,0:T(8,128)S(1)} %get-tuple-element.22, s32[]{:T(128)} %constant.61.clone.1, s32[]{:T(128)S(6)} %select_n.114) | dynamic-update-slice | bytes 69636 | tf_op jit(solution)/shard_map/dynamic_update_slice | solution.py:163
  22.8 0.2 copy.83
  23.1 0.3 reshape.124
  23.4 0.6 constant_dynamic-slice_fusion.7
  24.0 0.1 copy.93
  24.2 0.5 collective-permute-start
  24.7 1.2 %collective-permute-done = f32[2,2,2,34,256]{4,2,3,1,0:T(2,128)S(1)} collective-permute-done((f32[2,2,2,34,256]{4,2,3,1,0:T(2,128)S(1)}, f32[2,2,2,34,256]{4,2,3,1,0:T(2,128)S(1)}, u32[]{:S(2)}, u32[]{:S(2)}) %collective-permute-start) | collective-permute-done | bytes 278560 | tf_op jit(solution)/shard_map/ppermute | solution.py:119
  25.9 0.2 bitcast_add_fusion
  26.1 0.2 constant_dynamic-slice_fusion.5
  26.4 3.0 %collective-permute-start.1 = (f32[2,2,34,256]{3,1,2,0:T(2,128)S(1)}, f32[2,2,34,256]{3,1,2,0:T(2,128)S(1)}, u32[]{:S(2)}, u32[]{:S(2)}) collective-permute-start(f32[2,2,34,256]{3,1,2,0:T(2,128)S(1)} %bitcast.109), channel_id=1, source_target_pairs={{0,4},{2,6},{4,0},{6,2},{8,12},{10,14},{12,8},{14,10},{16,20},{18,... | collective-permute-start | bytes 417800 | tf_op jit(solution)/shard_map/ppermute | solution.py:119
  29.4 4.0 %collective-permute-done.1 = f32[2,2,34,256]{3,1,2,0:T(2,128)S(1)} collective-permute-done((f32[2,2,34,256]{3,1,2,0:T(2,128)S(1)}, f32[2,2,34,256]{3,1,2,0:T(2,128)S(1)}, u32[]{:S(2)}, u32[]{:S(2)}) %collective-permute-start.1) | collective-permute-done | bytes 139296 | tf_op jit(solution)/shard_map/ppermute | solution.py:119
  33.3 0.1 bitcast_add_fusion.1
  33.4 0.1 constant_dynamic-slice_fusion.3
  33.6 1.6 %collective-permute-start.2 = (f32[2,34,256]{2,0,1:T(2,128)S(1)}, f32[2,34,256]{2,0,1:T(2,128)S(1)}, u32[]{:S(2)}, u32[]{:S(2)}) collective-permute-start(f32[2,34,256]{2,0,1:T(2,128)S(1)} %bitcast.111), channel_id=1, source_target_pairs={{0,8},{2,10},{4,12},{6,14},{8,0},{10,2},{12,4},{14,6},{16,24},{18,... | collective-permute-start | bytes 208904 | tf_op jit(solution)/shard_map/ppermute | solution.py:119
  35.3 2.7 %collective-permute-done.2 = f32[2,34,256]{2,0,1:T(2,128)S(1)} collective-permute-done((f32[2,34,256]{2,0,1:T(2,128)S(1)}, f32[2,34,256]{2,0,1:T(2,128)S(1)}, u32[]{:S(2)}, u32[]{:S(2)}) %collective-permute-start.2) | collective-permute-done | bytes 69664 | tf_op jit(solution)/shard_map/ppermute | solution.py:119
  38.1 2.9 %collective-permute-start.3 = (f32[34,256]{1,0:T(8,128)S(1)}, f32[34,256]{1,0:T(8,128)S(1)}, u32[]{:S(2)}, u32[]{:S(2)}) collective-permute-start(f32[34,256]{1,0:T(8,128)S(1)} %bitcast.112), channel_id=1, source_target_pairs={{0,16},{2,18},{4,20},{6,22},{8,24},{10,26},{12,28},{14,30},{16,0},... | collective-permute-start | bytes 104456 | tf_op jit(solution)/shard_map/ppermute | solution.py:119
  41.0 0.1 reshape.126
  41.1 0.1 reshape.127
  41.2 1.9 %collective-permute-done.3 = f32[34,256]{1,0:T(8,128)S(1)} collective-permute-done((f32[34,256]{1,0:T(8,128)S(1)}, f32[34,256]{1,0:T(8,128)S(1)}, u32[]{:S(2)}, u32[]{:S(2)}) %collective-permute-start.3) | collective-permute-done | bytes 34848 | tf_op jit(solution)/shard_map/ppermute | solution.py:119
  43.2 3.6 %collective-permute-start.4 = (f32[2,4,256]{2,1,0:T(4,128)S(1)}, f32[2,4,256]{2,1,0:T(4,128)S(1)}, u32[]{:S(2)}, u32[]{:S(2)}) collective-permute-start(f32[2,4,256]{2,1,0:T(4,128)S(1)} %select_maximum_fusion.1), channel_id=1, source_target_pairs={{0,1},{2,3},{4,5},{6,7},{8,9},{10,11},{12,13},{14,15},{16,17},{18,... | collective-permute-start | bytes 24584 | tf_op jit(solution)/shard_map/ppermute | solution.py:167
  46.8 1.3 %collective-permute-start.5 = (f32[2,4,256]{2,1,0:T(4,128)S(1)}, f32[2,4,256]{2,1,0:T(4,128)S(1)}, u32[]{:S(2)}, u32[]{:S(2)}) collective-permute-start(f32[2,4,256]{2,1,0:T(4,128)S(1)} %select_maximum_fusion), channel_id=1, source_target_pairs={{1,0},{3,2},{5,4},{7,6},{9,8},{11,10},{13,12},{15,14},{17,16},{19,... | collective-permute-start | bytes 24584 | tf_op jit(solution)/shard_map/ppermute | solution.py:175
  48.2 4.2 %collective-permute-done.5 = f32[2,4,256]{2,1,0:T(4,128)S(1)} collective-permute-done((f32[2,4,256]{2,1,0:T(4,128)S(1)}, f32[2,4,256]{2,1,0:T(4,128)S(1)}, u32[]{:S(2)}, u32[]{:S(2)}) %collective-permute-start.5) | collective-permute-done | bytes 8224 | tf_op jit(solution)/shard_map/ppermute | solution.py:175
  52.4 0.1 reshape_squeeze.6
  52.5 0.1 reshape_squeeze.7
  52.7 0.3 copy-done.4
  53.0 0.3 slice-done
  53.2 0.4 slice-done.2
  53.7 0.1 fusion.5
  53.8 0.6 fusion.6
  54.4 2.7 %collective-permute-start.6 = (f32[32,256]{1,0:T(8,128)S(1)}, f32[32,256]{1,0:T(8,128)S(1)}, u32[]{:S(2)}, u32[]{:S(2)}) collective-permute-start(f32[32,256]{1,0:T(8,128)S(1)} %bitcast.110), channel_id=1, source_target_pairs={{0,16},{2,18},{4,20},{6,22},{8,24},{10,26},{12,28},{14,30},{16,0},... | collective-permute-start | bytes 98312 | tf_op jit(solution)/shard_map/ppermute | solution.py:130
  57.1 2.1 %collective-permute-done.6 = f32[32,256]{1,0:T(8,128)S(1)} collective-permute-done((f32[32,256]{1,0:T(8,128)S(1)}, f32[32,256]{1,0:T(8,128)S(1)}, u32[]{:S(2)}, u32[]{:S(2)}) %collective-permute-start.6) | collective-permute-done | bytes 32800 | tf_op jit(solution)/shard_map/ppermute | solution.py:130
  59.2 1.6 %collective-permute-start.7 = (f32[2,32,256]{2,1,0:T(8,128)S(1)}, f32[2,32,256]{2,1,0:T(8,128)S(1)}, u32[]{:S(2)}, u32[]{:S(2)}) collective-permute-start(f32[2,32,256]{2,1,0:T(8,128)S(1)} %pad_maximum_fusion.3), channel_id=1, source_target_pairs={{0,8},{2,10},{4,12},{6,14},{8,0},{10,2},{12,4},{14,6},{16,24},{18,... | collective-permute-start | bytes 196616 | tf_op jit(solution)/shard_map/ppermute | solution.py:130
  60.9 2.7 %collective-permute-done.7 = f32[2,32,256]{2,1,0:T(8,128)S(1)} collective-permute-done((f32[2,32,256]{2,1,0:T(8,128)S(1)}, f32[2,32,256]{2,1,0:T(8,128)S(1)}, u32[]{:S(2)}, u32[]{:S(2)}) %collective-permute-start.7) | collective-permute-done | bytes 65568 | tf_op jit(solution)/shard_map/ppermute | solution.py:130
  63.6 1.6 %collective-permute-start.8 = (f32[2,2,32,256]{3,2,1,0:T(8,128)S(1)}, f32[2,2,32,256]{3,2,1,0:T(8,128)S(1)}, u32[]{:S(2)}, u32[]{:S(2)}) collective-permute-start(f32[2,2,32,256]{3,2,1,0:T(8,128)S(1)} %pad_maximum_fusion.2), channel_id=1, source_target_pairs={{0,4},{2,6},{4,0},{6,2},{8,12},{10,14},{12,8},{14,10},{16,20},{18,... | collective-permute-start | bytes 393224 | tf_op jit(solution)/shard_map/ppermute | solution.py:130
  65.2 3.4 %collective-permute-done.8 = f32[2,2,32,256]{3,2,1,0:T(8,128)S(1)} collective-permute-done((f32[2,2,32,256]{3,2,1,0:T(8,128)S(1)}, f32[2,2,32,256]{3,2,1,0:T(8,128)S(1)}, u32[]{:S(2)}, u32[]{:S(2)}) %collective-permute-start.8) | collective-permute-done | bytes 131104 | tf_op jit(solution)/shard_map/ppermute | solution.py:130
  68.8 0.1 copy.73
  68.9 0.1 copy.74
  69.0 0.1 copy.75
  69.1 0.7 select_add_fusion.rw_ref
  69.7 0.6 collective-permute-done.9
  70.5 0.1 dynamic-slice_bitcast_fusion.1
  70.6 0.6 pad_maximum_fusion.4.back_ref
  71.3 9.7 %shard_map.87 = f32[16,16384]{1,0:T(8,128)} custom-call(f32[2,16,512]{2,1,0:T(8,128)} %pad_maximum_fusion.4.back_ref, f32[16,16384]{1,0:T(8,128)} %vol_ref.3, f32[2,16384]{1,0:T(2,128)} %amp_ref.3, s32[2,16384]{1,0:T(2,128)} %off_ref.3, s32[2,16384]{1,0:T(2,128)} %wid_ref.3, f32[2,16,1]{2,1,0:T(8,128)} %select_add_fusion.rw_ref), custom_call_target="tpu_custom_call" | custom-call | tf_op jit(solution)/shard_map/pallas_call | solution.py:94
  (56 shorter events, 1.0 us)
Async XLA Ops:
  0.6 0.7 copy-start.5
  24.2 1.7 %collective-permute-start = (f32[2,2,2,34,256]{4,2,3,1,0:T(2,128)S(1)}, f32[2,2,2,34,256]{4,2,3,1,0:T(2,128)S(1)}, u32[]{:S(2)}, u32[]{:S(2)}) collective-permute-start(f32[2,2,2,34,256]{4,2,3,1,0:T(2,128)S(1)} %bitcast.108), channel_id=1, source_target_pairs={{0,2},{2,0},{4,6},{6,4},{8,10},{10,8},{12,14},{14,12},{16,18},{18,... | collective-permute-start | bytes 835592 | tf_op jit(solution)/shard_map/ppermute | solution.py:119
  26.3 3.0 %copy-start.2 = (f32[2,16,256]{2,1,0:T(8,128)S(1)}, f32[2,16,256]{2,1,0:T(8,128)}, u32[]{:S(2)}) copy-start(f32[2,16,256]{2,1,0:T(8,128)} %param.8) | copy-start | bytes 98308
  26.4 6.9 %collective-permute-start.1 = (f32[2,2,34,256]{3,1,2,0:T(2,128)S(1)}, f32[2,2,34,256]{3,1,2,0:T(2,128)S(1)}, u32[]{:S(2)}, u32[]{:S(2)}) collective-permute-start(f32[2,2,34,256]{3,1,2,0:T(2,128)S(1)} %bitcast.109), channel_id=1, source_target_pairs={{0,4},{2,6},{4,0},{6,2},{8,12},{10,14},{12,8},{14,10},{16,20},{18,... | collective-permute-start | bytes 417800 | tf_op jit(solution)/shard_map/ppermute | solution.py:119
  33.6 1.7 %copy-start.1 = (f32[3,2,16]{2,1,0:T(2,128)S(1)}, f32[3,2,16]{2,1,0:T(2,128)}, u32[]{:S(2)}) copy-start(f32[3,2,16]{2,1,0:T(2,128)} %param.13) | copy-start | bytes 1156
  33.6 4.4 %collective-permute-start.2 = (f32[2,34,256]{2,0,1:T(2,128)S(1)}, f32[2,34,256]{2,0,1:T(2,128)S(1)}, u32[]{:S(2)}, u32[]{:S(2)}) collective-permute-start(f32[2,34,256]{2,0,1:T(2,128)S(1)} %bitcast.111), channel_id=1, source_target_pairs={{0,8},{2,10},{4,12},{6,14},{8,0},{10,2},{12,4},{14,6},{16,24},{18,... | collective-permute-start | bytes 208904 | tf_op jit(solution)/shard_map/ppermute | solution.py:119
  38.1 5.0 %collective-permute-start.3 = (f32[34,256]{1,0:T(8,128)S(1)}, f32[34,256]{1,0:T(8,128)S(1)}, u32[]{:S(2)}, u32[]{:S(2)}) collective-permute-start(f32[34,256]{1,0:T(8,128)S(1)} %bitcast.112), channel_id=1, source_target_pairs={{0,16},{2,18},{4,20},{6,22},{8,24},{10,26},{12,28},{14,30},{16,0},... | collective-permute-start | bytes 104456 | tf_op jit(solution)/shard_map/ppermute | solution.py:119
  43.1 5.0 %copy-start = (f32[2,17,256]{2,1,0:T(8,128)}, f32[2,17,256]{2,1,0:T(8,128)S(1)}, u32[]{:S(2)}) copy-start(f32[2,17,256]{2,1,0:T(8,128)S(1)} %reshape.125) | copy-start | bytes 104452
  43.2 5.0 %collective-permute-start.4 = (f32[2,4,256]{2,1,0:T(4,128)S(1)}, f32[2,4,256]{2,1,0:T(4,128)S(1)}, u32[]{:S(2)}, u32[]{:S(2)}) collective-permute-start(f32[2,4,256]{2,1,0:T(4,128)S(1)} %select_maximum_fusion.1), channel_id=1, source_target_pairs={{0,1},{2,3},{4,5},{6,7},{8,9},{10,11},{12,13},{14,15},{16,17},{18,... | collective-permute-start | bytes 24584 | tf_op jit(solution)/shard_map/ppermute | solution.py:167
  46.8 5.5 %collective-permute-start.5 = (f32[2,4,256]{2,1,0:T(4,128)S(1)}, f32[2,4,256]{2,1,0:T(4,128)S(1)}, u32[]{:S(2)}, u32[]{:S(2)}) collective-permute-start(f32[2,4,256]{2,1,0:T(4,128)S(1)} %select_maximum_fusion), channel_id=1, source_target_pairs={{1,0},{3,2},{5,4},{7,6},{9,8},{11,10},{13,12},{15,14},{17,16},{19,... | collective-permute-start | bytes 24584 | tf_op jit(solution)/shard_map/ppermute | solution.py:175
  48.2 4.5 %copy-start.3 = (f32[2,4,256]{2,1,0:T(4,128)}, f32[2,4,256]{2,1,0:T(4,128)S(1)}, u32[]{:S(2)}) copy-start(f32[2,4,256]{2,1,0:T(4,128)S(1)} %collective-permute-done.4) | copy-start | bytes 24580
  52.4 0.6 copy-start.4
  52.5 0.8 slice-start
  53.0 0.7 slice-start.2
  53.0 0.7 slice-start.1
  54.4 4.8 %collective-permute-start.6 = (f32[32,256]{1,0:T(8,128)S(1)}, f32[32,256]{1,0:T(8,128)S(1)}, u32[]{:S(2)}, u32[]{:S(2)}) collective-permute-start(f32[32,256]{1,0:T(8,128)S(1)} %bitcast.110), channel_id=1, source_target_pairs={{0,16},{2,18},{4,20},{6,22},{8,24},{10,26},{12,28},{14,30},{16,0},... | collective-permute-start | bytes 98312 | tf_op jit(solution)/shard_map/ppermute | solution.py:130
  59.2 4.3 %collective-permute-start.7 = (f32[2,32,256]{2,1,0:T(8,128)S(1)}, f32[2,32,256]{2,1,0:T(8,128)S(1)}, u32[]{:S(2)}, u32[]{:S(2)}) collective-permute-start(f32[2,32,256]{2,1,0:T(8,128)S(1)} %pad_maximum_fusion.3), channel_id=1, source_target_pairs={{0,8},{2,10},{4,12},{6,14},{8,0},{10,2},{12,4},{14,6},{16,24},{18,... | collective-permute-start | bytes 196616 | tf_op jit(solution)/shard_map/ppermute | solution.py:130
  63.6 5.0 %collective-permute-start.8 = (f32[2,2,32,256]{3,2,1,0:T(8,128)S(1)}, f32[2,2,32,256]{3,2,1,0:T(8,128)S(1)}, u32[]{:S(2)}, u32[]{:S(2)}) collective-permute-start(f32[2,2,32,256]{3,2,1,0:T(8,128)S(1)} %pad_maximum_fusion.2), channel_id=1, source_target_pairs={{0,4},{2,6},{4,0},{6,2},{8,12},{10,14},{12,8},{14,10},{16,20},{18,... | collective-permute-start | bytes 393224 | tf_op jit(solution)/shard_map/ppermute | solution.py:130
  68.7 1.6 %collective-permute-start.9 = (f32[2,2,2,32,256]{4,3,2,1,0:T(8,128)S(1)}, f32[2,2,2,32,256]{4,3,2,1,0:T(8,128)S(1)}, u32[]{:S(2)}, u32[]{:S(2)}) collective-permute-start(f32[2,2,2,32,256]{4,3,2,1,0:T(8,128)S(1)} %pad_maximum_fusion.1), channel_id=1, source_target_pairs={{0,2},{2,0},{4,6},{6,4},{8,10},{10,8},{12,14},{14,12},{16,18},{18,... | collective-permute-start | bytes 786440 | tf_op jit(solution)/shard_map/ppermute | solution.py:130

commit v9 on v7

--- a/solution.py
+++ b/solution.py
@@ -23,11 +23,13 @@
     return hi, lo
 
 
-def _forward_kernel(vol_ref, amp_ref, off_ref, wid_ref, out_ref):
+def _forward_kernel(start_ref, vol_ref, amp_ref, off_ref, wid_ref, out_ref, acc_ref):
     slab_rows, columns = vol_ref.shape
     view_count = amp_ref.shape[0]
-    band = out_ref.shape[2]
-    out_ref[...] = jnp.zeros(out_ref.shape, jnp.float32)
+    band = acc_ref.shape[2]
+    chunks, _, shard_width = out_ref.shape
+    detector_width = chunks * shard_width
+    acc_ref[...] = jnp.zeros(acc_ref.shape, jnp.float32)
     row = lax.broadcasted_iota(jnp.int32, (slab_rows, CHUNK), 0)
 
     def body(j, carry):
@@ -41,24 +43,41 @@
             hi, lo = _split(x)
             lhs = jnp.concatenate([hi, lo], axis=0)
             mask = _band_mask(off, wid, band, CHUNK)
-            out_ref[v] += lax.dot_general(
+            acc_ref[v] += lax.dot_general(
                 lhs, mask, (((1,), (1,)), ((), ())), preferred_element_type=jnp.float32
             )
         return carry
 
     lax.fori_loop(0, columns // CHUNK, body, 0)
-
-
-def forward_band(volume, amplitude, column_offset, column_width):
+    height = slab_rows + 1
+    placed = []
+    for v in range(view_count):
+        acc = acc_ref[v]
+        summed = (acc[: 2 * slab_rows] + acc[2 * slab_rows :])[:height]
+        ext = jnp.concatenate([summed, jnp.zeros((height, detector_width - band), jnp.float32)], axis=1)
+        placed.append(pltpu.roll(ext, start_ref[v, 0], 1))
+    joined = jnp.concatenate(placed, axis=0)
+    for k in range(chunks):
+        out_ref[k] = joined[:, k * shard_width : (k + 1) * shard_width]
+
+
+def forward_band(volume, amplitude, column_offset, column_width, band_start, chunks, shard_width):
     slab_rows = volume.shape[0]
     view_count = amplitude.shape[0]
-    acc = pl.pallas_call(
+    smem = pl.BlockSpec(memory_space=pltpu.SMEM)
+    vmem = pl.BlockSpec(memory_space=pltpu.VMEM)
+    return pl.pallas_call(
         _forward_kernel,
-        out_shape=jax.ShapeDtypeStruct((view_count, 4 * slab_rows, B), jnp.float32),
+        out_shape=jax.ShapeDtypeStruct((chunks, view_count * (slab_rows + 1), shard_width), jnp.float32),
+        in_specs=[smem, vmem, vmem, vmem, vmem],
+        scratch_shapes=[pltpu.VMEM((view_count, 4 * slab_rows, B), jnp.float32)],
+        cost_estimate=pl.CostEstimate(
+            flops=2 * view_count * 4 * slab_rows * B * volume.shape[1],
+            transcendentals=0,
+            bytes_accessed=4 * (volume.size + 3 * amplitude.size),
+        ),
         interpret=INTERPRET,
-    )(volume, amplitude, column_offset, column_width)
-    summed = acc[:, : 2 * slab_rows] + acc[:, 2 * slab_rows :]
-    return summed[:, : slab_rows + 1]
+    )(band_start, volume, amplitude, column_offset, column_width)
 
 
 def _backward_kernel(back_ref, vol_ref, amp_ref, off_ref, wid_ref, rw_ref, out_ref, split_ref):
@@ -106,11 +125,10 @@
 
 
 def reduce_scatter_xy(x, count):
-    rows = x.shape[0]
-    width = x.shape[1] // count
+    _, rows, width = x.shape
     bits = _bit_count(count)
     idx = lax.axis_index("xy")
-    y = jnp.transpose(x.reshape(rows, count, width), (1, 0, 2)).reshape((2,) * bits + (rows, width))
+    y = x.reshape((2,) * bits + (rows, width))
     for j in range(bits):
         axis = bits - 1 - j
         bit = (idx >> j) & 1
@@ -164,11 +182,8 @@
     measured_ext = jnp.concatenate([meas_below, measured, meas_above], axis=1)
     weight_ext = jnp.concatenate([weight_below, axial_weight, weight_above], axis=2)
 
-    band_rows = forward_band(volume, amplitude, column_offset, column_width)
+    placed = forward_band(volume, amplitude, column_offset, column_width, band_start, xy_count, shard_width)
     band_height = slab_rows + 1
-    placed = jnp.zeros((view_count * band_height, detector_width), jnp.float32)
-    for v in range(view_count):
-        placed = lax.dynamic_update_slice(placed, band_rows[v], (jnp.int32(v * band_height), band_start[v, 0]))
     reduced = reduce_scatter_xy(placed, xy_count).reshape(view_count, band_height, shard_width)
     proj_cols = reduced[:, :slab_rows]
     cover = reduced[:, slab_rows : slab_rows + 1]

time: 79.9 us -> 77.6 us (0.971)
  waiting for transfers between devices: 15.4 us -> 18.5 us
  local copies, waits for them, and re-layouts: 7.58 us -> 4.54 us
  starting transfers between devices: 25.2 us -> 23.2 us
  other arithmetic: 3.64 us -> 2.7 us
    ppermute x1, waiting for transfers between devices: 0.01 us -> 4.05 us  [local(): lax.ppermute(proj_cols[:, :2], 'gz', down_pairs)]
    dynamic_update_slice x2 -> x0, local copies, waits for them, and re-layouts: 3.06 us -> none  [local(): lax.dynamic_update_slice(placed, band_rows[v], (jnp.int32(v * band_height...]
    ppermute x1, waiting for transfers between devices: 1.16 us -> 0.01 us  [local(): lax.ppermute(proj_cols[:, slab_rows - 2:], 'gz', up_pairs)]
    ppermute x1, starting transfers between devices: 4.54 us -> 3.39 us  [local(): lax.ppermute(pack(measured[:, slab_rows - 1:], axial_weight[:, :, slab_ro...]
    add x1 -> x0, other arithmetic: 0.99 us -> none  [forward_band(): summed = acc[:, :2 * slab_rows] + acc[:, 2 * slab_rows:]]
    ppermute x4, waiting for transfers between devices: 4.93 us -> 5.78 us  [reduce_scatter_xy(): y = keep + lax.ppermute(send, 'xy', [(i, i ^ 1 << j) for i in range(count)])]
  transfers between devices with their start and end apart: 12 -> 12, of which waited for: 8 -> 7; matrix products, arithmetic and copies ran while one was open for 2% -> 3% of each run, Pallas kernels for 0% -> 0%
where the time goes in v9:
time: 77.6 us; the launch traced here: 77.1 us
  Pallas kernels  23.2 us (30%)
  starting transfers between devices  23.2 us (30%)
  waiting for transfers between devices  18.5 us (24%)
  between operations  4.99 us (6%)
  local copies, waits for them, and re-layouts  4.54 us (6%)
  other arithmetic  2.7 us (3%)
    pallas_call x1, Pallas kernels, forward_band(): pl.pallas_call(_forward_kernel, out_shape=jax.ShapeDtypeStruct((chunks, v...  13.5 us
    pallas_call x1, Pallas kernels, backward_update(): pl.pallas_call(_backward_kernel, out_shape=jax.ShapeDtypeStruct(volume.sh...  9.66 us
    ppermute x4, waiting for transfers between devices, all_gather_xy(): other = lax.ppermute(y, 'xy', [(i, i ^ 1 << j) for i in range(count)])  8.69 us
    ppermute x4, starting transfers between devices, reduce_scatter_xy(): y = keep + lax.ppermute(send, 'xy', [(i, i ^ 1 << j) for i in range(count)])  7.76 us
    ppermute x4, waiting for transfers between devices, reduce_scatter_xy(): y = keep + lax.ppermute(send, 'xy', [(i, i ^ 1 << j) for i in range(count)])  5.78 us
    ppermute x4, starting transfers between devices, all_gather_xy(): other = lax.ppermute(y, 'xy', [(i, i ^ 1 << j) for i in range(count)])  4.9 us
    ppermute x1, starting transfers between devices, local(): lax.ppermute(proj_cols[:, slab_rows - 2:], 'gz', up_pairs)  4.54 us
    ppermute x1, waiting for transfers between devices, local(): lax.ppermute(proj_cols[:, :2], 'gz', down_pairs)  4.05 us
  transfers between devices with their start and end apart: 12, of which 7 were waited for; matrix products, arithmetic and copies ran while one was open for 3% of the time, Pallas kernels for 0%

profile of v9, /device:TPU:0, one launch (start us, length us, event | category | flops | bytes accessed | tf_op | source)
XLA Modules:
  0.0 77.1 jit_solution(6709678024703590754)
XLA Ops:
  0.6 0.6 copy-done.2
  1.3 0.6 copy.50.start_ref
  1.9 13.5 %shard_map.86 = f32[16,34,256]{2,1,0:T(8,128)} custom-call(s32[2,1]{1,0:T(2,128)} %copy.50.start_ref, f32[16,16384]{1,0:T(8,128)} %vol_ref.3, f32[2,16384]{1,0:T(2,128)} %amp_ref.3, s32[2,16384]{1,0:T(2,128)} %off_ref.3, s32[2,16384]{1,0:T(2,128)} %wid_ref.3), custom_call_target="tpu_custom_call" | custom-call | flops 2147483648 | bytes 1441792 | tf_op jit(solution)/shard_map/pallas_call | solution.py:69
  15.5 1.1 %constant_dynamic-slice_fusion.5 = (f32[2,2,2,1,34,256]{5,4,3,2,1,0:T(8,128)S(1)}, f32[2,2,2,1,34,256]{5,4,3,2,1,0:T(8,128)S(1)}) fusion(f32[2,2,2,2,34,256]{5,4,3,2,1,0:T(8,128)} %bitcast.95, s32[]{:T(128)S(6)} %select_n.111, s32[]{:T(128)S(6)} %select_n.112), kind=kLoop, calls=%fused_computation.51 | loop fusion | bytes 1114120 | tf_op jit(solution)/shard_map/jit(dynamic_index_in_dim)/dynamic_slice | solution.py:135
  16.6 0.0 copy-start
  16.6 0.2 copy.79
  16.8 0.0 copy-start.1
  16.8 0.5 collective-permute-start.2
  17.4 0.1 slice_bitcast_fusion.3
  17.4 0.1 reshape.120
  17.5 0.1 copy-done.1
  17.6 0.9 %collective-permute-done.2 = f32[2,2,2,34,256]{4,1,3,0,2:T(2,128)S(1)} collective-permute-done((f32[2,2,2,34,256]{4,1,3,0,2:T(2,128)S(1)}, f32[2,2,2,34,256]{4,1,3,0,2:T(2,128)S(1)}, u32[]{:S(2)}, u32[]{:S(2)}) %collective-permute-start.2) | collective-permute-done | bytes 278560 | tf_op jit(solution)/shard_map/ppermute | solution.py:137
  18.6 0.3 bitcast_add_fusion
  18.9 3.0 %collective-permute-start.3 = (f32[2,2,34,256]{3,1,2,0:T(2,128)S(1)}, f32[2,2,34,256]{3,1,2,0:T(2,128)S(1)}, u32[]{:S(2)}, u32[]{:S(2)}) collective-permute-start(f32[2,2,34,256]{3,1,2,0:T(2,128)S(1)} %dynamic-slice_bitcast_fusion), channel_id=1, source_target_pairs={{0,4},{2,6},{4,0},{6,2},{8,12},{10,14},{12,8},{14,10},{16,20},{18,... | collective-permute-start | bytes 417800 | tf_op jit(solution)/shard_map/ppermute | solution.py:137
  21.8 3.4 %collective-permute-start = (f32[2,2,256]{2,0,1:T(2,128)S(1)}, f32[2,2,256]{2,0,1:T(2,128)S(1)}, u32[]{:S(2)}, u32[]{:S(2)}) collective-permute-start(f32[2,2,256]{2,0,1:T(2,128)S(1)} %select_maximum_fusion.1), channel_id=1, source_target_pairs={{0,1},{2,3},{4,5},{6,7},{8,9},{10,11},{12,13},{14,15},{16,17},{18,... | collective-permute-start | bytes 12296 | tf_op jit(solution)/shard_map/ppermute | solution.py:176
  25.2 0.1 reshape.121
  25.3 1.3 %collective-permute-start.1 = (f32[2,2,256]{2,0,1:T(2,128)S(1)}, f32[2,2,256]{2,0,1:T(2,128)S(1)}, u32[]{:S(2)}, u32[]{:S(2)}) collective-permute-start(f32[2,2,256]{2,0,1:T(2,128)S(1)} %select_maximum_fusion), channel_id=1, source_target_pairs={{1,0},{3,2},{5,4},{7,6},{9,8},{11,10},{13,12},{15,14},{17,16},{19,... | collective-permute-start | bytes 12296 | tf_op jit(solution)/shard_map/ppermute | solution.py:179
  26.6 0.1 bitcast_add_fusion.1
  26.7 0.1 constant_dynamic-slice_fusion.3
  26.9 1.6 %collective-permute-start.4 = (f32[2,34,256]{2,0,1:T(2,128)S(1)}, f32[2,34,256]{2,0,1:T(2,128)S(1)}, u32[]{:S(2)}, u32[]{:S(2)}) collective-permute-start(f32[2,34,256]{2,0,1:T(2,128)S(1)} %bitcast.100), channel_id=1, source_target_pairs={{0,8},{2,10},{4,12},{6,14},{8,0},{10,2},{12,4},{14,6},{16,24},{18,... | collective-permute-start | bytes 208904 | tf_op jit(solution)/shard_map/ppermute | solution.py:137
  28.5 2.7 %collective-permute-done.4 = f32[2,34,256]{2,0,1:T(2,128)S(1)} collective-permute-done((f32[2,34,256]{2,0,1:T(2,128)S(1)}, f32[2,34,256]{2,0,1:T(2,128)S(1)}, u32[]{:S(2)}, u32[]{:S(2)}) %collective-permute-start.4) | collective-permute-done | bytes 69664 | tf_op jit(solution)/shard_map/ppermute | solution.py:137
  31.3 0.1 bitcast_add_fusion.2
  31.3 0.1 constant_dynamic-slice_fusion.1
  31.4 2.7 %collective-permute-start.5 = (f32[34,256]{1,0:T(8,128)S(1)}, f32[34,256]{1,0:T(8,128)S(1)}, u32[]{:S(2)}, u32[]{:S(2)}) collective-permute-start(f32[34,256]{1,0:T(8,128)S(1)} %bitcast.101), channel_id=1, source_target_pairs={{0,16},{2,18},{4,20},{6,22},{8,24},{10,26},{12,28},{14,30},{16,0},... | collective-permute-start | bytes 104456 | tf_op jit(solution)/shard_map/ppermute | solution.py:137
  34.1 0.1 reshape_squeeze.6
  34.2 0.1 reshape_squeeze.7
  34.3 2.1 %collective-permute-done.5 = f32[34,256]{1,0:T(8,128)S(1)} collective-permute-done((f32[34,256]{1,0:T(8,128)S(1)}, f32[34,256]{1,0:T(8,128)S(1)}, u32[]{:S(2)}, u32[]{:S(2)}) %collective-permute-start.5) | collective-permute-done | bytes 34848 | tf_op jit(solution)/shard_map/ppermute | solution.py:137
  36.4 4.5 %collective-permute-start.6 = (f32[2,2,256]{2,1,0:T(2,128)S(1)}, f32[2,2,256]{2,1,0:T(2,128)S(1)}, u32[]{:S(2)}, u32[]{:S(2)}) collective-permute-start(f32[2,2,256]{2,1,0:T(2,128)S(1)} %get-tuple-element.24), channel_id=1, source_target_pairs={{0,1},{2,3},{4,5},{6,7},{8,9},{10,11},{12,13},{14,15},{16,17},{18,... | collective-permute-start | bytes 12296 | tf_op jit(solution)/shard_map/ppermute | solution.py:192
  41.0 1.3 %collective-permute-start.7 = (f32[2,2,256]{2,1,0:T(2,128)S(1)}, f32[2,2,256]{2,1,0:T(2,128)S(1)}, u32[]{:S(2)}, u32[]{:S(2)}) collective-permute-start(f32[2,2,256]{2,1,0:T(2,128)S(1)} %get-tuple-element.25), channel_id=1, source_target_pairs={{1,0},{3,2},{5,4},{7,6},{9,8},{11,10},{13,12},{15,14},{17,16},{19,... | collective-permute-start | bytes 12296 | tf_op jit(solution)/shard_map/ppermute | solution.py:194
  42.3 0.1 add_add_fusion
  42.4 4.0 %collective-permute-done.7 = f32[2,2,256]{2,1,0:T(2,128)S(1)} collective-permute-done((f32[2,2,256]{2,1,0:T(2,128)S(1)}, f32[2,2,256]{2,1,0:T(2,128)S(1)}, u32[]{:S(2)}, u32[]{:S(2)}) %collective-permute-start.7) | collective-permute-done | bytes 4128 | tf_op jit(solution)/shard_map/ppermute | solution.py:194
  46.5 0.1 fusion.5
  46.6 0.6 fusion.6
  47.2 2.6 %collective-permute-start.8 = (f32[32,256]{1,0:T(8,128)S(1)}, f32[32,256]{1,0:T(8,128)S(1)}, u32[]{:S(2)}, u32[]{:S(2)}) collective-permute-start(f32[32,256]{1,0:T(8,128)S(1)} %bitcast.99), channel_id=1, source_target_pairs={{0,16},{2,18},{4,20},{6,22},{8,24},{10,26},{12,28},{14,30},{16,0},... | collective-permute-start | bytes 98312 | tf_op jit(solution)/shard_map/ppermute | solution.py:148
  49.8 2.2 %collective-permute-done.8 = f32[32,256]{1,0:T(8,128)S(1)} collective-permute-done((f32[32,256]{1,0:T(8,128)S(1)}, f32[32,256]{1,0:T(8,128)S(1)}, u32[]{:S(2)}, u32[]{:S(2)}) %collective-permute-start.8) | collective-permute-done | bytes 32800 | tf_op jit(solution)/shard_map/ppermute | solution.py:148
  52.0 1.6 %collective-permute-start.9 = (f32[2,32,256]{2,1,0:T(8,128)S(1)}, f32[2,32,256]{2,1,0:T(8,128)S(1)}, u32[]{:S(2)}, u32[]{:S(2)}) collective-permute-start(f32[2,32,256]{2,1,0:T(8,128)S(1)} %pad_maximum_fusion.3), channel_id=1, source_target_pairs={{0,8},{2,10},{4,12},{6,14},{8,0},{10,2},{12,4},{14,6},{16,24},{18,... | collective-permute-start | bytes 196616 | tf_op jit(solution)/shard_map/ppermute | solution.py:148
  53.7 2.7 %collective-permute-done.9 = f32[2,32,256]{2,1,0:T(8,128)S(1)} collective-permute-done((f32[2,32,256]{2,1,0:T(8,128)S(1)}, f32[2,32,256]{2,1,0:T(8,128)S(1)}, u32[]{:S(2)}, u32[]{:S(2)}) %collective-permute-start.9) | collective-permute-done | bytes 65568 | tf_op jit(solution)/shard_map/ppermute | solution.py:148
  56.4 0.6 collective-permute-start.10
  57.0 0.7 fusion.18
  57.6 3.8 %collective-permute-done.10 = f32[2,2,32,256]{3,2,1,0:T(8,128)S(1)} collective-permute-done((f32[2,2,32,256]{3,2,1,0:T(8,128)S(1)}, f32[2,2,32,256]{3,2,1,0:T(8,128)S(1)}, u32[]{:S(2)}, u32[]{:S(2)}) %collective-permute-start.10) | collective-permute-done | bytes 131104 | tf_op jit(solution)/shard_map/ppermute | solution.py:148
  61.5 0.1 collective-permute-start.11
  64.3 0.1 copy.62
  64.3 0.1 copy.63
  64.4 0.1 copy.64
  65.9 0.7 select_add_fusion.rw_ref
  66.7 0.1 dynamic-slice_bitcast_fusion.1
  66.8 0.6 pad_maximum_fusion.4.back_ref
  67.5 9.7 %shard_map.87 = f32[16,16384]{1,0:T(8,128)} custom-call(f32[2,16,512]{2,1,0:T(8,128)} %pad_maximum_fusion.4.back_ref, f32[16,16384]{1,0:T(8,128)} %vol_ref.3, f32[2,16384]{1,0:T(2,128)} %amp_ref.3, s32[2,16384]{1,0:T(2,128)} %off_ref.3, s32[2,16384]{1,0:T(2,128)} %wid_ref.3, f32[2,16,1]{2,1,0:T(8,128)} %select_add_fusion.rw_ref), custom_call_target="tpu_custom_call" | custom-call | tf_op jit(solution)/shard_map/pallas_call | solution.py:113
  (45 shorter events, 0.4 us)
Async XLA Ops:
  0.6 0.7 copy-start.2
  16.6 0.8 copy-start
  16.8 0.8 copy-start.1
  16.8 1.7 %collective-permute-start.2 = (f32[2,2,2,34,256]{4,1,3,0,2:T(2,128)S(1)}, f32[2,2,2,34,256]{4,1,3,0,2:T(2,128)S(1)}, u32[]{:S(2)}, u32[]{:S(2)}) collective-permute-start(f32[2,2,2,34,256]{4,1,3,0,2:T(2,128)S(1)} %bitcast.98), channel_id=1, source_target_pairs={{0,2},{2,0},{4,6},{6,4},{8,10},{10,8},{12,14},{14,12},{16,18},{18,... | collective-permute-start | bytes 835592 | tf_op jit(solution)/shard_map/ppermute | solution.py:137
  18.9 7.8 %collective-permute-start.3 = (f32[2,2,34,256]{3,1,2,0:T(2,128)S(1)}, f32[2,2,34,256]{3,1,2,0:T(2,128)S(1)}, u32[]{:S(2)}, u32[]{:S(2)}) collective-permute-start(f32[2,2,34,256]{3,1,2,0:T(2,128)S(1)} %dynamic-slice_bitcast_fusion), channel_id=1, source_target_pairs={{0,4},{2,6},{4,0},{6,2},{8,12},{10,14},{12,8},{14,10},{16,20},{18,... | collective-permute-start | bytes 417800 | tf_op jit(solution)/shard_map/ppermute | solution.py:137
  21.8 12.3 %collective-permute-start = (f32[2,2,256]{2,0,1:T(2,128)S(1)}, f32[2,2,256]{2,0,1:T(2,128)S(1)}, u32[]{:S(2)}, u32[]{:S(2)}) collective-permute-start(f32[2,2,256]{2,0,1:T(2,128)S(1)} %select_maximum_fusion.1), channel_id=1, source_target_pairs={{0,1},{2,3},{4,5},{6,7},{8,9},{10,11},{12,13},{14,15},{16,17},{18,... | collective-permute-start | bytes 12296 | tf_op jit(solution)/shard_map/ppermute | solution.py:176
  25.3 8.9 %collective-permute-start.1 = (f32[2,2,256]{2,0,1:T(2,128)S(1)}, f32[2,2,256]{2,0,1:T(2,128)S(1)}, u32[]{:S(2)}, u32[]{:S(2)}) collective-permute-start(f32[2,2,256]{2,0,1:T(2,128)S(1)} %select_maximum_fusion), channel_id=1, source_target_pairs={{1,0},{3,2},{5,4},{7,6},{9,8},{11,10},{13,12},{15,14},{17,16},{19,... | collective-permute-start | bytes 12296 | tf_op jit(solution)/shard_map/ppermute | solution.py:179
  26.9 4.4 %collective-permute-start.4 = (f32[2,34,256]{2,0,1:T(2,128)S(1)}, f32[2,34,256]{2,0,1:T(2,128)S(1)}, u32[]{:S(2)}, u32[]{:S(2)}) collective-permute-start(f32[2,34,256]{2,0,1:T(2,128)S(1)} %bitcast.100), channel_id=1, source_target_pairs={{0,8},{2,10},{4,12},{6,14},{8,0},{10,2},{12,4},{14,6},{16,24},{18,... | collective-permute-start | bytes 208904 | tf_op jit(solution)/shard_map/ppermute | solution.py:137
  31.4 5.0 %collective-permute-start.5 = (f32[34,256]{1,0:T(8,128)S(1)}, f32[34,256]{1,0:T(8,128)S(1)}, u32[]{:S(2)}, u32[]{:S(2)}) collective-permute-start(f32[34,256]{1,0:T(8,128)S(1)} %bitcast.101), channel_id=1, source_target_pairs={{0,16},{2,18},{4,20},{6,22},{8,24},{10,26},{12,28},{14,30},{16,0},... | collective-permute-start | bytes 104456 | tf_op jit(solution)/shard_map/ppermute | solution.py:137
  36.4 6.0 %collective-permute-start.6 = (f32[2,2,256]{2,1,0:T(2,128)S(1)}, f32[2,2,256]{2,1,0:T(2,128)S(1)}, u32[]{:S(2)}, u32[]{:S(2)}) collective-permute-start(f32[2,2,256]{2,1,0:T(2,128)S(1)} %get-tuple-element.24), channel_id=1, source_target_pairs={{0,1},{2,3},{4,5},{6,7},{8,9},{10,11},{12,13},{14,15},{16,17},{18,... | collective-permute-start | bytes 12296 | tf_op jit(solution)/shard_map/ppermute | solution.py:192
  41.0 5.5 %collective-permute-start.7 = (f32[2,2,256]{2,1,0:T(2,128)S(1)}, f32[2,2,256]{2,1,0:T(2,128)S(1)}, u32[]{:S(2)}, u32[]{:S(2)}) collective-permute-start(f32[2,2,256]{2,1,0:T(2,128)S(1)} %get-tuple-element.25), channel_id=1, source_target_pairs={{1,0},{3,2},{5,4},{7,6},{9,8},{11,10},{13,12},{15,14},{17,16},{19,... | collective-permute-start | bytes 12296 | tf_op jit(solution)/shard_map/ppermute | solution.py:194
  47.2 4.8 %collective-permute-start.8 = (f32[32,256]{1,0:T(8,128)S(1)}, f32[32,256]{1,0:T(8,128)S(1)}, u32[]{:S(2)}, u32[]{:S(2)}) collective-permute-start(f32[32,256]{1,0:T(8,128)S(1)} %bitcast.99), channel_id=1, source_target_pairs={{0,16},{2,18},{4,20},{6,22},{8,24},{10,26},{12,28},{14,30},{16,0},... | collective-permute-start | bytes 98312 | tf_op jit(solution)/shard_map/ppermute | solution.py:148
  52.0 4.3 %collective-permute-start.9 = (f32[2,32,256]{2,1,0:T(8,128)S(1)}, f32[2,32,256]{2,1,0:T(8,128)S(1)}, u32[]{:S(2)}, u32[]{:S(2)}) collective-permute-start(f32[2,32,256]{2,1,0:T(8,128)S(1)} %pad_maximum_fusion.3), channel_id=1, source_target_pairs={{0,8},{2,10},{4,12},{6,14},{8,0},{10,2},{12,4},{14,6},{16,24},{18,... | collective-permute-start | bytes 196616 | tf_op jit(solution)/shard_map/ppermute | solution.py:148
  56.4 5.0 %collective-permute-start.10 = (f32[2,2,32,256]{3,2,1,0:T(8,128)S(1)}, f32[2,2,32,256]{3,2,1,0:T(8,128)S(1)}, u32[]{:S(2)}, u32[]{:S(2)}) collective-permute-start(f32[2,2,32,256]{3,2,1,0:T(8,128)S(1)} %pad_maximum_fusion.2), channel_id=1, source_target_pairs={{0,4},{2,6},{4,0},{6,2},{8,12},{10,14},{12,8},{14,10},{16,20},{18,... | collective-permute-start | bytes 393224 | tf_op jit(solution)/shard_map/ppermute | solution.py:148
  61.5 5.1 %collective-permute-start.11 = (f32[2,2,2,32,256]{4,3,2,1,0:T(8,128)S(1)}, f32[2,2,2,32,256]{4,3,2,1,0:T(8,128)S(1)}, u32[]{:S(2)}, u32[]{:S(2)}) collective-permute-start(f32[2,2,2,32,256]{4,3,2,1,0:T(8,128)S(1)} %pad_maximum_fusion.1), channel_id=1, source_target_pairs={{0,2},{2,0},{4,6},{6,4},{8,10},{10,8},{12,14},{14,12},{16,18},{18,... | collective-permute-start | bytes 786440 | tf_op jit(solution)/shard_map/ppermute | solution.py:148

commit v10 on v9

--- a/solution.py
+++ b/solution.py
@@ -152,6 +152,47 @@
     return jnp.transpose(y.reshape(count, rows, width), (1, 0, 2)).reshape(rows, count * width)
 
 
+def gather_band(rows, count, own_starts, partner_starts, band):
+    views, slab_rows, width = rows.shape
+    bits = _bit_count(count)
+    idx = lax.axis_index("xy")
+    y = rows
+    for step, j in enumerate(reversed(range(1, bits))):
+        bit = (idx >> j) & 1
+        other = lax.ppermute(y, "xy", [(i, i ^ (1 << j)) for i in range(count)])
+        low = jnp.where(bit == 0, y, other)
+        high = jnp.where(bit == 0, other, y)
+        y = jnp.stack([low, high], axis=step)
+    half = count // 2
+    y = y.reshape(half, views, slab_rows, width)
+    parity = idx & 1
+    needed = band // width + 1
+    sent = (needed + 1) // 2
+
+    def first_index(start, block_parity):
+        k0 = start // width
+        return jnp.minimum((k0 + (k0 + block_parity) % 2) // 2, half - sent)
+
+    send = jnp.stack(
+        [lax.dynamic_slice_in_dim(y[:, v], first_index(partner_starts[v], parity), sent, 0) for v in range(views)]
+    )
+    recv = lax.ppermute(send, "xy", [(i, i ^ 1) for i in range(count)])
+    out = []
+    for v in range(views):
+        start = own_starts[v]
+        k0 = start // width
+        base = first_index(start, 1 - parity)
+        pieces = []
+        for i in range(needed):
+            k = k0 + i
+            own = lax.dynamic_index_in_dim(y[:, v], jnp.minimum(k // 2, half - 1), 0, keepdims=False)
+            got = lax.dynamic_index_in_dim(recv[v], jnp.clip(k // 2 - base, 0, sent - 1), 0, keepdims=False)
+            pieces.append(jnp.where(k % 2 == parity, own, got))
+        window = jnp.concatenate(pieces, axis=1)
+        out.append(lax.dynamic_slice(window, (jnp.int32(0), start - k0 * width), (slab_rows, band)))
+    return jnp.stack(out)
+
+
 def local(volume, measured, band_start, column_offset, column_width, amplitude, axial_weight):
     slab_rows = volume.shape[0]
     view_count = amplitude.shape[0]
@@ -182,6 +223,7 @@
     measured_ext = jnp.concatenate([meas_below, measured, meas_above], axis=1)
     weight_ext = jnp.concatenate([weight_below, axial_weight, weight_above], axis=2)
 
+    partner_start = lax.ppermute(band_start, "xy", [(i, i ^ 1) for i in range(xy_count)])
     placed = forward_band(volume, amplitude, column_offset, column_width, band_start, xy_count, shard_width)
     band_height = slab_rows + 1
     reduced = reduce_scatter_xy(placed, xy_count).reshape(view_count, band_height, shard_width)
@@ -216,13 +258,9 @@
         + axial_weight[1][:, :, None] * residual
         + axial_weight[2][:, :, None] * residual_ext[:, 2 : slab_rows + 2]
     )
-    back_full = all_gather_xy(back_rows.reshape(view_count * slab_rows, shard_width), xy_count)
-    back_full = back_full.reshape(view_count, slab_rows, detector_width)
-    back_band = jnp.stack(
-        [
-            lax.dynamic_slice(back_full[v], (jnp.int32(0), band_start[v, 0]), (slab_rows, B))
-            for v in range(view_count)
-        ]
+    back_band = gather_band(
+        back_rows, xy_count, [band_start[v, 0] for v in range(view_count)],
+        [partner_start[v, 0] for v in range(view_count)], B,
     )
 
     own_rows = first_row + jnp.arange(slab_rows, dtype=jnp.int32)

time: 77.6 us -> 80 us (1.031)
  between operations: 4.99 us -> 12.4 us
  waiting for transfers between devices: 18.5 us -> 11.6 us
  starting transfers between devices: 23.2 us -> 24 us
    ppermute x4 -> x5, waiting for transfers between devices: 8.69 us -> 4.62 us  [the longest x3 4.61 us: gather_band(): other = lax.ppermute(y, 'xy', [(i, i ^ 1 << j) for i in range(count)])]
    ppermute x1, waiting for transfers between devices: 4.05 us -> 0.01 us  [local(): lax.ppermute(proj_cols[:, :2], 'gz', down_pairs)]
    ppermute x1, waiting for transfers between devices: 0.01 us -> 1.16 us  [local(): lax.ppermute(proj_cols[:, slab_rows - 2:], 'gz', up_pairs)]
    ppermute x1, starting transfers between devices: 3.39 us -> 4.54 us  [local(): lax.ppermute(pack(measured[:, slab_rows - 1:], axial_weight[:, :, slab_ro...]
    ppermute x4 -> x5, starting transfers between devices: 4.9 us -> 4.62 us  [the longest x3 4.54 us: gather_band(): other = lax.ppermute(y, 'xy', [(i, i ^ 1 << j) for i in range(count)])]
  transfers between devices with their start and end apart: 12 -> 13, of which waited for: 7 -> 6; matrix products, arithmetic and copies ran while one was open for 3% -> 4% of each run, Pallas kernels for 0% -> 0%
where the time goes in v10:
time: 80 us; the launch traced here: 78.9 us
  starting transfers between devices  24 us (30%)
  Pallas kernels  23.2 us (29%)
  between operations  12.4 us (16%)
  waiting for transfers between devices  11.6 us (14%)
  local copies, waits for them, and re-layouts  4.92 us (6%)
  other arithmetic  2.87 us (4%)
    pallas_call x1, Pallas kernels, forward_band(): pl.pallas_call(_forward_kernel, out_shape=jax.ShapeDtypeStruct((chunks, v...  13.5 us
    pallas_call x1, Pallas kernels, backward_update(): pl.pallas_call(_backward_kernel, out_shape=jax.ShapeDtypeStruct(volume.sh...  9.65 us
    ppermute x4, starting transfers between devices, reduce_scatter_xy(): y = keep + lax.ppermute(send, 'xy', [(i, i ^ 1 << j) for i in range(count)])  7.76 us
    ppermute x4, waiting for transfers between devices, reduce_scatter_xy(): y = keep + lax.ppermute(send, 'xy', [(i, i ^ 1 << j) for i in range(count)])  5.78 us
    ppermute x3, waiting for transfers between devices, gather_band(): other = lax.ppermute(y, 'xy', [(i, i ^ 1 << j) for i in range(count)])  4.61 us
    ppermute x3, starting transfers between devices, gather_band(): other = lax.ppermute(y, 'xy', [(i, i ^ 1 << j) for i in range(count)])  4.54 us
    ppermute x1, starting transfers between devices, local(): lax.ppermute(proj_cols[:, slab_rows - 2:], 'gz', up_pairs)  4.54 us
    ppermute x1, starting transfers between devices, local(): lax.ppermute(pack(measured[:, slab_rows - 1:], axial_weight[:, :, slab_ro...  4.54 us
  transfers between devices with their start and end apart: 13, of which 6 were waited for; matrix products, arithmetic and copies ran while one was open for 4% of the time, Pallas kernels for 0%

profile of v10, /device:TPU:0, one launch (start us, length us, event | category | flops | bytes accessed | tf_op | source)
XLA Modules:
  0.0 78.9 jit_solution(2386440686312378980)
XLA Ops:
  0.6 0.6 copy-done.2
  1.3 0.6 copy.49.start_ref
  1.9 13.5 %shard_map.86 = f32[16,34,256]{2,1,0:T(8,128)} custom-call(s32[2,1]{1,0:T(2,128)} %copy.49.start_ref, f32[16,16384]{1,0:T(8,128)} %vol_ref.3, f32[2,16384]{1,0:T(2,128)} %amp_ref.3, s32[2,16384]{1,0:T(2,128)} %off_ref.3, s32[2,16384]{1,0:T(2,128)} %wid_ref.3), custom_call_target="tpu_custom_call" | custom-call | flops 2147483648 | bytes 1441792 | tf_op jit(solution)/shard_map/pallas_call | solution.py:69
  15.5 1.1 %constant_dynamic-slice_fusion.5 = (f32[2,2,2,1,34,256]{5,4,3,2,1,0:T(8,128)S(1)}, f32[2,2,2,1,34,256]{5,4,3,2,1,0:T(8,128)S(1)}) fusion(f32[2,2,2,2,34,256]{5,4,3,2,1,0:T(8,128)} %bitcast.92, s32[]{:T(128)S(6)} %select_n.283, s32[]{:T(128)S(6)} %select_n.284), kind=kLoop, calls=%fused_computation.60 | loop fusion | bytes 1114120 | tf_op jit(solution)/shard_map/jit(dynamic_index_in_dim)/dynamic_slice | solution.py:135
  16.6 0.0 copy-start
  16.6 0.2 copy.72
  16.8 0.5 collective-permute-start.2
  17.4 0.1 slice_bitcast_fusion.1
  17.4 0.1 reshape.154
  17.5 0.1 copy-done.1
  17.6 0.9 %collective-permute-done.2 = f32[2,2,2,34,256]{4,1,3,0,2:T(2,128)S(1)} collective-permute-done((f32[2,2,2,34,256]{4,1,3,0,2:T(2,128)S(1)}, f32[2,2,2,34,256]{4,1,3,0,2:T(2,128)S(1)}, u32[]{:S(2)}, u32[]{:S(2)}) %collective-permute-start.2) | collective-permute-done | bytes 278560 | tf_op jit(solution)/shard_map/ppermute | solution.py:137
  18.6 0.3 bitcast_add_fusion
  18.9 3.0 %collective-permute-start.3 = (f32[2,2,34,256]{3,1,2,0:T(2,128)S(1)}, f32[2,2,34,256]{3,1,2,0:T(2,128)S(1)}, u32[]{:S(2)}, u32[]{:S(2)}) collective-permute-start(f32[2,2,34,256]{3,1,2,0:T(2,128)S(1)} %dynamic-slice_bitcast_fusion), channel_id=1, source_target_pairs={{0,4},{2,6},{4,0},{6,2},{8,12},{10,14},{12,8},{14,10},{16,20},{18,... | collective-permute-start | bytes 417800 | tf_op jit(solution)/shard_map/ppermute | solution.py:137
  21.8 1.3 %collective-permute-start.1 = (f32[2,2,256]{2,0,1:T(2,128)S(1)}, f32[2,2,256]{2,0,1:T(2,128)S(1)}, u32[]{:S(2)}, u32[]{:S(2)}) collective-permute-start(f32[2,2,256]{2,0,1:T(2,128)S(1)} %select_maximum_fusion), channel_id=1, source_target_pairs={{1,0},{3,2},{5,4},{7,6},{9,8},{11,10},{13,12},{15,14},{17,16},{19,... | collective-permute-start | bytes 12296 | tf_op jit(solution)/shard_map/ppermute | solution.py:220
  23.1 0.1 reshape.153
  23.2 4.5 %collective-permute-start = (f32[2,2,256]{2,0,1:T(2,128)S(1)}, f32[2,2,256]{2,0,1:T(2,128)S(1)}, u32[]{:S(2)}, u32[]{:S(2)}) collective-permute-start(f32[2,2,256]{2,0,1:T(2,128)S(1)} %select_maximum_fusion.1), channel_id=1, source_target_pairs={{0,1},{2,3},{4,5},{6,7},{8,9},{10,11},{12,13},{14,15},{16,17},{18,... | collective-permute-start | bytes 12296 | tf_op jit(solution)/shard_map/ppermute | solution.py:217
  27.8 0.1 bitcast_add_fusion.1
  27.9 0.1 constant_dynamic-slice_fusion.3
  28.0 1.6 %collective-permute-start.4 = (f32[2,34,256]{2,0,1:T(2,128)S(1)}, f32[2,34,256]{2,0,1:T(2,128)S(1)}, u32[]{:S(2)}, u32[]{:S(2)}) collective-permute-start(f32[2,34,256]{2,0,1:T(2,128)S(1)} %bitcast.94), channel_id=1, source_target_pairs={{0,8},{2,10},{4,12},{6,14},{8,0},{10,2},{12,4},{14,6},{16,24},{18,... | collective-permute-start | bytes 208904 | tf_op jit(solution)/shard_map/ppermute | solution.py:137
  29.7 2.7 %collective-permute-done.4 = f32[2,34,256]{2,0,1:T(2,128)S(1)} collective-permute-done((f32[2,34,256]{2,0,1:T(2,128)S(1)}, f32[2,34,256]{2,0,1:T(2,128)S(1)}, u32[]{:S(2)}, u32[]{:S(2)}) %collective-permute-start.4) | collective-permute-done | bytes 69664 | tf_op jit(solution)/shard_map/ppermute | solution.py:137
  32.4 0.1 bitcast_add_fusion.2
  32.5 0.1 constant_dynamic-slice_fusion.1
  32.6 2.7 %collective-permute-start.5 = (f32[34,256]{1,0:T(8,128)S(1)}, f32[34,256]{1,0:T(8,128)S(1)}, u32[]{:S(2)}, u32[]{:S(2)}) collective-permute-start(f32[34,256]{1,0:T(8,128)S(1)} %bitcast.95), channel_id=1, source_target_pairs={{0,16},{2,18},{4,20},{6,22},{8,24},{10,26},{12,28},{14,30},{16,0},... | collective-permute-start | bytes 104456 | tf_op jit(solution)/shard_map/ppermute | solution.py:137
  35.2 0.1 reshape_squeeze.7
  35.3 0.1 reshape_squeeze.6
  35.4 2.1 %collective-permute-done.5 = f32[34,256]{1,0:T(8,128)S(1)} collective-permute-done((f32[34,256]{1,0:T(8,128)S(1)}, f32[34,256]{1,0:T(8,128)S(1)}, u32[]{:S(2)}, u32[]{:S(2)}) %collective-permute-start.5) | collective-permute-done | bytes 34848 | tf_op jit(solution)/shard_map/ppermute | solution.py:137
  37.6 1.3 %collective-permute-start.7 = (f32[2,2,256]{2,1,0:T(2,128)S(1)}, f32[2,2,256]{2,1,0:T(2,128)S(1)}, u32[]{:S(2)}, u32[]{:S(2)}) collective-permute-start(f32[2,2,256]{2,1,0:T(2,128)S(1)} %get-tuple-element.31), channel_id=1, source_target_pairs={{1,0},{3,2},{5,4},{7,6},{9,8},{11,10},{13,12},{15,14},{17,16},{19,... | collective-permute-start | bytes 12296 | tf_op jit(solution)/shard_map/ppermute | solution.py:236
  38.9 4.5 %collective-permute-start.6 = (f32[2,2,256]{2,1,0:T(2,128)S(1)}, f32[2,2,256]{2,1,0:T(2,128)S(1)}, u32[]{:S(2)}, u32[]{:S(2)}) collective-permute-start(f32[2,2,256]{2,1,0:T(2,128)S(1)} %get-tuple-element.30), channel_id=1, source_target_pairs={{0,1},{2,3},{4,5},{6,7},{8,9},{10,11},{12,13},{14,15},{16,17},{18,... | collective-permute-start | bytes 12296 | tf_op jit(solution)/shard_map/ppermute | solution.py:234
  43.4 0.1 add_add_fusion
  43.6 1.2 %collective-permute-done.6 = f32[2,2,256]{2,1,0:T(2,128)S(1)} collective-permute-done((f32[2,2,256]{2,1,0:T(2,128)S(1)}, f32[2,2,256]{2,1,0:T(2,128)S(1)}, u32[]{:S(2)}, u32[]{:S(2)}) %collective-permute-start.6) | collective-permute-done | bytes 4128 | tf_op jit(solution)/shard_map/ppermute | solution.py:234
  44.7 0.1 fusion.5
  44.8 0.6 fusion.12
  45.4 2.6 %collective-permute-start.8 = (f32[2,16,256]{2,1,0:T(8,128)S(1)}, f32[2,16,256]{2,1,0:T(8,128)S(1)}, u32[]{:S(2)}, u32[]{:S(2)}) collective-permute-start(f32[2,16,256]{2,1,0:T(8,128)S(1)} %get-tuple-element.2), channel_id=1, source_target_pairs={{0,16},{2,18},{4,20},{6,22},{8,24},{10,26},{12,28},{14,30},{16,0},... | collective-permute-start | bytes 98312 | tf_op jit(solution)/shard_map/ppermute | solution.py:162
  48.1 0.1 copy.59
  48.2 0.1 copy.58
  48.2 0.1 copy.57
  48.3 1.9 %collective-permute-done.8 = f32[2,16,256]{2,1,0:T(8,128)S(1)} collective-permute-done((f32[2,16,256]{2,1,0:T(8,128)S(1)}, f32[2,16,256]{2,1,0:T(8,128)S(1)}, u32[]{:S(2)}, u32[]{:S(2)}) %collective-permute-start.8) | collective-permute-done | bytes 32800 | tf_op jit(solution)/shard_map/ppermute | solution.py:162
  50.3 1.6 %collective-permute-start.9 = (f32[2,2,16,256]{3,2,1,0:T(8,128)S(1)}, f32[2,2,16,256]{3,2,1,0:T(8,128)S(1)}, u32[]{:S(2)}, u32[]{:S(2)}) collective-permute-start(f32[2,2,16,256]{3,2,1,0:T(8,128)S(1)} %pad_maximum_fusion.2), channel_id=1, source_target_pairs={{0,8},{2,10},{4,12},{6,14},{8,0},{10,2},{12,4},{14,6},{16,24},{18,... | collective-permute-start | bytes 196616 | tf_op jit(solution)/shard_map/ppermute | solution.py:162
  51.9 2.7 %collective-permute-done.9 = f32[2,2,16,256]{3,2,1,0:T(8,128)S(1)} collective-permute-done((f32[2,2,16,256]{3,2,1,0:T(8,128)S(1)}, f32[2,2,16,256]{3,2,1,0:T(8,128)S(1)}, u32[]{:S(2)}, u32[]{:S(2)}) %collective-permute-start.9) | collective-permute-done | bytes 65568 | tf_op jit(solution)/shard_map/ppermute | solution.py:162
  54.7 0.3 collective-permute-start.10
  54.9 0.7 select_add_fusion.rw_ref
  55.6 0.6 fusion.27
  61.3 0.1 collective-permute-start.12
  61.4 0.6 fusion.26
  68.4 0.1 fusion.8
  68.5 0.1 fusion.11
  68.6 0.6 pad_maximum_fusion.4.back_ref
  69.3 9.7 %shard_map.87 = f32[16,16384]{1,0:T(8,128)} custom-call(f32[2,16,512]{2,1,0:T(8,128)} %pad_maximum_fusion.4.back_ref, f32[16,16384]{1,0:T(8,128)} %vol_ref.3, f32[2,16384]{1,0:T(2,128)} %amp_ref.3, s32[2,16384]{1,0:T(2,128)} %off_ref.3, s32[2,16384]{1,0:T(2,128)} %wid_ref.3, f32[2,16,1]{2,1,0:T(8,128)} %select_add_fusion.rw_ref), custom_call_target="tpu_custom_call" | custom-call | tf_op jit(solution)/shard_map/pallas_call | solution.py:113
  (51 shorter events, 0.4 us)
Async XLA Ops:
  0.6 0.7 copy-start.2
  16.6 0.8 copy-start
  16.8 0.8 copy-start.1
  16.8 1.7 %collective-permute-start.2 = (f32[2,2,2,34,256]{4,1,3,0,2:T(2,128)S(1)}, f32[2,2,2,34,256]{4,1,3,0,2:T(2,128)S(1)}, u32[]{:S(2)}, u32[]{:S(2)}) collective-permute-start(f32[2,2,2,34,256]{4,1,3,0,2:T(2,128)S(1)} %bitcast.93), channel_id=1, source_target_pairs={{0,2},{2,0},{4,6},{6,4},{8,10},{10,8},{12,14},{14,12},{16,18},{18,... | collective-permute-start | bytes 835592 | tf_op jit(solution)/shard_map/ppermute | solution.py:137
  18.9 8.9 %collective-permute-start.3 = (f32[2,2,34,256]{3,1,2,0:T(2,128)S(1)}, f32[2,2,34,256]{3,1,2,0:T(2,128)S(1)}, u32[]{:S(2)}, u32[]{:S(2)}) collective-permute-start(f32[2,2,34,256]{3,1,2,0:T(2,128)S(1)} %dynamic-slice_bitcast_fusion), channel_id=1, source_target_pairs={{0,4},{2,6},{4,0},{6,2},{8,12},{10,14},{12,8},{14,10},{16,20},{18,... | collective-permute-start | bytes 417800 | tf_op jit(solution)/shard_map/ppermute | solution.py:137
  21.8 13.4 %collective-permute-start.1 = (f32[2,2,256]{2,0,1:T(2,128)S(1)}, f32[2,2,256]{2,0,1:T(2,128)S(1)}, u32[]{:S(2)}, u32[]{:S(2)}) collective-permute-start(f32[2,2,256]{2,0,1:T(2,128)S(1)} %select_maximum_fusion), channel_id=1, source_target_pairs={{1,0},{3,2},{5,4},{7,6},{9,8},{11,10},{13,12},{15,14},{17,16},{19,... | collective-permute-start | bytes 12296 | tf_op jit(solution)/shard_map/ppermute | solution.py:220
  23.2 12.1 %collective-permute-start = (f32[2,2,256]{2,0,1:T(2,128)S(1)}, f32[2,2,256]{2,0,1:T(2,128)S(1)}, u32[]{:S(2)}, u32[]{:S(2)}) collective-permute-start(f32[2,2,256]{2,0,1:T(2,128)S(1)} %select_maximum_fusion.1), channel_id=1, source_target_pairs={{0,1},{2,3},{4,5},{6,7},{8,9},{10,11},{12,13},{14,15},{16,17},{18,... | collective-permute-start | bytes 12296 | tf_op jit(solution)/shard_map/ppermute | solution.py:217
  28.0 4.4 %collective-permute-start.4 = (f32[2,34,256]{2,0,1:T(2,128)S(1)}, f32[2,34,256]{2,0,1:T(2,128)S(1)}, u32[]{:S(2)}, u32[]{:S(2)}) collective-permute-start(f32[2,34,256]{2,0,1:T(2,128)S(1)} %bitcast.94), channel_id=1, source_target_pairs={{0,8},{2,10},{4,12},{6,14},{8,0},{10,2},{12,4},{14,6},{16,24},{18,... | collective-permute-start | bytes 208904 | tf_op jit(solution)/shard_map/ppermute | solution.py:137
  32.6 5.0 %collective-permute-start.5 = (f32[34,256]{1,0:T(8,128)S(1)}, f32[34,256]{1,0:T(8,128)S(1)}, u32[]{:S(2)}, u32[]{:S(2)}) collective-permute-start(f32[34,256]{1,0:T(8,128)S(1)} %bitcast.95), channel_id=1, source_target_pairs={{0,16},{2,18},{4,20},{6,22},{8,24},{10,26},{12,28},{14,30},{16,0},... | collective-permute-start | bytes 104456 | tf_op jit(solution)/shard_map/ppermute | solution.py:137
  37.6 6.0 %collective-permute-start.7 = (f32[2,2,256]{2,1,0:T(2,128)S(1)}, f32[2,2,256]{2,1,0:T(2,128)S(1)}, u32[]{:S(2)}, u32[]{:S(2)}) collective-permute-start(f32[2,2,256]{2,1,0:T(2,128)S(1)} %get-tuple-element.31), channel_id=1, source_target_pairs={{1,0},{3,2},{5,4},{7,6},{9,8},{11,10},{13,12},{15,14},{17,16},{19,... | collective-permute-start | bytes 12296 | tf_op jit(solution)/shard_map/ppermute | solution.py:236
  38.9 5.9 %collective-permute-start.6 = (f32[2,2,256]{2,1,0:T(2,128)S(1)}, f32[2,2,256]{2,1,0:T(2,128)S(1)}, u32[]{:S(2)}, u32[]{:S(2)}) collective-permute-start(f32[2,2,256]{2,1,0:T(2,128)S(1)} %get-tuple-element.30), channel_id=1, source_target_pairs={{0,1},{2,3},{4,5},{6,7},{8,9},{10,11},{12,13},{14,15},{16,17},{18,... | collective-permute-start | bytes 12296 | tf_op jit(solution)/shard_map/ppermute | solution.py:234
  45.4 4.8 %collective-permute-start.8 = (f32[2,16,256]{2,1,0:T(8,128)S(1)}, f32[2,16,256]{2,1,0:T(8,128)S(1)}, u32[]{:S(2)}, u32[]{:S(2)}) collective-permute-start(f32[2,16,256]{2,1,0:T(8,128)S(1)} %get-tuple-element.2), channel_id=1, source_target_pairs={{0,16},{2,18},{4,20},{6,22},{8,24},{10,26},{12,28},{14,30},{16,0},... | collective-permute-start | bytes 98312 | tf_op jit(solution)/shard_map/ppermute | solution.py:162
  48.1 7.5 %collective-permute-start.11 = (s32[2,1]{0,1:T(1,128)S(1)}, s32[2,1]{0,1:T(1,128)S(1)}, u32[]{:S(2)}, u32[]{:S(2)}) collective-permute-start(s32[2,1]{0,1:T(1,128)S(1)} %copy-done.2), channel_id=1, source_target_pairs={{0,2},{2,0},{4,6},{6,4},{8,10},{10,8},{12,14},{14,12},{16,18},{18,... | collective-permute-start | bytes 32 | tf_op jit(solution)/shard_map/ppermute | solution.py:226
  50.3 4.3 %collective-permute-start.9 = (f32[2,2,16,256]{3,2,1,0:T(8,128)S(1)}, f32[2,2,16,256]{3,2,1,0:T(8,128)S(1)}, u32[]{:S(2)}, u32[]{:S(2)}) collective-permute-start(f32[2,2,16,256]{3,2,1,0:T(8,128)S(1)} %pad_maximum_fusion.2), channel_id=1, source_target_pairs={{0,8},{2,10},{4,12},{6,14},{8,0},{10,2},{12,4},{14,6},{16,24},{18,... | collective-permute-start | bytes 196616 | tf_op jit(solution)/shard_map/ppermute | solution.py:162
  54.7 6.5 %collective-permute-start.10 = (f32[2,2,2,16,256]{4,3,2,0,1:T(8,128)S(1)}, f32[2,2,2,16,256]{4,3,2,0,1:T(8,128)S(1)}, u32[]{:S(2)}, u32[]{:S(2)}) collective-permute-start(f32[2,2,2,16,256]{4,3,2,0,1:T(8,128)S(1)} %pad_maximum_fusion.1), channel_id=1, source_target_pairs={{0,4},{2,6},{4,0},{6,2},{8,12},{10,14},{12,8},{14,10},{16,20},{18,... | collective-permute-start | bytes 393224 | tf_op jit(solution)/shard_map/ppermute | solution.py:162
  61.3 7.1 %collective-permute-start.12 = (f32[2,2,16,256]{3,2,1,0:T(8,128)S(1)}, f32[2,2,16,256]{3,2,1,0:T(8,128)S(1)}, u32[]{:S(2)}, u32[]{:S(2)}) collective-permute-start(f32[2,2,16,256]{3,2,1,0:T(8,128)S(1)} %pad_maximum_fusion.3), channel_id=1, source_target_pairs={{0,2},{2,0},{4,6},{6,4},{8,10},{10,8},{12,14},{14,12},{16,18},{18,... | collective-permute-start | bytes 196616 | tf_op jit(solution)/shard_map/ppermute | solution.py:179

commit v11 on v9

--- a/solution.py
+++ b/solution.py
@@ -39,9 +39,14 @@
             amp = amp_ref[pl.ds(v, 1), pl.ds(c0, CHUNK)]
             off = off_ref[pl.ds(v, 1), pl.ds(c0, CHUNK)]
             wid = wid_ref[pl.ds(v, 1), pl.ds(c0, CHUNK)]
-            x = jnp.concatenate([cells * amp, jnp.where(row == 0, amp, 0.0)], axis=0)
-            hi, lo = _split(x)
-            lhs = jnp.concatenate([hi, lo], axis=0)
+            cells_hi, cells_lo = _split(cells * amp)
+            amp_hi, amp_lo = _split(amp)
+            amp_rows = jnp.where(
+                row == 0,
+                amp_hi.astype(jnp.float32),
+                jnp.where(row == 1, amp_lo.astype(jnp.float32), 0.0),
+            ).astype(jnp.bfloat16)
+            lhs = jnp.concatenate([cells_hi, cells_lo, amp_rows], axis=0)
             mask = _band_mask(off, wid, band, CHUNK)
             acc_ref[v] += lax.dot_general(
                 lhs, mask, (((1,), (1,)), ((), ())), preferred_element_type=jnp.float32
@@ -53,7 +58,13 @@
     placed = []
     for v in range(view_count):
         acc = acc_ref[v]
-        summed = (acc[: 2 * slab_rows] + acc[2 * slab_rows :])[:height]
+        summed = jnp.concatenate(
+            [
+                acc[:slab_rows] + acc[slab_rows : 2 * slab_rows],
+                acc[2 * slab_rows : 2 * slab_rows + 1] + acc[2 * slab_rows + 1 : 2 * slab_rows + 2],
+            ],
+            axis=0,
+        )
         ext = jnp.concatenate([summed, jnp.zeros((height, detector_width - band), jnp.float32)], axis=1)
         placed.append(pltpu.roll(ext, start_ref[v, 0], 1))
     joined = jnp.concatenate(placed, axis=0)
@@ -70,9 +81,9 @@
         _forward_kernel,
         out_shape=jax.ShapeDtypeStruct((chunks, view_count * (slab_rows + 1), shard_width), jnp.float32),
         in_specs=[smem, vmem, vmem, vmem, vmem],
-        scratch_shapes=[pltpu.VMEM((view_count, 4 * slab_rows, B), jnp.float32)],
+        scratch_shapes=[pltpu.VMEM((view_count, 3 * slab_rows, B), jnp.float32)],
         cost_estimate=pl.CostEstimate(
-            flops=2 * view_count * 4 * slab_rows * B * volume.shape[1],
+            flops=2 * view_count * 3 * slab_rows * B * volume.shape[1],
             transcendentals=0,
             bytes_accessed=4 * (volume.size + 3 * amplitude.size),
         ),

time: 77.6 us -> 77.4 us (level)
  no operation moved by 1% of the time
where the time goes in v11:
time: 77.4 us; the launch traced here: 77 us
  starting transfers between devices  23.2 us (30%)
  Pallas kernels  23 us (30%)
  waiting for transfers between devices  18.5 us (24%)
  between operations  4.99 us (6%)
  local copies, waits for them, and re-layouts  4.54 us (6%)
  other arithmetic  2.7 us (3%)
    pallas_call x1, Pallas kernels, forward_band(): pl.pallas_call(_forward_kernel, out_shape=jax.ShapeDtypeStruct((chunks, v...  13.4 us
    pallas_call x1, Pallas kernels, backward_update(): pl.pallas_call(_backward_kernel, out_shape=jax.ShapeDtypeStruct(volume.sh...  9.66 us
    ppermute x4, waiting for transfers between devices, all_gather_xy(): other = lax.ppermute(y, 'xy', [(i, i ^ 1 << j) for i in range(count)])  8.68 us
    ppermute x4, starting transfers between devices, reduce_scatter_xy(): y = keep + lax.ppermute(send, 'xy', [(i, i ^ 1 << j) for i in range(count)])  7.77 us
    ppermute x4, waiting for transfers between devices, reduce_scatter_xy(): y = keep + lax.ppermute(send, 'xy', [(i, i ^ 1 << j) for i in range(count)])  5.78 us
    ppermute x4, starting transfers between devices, all_gather_xy(): other = lax.ppermute(y, 'xy', [(i, i ^ 1 << j) for i in range(count)])  4.9 us
    ppermute x1, starting transfers between devices, local(): lax.ppermute(proj_cols[:, slab_rows - 2:], 'gz', up_pairs)  4.54 us
    ppermute x1, waiting for transfers between devices, local(): lax.ppermute(proj_cols[:, :2], 'gz', down_pairs)  4.05 us
  transfers between devices with their start and end apart: 12, of which 7 were waited for; matrix products, arithmetic and copies ran while one was open for 3% of the time, Pallas kernels for 0%

profile of v11, /device:TPU:0, one launch (start us, length us, event | category | flops | bytes accessed | tf_op | source)
XLA Modules:
  0.0 77.0 jit_solution(7753357137362167959)
XLA Ops:
  0.6 0.6 copy-done.2
  1.3 0.6 copy.50.start_ref
  1.9 13.4 %shard_map.86 = f32[16,34,256]{2,1,0:T(8,128)} custom-call(s32[2,1]{1,0:T(2,128)} %copy.50.start_ref, f32[16,16384]{1,0:T(8,128)} %vol_ref.3, f32[2,16384]{1,0:T(2,128)} %amp_ref.3, s32[2,16384]{1,0:T(2,128)} %off_ref.3, s32[2,16384]{1,0:T(2,128)} %wid_ref.3), custom_call_target="tpu_custom_call" | custom-call | flops 1610612736 | bytes 1441792 | tf_op jit(solution)/shard_map/pallas_call | solution.py:80
  15.3 1.1 %constant_dynamic-slice_fusion.5 = (f32[2,2,2,1,34,256]{5,4,3,2,1,0:T(8,128)S(1)}, f32[2,2,2,1,34,256]{5,4,3,2,1,0:T(8,128)S(1)}) fusion(f32[2,2,2,2,34,256]{5,4,3,2,1,0:T(8,128)} %bitcast.95, s32[]{:T(128)S(6)} %select_n.111, s32[]{:T(128)S(6)} %select_n.112), kind=kLoop, calls=%fused_computation.51 | loop fusion | bytes 1114120 | tf_op jit(solution)/shard_map/jit(dynamic_index_in_dim)/dynamic_slice | solution.py:146
  16.4 0.0 copy-start
  16.4 0.2 copy.79
  16.7 0.0 copy-start.1
  16.7 0.5 collective-permute-start.2
  17.2 0.1 slice_bitcast_fusion.3
  17.3 0.1 reshape.120
  17.4 0.1 copy-done.1
  17.4 0.9 %collective-permute-done.2 = f32[2,2,2,34,256]{4,1,3,0,2:T(2,128)S(1)} collective-permute-done((f32[2,2,2,34,256]{4,1,3,0,2:T(2,128)S(1)}, f32[2,2,2,34,256]{4,1,3,0,2:T(2,128)S(1)}, u32[]{:S(2)}, u32[]{:S(2)}) %collective-permute-start.2) | collective-permute-done | bytes 278560 | tf_op jit(solution)/shard_map/ppermute | solution.py:148
  18.4 0.3 bitcast_add_fusion
  18.7 3.0 %collective-permute-start.3 = (f32[2,2,34,256]{3,1,2,0:T(2,128)S(1)}, f32[2,2,34,256]{3,1,2,0:T(2,128)S(1)}, u32[]{:S(2)}, u32[]{:S(2)}) collective-permute-start(f32[2,2,34,256]{3,1,2,0:T(2,128)S(1)} %dynamic-slice_bitcast_fusion), channel_id=1, source_target_pairs={{0,4},{2,6},{4,0},{6,2},{8,12},{10,14},{12,8},{14,10},{16,20},{18,... | collective-permute-start | bytes 417800 | tf_op jit(solution)/shard_map/ppermute | solution.py:148
  21.7 3.4 %collective-permute-start = (f32[2,2,256]{2,0,1:T(2,128)S(1)}, f32[2,2,256]{2,0,1:T(2,128)S(1)}, u32[]{:S(2)}, u32[]{:S(2)}) collective-permute-start(f32[2,2,256]{2,0,1:T(2,128)S(1)} %select_maximum_fusion.1), channel_id=1, source_target_pairs={{0,1},{2,3},{4,5},{6,7},{8,9},{10,11},{12,13},{14,15},{16,17},{18,... | collective-permute-start | bytes 12296 | tf_op jit(solution)/shard_map/ppermute | solution.py:187
  25.1 0.1 reshape.121
  25.2 1.3 %collective-permute-start.1 = (f32[2,2,256]{2,0,1:T(2,128)S(1)}, f32[2,2,256]{2,0,1:T(2,128)S(1)}, u32[]{:S(2)}, u32[]{:S(2)}) collective-permute-start(f32[2,2,256]{2,0,1:T(2,128)S(1)} %select_maximum_fusion), channel_id=1, source_target_pairs={{1,0},{3,2},{5,4},{7,6},{9,8},{11,10},{13,12},{15,14},{17,16},{19,... | collective-permute-start | bytes 12296 | tf_op jit(solution)/shard_map/ppermute | solution.py:190
  26.5 0.1 bitcast_add_fusion.1
  26.6 0.1 constant_dynamic-slice_fusion.3
  26.7 1.6 %collective-permute-start.4 = (f32[2,34,256]{2,0,1:T(2,128)S(1)}, f32[2,34,256]{2,0,1:T(2,128)S(1)}, u32[]{:S(2)}, u32[]{:S(2)}) collective-permute-start(f32[2,34,256]{2,0,1:T(2,128)S(1)} %bitcast.100), channel_id=1, source_target_pairs={{0,8},{2,10},{4,12},{6,14},{8,0},{10,2},{12,4},{14,6},{16,24},{18,... | collective-permute-start | bytes 208904 | tf_op jit(solution)/shard_map/ppermute | solution.py:148
  28.4 2.7 %collective-permute-done.4 = f32[2,34,256]{2,0,1:T(2,128)S(1)} collective-permute-done((f32[2,34,256]{2,0,1:T(2,128)S(1)}, f32[2,34,256]{2,0,1:T(2,128)S(1)}, u32[]{:S(2)}, u32[]{:S(2)}) %collective-permute-start.4) | collective-permute-done | bytes 69664 | tf_op jit(solution)/shard_map/ppermute | solution.py:148
  31.1 0.1 bitcast_add_fusion.2
  31.2 0.1 constant_dynamic-slice_fusion.1
  31.2 2.7 %collective-permute-start.5 = (f32[34,256]{1,0:T(8,128)S(1)}, f32[34,256]{1,0:T(8,128)S(1)}, u32[]{:S(2)}, u32[]{:S(2)}) collective-permute-start(f32[34,256]{1,0:T(8,128)S(1)} %bitcast.101), channel_id=1, source_target_pairs={{0,16},{2,18},{4,20},{6,22},{8,24},{10,26},{12,28},{14,30},{16,0},... | collective-permute-start | bytes 104456 | tf_op jit(solution)/shard_map/ppermute | solution.py:148
  33.9 0.1 reshape_squeeze.6
  34.0 0.1 reshape_squeeze.7
  34.1 2.1 %collective-permute-done.5 = f32[34,256]{1,0:T(8,128)S(1)} collective-permute-done((f32[34,256]{1,0:T(8,128)S(1)}, f32[34,256]{1,0:T(8,128)S(1)}, u32[]{:S(2)}, u32[]{:S(2)}) %collective-permute-start.5) | collective-permute-done | bytes 34848 | tf_op jit(solution)/shard_map/ppermute | solution.py:148
  36.2 4.5 %collective-permute-start.6 = (f32[2,2,256]{2,1,0:T(2,128)S(1)}, f32[2,2,256]{2,1,0:T(2,128)S(1)}, u32[]{:S(2)}, u32[]{:S(2)}) collective-permute-start(f32[2,2,256]{2,1,0:T(2,128)S(1)} %get-tuple-element.24), channel_id=1, source_target_pairs={{0,1},{2,3},{4,5},{6,7},{8,9},{10,11},{12,13},{14,15},{16,17},{18,... | collective-permute-start | bytes 12296 | tf_op jit(solution)/shard_map/ppermute | solution.py:203
  40.8 1.3 %collective-permute-start.7 = (f32[2,2,256]{2,1,0:T(2,128)S(1)}, f32[2,2,256]{2,1,0:T(2,128)S(1)}, u32[]{:S(2)}, u32[]{:S(2)}) collective-permute-start(f32[2,2,256]{2,1,0:T(2,128)S(1)} %get-tuple-element.25), channel_id=1, source_target_pairs={{1,0},{3,2},{5,4},{7,6},{9,8},{11,10},{13,12},{15,14},{17,16},{19,... | collective-permute-start | bytes 12296 | tf_op jit(solution)/shard_map/ppermute | solution.py:205
  42.1 0.1 add_add_fusion
  42.2 4.0 %collective-permute-done.7 = f32[2,2,256]{2,1,0:T(2,128)S(1)} collective-permute-done((f32[2,2,256]{2,1,0:T(2,128)S(1)}, f32[2,2,256]{2,1,0:T(2,128)S(1)}, u32[]{:S(2)}, u32[]{:S(2)}) %collective-permute-start.7) | collective-permute-done | bytes 4128 | tf_op jit(solution)/shard_map/ppermute | solution.py:205
  46.3 0.1 fusion.5
  46.4 0.6 fusion.6
  47.0 2.6 %collective-permute-start.8 = (f32[32,256]{1,0:T(8,128)S(1)}, f32[32,256]{1,0:T(8,128)S(1)}, u32[]{:S(2)}, u32[]{:S(2)}) collective-permute-start(f32[32,256]{1,0:T(8,128)S(1)} %bitcast.99), channel_id=1, source_target_pairs={{0,16},{2,18},{4,20},{6,22},{8,24},{10,26},{12,28},{14,30},{16,0},... | collective-permute-start | bytes 98312 | tf_op jit(solution)/shard_map/ppermute | solution.py:159
  49.6 2.2 %collective-permute-done.8 = f32[32,256]{1,0:T(8,128)S(1)} collective-permute-done((f32[32,256]{1,0:T(8,128)S(1)}, f32[32,256]{1,0:T(8,128)S(1)}, u32[]{:S(2)}, u32[]{:S(2)}) %collective-permute-start.8) | collective-permute-done | bytes 32800 | tf_op jit(solution)/shard_map/ppermute | solution.py:159
  51.9 1.6 %collective-permute-start.9 = (f32[2,32,256]{2,1,0:T(8,128)S(1)}, f32[2,32,256]{2,1,0:T(8,128)S(1)}, u32[]{:S(2)}, u32[]{:S(2)}) collective-permute-start(f32[2,32,256]{2,1,0:T(8,128)S(1)} %pad_maximum_fusion.3), channel_id=1, source_target_pairs={{0,8},{2,10},{4,12},{6,14},{8,0},{10,2},{12,4},{14,6},{16,24},{18,... | collective-permute-start | bytes 196616 | tf_op jit(solution)/shard_map/ppermute | solution.py:159
  53.5 2.7 %collective-permute-done.9 = f32[2,32,256]{2,1,0:T(8,128)S(1)} collective-permute-done((f32[2,32,256]{2,1,0:T(8,128)S(1)}, f32[2,32,256]{2,1,0:T(8,128)S(1)}, u32[]{:S(2)}, u32[]{:S(2)}) %collective-permute-start.9) | collective-permute-done | bytes 65568 | tf_op jit(solution)/shard_map/ppermute | solution.py:159
  56.2 0.6 collective-permute-start.10
  56.8 0.7 fusion.18
  57.5 3.8 %collective-permute-done.10 = f32[2,2,32,256]{3,2,1,0:T(8,128)S(1)} collective-permute-done((f32[2,2,32,256]{3,2,1,0:T(8,128)S(1)}, f32[2,2,32,256]{3,2,1,0:T(8,128)S(1)}, u32[]{:S(2)}, u32[]{:S(2)}) %collective-permute-start.10) | collective-permute-done | bytes 131104 | tf_op jit(solution)/shard_map/ppermute | solution.py:159
  61.3 0.1 collective-permute-start.11
  64.1 0.1 copy.62
  64.2 0.1 copy.63
  64.3 0.1 copy.64
  65.7 0.7 select_add_fusion.rw_ref
  66.6 0.1 dynamic-slice_bitcast_fusion.1
  66.7 0.6 pad_maximum_fusion.4.back_ref
  67.3 9.7 %shard_map.87 = f32[16,16384]{1,0:T(8,128)} custom-call(f32[2,16,512]{2,1,0:T(8,128)} %pad_maximum_fusion.4.back_ref, f32[16,16384]{1,0:T(8,128)} %vol_ref.3, f32[2,16384]{1,0:T(2,128)} %amp_ref.3, s32[2,16384]{1,0:T(2,128)} %off_ref.3, s32[2,16384]{1,0:T(2,128)} %wid_ref.3, f32[2,16,1]{2,1,0:T(8,128)} %select_add_fusion.rw_ref), custom_call_target="tpu_custom_call" | custom-call | tf_op jit(solution)/shard_map/pallas_call | solution.py:124
  (45 shorter events, 0.4 us)
Async XLA Ops:
  0.6 0.7 copy-start.2
  16.4 0.8 %copy-start = (f32[3,2,16]{2,1,0:T(2,128)S(1)}, f32[3,2,16]{2,1,0:T(2,128)}, u32[]{:S(2)}) copy-start(f32[3,2,16]{2,1,0:T(2,128)} %param.13) | copy-start | bytes 1156
  16.7 0.8 copy-start.1
  16.7 1.7 %collective-permute-start.2 = (f32[2,2,2,34,256]{4,1,3,0,2:T(2,128)S(1)}, f32[2,2,2,34,256]{4,1,3,0,2:T(2,128)S(1)}, u32[]{:S(2)}, u32[]{:S(2)}) collective-permute-start(f32[2,2,2,34,256]{4,1,3,0,2:T(2,128)S(1)} %bitcast.98), channel_id=1, source_target_pairs={{0,2},{2,0},{4,6},{6,4},{8,10},{10,8},{12,14},{14,12},{16,18},{18,... | collective-permute-start | bytes 835592 | tf_op jit(solution)/shard_map/ppermute | solution.py:148
  18.7 7.8 %collective-permute-start.3 = (f32[2,2,34,256]{3,1,2,0:T(2,128)S(1)}, f32[2,2,34,256]{3,1,2,0:T(2,128)S(1)}, u32[]{:S(2)}, u32[]{:S(2)}) collective-permute-start(f32[2,2,34,256]{3,1,2,0:T(2,128)S(1)} %dynamic-slice_bitcast_fusion), channel_id=1, source_target_pairs={{0,4},{2,6},{4,0},{6,2},{8,12},{10,14},{12,8},{14,10},{16,20},{18,... | collective-permute-start | bytes 417800 | tf_op jit(solution)/shard_map/ppermute | solution.py:148
  21.7 12.3 %collective-permute-start = (f32[2,2,256]{2,0,1:T(2,128)S(1)}, f32[2,2,256]{2,0,1:T(2,128)S(1)}, u32[]{:S(2)}, u32[]{:S(2)}) collective-permute-start(f32[2,2,256]{2,0,1:T(2,128)S(1)} %select_maximum_fusion.1), channel_id=1, source_target_pairs={{0,1},{2,3},{4,5},{6,7},{8,9},{10,11},{12,13},{14,15},{16,17},{18,... | collective-permute-start | bytes 12296 | tf_op jit(solution)/shard_map/ppermute | solution.py:187
  25.2 8.9 %collective-permute-start.1 = (f32[2,2,256]{2,0,1:T(2,128)S(1)}, f32[2,2,256]{2,0,1:T(2,128)S(1)}, u32[]{:S(2)}, u32[]{:S(2)}) collective-permute-start(f32[2,2,256]{2,0,1:T(2,128)S(1)} %select_maximum_fusion), channel_id=1, source_target_pairs={{1,0},{3,2},{5,4},{7,6},{9,8},{11,10},{13,12},{15,14},{17,16},{19,... | collective-permute-start | bytes 12296 | tf_op jit(solution)/shard_map/ppermute | solution.py:190
  26.7 4.4 %collective-permute-start.4 = (f32[2,34,256]{2,0,1:T(2,128)S(1)}, f32[2,34,256]{2,0,1:T(2,128)S(1)}, u32[]{:S(2)}, u32[]{:S(2)}) collective-permute-start(f32[2,34,256]{2,0,1:T(2,128)S(1)} %bitcast.100), channel_id=1, source_target_pairs={{0,8},{2,10},{4,12},{6,14},{8,0},{10,2},{12,4},{14,6},{16,24},{18,... | collective-permute-start | bytes 208904 | tf_op jit(solution)/shard_map/ppermute | solution.py:148
  31.2 5.0 %collective-permute-start.5 = (f32[34,256]{1,0:T(8,128)S(1)}, f32[34,256]{1,0:T(8,128)S(1)}, u32[]{:S(2)}, u32[]{:S(2)}) collective-permute-start(f32[34,256]{1,0:T(8,128)S(1)} %bitcast.101), channel_id=1, source_target_pairs={{0,16},{2,18},{4,20},{6,22},{8,24},{10,26},{12,28},{14,30},{16,0},... | collective-permute-start | bytes 104456 | tf_op jit(solution)/shard_map/ppermute | solution.py:148
  36.2 6.0 %collective-permute-start.6 = (f32[2,2,256]{2,1,0:T(2,128)S(1)}, f32[2,2,256]{2,1,0:T(2,128)S(1)}, u32[]{:S(2)}, u32[]{:S(2)}) collective-permute-start(f32[2,2,256]{2,1,0:T(2,128)S(1)} %get-tuple-element.24), channel_id=1, source_target_pairs={{0,1},{2,3},{4,5},{6,7},{8,9},{10,11},{12,13},{14,15},{16,17},{18,... | collective-permute-start | bytes 12296 | tf_op jit(solution)/shard_map/ppermute | solution.py:203
  40.8 5.5 %collective-permute-start.7 = (f32[2,2,256]{2,1,0:T(2,128)S(1)}, f32[2,2,256]{2,1,0:T(2,128)S(1)}, u32[]{:S(2)}, u32[]{:S(2)}) collective-permute-start(f32[2,2,256]{2,1,0:T(2,128)S(1)} %get-tuple-element.25), channel_id=1, source_target_pairs={{1,0},{3,2},{5,4},{7,6},{9,8},{11,10},{13,12},{15,14},{17,16},{19,... | collective-permute-start | bytes 12296 | tf_op jit(solution)/shard_map/ppermute | solution.py:205
  47.0 4.8 %collective-permute-start.8 = (f32[32,256]{1,0:T(8,128)S(1)}, f32[32,256]{1,0:T(8,128)S(1)}, u32[]{:S(2)}, u32[]{:S(2)}) collective-permute-start(f32[32,256]{1,0:T(8,128)S(1)} %bitcast.99), channel_id=1, source_target_pairs={{0,16},{2,18},{4,20},{6,22},{8,24},{10,26},{12,28},{14,30},{16,0},... | collective-permute-start | bytes 98312 | tf_op jit(solution)/shard_map/ppermute | solution.py:159
  51.9 4.3 %collective-permute-start.9 = (f32[2,32,256]{2,1,0:T(8,128)S(1)}, f32[2,32,256]{2,1,0:T(8,128)S(1)}, u32[]{:S(2)}, u32[]{:S(2)}) collective-permute-start(f32[2,32,256]{2,1,0:T(8,128)S(1)} %pad_maximum_fusion.3), channel_id=1, source_target_pairs={{0,8},{2,10},{4,12},{6,14},{8,0},{10,2},{12,4},{14,6},{16,24},{18,... | collective-permute-start | bytes 196616 | tf_op jit(solution)/shard_map/ppermute | solution.py:159
  56.2 5.0 %collective-permute-start.10 = (f32[2,2,32,256]{3,2,1,0:T(8,128)S(1)}, f32[2,2,32,256]{3,2,1,0:T(8,128)S(1)}, u32[]{:S(2)}, u32[]{:S(2)}) collective-permute-start(f32[2,2,32,256]{3,2,1,0:T(8,128)S(1)} %pad_maximum_fusion.2), channel_id=1, source_target_pairs={{0,4},{2,6},{4,0},{6,2},{8,12},{10,14},{12,8},{14,10},{16,20},{18,... | collective-permute-start | bytes 393224 | tf_op jit(solution)/shard_map/ppermute | solution.py:159
  61.3 5.1 %collective-permute-start.11 = (f32[2,2,2,32,256]{4,3,2,1,0:T(8,128)S(1)}, f32[2,2,2,32,256]{4,3,2,1,0:T(8,128)S(1)}, u32[]{:S(2)}, u32[]{:S(2)}) collective-permute-start(f32[2,2,2,32,256]{4,3,2,1,0:T(8,128)S(1)} %pad_maximum_fusion.1), channel_id=1, source_target_pairs={{0,2},{2,0},{4,6},{6,4},{8,10},{10,8},{12,14},{14,12},{16,18},{18,... | collective-permute-start | bytes 786440 | tf_op jit(solution)/shard_map/ppermute | solution.py:159

commit v12 on v11

--- a/solution.py
+++ b/solution.py
@@ -184,10 +184,18 @@
         cols = packed[:, 1, : 3 * 2].reshape(view_count, 3, 2)
         return packed[:, :1], jnp.transpose(cols, (1, 0, 2))
 
-    from_below = lax.ppermute(
-        pack(measured[:, slab_rows - 1 :], axial_weight[:, :, slab_rows - 2 :]), "gz", up_pairs
-    )
-    from_above = lax.ppermute(pack(measured[:, :1], axial_weight[:, :, :2]), "gz", down_pairs)
+    gz_index = lax.axis_index("gz")
+
+    def exchange(upward, downward):
+        if gz_count != 2:
+            return lax.ppermute(upward, "gz", up_pairs), lax.ppermute(downward, "gz", down_pairs)
+        got = lax.ppermute(jnp.where(gz_index == 0, upward, downward), "gz", [(0, 1), (1, 0)])
+        return jnp.where(gz_index == 1, got, 0.0), jnp.where(gz_index == 0, got, 0.0)
+
+    from_below, from_above = exchange(
+        pack(measured[:, slab_rows - 1 :], axial_weight[:, :, slab_rows - 2 :]),
+        pack(measured[:, :1], axial_weight[:, :, :2]),
+    )
     meas_below, weight_below = unpack(from_below)
     meas_above, weight_above = unpack(from_above)
     measured_ext = jnp.concatenate([meas_below, measured, meas_above], axis=1)
@@ -198,14 +206,8 @@
     reduced = reduce_scatter_xy(placed, xy_count).reshape(view_count, band_height, shard_width)
     proj_cols = reduced[:, :slab_rows]
     cover = reduced[:, slab_rows : slab_rows + 1]
-    proj_ext = jnp.concatenate(
-        [
-            lax.ppermute(proj_cols[:, slab_rows - 2 :], "gz", up_pairs),
-            proj_cols,
-            lax.ppermute(proj_cols[:, :2], "gz", down_pairs),
-        ],
-        axis=1,
-    )
+    proj_below, proj_above = exchange(proj_cols[:, slab_rows - 2 :], proj_cols[:, :2])
+    proj_ext = jnp.concatenate([proj_below, proj_cols, proj_above], axis=1)
 
     ext_rows = slab_rows + 2
     mid_w = weight_ext[1, :, 1 : ext_rows + 1][:, :, None]

time: 77.4 us -> 70.5 us (0.911)
  starting transfers between devices: 23.2 us -> 16.5 us
    ppermute x4 -> x2, starting transfers between devices: 10.5 us -> 4.16 us  [exchange(): lax.ppermute(jnp.where(gz_index == 0, upward, downward), 'gz', [(0, 1), (...]
    ppermute x4, waiting for transfers between devices: 5.78 us -> 8.52 us  [reduce_scatter_xy(): y = keep + lax.ppermute(send, 'xy', [(i, i ^ 1 << j) for i in range(count)])]
    ppermute x4 -> x2, waiting for transfers between devices: 4.05 us -> 2.37 us  [exchange(): lax.ppermute(jnp.where(gz_index == 0, upward, downward), 'gz', [(0, 1), (...]
    ppermute x4, starting transfers between devices: 7.77 us -> 6.4 us  [reduce_scatter_xy(): y = keep + lax.ppermute(send, 'xy', [(i, i ^ 1 << j) for i in range(count)])]
    ppermute x4, starting transfers between devices: 4.9 us -> 5.92 us  [all_gather_xy(): other = lax.ppermute(y, 'xy', [(i, i ^ 1 << j) for i in range(count)])]
    ppermute x4, waiting for transfers between devices: 8.68 us -> 7.71 us  [all_gather_xy(): other = lax.ppermute(y, 'xy', [(i, i ^ 1 << j) for i in range(count)])]
  transfers between devices with their start and end apart: 12 -> 10, of which waited for: 7 -> 7; matrix products, arithmetic and copies ran while one was open for 3% -> 4% of each run, Pallas kernels for 0% -> 0%
where the time goes in v12:
time: 70.5 us; the launch traced here: 70.2 us
  Pallas kernels  23 us (33%)
  waiting for transfers between devices  18.6 us (26%)
  starting transfers between devices  16.5 us (23%)
  between operations  4.75 us (7%)
  local copies, waits for them, and re-layouts  4.62 us (7%)
  other arithmetic  2.71 us (4%)
    pallas_call x1, Pallas kernels, forward_band(): pl.pallas_call(_forward_kernel, out_shape=jax.ShapeDtypeStruct((chunks, v...  13.4 us
    pallas_call x1, Pallas kernels, backward_update(): pl.pallas_call(_backward_kernel, out_shape=jax.ShapeDtypeStruct(volume.sh...  9.65 us
    ppermute x4, waiting for transfers between devices, reduce_scatter_xy(): y = keep + lax.ppermute(send, 'xy', [(i, i ^ 1 << j) for i in range(count)])  8.52 us
    ppermute x4, waiting for transfers between devices, all_gather_xy(): other = lax.ppermute(y, 'xy', [(i, i ^ 1 << j) for i in range(count)])  7.71 us
    ppermute x4, starting transfers between devices, reduce_scatter_xy(): y = keep + lax.ppermute(send, 'xy', [(i, i ^ 1 << j) for i in range(count)])  6.4 us
    ppermute x4, starting transfers between devices, all_gather_xy(): other = lax.ppermute(y, 'xy', [(i, i ^ 1 << j) for i in range(count)])  5.92 us
    ppermute x2, starting transfers between devices, exchange(): lax.ppermute(jnp.where(gz_index == 0, upward, downward), 'gz', [(0, 1), (...  4.16 us
    ppermute x2, waiting for transfers between devices, exchange(): lax.ppermute(jnp.where(gz_index == 0, upward, downward), 'gz', [(0, 1), (...  2.37 us
  transfers between devices with their start and end apart: 10, of which 7 were waited for; matrix products, arithmetic and copies ran while one was open for 4% of the time, Pallas kernels for 0%

profile of v12, /device:TPU:0, one launch (start us, length us, event | category | flops | bytes accessed | tf_op | source)
XLA Modules:
  0.0 70.2 jit_solution(16451012526904969332)
XLA Ops:
  0.6 0.6 copy-done.3
  1.3 0.6 copy.85.start_ref
  1.9 13.4 %shard_map.86 = f32[16,34,256]{2,1,0:T(8,128)} custom-call(s32[2,1]{1,0:T(2,128)} %copy.85.start_ref, f32[16,16384]{1,0:T(8,128)} %vol_ref.3, f32[2,16384]{1,0:T(2,128)} %amp_ref.3, s32[2,16384]{1,0:T(2,128)} %off_ref.3, s32[2,16384]{1,0:T(2,128)} %wid_ref.3), custom_call_target="tpu_custom_call" | custom-call | flops 1610612736 | bytes 1441792 | tf_op jit(solution)/shard_map/pallas_call | solution.py:80
  15.3 1.1 %constant_dynamic-slice_fusion.5 = (f32[2,2,2,1,34,256]{5,4,3,2,1,0:T(8,128)S(1)}, f32[2,2,2,1,34,256]{5,4,3,2,1,0:T(8,128)S(1)}) fusion(f32[2,2,2,2,34,256]{5,4,3,2,1,0:T(8,128)} %bitcast.89, s32[]{:T(128)S(6)} %select_n.148, s32[]{:T(128)S(6)} %select_n.149), kind=kLoop, calls=%fused_computation.56 | loop fusion | bytes 1114120 | tf_op jit(solution)/shard_map/jit(dynamic_index_in_dim)/dynamic_slice | solution.py:146
  16.4 0.2 copy.122
  16.7 0.0 copy-start.1
  16.7 0.0 copy-start.2
  16.7 0.5 collective-permute-start.1
  17.2 0.1 copy-done.1
  17.3 0.1 slice_bitcast_fusion.3
  17.4 0.1 reshape.120
  17.5 0.1 reshape.121
  17.6 3.0 %collective-permute-start = (f32[2,2,256]{2,0,1:T(2,128)S(1)}, f32[2,2,256]{2,0,1:T(2,128)S(1)}, u32[]{:S(2)}, u32[]{:S(2)}) collective-permute-start(f32[2,2,256]{2,0,1:T(2,128)S(1)} %fusion.8), channel_id=1, source_target_pairs={{0,1},{1,0},{2,3},{3,2},{4,5},{5,4},{6,7},{7,6},{8,9},{9,8},{10,11... | collective-permute-start | bytes 12296 | tf_op jit(solution)/shard_map/ppermute | solution.py:192
  20.6 0.3 bitcast_add_fusion
  21.0 1.6 %collective-permute-start.2 = (f32[2,2,34,256]{3,1,2,0:T(2,128)S(1)}, f32[2,2,34,256]{3,1,2,0:T(2,128)S(1)}, u32[]{:S(2)}, u32[]{:S(2)}) collective-permute-start(f32[2,2,34,256]{3,1,2,0:T(2,128)S(1)} %dynamic-slice_bitcast_fusion), channel_id=1, source_target_pairs={{0,4},{2,6},{4,0},{6,2},{8,12},{10,14},{12,8},{14,10},{16,20},{18,... | collective-permute-start | bytes 417800 | tf_op jit(solution)/shard_map/ppermute | solution.py:148
  22.6 3.7 %collective-permute-done.2 = f32[2,2,34,256]{3,1,2,0:T(2,128)S(1)} collective-permute-done((f32[2,2,34,256]{3,1,2,0:T(2,128)S(1)}, f32[2,2,34,256]{3,1,2,0:T(2,128)S(1)}, u32[]{:S(2)}, u32[]{:S(2)}) %collective-permute-start.2) | collective-permute-done | bytes 139296 | tf_op jit(solution)/shard_map/ppermute | solution.py:148
  26.2 0.1 bitcast_add_fusion.1
  26.3 0.1 constant_dynamic-slice_fusion.3
  26.5 1.6 %collective-permute-start.3 = (f32[2,34,256]{2,0,1:T(2,128)S(1)}, f32[2,34,256]{2,0,1:T(2,128)S(1)}, u32[]{:S(2)}, u32[]{:S(2)}) collective-permute-start(f32[2,34,256]{2,0,1:T(2,128)S(1)} %bitcast.94), channel_id=1, source_target_pairs={{0,8},{2,10},{4,12},{6,14},{8,0},{10,2},{12,4},{14,6},{16,24},{18,... | collective-permute-start | bytes 208904 | tf_op jit(solution)/shard_map/ppermute | solution.py:148
  28.2 2.7 %collective-permute-done.3 = f32[2,34,256]{2,0,1:T(2,128)S(1)} collective-permute-done((f32[2,34,256]{2,0,1:T(2,128)S(1)}, f32[2,34,256]{2,0,1:T(2,128)S(1)}, u32[]{:S(2)}, u32[]{:S(2)}) %collective-permute-start.3) | collective-permute-done | bytes 69664 | tf_op jit(solution)/shard_map/ppermute | solution.py:148
  30.9 0.1 bitcast_add_fusion.2
  30.9 0.1 constant_dynamic-slice_fusion.1
  31.0 2.7 %collective-permute-start.4 = (f32[34,256]{1,0:T(8,128)S(1)}, f32[34,256]{1,0:T(8,128)S(1)}, u32[]{:S(2)}, u32[]{:S(2)}) collective-permute-start(f32[34,256]{1,0:T(8,128)S(1)} %bitcast.95), channel_id=1, source_target_pairs={{0,16},{2,18},{4,20},{6,22},{8,24},{10,26},{12,28},{14,30},{16,0},... | collective-permute-start | bytes 104456 | tf_op jit(solution)/shard_map/ppermute | solution.py:148
  33.7 0.1 reshape_squeeze.6
  33.8 0.1 reshape_squeeze.7
  33.9 2.1 %collective-permute-done.4 = f32[34,256]{1,0:T(8,128)S(1)} collective-permute-done((f32[34,256]{1,0:T(8,128)S(1)}, f32[34,256]{1,0:T(8,128)S(1)}, u32[]{:S(2)}, u32[]{:S(2)}) %collective-permute-start.4) | collective-permute-done | bytes 34848 | tf_op jit(solution)/shard_map/ppermute | solution.py:148
  36.0 0.0 copy-start
  36.0 1.2 %collective-permute-start.5 = (f32[2,2,256]{2,0,1:T(2,128)S(1)}, f32[2,2,256]{2,0,1:T(2,128)S(1)}, u32[]{:S(2)}, u32[]{:S(2)}) collective-permute-start(f32[2,2,256]{2,0,1:T(2,128)S(1)} %copy_select_fusion), channel_id=1, source_target_pairs={{0,1},{1,0},{2,3},{3,2},{4,5},{5,4},{6,7},{7,6},{8,9},{9,8},{10,11... | collective-permute-start | bytes 12296 | tf_op jit(solution)/shard_map/ppermute | solution.py:192
  37.2 0.1 add_add_fusion
  37.3 0.0 slice-start
  37.3 2.4 %collective-permute-done.5 = f32[2,2,256]{2,0,1:T(2,128)S(1)} collective-permute-done((f32[2,2,256]{2,0,1:T(2,128)S(1)}, f32[2,2,256]{2,0,1:T(2,128)S(1)}, u32[]{:S(2)}, u32[]{:S(2)}) %collective-permute-start.5) | collective-permute-done | bytes 4128 | tf_op jit(solution)/shard_map/ppermute | solution.py:192
  39.7 0.1 fusion.5
  39.9 0.6 fusion.6
  40.5 2.6 %collective-permute-start.6 = (f32[32,256]{1,0:T(8,128)S(1)}, f32[32,256]{1,0:T(8,128)S(1)}, u32[]{:S(2)}, u32[]{:S(2)}) collective-permute-start(f32[32,256]{1,0:T(8,128)S(1)} %bitcast.93), channel_id=1, source_target_pairs={{0,16},{2,18},{4,20},{6,22},{8,24},{10,26},{12,28},{14,30},{16,0},... | collective-permute-start | bytes 98312 | tf_op jit(solution)/shard_map/ppermute | solution.py:159
  43.1 2.2 %collective-permute-done.6 = f32[32,256]{1,0:T(8,128)S(1)} collective-permute-done((f32[32,256]{1,0:T(8,128)S(1)}, f32[32,256]{1,0:T(8,128)S(1)}, u32[]{:S(2)}, u32[]{:S(2)}) %collective-permute-start.6) | collective-permute-done | bytes 32800 | tf_op jit(solution)/shard_map/ppermute | solution.py:159
  45.3 1.6 %collective-permute-start.7 = (f32[2,32,256]{2,1,0:T(8,128)S(1)}, f32[2,32,256]{2,1,0:T(8,128)S(1)}, u32[]{:S(2)}, u32[]{:S(2)}) collective-permute-start(f32[2,32,256]{2,1,0:T(8,128)S(1)} %pad_maximum_fusion.3), channel_id=1, source_target_pairs={{0,8},{2,10},{4,12},{6,14},{8,0},{10,2},{12,4},{14,6},{16,24},{18,... | collective-permute-start | bytes 196616 | tf_op jit(solution)/shard_map/ppermute | solution.py:159
  47.0 2.7 %collective-permute-done.7 = f32[2,32,256]{2,1,0:T(8,128)S(1)} collective-permute-done((f32[2,32,256]{2,1,0:T(8,128)S(1)}, f32[2,32,256]{2,1,0:T(8,128)S(1)}, u32[]{:S(2)}, u32[]{:S(2)}) %collective-permute-start.7) | collective-permute-done | bytes 65568 | tf_op jit(solution)/shard_map/ppermute | solution.py:159
  49.7 1.6 %collective-permute-start.8 = (f32[2,2,32,256]{3,2,0,1:T(8,128)S(1)}, f32[2,2,32,256]{3,2,0,1:T(8,128)S(1)}, u32[]{:S(2)}, u32[]{:S(2)}) collective-permute-start(f32[2,2,32,256]{3,2,0,1:T(8,128)S(1)} %pad_maximum_fusion.2), channel_id=1, source_target_pairs={{0,4},{2,6},{4,0},{6,2},{8,12},{10,14},{12,8},{14,10},{16,20},{18,... | collective-permute-start | bytes 393224 | tf_op jit(solution)/shard_map/ppermute | solution.py:159
  51.3 0.6 fusion.19
  51.9 2.8 %collective-permute-done.8 = f32[2,2,32,256]{3,2,0,1:T(8,128)S(1)} collective-permute-done((f32[2,2,32,256]{3,2,0,1:T(8,128)S(1)}, f32[2,2,32,256]{3,2,0,1:T(8,128)S(1)}, u32[]{:S(2)}, u32[]{:S(2)}) %collective-permute-start.8) | collective-permute-done | bytes 131104 | tf_op jit(solution)/shard_map/ppermute | solution.py:159
  54.8 0.1 collective-permute-start.9
  57.4 0.1 copy.101
  57.5 0.1 copy.102
  57.6 0.1 copy.103
  58.9 0.7 select_add_fusion.rw_ref
  59.8 0.1 dynamic-slice_bitcast_fusion.1
  59.9 0.6 pad_maximum_fusion.4.back_ref
  60.5 9.7 %shard_map.87 = f32[16,16384]{1,0:T(8,128)} custom-call(f32[2,16,512]{2,1,0:T(8,128)} %pad_maximum_fusion.4.back_ref, f32[16,16384]{1,0:T(8,128)} %vol_ref.3, f32[2,16384]{1,0:T(2,128)} %amp_ref.3, s32[2,16384]{1,0:T(2,128)} %off_ref.3, s32[2,16384]{1,0:T(2,128)} %wid_ref.3, f32[2,16,1]{2,1,0:T(8,128)} %select_add_fusion.rw_ref), custom_call_target="tpu_custom_call" | custom-call | tf_op jit(solution)/shard_map/pallas_call | solution.py:124
  (49 shorter events, 0.5 us)
Async XLA Ops:
  0.6 0.7 copy-start.3
  16.7 0.7 copy-start.1
  16.7 0.9 %copy-start.2 = (f32[2,16,256]{2,1,0:T(8,128)S(1)}, f32[2,16,256]{2,1,0:T(8,128)}, u32[]{:S(2)}) copy-start(f32[2,16,256]{2,1,0:T(8,128)} %param.8) | copy-start | bytes 98308
  16.7 4.0 %collective-permute-start.1 = (f32[2,2,2,34,256]{4,1,3,0,2:T(2,128)S(1)}, f32[2,2,2,34,256]{4,1,3,0,2:T(2,128)S(1)}, u32[]{:S(2)}, u32[]{:S(2)}) collective-permute-start(f32[2,2,2,34,256]{4,1,3,0,2:T(2,128)S(1)} %bitcast.92), channel_id=1, source_target_pairs={{0,2},{2,0},{4,6},{6,4},{8,10},{10,8},{12,14},{14,12},{16,18},{18,... | collective-permute-start | bytes 835592 | tf_op jit(solution)/shard_map/ppermute | solution.py:148
  17.6 16.0 %collective-permute-start = (f32[2,2,256]{2,0,1:T(2,128)S(1)}, f32[2,2,256]{2,0,1:T(2,128)S(1)}, u32[]{:S(2)}, u32[]{:S(2)}) collective-permute-start(f32[2,2,256]{2,0,1:T(2,128)S(1)} %fusion.8), channel_id=1, source_target_pairs={{0,1},{1,0},{2,3},{3,2},{4,5},{5,4},{6,7},{7,6},{8,9},{9,8},{10,11... | collective-permute-start | bytes 12296 | tf_op jit(solution)/shard_map/ppermute | solution.py:192
  21.0 5.3 %collective-permute-start.2 = (f32[2,2,34,256]{3,1,2,0:T(2,128)S(1)}, f32[2,2,34,256]{3,1,2,0:T(2,128)S(1)}, u32[]{:S(2)}, u32[]{:S(2)}) collective-permute-start(f32[2,2,34,256]{3,1,2,0:T(2,128)S(1)} %dynamic-slice_bitcast_fusion), channel_id=1, source_target_pairs={{0,4},{2,6},{4,0},{6,2},{8,12},{10,14},{12,8},{14,10},{16,20},{18,... | collective-permute-start | bytes 417800 | tf_op jit(solution)/shard_map/ppermute | solution.py:148
  26.5 4.4 %collective-permute-start.3 = (f32[2,34,256]{2,0,1:T(2,128)S(1)}, f32[2,34,256]{2,0,1:T(2,128)S(1)}, u32[]{:S(2)}, u32[]{:S(2)}) collective-permute-start(f32[2,34,256]{2,0,1:T(2,128)S(1)} %bitcast.94), channel_id=1, source_target_pairs={{0,8},{2,10},{4,12},{6,14},{8,0},{10,2},{12,4},{14,6},{16,24},{18,... | collective-permute-start | bytes 208904 | tf_op jit(solution)/shard_map/ppermute | solution.py:148
  31.0 5.0 %collective-permute-start.4 = (f32[34,256]{1,0:T(8,128)S(1)}, f32[34,256]{1,0:T(8,128)S(1)}, u32[]{:S(2)}, u32[]{:S(2)}) collective-permute-start(f32[34,256]{1,0:T(8,128)S(1)} %bitcast.95), channel_id=1, source_target_pairs={{0,16},{2,18},{4,20},{6,22},{8,24},{10,26},{12,28},{14,30},{16,0},... | collective-permute-start | bytes 104456 | tf_op jit(solution)/shard_map/ppermute | solution.py:148
  36.0 1.3 %copy-start = (f32[2,17,256]{2,1,0:T(8,128)}, f32[2,17,256]{2,1,0:T(8,128)S(1)}, u32[]{:S(2)}) copy-start(f32[2,17,256]{2,1,0:T(8,128)S(1)} %reshape.123) | copy-start | bytes 104452
  36.0 3.7 %collective-permute-start.5 = (f32[2,2,256]{2,0,1:T(2,128)S(1)}, f32[2,2,256]{2,0,1:T(2,128)S(1)}, u32[]{:S(2)}, u32[]{:S(2)}) collective-permute-start(f32[2,2,256]{2,0,1:T(2,128)S(1)} %copy_select_fusion), channel_id=1, source_target_pairs={{0,1},{1,0},{2,3},{3,2},{4,5},{5,4},{6,7},{7,6},{8,9},{9,8},{10,11... | collective-permute-start | bytes 12296 | tf_op jit(solution)/shard_map/ppermute | solution.py:192
  37.3 2.4 %slice-start = ((f32[2,17,256]{2,1,0:T(8,128)}), f32[2,16,256]{2,1,0:T(8,128)S(1)}, s32[]{:S(2)}) async-start(f32[2,17,256]{2,1,0:T(8,128)} %copy-done), calls=%async_computation | async-start | bytes 65536 | tf_op jit(solution)/shard_map/slice | solution.py:207
  40.5 4.8 %collective-permute-start.6 = (f32[32,256]{1,0:T(8,128)S(1)}, f32[32,256]{1,0:T(8,128)S(1)}, u32[]{:S(2)}, u32[]{:S(2)}) collective-permute-start(f32[32,256]{1,0:T(8,128)S(1)} %bitcast.93), channel_id=1, source_target_pairs={{0,16},{2,18},{4,20},{6,22},{8,24},{10,26},{12,28},{14,30},{16,0},... | collective-permute-start | bytes 98312 | tf_op jit(solution)/shard_map/ppermute | solution.py:159
  45.3 4.3 %collective-permute-start.7 = (f32[2,32,256]{2,1,0:T(8,128)S(1)}, f32[2,32,256]{2,1,0:T(8,128)S(1)}, u32[]{:S(2)}, u32[]{:S(2)}) collective-permute-start(f32[2,32,256]{2,1,0:T(8,128)S(1)} %pad_maximum_fusion.3), channel_id=1, source_target_pairs={{0,8},{2,10},{4,12},{6,14},{8,0},{10,2},{12,4},{14,6},{16,24},{18,... | collective-permute-start | bytes 196616 | tf_op jit(solution)/shard_map/ppermute | solution.py:159
  49.7 5.0 %collective-permute-start.8 = (f32[2,2,32,256]{3,2,0,1:T(8,128)S(1)}, f32[2,2,32,256]{3,2,0,1:T(8,128)S(1)}, u32[]{:S(2)}, u32[]{:S(2)}) collective-permute-start(f32[2,2,32,256]{3,2,0,1:T(8,128)S(1)} %pad_maximum_fusion.2), channel_id=1, source_target_pairs={{0,4},{2,6},{4,0},{6,2},{8,12},{10,14},{12,8},{14,10},{16,20},{18,... | collective-permute-start | bytes 393224 | tf_op jit(solution)/shard_map/ppermute | solution.py:159
  54.8 4.8 %collective-permute-start.9 = (f32[2,2,2,32,256]{4,3,0,1,2:T(8,128)S(1)}, f32[2,2,2,32,256]{4,3,0,1,2:T(8,128)S(1)}, u32[]{:S(2)}, u32[]{:S(2)}) collective-permute-start(f32[2,2,2,32,256]{4,3,0,1,2:T(8,128)S(1)} %pad_maximum_fusion.1), channel_id=1, source_target_pairs={{0,2},{2,0},{4,6},{6,4},{8,10},{10,8},{12,14},{14,12},{16,18},{18,... | collective-permute-start | bytes 786440 | tf_op jit(solution)/shard_map/ppermute | solution.py:159

commit v13 on v12

--- a/solution.py
+++ b/solution.py
@@ -192,22 +192,24 @@
         got = lax.ppermute(jnp.where(gz_index == 0, upward, downward), "gz", [(0, 1), (1, 0)])
         return jnp.where(gz_index == 1, got, 0.0), jnp.where(gz_index == 0, got, 0.0)
 
-    from_below, from_above = exchange(
-        pack(measured[:, slab_rows - 1 :], axial_weight[:, :, slab_rows - 2 :]),
-        pack(measured[:, :1], axial_weight[:, :, :2]),
-    )
-    meas_below, weight_below = unpack(from_below)
-    meas_above, weight_above = unpack(from_above)
-    measured_ext = jnp.concatenate([meas_below, measured, meas_above], axis=1)
-    weight_ext = jnp.concatenate([weight_below, axial_weight, weight_above], axis=2)
 
     placed = forward_band(volume, amplitude, column_offset, column_width, band_start, xy_count, shard_width)
     band_height = slab_rows + 1
     reduced = reduce_scatter_xy(placed, xy_count).reshape(view_count, band_height, shard_width)
     proj_cols = reduced[:, :slab_rows]
     cover = reduced[:, slab_rows : slab_rows + 1]
-    proj_below, proj_above = exchange(proj_cols[:, slab_rows - 2 :], proj_cols[:, :2])
-    proj_ext = jnp.concatenate([proj_below, proj_cols, proj_above], axis=1)
+    from_below, from_above = exchange(
+        jnp.concatenate(
+            [proj_cols[:, slab_rows - 2 :], pack(measured[:, slab_rows - 1 :], axial_weight[:, :, slab_rows - 2 :])],
+            axis=1,
+        ),
+        jnp.concatenate([proj_cols[:, :2], pack(measured[:, :1], axial_weight[:, :, :2])], axis=1),
+    )
+    proj_ext = jnp.concatenate([from_below[:, :2], proj_cols, from_above[:, :2]], axis=1)
+    meas_below, weight_below = unpack(from_below[:, 2:])
+    meas_above, weight_above = unpack(from_above[:, 2:])
+    measured_ext = jnp.concatenate([meas_below, measured, meas_above], axis=1)
+    weight_ext = jnp.concatenate([weight_below, axial_weight, weight_above], axis=2)
 
     ext_rows = slab_rows + 2
     mid_w = weight_ext[1, :, 1 : ext_rows + 1][:, :, None]

time: 70.5 us -> 71 us (level)
    ppermute x2 -> x1, starting transfers between devices: 4.16 us -> 1.78 us  [exchange(): lax.ppermute(jnp.where(gz_index == 0, upward, downward), 'gz', [(0, 1), (...]
    ppermute x4, starting transfers between devices: 6.4 us -> 8.21 us  [reduce_scatter_xy(): y = keep + lax.ppermute(send, 'xy', [(i, i ^ 1 << j) for i in range(count)])]
    ppermute x4, waiting for transfers between devices: 8.52 us -> 9.5 us  [reduce_scatter_xy(): y = keep + lax.ppermute(send, 'xy', [(i, i ^ 1 << j) for i in range(count)])]
    ppermute x2 -> x1, waiting for transfers between devices: 2.37 us -> 1.91 us  [exchange(): lax.ppermute(jnp.where(gz_index == 0, upward, downward), 'gz', [(0, 1), (...]
    unnamed x14 -> x12, local copies, waits for them, and re-layouts: 1.51 us -> 1.36 us
  transfers between devices with their start and end apart: 10 -> 9, of which waited for: 7 -> 8; matrix products, arithmetic and copies ran while one was open for 4% -> 3% of each run, Pallas kernels for 0% -> 0%
where the time goes in v13:
time: 71 us; the launch traced here: 70.6 us
  Pallas kernels  23 us (32%)
  waiting for transfers between devices  18.4 us (26%)
  starting transfers between devices  16.6 us (23%)
  local copies, waits for them, and re-layouts  5 us (7%)
  between operations  4.89 us (7%)
  other arithmetic  2.72 us (4%)
    pallas_call x1, Pallas kernels, forward_band(): pl.pallas_call(_forward_kernel, out_shape=jax.ShapeDtypeStruct((chunks, v...  13.4 us
    pallas_call x1, Pallas kernels, backward_update(): pl.pallas_call(_backward_kernel, out_shape=jax.ShapeDtypeStruct(volume.sh...  9.65 us
    ppermute x4, waiting for transfers between devices, reduce_scatter_xy(): y = keep + lax.ppermute(send, 'xy', [(i, i ^ 1 << j) for i in range(count)])  9.5 us
    ppermute x4, starting transfers between devices, reduce_scatter_xy(): y = keep + lax.ppermute(send, 'xy', [(i, i ^ 1 << j) for i in range(count)])  8.21 us
    ppermute x4, waiting for transfers between devices, all_gather_xy(): other = lax.ppermute(y, 'xy', [(i, i ^ 1 << j) for i in range(count)])  7.02 us
    ppermute x4, starting transfers between devices, all_gather_xy(): other = lax.ppermute(y, 'xy', [(i, i ^ 1 << j) for i in range(count)])  6.58 us
    ppermute x1, waiting for transfers between devices, exchange(): lax.ppermute(jnp.where(gz_index == 0, upward, downward), 'gz', [(0, 1), (...  1.91 us
    ppermute x1, starting transfers between devices, exchange(): lax.ppermute(jnp.where(gz_index == 0, upward, downward), 'gz', [(0, 1), (...  1.78 us
  transfers between devices with their start and end apart: 9, of which 8 were waited for; matrix products, arithmetic and copies ran while one was open for 3% of the time, Pallas kernels for 0%

profile of v13, /device:TPU:0, one launch (start us, length us, event | category | flops | bytes accessed | tf_op | source)
XLA Modules:
  0.0 70.6 jit_solution(6784205871411313337)
XLA Ops:
  0.6 0.6 copy-done.3
  1.3 0.6 copy.38.start_ref
  1.9 13.4 %shard_map.86 = f32[16,34,256]{2,1,0:T(8,128)} custom-call(s32[2,1]{1,0:T(2,128)} %copy.38.start_ref, f32[16,16384]{1,0:T(8,128)} %vol_ref.3, f32[2,16384]{1,0:T(2,128)} %amp_ref.3, s32[2,16384]{1,0:T(2,128)} %off_ref.3, s32[2,16384]{1,0:T(2,128)} %wid_ref.3), custom_call_target="tpu_custom_call" | custom-call | flops 1610612736 | bytes 1441792 | tf_op jit(solution)/shard_map/pallas_call | solution.py:80
  15.3 1.1 %constant_dynamic-slice_fusion.5 = (f32[2,2,2,1,34,256]{5,4,3,2,1,0:T(8,128)S(1)}, f32[2,2,2,1,34,256]{5,4,3,2,1,0:T(8,128)S(1)}) fusion(f32[2,2,2,2,34,256]{5,4,3,2,1,0:T(8,128)} %bitcast.93, s32[]{:T(128)S(6)} %select_n.133, s32[]{:T(128)S(6)} %select_n.134), kind=kLoop, calls=%fused_computation.54 | loop fusion | bytes 1114120 | tf_op jit(solution)/shard_map/jit(dynamic_index_in_dim)/dynamic_slice | solution.py:146
  16.4 0.2 copy.73
  16.7 0.5 collective-permute-start
  17.2 1.2 %collective-permute-done = f32[2,2,2,34,256]{4,1,3,0,2:T(2,128)S(1)} collective-permute-done((f32[2,2,2,34,256]{4,1,3,0,2:T(2,128)S(1)}, f32[2,2,2,34,256]{4,1,3,0,2:T(2,128)S(1)}, u32[]{:S(2)}, u32[]{:S(2)}) %collective-permute-start) | collective-permute-done | bytes 278560 | tf_op jit(solution)/shard_map/ppermute | solution.py:148
  18.4 0.3 bitcast_add_fusion
  18.7 0.0 copy-start.2
  18.7 3.0 %collective-permute-start.1 = (f32[2,2,34,256]{3,1,2,0:T(2,128)S(1)}, f32[2,2,34,256]{3,1,2,0:T(2,128)S(1)}, u32[]{:S(2)}, u32[]{:S(2)}) collective-permute-start(f32[2,2,34,256]{3,1,2,0:T(2,128)S(1)} %dynamic-slice_bitcast_fusion), channel_id=1, source_target_pairs={{0,4},{2,6},{4,0},{6,2},{8,12},{10,14},{12,8},{14,10},{16,20},{18,... | collective-permute-start | bytes 417800 | tf_op jit(solution)/shard_map/ppermute | solution.py:148
  21.7 4.0 %collective-permute-done.1 = f32[2,2,34,256]{3,1,2,0:T(2,128)S(1)} collective-permute-done((f32[2,2,34,256]{3,1,2,0:T(2,128)S(1)}, f32[2,2,34,256]{3,1,2,0:T(2,128)S(1)}, u32[]{:S(2)}, u32[]{:S(2)}) %collective-permute-start.1) | collective-permute-done | bytes 139296 | tf_op jit(solution)/shard_map/ppermute | solution.py:148
  25.6 0.1 bitcast_add_fusion.1
  25.7 0.1 constant_dynamic-slice_fusion.3
  25.8 0.0 copy-start.1
  25.9 1.9 %collective-permute-start.2 = (f32[2,34,256]{2,0,1:T(2,128)S(1)}, f32[2,34,256]{2,0,1:T(2,128)S(1)}, u32[]{:S(2)}, u32[]{:S(2)}) collective-permute-start(f32[2,34,256]{2,0,1:T(2,128)S(1)} %bitcast.98), channel_id=1, source_target_pairs={{0,8},{2,10},{4,12},{6,14},{8,0},{10,2},{12,4},{14,6},{16,24},{18,... | collective-permute-start | bytes 208904 | tf_op jit(solution)/shard_map/ppermute | solution.py:148
  27.8 0.1 slice_bitcast_fusion.3
  27.8 2.4 %collective-permute-done.2 = f32[2,34,256]{2,0,1:T(2,128)S(1)} collective-permute-done((f32[2,34,256]{2,0,1:T(2,128)S(1)}, f32[2,34,256]{2,0,1:T(2,128)S(1)}, u32[]{:S(2)}, u32[]{:S(2)}) %collective-permute-start.2) | collective-permute-done | bytes 69664 | tf_op jit(solution)/shard_map/ppermute | solution.py:148
  30.3 0.1 bitcast_add_fusion.2
  30.3 0.1 constant_dynamic-slice_fusion.1
  30.4 2.9 %collective-permute-start.3 = (f32[34,256]{1,0:T(8,128)S(1)}, f32[34,256]{1,0:T(8,128)S(1)}, u32[]{:S(2)}, u32[]{:S(2)}) collective-permute-start(f32[34,256]{1,0:T(8,128)S(1)} %bitcast.99), channel_id=1, source_target_pairs={{0,16},{2,18},{4,20},{6,22},{8,24},{10,26},{12,28},{14,30},{16,0},... | collective-permute-start | bytes 104456 | tf_op jit(solution)/shard_map/ppermute | solution.py:148
  33.3 0.1 reshape.122
  33.4 0.1 reshape.123
  33.5 1.9 %collective-permute-done.3 = f32[34,256]{1,0:T(8,128)S(1)} collective-permute-done((f32[34,256]{1,0:T(8,128)S(1)}, f32[34,256]{1,0:T(8,128)S(1)}, u32[]{:S(2)}, u32[]{:S(2)}) %collective-permute-start.3) | collective-permute-done | bytes 34848 | tf_op jit(solution)/shard_map/ppermute | solution.py:148
  35.4 1.8 %collective-permute-start.4 = (f32[2,4,256]{2,1,0:T(4,128)S(1)}, f32[2,4,256]{2,1,0:T(4,128)S(1)}, u32[]{:S(2)}, u32[]{:S(2)}) collective-permute-start(f32[2,4,256]{2,1,0:T(4,128)S(1)} %fusion.8), channel_id=1, source_target_pairs={{0,1},{1,0},{2,3},{3,2},{4,5},{5,4},{6,7},{7,6},{8,9},{9,8},{10,11... | collective-permute-start | bytes 24584 | tf_op jit(solution)/shard_map/ppermute | solution.py:192
  37.2 1.9 %collective-permute-done.4 = f32[2,4,256]{2,1,0:T(4,128)S(1)} collective-permute-done((f32[2,4,256]{2,1,0:T(4,128)S(1)}, f32[2,4,256]{2,1,0:T(4,128)S(1)}, u32[]{:S(2)}, u32[]{:S(2)}) %collective-permute-start.4) | collective-permute-done | bytes 8224 | tf_op jit(solution)/shard_map/ppermute | solution.py:192
  39.2 0.0 slice-start
  39.2 0.1 reshape_squeeze.6
  39.3 0.1 reshape_squeeze.7
  39.4 0.1 add_add_fusion
  39.5 0.5 slice-done
  40.0 0.1 fusion.5
  40.1 0.6 fusion.6
  40.7 2.8 %collective-permute-start.5 = (f32[32,256]{1,0:T(8,128)S(1)}, f32[32,256]{1,0:T(8,128)S(1)}, u32[]{:S(2)}, u32[]{:S(2)}) collective-permute-start(f32[32,256]{1,0:T(8,128)S(1)} %bitcast.97), channel_id=1, source_target_pairs={{0,16},{2,18},{4,20},{6,22},{8,24},{10,26},{12,28},{14,30},{16,0},... | collective-permute-start | bytes 98312 | tf_op jit(solution)/shard_map/ppermute | solution.py:159
  43.5 2.0 %collective-permute-done.5 = f32[32,256]{1,0:T(8,128)S(1)} collective-permute-done((f32[32,256]{1,0:T(8,128)S(1)}, f32[32,256]{1,0:T(8,128)S(1)}, u32[]{:S(2)}, u32[]{:S(2)}) %collective-permute-start.5) | collective-permute-done | bytes 32800 | tf_op jit(solution)/shard_map/ppermute | solution.py:159
  45.5 1.9 %collective-permute-start.6 = (f32[2,32,256]{2,1,0:T(8,128)S(1)}, f32[2,32,256]{2,1,0:T(8,128)S(1)}, u32[]{:S(2)}, u32[]{:S(2)}) collective-permute-start(f32[2,32,256]{2,1,0:T(8,128)S(1)} %pad_maximum_fusion.3), channel_id=1, source_target_pairs={{0,8},{2,10},{4,12},{6,14},{8,0},{10,2},{12,4},{14,6},{16,24},{18,... | collective-permute-start | bytes 196616 | tf_op jit(solution)/shard_map/ppermute | solution.py:159
  47.4 2.5 %collective-permute-done.6 = f32[2,32,256]{2,1,0:T(8,128)S(1)} collective-permute-done((f32[2,32,256]{2,1,0:T(8,128)S(1)}, f32[2,32,256]{2,1,0:T(8,128)S(1)}, u32[]{:S(2)}, u32[]{:S(2)}) %collective-permute-start.6) | collective-permute-done | bytes 65568 | tf_op jit(solution)/shard_map/ppermute | solution.py:159
  49.9 1.8 %collective-permute-start.7 = (f32[2,2,32,256]{3,2,1,0:T(8,128)S(1)}, f32[2,2,32,256]{3,2,1,0:T(8,128)S(1)}, u32[]{:S(2)}, u32[]{:S(2)}) collective-permute-start(f32[2,2,32,256]{3,2,1,0:T(8,128)S(1)} %pad_maximum_fusion.2), channel_id=1, source_target_pairs={{0,4},{2,6},{4,0},{6,2},{8,12},{10,14},{12,8},{14,10},{16,20},{18,... | collective-permute-start | bytes 393224 | tf_op jit(solution)/shard_map/ppermute | solution.py:159
  51.7 0.6 fusion.19
  52.3 2.6 %collective-permute-done.7 = f32[2,2,32,256]{3,2,1,0:T(8,128)S(1)} collective-permute-done((f32[2,2,32,256]{3,2,1,0:T(8,128)S(1)}, f32[2,2,32,256]{3,2,1,0:T(8,128)S(1)}, u32[]{:S(2)}, u32[]{:S(2)}) %collective-permute-start.7) | collective-permute-done | bytes 131104 | tf_op jit(solution)/shard_map/ppermute | solution.py:159
  55.0 0.1 collective-permute-start.8
  57.7 0.1 copy.56
  57.8 0.1 copy.57
  57.9 0.1 copy.58
  59.3 0.7 select_add_fusion.rw_ref
  60.2 0.1 dynamic-slice_bitcast_fusion.2
  60.3 0.1 dynamic-slice_bitcast_fusion.1
  60.3 0.6 pad_maximum_fusion.4.back_ref
  61.0 9.7 %shard_map.87 = f32[16,16384]{1,0:T(8,128)} custom-call(f32[2,16,512]{2,1,0:T(8,128)} %pad_maximum_fusion.4.back_ref, f32[16,16384]{1,0:T(8,128)} %vol_ref.3, f32[2,16384]{1,0:T(2,128)} %amp_ref.3, s32[2,16384]{1,0:T(2,128)} %off_ref.3, s32[2,16384]{1,0:T(2,128)} %wid_ref.3, f32[2,16,1]{2,1,0:T(8,128)} %select_add_fusion.rw_ref), custom_call_target="tpu_custom_call" | custom-call | tf_op jit(solution)/shard_map/pallas_call | solution.py:124
  (40 shorter events, 0.4 us)
Async XLA Ops:
  0.6 0.7 copy-start.3
  16.7 1.7 %collective-permute-start = (f32[2,2,2,34,256]{4,1,3,0,2:T(2,128)S(1)}, f32[2,2,2,34,256]{4,1,3,0,2:T(2,128)S(1)}, u32[]{:S(2)}, u32[]{:S(2)}) collective-permute-start(f32[2,2,2,34,256]{4,1,3,0,2:T(2,128)S(1)} %bitcast.96), channel_id=1, source_target_pairs={{0,2},{2,0},{4,6},{6,4},{8,10},{10,8},{12,14},{14,12},{16,18},{18,... | collective-permute-start | bytes 835592 | tf_op jit(solution)/shard_map/ppermute | solution.py:148
  18.7 3.0 %copy-start.2 = (f32[2,16,256]{2,1,0:T(8,128)S(1)}, f32[2,16,256]{2,1,0:T(8,128)}, u32[]{:S(2)}) copy-start(f32[2,16,256]{2,1,0:T(8,128)} %param.8) | copy-start | bytes 98308
  18.7 6.9 %collective-permute-start.1 = (f32[2,2,34,256]{3,1,2,0:T(2,128)S(1)}, f32[2,2,34,256]{3,1,2,0:T(2,128)S(1)}, u32[]{:S(2)}, u32[]{:S(2)}) collective-permute-start(f32[2,2,34,256]{3,1,2,0:T(2,128)S(1)} %dynamic-slice_bitcast_fusion), channel_id=1, source_target_pairs={{0,4},{2,6},{4,0},{6,2},{8,12},{10,14},{12,8},{14,10},{16,20},{18,... | collective-permute-start | bytes 417800 | tf_op jit(solution)/shard_map/ppermute | solution.py:148
  25.8 1.9 %copy-start.1 = (f32[3,2,16]{2,1,0:T(2,128)S(1)}, f32[3,2,16]{2,1,0:T(2,128)}, u32[]{:S(2)}) copy-start(f32[3,2,16]{2,1,0:T(2,128)} %param.13) | copy-start | bytes 1156
  25.9 4.4 %collective-permute-start.2 = (f32[2,34,256]{2,0,1:T(2,128)S(1)}, f32[2,34,256]{2,0,1:T(2,128)S(1)}, u32[]{:S(2)}, u32[]{:S(2)}) collective-permute-start(f32[2,34,256]{2,0,1:T(2,128)S(1)} %bitcast.98), channel_id=1, source_target_pairs={{0,8},{2,10},{4,12},{6,14},{8,0},{10,2},{12,4},{14,6},{16,24},{18,... | collective-permute-start | bytes 208904 | tf_op jit(solution)/shard_map/ppermute | solution.py:148
  30.4 5.0 %collective-permute-start.3 = (f32[34,256]{1,0:T(8,128)S(1)}, f32[34,256]{1,0:T(8,128)S(1)}, u32[]{:S(2)}, u32[]{:S(2)}) collective-permute-start(f32[34,256]{1,0:T(8,128)S(1)} %bitcast.99), channel_id=1, source_target_pairs={{0,16},{2,18},{4,20},{6,22},{8,24},{10,26},{12,28},{14,30},{16,0},... | collective-permute-start | bytes 104456 | tf_op jit(solution)/shard_map/ppermute | solution.py:148
  35.4 1.8 %copy-start = (f32[2,17,256]{2,1,0:T(8,128)}, f32[2,17,256]{2,1,0:T(8,128)S(1)}, u32[]{:S(2)}) copy-start(f32[2,17,256]{2,1,0:T(8,128)S(1)} %reshape.121) | copy-start | bytes 104452
  35.4 3.7 %collective-permute-start.4 = (f32[2,4,256]{2,1,0:T(4,128)S(1)}, f32[2,4,256]{2,1,0:T(4,128)S(1)}, u32[]{:S(2)}, u32[]{:S(2)}) collective-permute-start(f32[2,4,256]{2,1,0:T(4,128)S(1)} %fusion.8), channel_id=1, source_target_pairs={{0,1},{1,0},{2,3},{3,2},{4,5},{5,4},{6,7},{7,6},{8,9},{9,8},{10,11... | collective-permute-start | bytes 24584 | tf_op jit(solution)/shard_map/ppermute | solution.py:192
  39.2 0.8 %slice-start = ((f32[2,17,256]{2,1,0:T(8,128)}), f32[2,16,256]{2,1,0:T(8,128)S(1)}, s32[]{:S(2)}) async-start(f32[2,17,256]{2,1,0:T(8,128)} %copy-done), calls=%async_computation | async-start | bytes 65536 | tf_op jit(solution)/shard_map/slice | solution.py:199
  40.7 4.8 %collective-permute-start.5 = (f32[32,256]{1,0:T(8,128)S(1)}, f32[32,256]{1,0:T(8,128)S(1)}, u32[]{:S(2)}, u32[]{:S(2)}) collective-permute-start(f32[32,256]{1,0:T(8,128)S(1)} %bitcast.97), channel_id=1, source_target_pairs={{0,16},{2,18},{4,20},{6,22},{8,24},{10,26},{12,28},{14,30},{16,0},... | collective-permute-start | bytes 98312 | tf_op jit(solution)/shard_map/ppermute | solution.py:159
  45.5 4.3 %collective-permute-start.6 = (f32[2,32,256]{2,1,0:T(8,128)S(1)}, f32[2,32,256]{2,1,0:T(8,128)S(1)}, u32[]{:S(2)}, u32[]{:S(2)}) collective-permute-start(f32[2,32,256]{2,1,0:T(8,128)S(1)} %pad_maximum_fusion.3), channel_id=1, source_target_pairs={{0,8},{2,10},{4,12},{6,14},{8,0},{10,2},{12,4},{14,6},{16,24},{18,... | collective-permute-start | bytes 196616 | tf_op jit(solution)/shard_map/ppermute | solution.py:159
  49.9 5.0 %collective-permute-start.7 = (f32[2,2,32,256]{3,2,1,0:T(8,128)S(1)}, f32[2,2,32,256]{3,2,1,0:T(8,128)S(1)}, u32[]{:S(2)}, u32[]{:S(2)}) collective-permute-start(f32[2,2,32,256]{3,2,1,0:T(8,128)S(1)} %pad_maximum_fusion.2), channel_id=1, source_target_pairs={{0,4},{2,6},{4,0},{6,2},{8,12},{10,14},{12,8},{14,10},{16,20},{18,... | collective-permute-start | bytes 393224 | tf_op jit(solution)/shard_map/ppermute | solution.py:159
  55.0 5.0 %collective-permute-start.8 = (f32[2,2,2,32,256]{4,3,2,1,0:T(8,128)S(1)}, f32[2,2,2,32,256]{4,3,2,1,0:T(8,128)S(1)}, u32[]{:S(2)}, u32[]{:S(2)}) collective-permute-start(f32[2,2,2,32,256]{4,3,2,1,0:T(8,128)S(1)} %pad_maximum_fusion.1), channel_id=1, source_target_pairs={{0,2},{2,0},{4,6},{6,4},{8,10},{10,8},{12,14},{14,12},{16,18},{18,... | collective-permute-start | bytes 786440 | tf_op jit(solution)/shard_map/ppermute | solution.py:159

commit v14 on v12

--- a/solution.py
+++ b/solution.py
@@ -66,7 +66,7 @@
             axis=0,
         )
         ext = jnp.concatenate([summed, jnp.zeros((height, detector_width - band), jnp.float32)], axis=1)
-        placed.append(pltpu.roll(ext, start_ref[v, 0], 1))
+        placed.append(pltpu.roll(ext, start_ref[v], 1))
     joined = jnp.concatenate(placed, axis=0)
     for k in range(chunks):
         out_ref[k] = joined[:, k * shard_width : (k + 1) * shard_width]
@@ -88,7 +88,7 @@
             bytes_accessed=4 * (volume.size + 3 * amplitude.size),
         ),
         interpret=INTERPRET,
-    )(band_start, volume, amplitude, column_offset, column_width)
+    )(band_start.reshape(-1), volume, amplitude, column_offset, column_width)
 
 
 def _backward_kernel(back_ref, vol_ref, amp_ref, off_ref, wid_ref, rw_ref, out_ref, split_ref):

time: 70.5 us -> 69.3 us (0.983)
  local copies, waits for them, and re-layouts: 4.62 us -> 3.33 us
    unnamed x14 -> x13, local copies, waits for them, and re-layouts: 1.51 us -> 0.22 us
where the time goes in v14:
time: 69.3 us; the launch traced here: 68.9 us
  Pallas kernels  23 us (33%)
  waiting for transfers between devices  18.6 us (27%)
  starting transfers between devices  16.5 us (24%)
  between operations  4.75 us (7%)
  local copies, waits for them, and re-layouts  3.33 us (5%)
  other arithmetic  2.71 us (4%)
    pallas_call x1, Pallas kernels, forward_band(): pl.pallas_call(_forward_kernel, out_shape=jax.ShapeDtypeStruct((chunks, v...  13.4 us
    pallas_call x1, Pallas kernels, backward_update(): pl.pallas_call(_backward_kernel, out_shape=jax.ShapeDtypeStruct(volume.sh...  9.65 us
    ppermute x4, waiting for transfers between devices, reduce_scatter_xy(): y = keep + lax.ppermute(send, 'xy', [(i, i ^ 1 << j) for i in range(count)])  8.52 us
    ppermute x4, waiting for transfers between devices, all_gather_xy(): other = lax.ppermute(y, 'xy', [(i, i ^ 1 << j) for i in range(count)])  7.71 us
    ppermute x4, starting transfers between devices, reduce_scatter_xy(): y = keep + lax.ppermute(send, 'xy', [(i, i ^ 1 << j) for i in range(count)])  6.4 us
    ppermute x4, starting transfers between devices, all_gather_xy(): other = lax.ppermute(y, 'xy', [(i, i ^ 1 << j) for i in range(count)])  5.92 us
    ppermute x2, starting transfers between devices, exchange(): lax.ppermute(jnp.where(gz_index == 0, upward, downward), 'gz', [(0, 1), (...  4.16 us
    ppermute x2, waiting for transfers between devices, exchange(): lax.ppermute(jnp.where(gz_index == 0, upward, downward), 'gz', [(0, 1), (...  2.37 us
  transfers between devices with their start and end apart: 10, of which 7 were waited for; matrix products, arithmetic and copies ran while one was open for 4% of the time, Pallas kernels for 0%

profile of v14, /device:TPU:0, one launch (start us, length us, event | category | flops | bytes accessed | tf_op | source)
XLA Modules:
  0.0 68.9 jit_solution(13668979816772403062)
XLA Ops:
  0.6 13.4 %shard_map.86 = f32[16,34,256]{2,1,0:T(8,128)} custom-call(s32[2]{0:T(128)} %bitcast.100, f32[16,16384]{1,0:T(8,128)} %vol_ref.3, f32[2,16384]{1,0:T(2,128)} %amp_ref.3, s32[2,16384]{1,0:T(2,128)} %off_ref.3, s32[2,16384]{1,0:T(2,128)} %wid_ref.3), custom_call_target="tpu_custom_call" | custom-call | flops 1610612736 | bytes 1441792 | tf_op jit(solution)/shard_map/pallas_call | solution.py:80
  14.0 1.1 %constant_dynamic-slice_fusion.5 = (f32[2,2,2,1,34,256]{5,4,3,2,1,0:T(8,128)S(1)}, f32[2,2,2,1,34,256]{5,4,3,2,1,0:T(8,128)S(1)}) fusion(f32[2,2,2,2,34,256]{5,4,3,2,1,0:T(8,128)} %bitcast.90, s32[]{:T(128)S(6)} %select_n.148, s32[]{:T(128)S(6)} %select_n.149), kind=kLoop, calls=%fused_computation.56 | loop fusion | bytes 1114120 | tf_op jit(solution)/shard_map/jit(dynamic_index_in_dim)/dynamic_slice | solution.py:146
  15.1 0.2 copy.118
  15.4 0.0 copy-start.1
  15.4 0.0 copy-start.2
  15.4 0.5 collective-permute-start.1
  15.9 0.1 copy-done.1
  16.0 0.1 slice_bitcast_fusion.3
  16.1 0.1 reshape.123
  16.2 0.1 reshape.124
  16.3 3.0 %collective-permute-start = (f32[2,2,256]{2,0,1:T(2,128)S(1)}, f32[2,2,256]{2,0,1:T(2,128)S(1)}, u32[]{:S(2)}, u32[]{:S(2)}) collective-permute-start(f32[2,2,256]{2,0,1:T(2,128)S(1)} %fusion.8), channel_id=1, source_target_pairs={{0,1},{1,0},{2,3},{3,2},{4,5},{5,4},{6,7},{7,6},{8,9},{9,8},{10,11... | collective-permute-start | bytes 12296 | tf_op jit(solution)/shard_map/ppermute | solution.py:192
  19.3 0.3 bitcast_add_fusion
  19.7 1.6 %collective-permute-start.2 = (f32[2,2,34,256]{3,1,2,0:T(2,128)S(1)}, f32[2,2,34,256]{3,1,2,0:T(2,128)S(1)}, u32[]{:S(2)}, u32[]{:S(2)}) collective-permute-start(f32[2,2,34,256]{3,1,2,0:T(2,128)S(1)} %dynamic-slice_bitcast_fusion), channel_id=1, source_target_pairs={{0,4},{2,6},{4,0},{6,2},{8,12},{10,14},{12,8},{14,10},{16,20},{18,... | collective-permute-start | bytes 417800 | tf_op jit(solution)/shard_map/ppermute | solution.py:148
  21.3 3.7 %collective-permute-done.2 = f32[2,2,34,256]{3,1,2,0:T(2,128)S(1)} collective-permute-done((f32[2,2,34,256]{3,1,2,0:T(2,128)S(1)}, f32[2,2,34,256]{3,1,2,0:T(2,128)S(1)}, u32[]{:S(2)}, u32[]{:S(2)}) %collective-permute-start.2) | collective-permute-done | bytes 139296 | tf_op jit(solution)/shard_map/ppermute | solution.py:148
  24.9 0.1 bitcast_add_fusion.1
  25.0 0.1 constant_dynamic-slice_fusion.3
  25.2 1.6 %collective-permute-start.3 = (f32[2,34,256]{2,0,1:T(2,128)S(1)}, f32[2,34,256]{2,0,1:T(2,128)S(1)}, u32[]{:S(2)}, u32[]{:S(2)}) collective-permute-start(f32[2,34,256]{2,0,1:T(2,128)S(1)} %bitcast.95), channel_id=1, source_target_pairs={{0,8},{2,10},{4,12},{6,14},{8,0},{10,2},{12,4},{14,6},{16,24},{18,... | collective-permute-start | bytes 208904 | tf_op jit(solution)/shard_map/ppermute | solution.py:148
  26.9 2.7 %collective-permute-done.3 = f32[2,34,256]{2,0,1:T(2,128)S(1)} collective-permute-done((f32[2,34,256]{2,0,1:T(2,128)S(1)}, f32[2,34,256]{2,0,1:T(2,128)S(1)}, u32[]{:S(2)}, u32[]{:S(2)}) %collective-permute-start.3) | collective-permute-done | bytes 69664 | tf_op jit(solution)/shard_map/ppermute | solution.py:148
  29.6 0.1 bitcast_add_fusion.2
  29.6 0.1 constant_dynamic-slice_fusion.1
  29.7 2.7 %collective-permute-start.4 = (f32[34,256]{1,0:T(8,128)S(1)}, f32[34,256]{1,0:T(8,128)S(1)}, u32[]{:S(2)}, u32[]{:S(2)}) collective-permute-start(f32[34,256]{1,0:T(8,128)S(1)} %bitcast.96), channel_id=1, source_target_pairs={{0,16},{2,18},{4,20},{6,22},{8,24},{10,26},{12,28},{14,30},{16,0},... | collective-permute-start | bytes 104456 | tf_op jit(solution)/shard_map/ppermute | solution.py:148
  32.4 0.1 reshape_squeeze.6
  32.5 0.1 reshape_squeeze.7
  32.6 2.1 %collective-permute-done.4 = f32[34,256]{1,0:T(8,128)S(1)} collective-permute-done((f32[34,256]{1,0:T(8,128)S(1)}, f32[34,256]{1,0:T(8,128)S(1)}, u32[]{:S(2)}, u32[]{:S(2)}) %collective-permute-start.4) | collective-permute-done | bytes 34848 | tf_op jit(solution)/shard_map/ppermute | solution.py:148
  34.7 0.0 copy-start
  34.7 1.2 %collective-permute-start.5 = (f32[2,2,256]{2,0,1:T(2,128)S(1)}, f32[2,2,256]{2,0,1:T(2,128)S(1)}, u32[]{:S(2)}, u32[]{:S(2)}) collective-permute-start(f32[2,2,256]{2,0,1:T(2,128)S(1)} %copy_select_fusion), channel_id=1, source_target_pairs={{0,1},{1,0},{2,3},{3,2},{4,5},{5,4},{6,7},{7,6},{8,9},{9,8},{10,11... | collective-permute-start | bytes 12296 | tf_op jit(solution)/shard_map/ppermute | solution.py:192
  35.9 0.1 add_add_fusion
  36.0 0.0 slice-start
  36.0 2.4 %collective-permute-done.5 = f32[2,2,256]{2,0,1:T(2,128)S(1)} collective-permute-done((f32[2,2,256]{2,0,1:T(2,128)S(1)}, f32[2,2,256]{2,0,1:T(2,128)S(1)}, u32[]{:S(2)}, u32[]{:S(2)}) %collective-permute-start.5) | collective-permute-done | bytes 4128 | tf_op jit(solution)/shard_map/ppermute | solution.py:192
  38.4 0.1 fusion.5
  38.6 0.6 fusion.6
  39.2 2.6 %collective-permute-start.6 = (f32[32,256]{1,0:T(8,128)S(1)}, f32[32,256]{1,0:T(8,128)S(1)}, u32[]{:S(2)}, u32[]{:S(2)}) collective-permute-start(f32[32,256]{1,0:T(8,128)S(1)} %bitcast.94), channel_id=1, source_target_pairs={{0,16},{2,18},{4,20},{6,22},{8,24},{10,26},{12,28},{14,30},{16,0},... | collective-permute-start | bytes 98312 | tf_op jit(solution)/shard_map/ppermute | solution.py:159
  41.8 2.2 %collective-permute-done.6 = f32[32,256]{1,0:T(8,128)S(1)} collective-permute-done((f32[32,256]{1,0:T(8,128)S(1)}, f32[32,256]{1,0:T(8,128)S(1)}, u32[]{:S(2)}, u32[]{:S(2)}) %collective-permute-start.6) | collective-permute-done | bytes 32800 | tf_op jit(solution)/shard_map/ppermute | solution.py:159
  44.0 1.6 %collective-permute-start.7 = (f32[2,32,256]{2,1,0:T(8,128)S(1)}, f32[2,32,256]{2,1,0:T(8,128)S(1)}, u32[]{:S(2)}, u32[]{:S(2)}) collective-permute-start(f32[2,32,256]{2,1,0:T(8,128)S(1)} %pad_maximum_fusion.3), channel_id=1, source_target_pairs={{0,8},{2,10},{4,12},{6,14},{8,0},{10,2},{12,4},{14,6},{16,24},{18,... | collective-permute-start | bytes 196616 | tf_op jit(solution)/shard_map/ppermute | solution.py:159
  45.7 2.7 %collective-permute-done.7 = f32[2,32,256]{2,1,0:T(8,128)S(1)} collective-permute-done((f32[2,32,256]{2,1,0:T(8,128)S(1)}, f32[2,32,256]{2,1,0:T(8,128)S(1)}, u32[]{:S(2)}, u32[]{:S(2)}) %collective-permute-start.7) | collective-permute-done | bytes 65568 | tf_op jit(solution)/shard_map/ppermute | solution.py:159
  48.4 0.0 copy-start.3
  48.4 1.6 %collective-permute-start.8 = (f32[2,2,32,256]{3,2,0,1:T(8,128)S(1)}, f32[2,2,32,256]{3,2,0,1:T(8,128)S(1)}, u32[]{:S(2)}, u32[]{:S(2)}) collective-permute-start(f32[2,2,32,256]{3,2,0,1:T(8,128)S(1)} %pad_maximum_fusion.2), channel_id=1, source_target_pairs={{0,4},{2,6},{4,0},{6,2},{8,12},{10,14},{12,8},{14,10},{16,20},{18,... | collective-permute-start | bytes 393224 | tf_op jit(solution)/shard_map/ppermute | solution.py:159
  50.0 0.6 fusion.19
  50.6 2.8 %collective-permute-done.8 = f32[2,2,32,256]{3,2,0,1:T(8,128)S(1)} collective-permute-done((f32[2,2,32,256]{3,2,0,1:T(8,128)S(1)}, f32[2,2,32,256]{3,2,0,1:T(8,128)S(1)}, u32[]{:S(2)}, u32[]{:S(2)}) %collective-permute-start.8) | collective-permute-done | bytes 131104 | tf_op jit(solution)/shard_map/ppermute | solution.py:159
  53.5 0.1 collective-permute-start.9
  56.1 0.1 copy.97
  56.2 0.1 copy.98
  56.3 0.1 copy.99
  57.6 0.7 select_add_fusion.rw_ref
  58.3 0.0 collective-permute-done.9
  58.5 0.1 dynamic-slice_bitcast_fusion.1
  58.6 0.6 pad_maximum_fusion.4.back_ref
  59.3 9.7 %shard_map.87 = f32[16,16384]{1,0:T(8,128)} custom-call(f32[2,16,512]{2,1,0:T(8,128)} %pad_maximum_fusion.4.back_ref, f32[16,16384]{1,0:T(8,128)} %vol_ref.3, f32[2,16384]{1,0:T(2,128)} %amp_ref.3, s32[2,16384]{1,0:T(2,128)} %off_ref.3, s32[2,16384]{1,0:T(2,128)} %wid_ref.3, f32[2,16,1]{2,1,0:T(8,128)} %select_add_fusion.rw_ref), custom_call_target="tpu_custom_call" | custom-call | tf_op jit(solution)/shard_map/pallas_call | solution.py:124
  (48 shorter events, 0.5 us)
Async XLA Ops:
  15.4 0.7 copy-start.1
  15.4 0.9 %copy-start.2 = (f32[2,16,256]{2,1,0:T(8,128)S(1)}, f32[2,16,256]{2,1,0:T(8,128)}, u32[]{:S(2)}) copy-start(f32[2,16,256]{2,1,0:T(8,128)} %param.8) | copy-start | bytes 98308
  15.4 4.0 %collective-permute-start.1 = (f32[2,2,2,34,256]{4,1,3,0,2:T(2,128)S(1)}, f32[2,2,2,34,256]{4,1,3,0,2:T(2,128)S(1)}, u32[]{:S(2)}, u32[]{:S(2)}) collective-permute-start(f32[2,2,2,34,256]{4,1,3,0,2:T(2,128)S(1)} %bitcast.93), channel_id=1, source_target_pairs={{0,2},{2,0},{4,6},{6,4},{8,10},{10,8},{12,14},{14,12},{16,18},{18,... | collective-permute-start | bytes 835592 | tf_op jit(solution)/shard_map/ppermute | solution.py:148
  16.3 16.0 %collective-permute-start = (f32[2,2,256]{2,0,1:T(2,128)S(1)}, f32[2,2,256]{2,0,1:T(2,128)S(1)}, u32[]{:S(2)}, u32[]{:S(2)}) collective-permute-start(f32[2,2,256]{2,0,1:T(2,128)S(1)} %fusion.8), channel_id=1, source_target_pairs={{0,1},{1,0},{2,3},{3,2},{4,5},{5,4},{6,7},{7,6},{8,9},{9,8},{10,11... | collective-permute-start | bytes 12296 | tf_op jit(solution)/shard_map/ppermute | solution.py:192
  19.7 5.3 %collective-permute-start.2 = (f32[2,2,34,256]{3,1,2,0:T(2,128)S(1)}, f32[2,2,34,256]{3,1,2,0:T(2,128)S(1)}, u32[]{:S(2)}, u32[]{:S(2)}) collective-permute-start(f32[2,2,34,256]{3,1,2,0:T(2,128)S(1)} %dynamic-slice_bitcast_fusion), channel_id=1, source_target_pairs={{0,4},{2,6},{4,0},{6,2},{8,12},{10,14},{12,8},{14,10},{16,20},{18,... | collective-permute-start | bytes 417800 | tf_op jit(solution)/shard_map/ppermute | solution.py:148
  25.2 4.4 %collective-permute-start.3 = (f32[2,34,256]{2,0,1:T(2,128)S(1)}, f32[2,34,256]{2,0,1:T(2,128)S(1)}, u32[]{:S(2)}, u32[]{:S(2)}) collective-permute-start(f32[2,34,256]{2,0,1:T(2,128)S(1)} %bitcast.95), channel_id=1, source_target_pairs={{0,8},{2,10},{4,12},{6,14},{8,0},{10,2},{12,4},{14,6},{16,24},{18,... | collective-permute-start | bytes 208904 | tf_op jit(solution)/shard_map/ppermute | solution.py:148
  29.7 5.0 %collective-permute-start.4 = (f32[34,256]{1,0:T(8,128)S(1)}, f32[34,256]{1,0:T(8,128)S(1)}, u32[]{:S(2)}, u32[]{:S(2)}) collective-permute-start(f32[34,256]{1,0:T(8,128)S(1)} %bitcast.96), channel_id=1, source_target_pairs={{0,16},{2,18},{4,20},{6,22},{8,24},{10,26},{12,28},{14,30},{16,0},... | collective-permute-start | bytes 104456 | tf_op jit(solution)/shard_map/ppermute | solution.py:148
  34.7 1.3 %copy-start = (f32[2,17,256]{2,1,0:T(8,128)}, f32[2,17,256]{2,1,0:T(8,128)S(1)}, u32[]{:S(2)}) copy-start(f32[2,17,256]{2,1,0:T(8,128)S(1)} %reshape.127) | copy-start | bytes 104452
  34.7 3.7 %collective-permute-start.5 = (f32[2,2,256]{2,0,1:T(2,128)S(1)}, f32[2,2,256]{2,0,1:T(2,128)S(1)}, u32[]{:S(2)}, u32[]{:S(2)}) collective-permute-start(f32[2,2,256]{2,0,1:T(2,128)S(1)} %copy_select_fusion), channel_id=1, source_target_pairs={{0,1},{1,0},{2,3},{3,2},{4,5},{5,4},{6,7},{7,6},{8,9},{9,8},{10,11... | collective-permute-start | bytes 12296 | tf_op jit(solution)/shard_map/ppermute | solution.py:192
  36.0 2.4 %slice-start = ((f32[2,17,256]{2,1,0:T(8,128)}), f32[2,16,256]{2,1,0:T(8,128)S(1)}, s32[]{:S(2)}) async-start(f32[2,17,256]{2,1,0:T(8,128)} %copy-done), calls=%async_computation | async-start | bytes 65536 | tf_op jit(solution)/shard_map/slice | solution.py:207
  39.2 4.8 %collective-permute-start.6 = (f32[32,256]{1,0:T(8,128)S(1)}, f32[32,256]{1,0:T(8,128)S(1)}, u32[]{:S(2)}, u32[]{:S(2)}) collective-permute-start(f32[32,256]{1,0:T(8,128)S(1)} %bitcast.94), channel_id=1, source_target_pairs={{0,16},{2,18},{4,20},{6,22},{8,24},{10,26},{12,28},{14,30},{16,0},... | collective-permute-start | bytes 98312 | tf_op jit(solution)/shard_map/ppermute | solution.py:159
  44.0 4.3 %collective-permute-start.7 = (f32[2,32,256]{2,1,0:T(8,128)S(1)}, f32[2,32,256]{2,1,0:T(8,128)S(1)}, u32[]{:S(2)}, u32[]{:S(2)}) collective-permute-start(f32[2,32,256]{2,1,0:T(8,128)S(1)} %pad_maximum_fusion.3), channel_id=1, source_target_pairs={{0,8},{2,10},{4,12},{6,14},{8,0},{10,2},{12,4},{14,6},{16,24},{18,... | collective-permute-start | bytes 196616 | tf_op jit(solution)/shard_map/ppermute | solution.py:159
  48.4 1.6 %copy-start.3 = (s32[2,1]{0,1:T(1,128)S(1)}, s32[2,1]{0,1:T(1,128)}, u32[]{:S(2)}) copy-start(s32[2,1]{0,1:T(1,128)} %param.9) | copy-start | bytes 28
  48.4 5.0 %collective-permute-start.8 = (f32[2,2,32,256]{3,2,0,1:T(8,128)S(1)}, f32[2,2,32,256]{3,2,0,1:T(8,128)S(1)}, u32[]{:S(2)}, u32[]{:S(2)}) collective-permute-start(f32[2,2,32,256]{3,2,0,1:T(8,128)S(1)} %pad_maximum_fusion.2), channel_id=1, source_target_pairs={{0,4},{2,6},{4,0},{6,2},{8,12},{10,14},{12,8},{14,10},{16,20},{18,... | collective-permute-start | bytes 393224 | tf_op jit(solution)/shard_map/ppermute | solution.py:159
  53.5 4.8 %collective-permute-start.9 = (f32[2,2,2,32,256]{4,3,0,1,2:T(8,128)S(1)}, f32[2,2,2,32,256]{4,3,0,1,2:T(8,128)S(1)}, u32[]{:S(2)}, u32[]{:S(2)}) collective-permute-start(f32[2,2,2,32,256]{4,3,0,1,2:T(8,128)S(1)} %pad_maximum_fusion.1), channel_id=1, source_target_pairs={{0,2},{2,0},{4,6},{6,4},{8,10},{10,8},{12,14},{14,12},{16,18},{18,... | collective-permute-start | bytes 786440 | tf_op jit(solution)/shard_map/ppermute | solution.py:159

commit v15 on v14

--- a/solution.py
+++ b/solution.py
@@ -27,7 +27,8 @@
     slab_rows, columns = vol_ref.shape
     view_count = amp_ref.shape[0]
     band = acc_ref.shape[2]
-    chunks, _, shard_width = out_ref.shape
+    _, half, _, shard_width = out_ref.shape
+    chunks = 2 * half
     detector_width = chunks * shard_width
     acc_ref[...] = jnp.zeros(acc_ref.shape, jnp.float32)
     row = lax.broadcasted_iota(jnp.int32, (slab_rows, CHUNK), 0)
@@ -68,8 +69,9 @@
         ext = jnp.concatenate([summed, jnp.zeros((height, detector_width - band), jnp.float32)], axis=1)
         placed.append(pltpu.roll(ext, start_ref[v], 1))
     joined = jnp.concatenate(placed, axis=0)
+    parity = lax.axis_index("xy") & 1
     for k in range(chunks):
-        out_ref[k] = joined[:, k * shard_width : (k + 1) * shard_width]
+        out_ref[(k % 2) ^ parity, k // 2] = joined[:, k * shard_width : (k + 1) * shard_width]
 
 
 def forward_band(volume, amplitude, column_offset, column_width, band_start, chunks, shard_width):
@@ -79,7 +81,7 @@
     vmem = pl.BlockSpec(memory_space=pltpu.VMEM)
     return pl.pallas_call(
         _forward_kernel,
-        out_shape=jax.ShapeDtypeStruct((chunks, view_count * (slab_rows + 1), shard_width), jnp.float32),
+        out_shape=jax.ShapeDtypeStruct((2, chunks // 2, view_count * (slab_rows + 1), shard_width), jnp.float32),
         in_specs=[smem, vmem, vmem, vmem, vmem],
         scratch_shapes=[pltpu.VMEM((view_count, 3 * slab_rows, B), jnp.float32)],
         cost_estimate=pl.CostEstimate(
@@ -135,12 +137,13 @@
     return bits
 
 
-def reduce_scatter_xy(x, count):
-    _, rows, width = x.shape
+def reduce_scatter_xy(halves, count):
+    _, _, rows, width = halves.shape
     bits = _bit_count(count)
     idx = lax.axis_index("xy")
-    y = x.reshape((2,) * bits + (rows, width))
-    for j in range(bits):
+    y = halves[0] + lax.ppermute(halves[1], "xy", [(i, i ^ 1) for i in range(count)])
+    y = y.reshape((2,) * (bits - 1) + (rows, width))
+    for j in range(1, bits):
         axis = bits - 1 - j
         bit = (idx >> j) & 1
         keep = lax.dynamic_index_in_dim(y, bit, axis, keepdims=False)

time: 69.3 us -> 69 us (level)
    dynamic_slice x5 -> x0, local copies, waits for them, and re-layouts: 1.56 us -> none  [the longest x3 1.31 us: reduce_scatter_xy(): keep = lax.dynamic_index_in_dim(y, bit, axis, keepdims=False)]
    squeeze x0 -> x1, local copies, waits for them, and re-layouts: none -> 1.07 us  [reduce_scatter_xy(): halves[1]]
    ppermute x4 -> x3, waiting for transfers between devices: 8.52 us -> 9.18 us  [reduce_scatter_xy(): y = keep + lax.ppermute(send, 'xy', [(i, i ^ 1 << j) for i in range(count)])]
    ppermute x4 -> x3, starting transfers between devices: 6.4 us -> 5.88 us  [reduce_scatter_xy(): y = keep + lax.ppermute(send, 'xy', [(i, i ^ 1 << j) for i in range(count)])]
  transfers between devices with their start and end apart: 10 -> 10, of which waited for: 7 -> 7; matrix products, arithmetic and copies ran while one was open for 4% -> 3% of each run, Pallas kernels for 0% -> 0%
where the time goes in v15:
time: 69 us; the launch traced here: 68.7 us
  Pallas kernels  23.1 us (33%)
  waiting for transfers between devices  19.2 us (28%)
  starting transfers between devices  16.5 us (24%)
  between operations  4.61 us (7%)
  local copies, waits for them, and re-layouts  2.82 us (4%)
  other arithmetic  2.39 us (3%)
    pallas_call x1, Pallas kernels, forward_band(): pl.pallas_call(_forward_kernel, out_shape=jax.ShapeDtypeStruct((2, chunks...  13.4 us
    pallas_call x1, Pallas kernels, backward_update(): pl.pallas_call(_backward_kernel, out_shape=jax.ShapeDtypeStruct(volume.sh...  9.65 us
    ppermute x3, waiting for transfers between devices, reduce_scatter_xy(): y = keep + lax.ppermute(send, 'xy', [(i, i ^ 1 << j) for i in range(count)])  9.18 us
    ppermute x4, waiting for transfers between devices, all_gather_xy(): other = lax.ppermute(y, 'xy', [(i, i ^ 1 << j) for i in range(count)])  7.76 us
    ppermute x4, starting transfers between devices, all_gather_xy(): other = lax.ppermute(y, 'xy', [(i, i ^ 1 << j) for i in range(count)])  5.92 us
    ppermute x3, starting transfers between devices, reduce_scatter_xy(): y = keep + lax.ppermute(send, 'xy', [(i, i ^ 1 << j) for i in range(count)])  5.88 us
    ppermute x2, starting transfers between devices, exchange(): lax.ppermute(jnp.where(gz_index == 0, upward, downward), 'gz', [(0, 1), (...  4.23 us
    ppermute x2, waiting for transfers between devices, exchange(): lax.ppermute(jnp.where(gz_index == 0, upward, downward), 'gz', [(0, 1), (...  2.3 us
  transfers between devices with their start and end apart: 10, of which 7 were waited for; matrix products, arithmetic and copies ran while one was open for 3% of the time, Pallas kernels for 0%

profile of v15, /device:TPU:0, one launch (start us, length us, event | category | flops | bytes accessed | tf_op | source)
XLA Modules:
  0.0 68.7 jit_solution(1308820948761841102)
XLA Ops:
  0.6 13.4 %shard_map.86 = f32[2,8,34,256]{3,2,1,0:T(8,128)} custom-call(s32[2]{0:T(128)} %bitcast.97, f32[16,16384]{1,0:T(8,128)} %vol_ref.3, f32[2,16384]{1,0:T(2,128)} %amp_ref.3, s32[2,16384]{1,0:T(2,128)} %off_ref.3, s32[2,16384]{1,0:T(2,128)} %wid_ref.3), custom_call_target="tpu_custom_call" | custom-call | flops 1610612736 | bytes 1441792 | tf_op jit(solution)/shard_map/pallas_call | solution.py:82
  14.0 1.1 %slice_bitcast_fusion = f32[8,34,256]{2,1,0:T(8,128)S(1)} fusion(f32[2,8,34,256]{3,2,1,0:T(8,128)} %shard_map.86), kind=kLoop, calls=%fused_computation.1 | loop fusion | bytes 557056 | tf_op jit(solution)/shard_map/squeeze | solution.py:144
  15.1 0.0 copy-start.2
  15.1 0.0 copy-start.3
  15.1 0.5 collective-permute-start.1
  15.7 0.1 copy-done.2
  15.8 0.1 slice_bitcast_fusion.5
  15.9 0.1 reshape.124
  16.0 0.1 reshape.123
  16.0 0.0 copy-done.3
  16.1 3.0 %collective-permute-start = (f32[2,2,256]{2,0,1:T(2,128)S(1)}, f32[2,2,256]{2,0,1:T(2,128)S(1)}, u32[]{:S(2)}, u32[]{:S(2)}) collective-permute-start(f32[2,2,256]{2,0,1:T(2,128)S(1)} %fusion.9), channel_id=1, source_target_pairs={{0,1},{1,0},{2,3},{3,2},{4,5},{5,4},{6,7},{7,6},{8,9},{9,8},{10,11... | collective-permute-start | bytes 12296 | tf_op jit(solution)/shard_map/ppermute | solution.py:195
  19.1 0.0 collective-permute-done.1
  19.1 0.0 copy-done
  19.2 1.6 %collective-permute-start.2 = (f32[2,2,34,256]{3,2,1,0:T(8,128)S(1)}, f32[2,2,34,256]{3,2,1,0:T(8,128)S(1)}, u32[]{:S(2)}, u32[]{:S(2)}) collective-permute-start(f32[2,2,34,256]{3,2,1,0:T(8,128)S(1)} %dynamic-slice_bitcast_fusion), channel_id=1, source_target_pairs={{0,4},{2,6},{4,0},{6,2},{8,12},{10,14},{12,8},{14,10},{16,20},{18,... | collective-permute-start | bytes 417800 | tf_op jit(solution)/shard_map/ppermute | solution.py:151
  20.8 4.2 %collective-permute-done.2 = f32[2,2,34,256]{3,2,1,0:T(8,128)S(1)} collective-permute-done((f32[2,2,34,256]{3,2,1,0:T(8,128)S(1)}, f32[2,2,34,256]{3,2,1,0:T(8,128)S(1)}, u32[]{:S(2)}, u32[]{:S(2)}) %collective-permute-start.2) | collective-permute-done | bytes 139296 | tf_op jit(solution)/shard_map/ppermute | solution.py:151
  25.0 1.6 %collective-permute-start.3 = (f32[2,34,256]{2,1,0:T(8,128)S(1)}, f32[2,34,256]{2,1,0:T(8,128)S(1)}, u32[]{:S(2)}, u32[]{:S(2)}) collective-permute-start(f32[2,34,256]{2,1,0:T(8,128)S(1)} %dynamic-slice_bitcast_fusion.1), channel_id=1, source_target_pairs={{0,8},{2,10},{4,12},{6,14},{8,0},{10,2},{12,4},{14,6},{16,24},{18,... | collective-permute-start | bytes 208904 | tf_op jit(solution)/shard_map/ppermute | solution.py:151
  26.7 2.9 %collective-permute-done.3 = f32[2,34,256]{2,1,0:T(8,128)S(1)} collective-permute-done((f32[2,34,256]{2,1,0:T(8,128)S(1)}, f32[2,34,256]{2,1,0:T(8,128)S(1)}, u32[]{:S(2)}, u32[]{:S(2)}) %collective-permute-start.3) | collective-permute-done | bytes 69664 | tf_op jit(solution)/shard_map/ppermute | solution.py:151
  29.6 2.7 %collective-permute-start.4 = (f32[34,256]{1,0:T(8,128)S(1)}, f32[34,256]{1,0:T(8,128)S(1)}, u32[]{:S(2)}, u32[]{:S(2)}) collective-permute-start(f32[34,256]{1,0:T(8,128)S(1)} %dynamic-slice_bitcast_fusion.2), channel_id=1, source_target_pairs={{0,16},{2,18},{4,20},{6,22},{8,24},{10,26},{12,28},{14,30},{16,0},... | collective-permute-start | bytes 104456 | tf_op jit(solution)/shard_map/ppermute | solution.py:151
  32.2 0.0 collective-permute-done
  32.3 0.1 reshape_squeeze.7
  32.3 0.1 reshape_squeeze.6
  32.4 2.1 %collective-permute-done.4 = f32[34,256]{1,0:T(8,128)S(1)} collective-permute-done((f32[34,256]{1,0:T(8,128)S(1)}, f32[34,256]{1,0:T(8,128)S(1)}, u32[]{:S(2)}, u32[]{:S(2)}) %collective-permute-start.4) | collective-permute-done | bytes 34848 | tf_op jit(solution)/shard_map/ppermute | solution.py:151
  34.6 0.0 copy-start.1
  34.6 1.2 %collective-permute-start.5 = (f32[2,2,256]{2,0,1:T(2,128)S(1)}, f32[2,2,256]{2,0,1:T(2,128)S(1)}, u32[]{:S(2)}, u32[]{:S(2)}) collective-permute-start(f32[2,2,256]{2,0,1:T(2,128)S(1)} %copy_select_fusion), channel_id=1, source_target_pairs={{0,1},{1,0},{2,3},{3,2},{4,5},{5,4},{6,7},{7,6},{8,9},{9,8},{10,11... | collective-permute-start | bytes 12296 | tf_op jit(solution)/shard_map/ppermute | solution.py:195
  35.8 0.1 add_add_fusion
  35.9 0.0 copy-done.1
  36.0 0.0 slice-start
  36.0 2.3 %collective-permute-done.5 = f32[2,2,256]{2,0,1:T(2,128)S(1)} collective-permute-done((f32[2,2,256]{2,0,1:T(2,128)S(1)}, f32[2,2,256]{2,0,1:T(2,128)S(1)}, u32[]{:S(2)}, u32[]{:S(2)}) %collective-permute-start.5) | collective-permute-done | bytes 4128 | tf_op jit(solution)/shard_map/ppermute | solution.py:195
  38.3 0.0 slice-done
  38.3 0.1 fusion.6
  38.4 0.6 fusion.7
  39.0 2.6 %collective-permute-start.6 = (f32[32,256]{1,0:T(8,128)S(1)}, f32[32,256]{1,0:T(8,128)S(1)}, u32[]{:S(2)}, u32[]{:S(2)}) collective-permute-start(f32[32,256]{1,0:T(8,128)S(1)} %bitcast.93), channel_id=1, source_target_pairs={{0,16},{2,18},{4,20},{6,22},{8,24},{10,26},{12,28},{14,30},{16,0},... | collective-permute-start | bytes 98312 | tf_op jit(solution)/shard_map/ppermute | solution.py:162
  41.7 2.2 %collective-permute-done.6 = f32[32,256]{1,0:T(8,128)S(1)} collective-permute-done((f32[32,256]{1,0:T(8,128)S(1)}, f32[32,256]{1,0:T(8,128)S(1)}, u32[]{:S(2)}, u32[]{:S(2)}) %collective-permute-start.6) | collective-permute-done | bytes 32800 | tf_op jit(solution)/shard_map/ppermute | solution.py:162
  43.9 1.6 %collective-permute-start.7 = (f32[2,32,256]{2,1,0:T(8,128)S(1)}, f32[2,32,256]{2,1,0:T(8,128)S(1)}, u32[]{:S(2)}, u32[]{:S(2)}) collective-permute-start(f32[2,32,256]{2,1,0:T(8,128)S(1)} %pad_maximum_fusion.3), channel_id=1, source_target_pairs={{0,8},{2,10},{4,12},{6,14},{8,0},{10,2},{12,4},{14,6},{16,24},{18,... | collective-permute-start | bytes 196616 | tf_op jit(solution)/shard_map/ppermute | solution.py:162
  45.5 2.7 %collective-permute-done.7 = f32[2,32,256]{2,1,0:T(8,128)S(1)} collective-permute-done((f32[2,32,256]{2,1,0:T(8,128)S(1)}, f32[2,32,256]{2,1,0:T(8,128)S(1)}, u32[]{:S(2)}, u32[]{:S(2)}) %collective-permute-start.7) | collective-permute-done | bytes 65568 | tf_op jit(solution)/shard_map/ppermute | solution.py:162
  48.2 0.0 copy-start.4
  48.3 1.6 %collective-permute-start.8 = (f32[2,2,32,256]{3,2,0,1:T(8,128)S(1)}, f32[2,2,32,256]{3,2,0,1:T(8,128)S(1)}, u32[]{:S(2)}, u32[]{:S(2)}) collective-permute-start(f32[2,2,32,256]{3,2,0,1:T(8,128)S(1)} %pad_maximum_fusion.2), channel_id=1, source_target_pairs={{0,4},{2,6},{4,0},{6,2},{8,12},{10,14},{12,8},{14,10},{16,20},{18,... | collective-permute-start | bytes 393224 | tf_op jit(solution)/shard_map/ppermute | solution.py:162
  49.8 0.6 fusion.20
  50.4 2.9 %collective-permute-done.8 = f32[2,2,32,256]{3,2,0,1:T(8,128)S(1)} collective-permute-done((f32[2,2,32,256]{3,2,0,1:T(8,128)S(1)}, f32[2,2,32,256]{3,2,0,1:T(8,128)S(1)}, u32[]{:S(2)}, u32[]{:S(2)}) %collective-permute-start.8) | collective-permute-done | bytes 131104 | tf_op jit(solution)/shard_map/ppermute | solution.py:162
  53.3 0.1 collective-permute-start.9
  55.9 0.1 copy.93
  56.0 0.1 copy.92
  56.1 0.1 copy.91
  57.4 0.7 select_add_fusion.rw_ref
  58.0 0.0 collective-permute-done.9
  58.3 0.1 dynamic-slice_bitcast_fusion.3
  58.4 0.6 pad_maximum_fusion.4.back_ref
  59.0 9.7 %shard_map.87 = f32[16,16384]{1,0:T(8,128)} custom-call(f32[2,16,512]{2,1,0:T(8,128)} %pad_maximum_fusion.4.back_ref, f32[16,16384]{1,0:T(8,128)} %vol_ref.3, f32[2,16384]{1,0:T(2,128)} %amp_ref.3, s32[2,16384]{1,0:T(2,128)} %off_ref.3, s32[2,16384]{1,0:T(2,128)} %wid_ref.3, f32[2,16,1]{2,1,0:T(8,128)} %select_add_fusion.rw_ref), custom_call_target="tpu_custom_call" | custom-call | tf_op jit(solution)/shard_map/pallas_call | solution.py:126
  (47 shorter events, 0.5 us)
Async XLA Ops:
  14.0 5.1 %copy-start = (f32[2,8,34,256]{3,2,1,0:T(8,128)S(1)}, f32[2,8,34,256]{3,2,1,0:T(8,128)}, u32[]{:S(2)}) copy-start(f32[2,8,34,256]{3,2,1,0:T(8,128)} %shard_map.86) | copy-start | bytes 1671172
  15.1 0.7 %copy-start.2 = (f32[3,2,16]{2,1,0:T(2,128)S(1)}, f32[3,2,16]{2,1,0:T(2,128)}, u32[]{:S(2)}) copy-start(f32[3,2,16]{2,1,0:T(2,128)} %param.13) | copy-start | bytes 1156
  15.1 0.9 %copy-start.3 = (f32[2,16,256]{2,1,0:T(8,128)S(1)}, f32[2,16,256]{2,1,0:T(8,128)}, u32[]{:S(2)}) copy-start(f32[2,16,256]{2,1,0:T(8,128)} %param.8) | copy-start | bytes 98308
  15.1 4.0 %collective-permute-start.1 = (f32[8,34,256]{2,1,0:T(8,128)S(1)}, f32[8,34,256]{2,1,0:T(8,128)S(1)}, u32[]{:S(2)}, u32[]{:S(2)}) collective-permute-start(f32[8,34,256]{2,1,0:T(8,128)S(1)} %slice_bitcast_fusion), channel_id=1, source_target_pairs={{0,2},{2,0},{4,6},{6,4},{8,10},{10,8},{12,14},{14,12},{16,18},{18,... | collective-permute-start | bytes 835592 | tf_op jit(solution)/shard_map/ppermute | solution.py:144
  16.1 16.1 %collective-permute-start = (f32[2,2,256]{2,0,1:T(2,128)S(1)}, f32[2,2,256]{2,0,1:T(2,128)S(1)}, u32[]{:S(2)}, u32[]{:S(2)}) collective-permute-start(f32[2,2,256]{2,0,1:T(2,128)S(1)} %fusion.9), channel_id=1, source_target_pairs={{0,1},{1,0},{2,3},{3,2},{4,5},{5,4},{6,7},{7,6},{8,9},{9,8},{10,11... | collective-permute-start | bytes 12296 | tf_op jit(solution)/shard_map/ppermute | solution.py:195
  19.2 5.8 %collective-permute-start.2 = (f32[2,2,34,256]{3,2,1,0:T(8,128)S(1)}, f32[2,2,34,256]{3,2,1,0:T(8,128)S(1)}, u32[]{:S(2)}, u32[]{:S(2)}) collective-permute-start(f32[2,2,34,256]{3,2,1,0:T(8,128)S(1)} %dynamic-slice_bitcast_fusion), channel_id=1, source_target_pairs={{0,4},{2,6},{4,0},{6,2},{8,12},{10,14},{12,8},{14,10},{16,20},{18,... | collective-permute-start | bytes 417800 | tf_op jit(solution)/shard_map/ppermute | solution.py:151
  25.0 4.5 %collective-permute-start.3 = (f32[2,34,256]{2,1,0:T(8,128)S(1)}, f32[2,34,256]{2,1,0:T(8,128)S(1)}, u32[]{:S(2)}, u32[]{:S(2)}) collective-permute-start(f32[2,34,256]{2,1,0:T(8,128)S(1)} %dynamic-slice_bitcast_fusion.1), channel_id=1, source_target_pairs={{0,8},{2,10},{4,12},{6,14},{8,0},{10,2},{12,4},{14,6},{16,24},{18,... | collective-permute-start | bytes 208904 | tf_op jit(solution)/shard_map/ppermute | solution.py:151
  29.6 5.0 %collective-permute-start.4 = (f32[34,256]{1,0:T(8,128)S(1)}, f32[34,256]{1,0:T(8,128)S(1)}, u32[]{:S(2)}, u32[]{:S(2)}) collective-permute-start(f32[34,256]{1,0:T(8,128)S(1)} %dynamic-slice_bitcast_fusion.2), channel_id=1, source_target_pairs={{0,16},{2,18},{4,20},{6,22},{8,24},{10,26},{12,28},{14,30},{16,0},... | collective-permute-start | bytes 104456 | tf_op jit(solution)/shard_map/ppermute | solution.py:151
  34.6 1.4 %copy-start.1 = (f32[2,17,256]{2,1,0:T(8,128)}, f32[2,17,256]{2,1,0:T(8,128)S(1)}, u32[]{:S(2)}) copy-start(f32[2,17,256]{2,1,0:T(8,128)S(1)} %reshape.127) | copy-start | bytes 104452
  34.6 3.7 %collective-permute-start.5 = (f32[2,2,256]{2,0,1:T(2,128)S(1)}, f32[2,2,256]{2,0,1:T(2,128)S(1)}, u32[]{:S(2)}, u32[]{:S(2)}) collective-permute-start(f32[2,2,256]{2,0,1:T(2,128)S(1)} %copy_select_fusion), channel_id=1, source_target_pairs={{0,1},{1,0},{2,3},{3,2},{4,5},{5,4},{6,7},{7,6},{8,9},{9,8},{10,11... | collective-permute-start | bytes 12296 | tf_op jit(solution)/shard_map/ppermute | solution.py:195
  36.0 2.3 %slice-start = ((f32[2,17,256]{2,1,0:T(8,128)}), f32[2,16,256]{2,1,0:T(8,128)S(1)}, s32[]{:S(2)}) async-start(f32[2,17,256]{2,1,0:T(8,128)} %copy-done.1), calls=%async_computation | async-start | bytes 65536 | tf_op jit(solution)/shard_map/slice | solution.py:210
  39.0 4.8 %collective-permute-start.6 = (f32[32,256]{1,0:T(8,128)S(1)}, f32[32,256]{1,0:T(8,128)S(1)}, u32[]{:S(2)}, u32[]{:S(2)}) collective-permute-start(f32[32,256]{1,0:T(8,128)S(1)} %bitcast.93), channel_id=1, source_target_pairs={{0,16},{2,18},{4,20},{6,22},{8,24},{10,26},{12,28},{14,30},{16,0},... | collective-permute-start | bytes 98312 | tf_op jit(solution)/shard_map/ppermute | solution.py:162
  43.9 4.3 %collective-permute-start.7 = (f32[2,32,256]{2,1,0:T(8,128)S(1)}, f32[2,32,256]{2,1,0:T(8,128)S(1)}, u32[]{:S(2)}, u32[]{:S(2)}) collective-permute-start(f32[2,32,256]{2,1,0:T(8,128)S(1)} %pad_maximum_fusion.3), channel_id=1, source_target_pairs={{0,8},{2,10},{4,12},{6,14},{8,0},{10,2},{12,4},{14,6},{16,24},{18,... | collective-permute-start | bytes 196616 | tf_op jit(solution)/shard_map/ppermute | solution.py:162
  48.2 1.6 %copy-start.4 = (s32[2,1]{0,1:T(1,128)S(1)}, s32[2,1]{0,1:T(1,128)}, u32[]{:S(2)}) copy-start(s32[2,1]{0,1:T(1,128)} %param.9) | copy-start | bytes 28
  48.3 5.0 %collective-permute-start.8 = (f32[2,2,32,256]{3,2,0,1:T(8,128)S(1)}, f32[2,2,32,256]{3,2,0,1:T(8,128)S(1)}, u32[]{:S(2)}, u32[]{:S(2)}) collective-permute-start(f32[2,2,32,256]{3,2,0,1:T(8,128)S(1)} %pad_maximum_fusion.2), channel_id=1, source_target_pairs={{0,4},{2,6},{4,0},{6,2},{8,12},{10,14},{12,8},{14,10},{16,20},{18,... | collective-permute-start | bytes 393224 | tf_op jit(solution)/shard_map/ppermute | solution.py:162
  53.3 4.7 %collective-permute-start.9 = (f32[2,2,2,32,256]{4,3,0,1,2:T(8,128)S(1)}, f32[2,2,2,32,256]{4,3,0,1,2:T(8,128)S(1)}, u32[]{:S(2)}, u32[]{:S(2)}) collective-permute-start(f32[2,2,2,32,256]{4,3,0,1,2:T(8,128)S(1)} %pad_maximum_fusion.1), channel_id=1, source_target_pairs={{0,2},{2,0},{4,6},{6,4},{8,10},{10,8},{12,14},{14,12},{16,18},{18,... | collective-permute-start | bytes 786440 | tf_op jit(solution)/shard_map/ppermute | solution.py:162

commit v16 on v14

--- a/solution.py
+++ b/solution.py
@@ -91,11 +91,16 @@
     )(band_start.reshape(-1), volume, amplitude, column_offset, column_width)
 
 
-def _backward_kernel(back_ref, vol_ref, amp_ref, off_ref, wid_ref, rw_ref, out_ref, split_ref):
+def _backward_kernel(start_ref, back_ref, vol_ref, amp_ref, off_ref, wid_ref, rw_ref, out_ref, split_ref):
     slab_rows, columns = vol_ref.shape
-    view_count, _, band = back_ref.shape
+    view_count, _, band = split_ref.shape
+    chunks = back_ref.shape[0]
+    detector_width = chunks * back_ref.shape[2]
     for v in range(view_count):
-        hi, lo = _split(back_ref[v])
+        rows = slice(v * slab_rows, (v + 1) * slab_rows)
+        full = jnp.concatenate([back_ref[k, rows, :] for k in range(chunks)], axis=1)
+        rolled = pltpu.roll(full, (detector_width - start_ref[v]) % detector_width, 1)
+        hi, lo = _split(rolled[:, :band])
         split_ref[v] = jnp.concatenate([hi, lo], axis=0)
 
     def body(j, carry):
@@ -119,14 +124,18 @@
     lax.fori_loop(0, columns // CHUNK, body, 0)
 
 
-def backward_update(back_band, volume, amplitude, column_offset, column_width, row_weight):
-    view_count, slab_rows, band = back_band.shape
+def backward_update(back_chunks, band_start, volume, amplitude, column_offset, column_width, row_weight):
+    view_count = amplitude.shape[0]
+    slab_rows = volume.shape[0]
+    smem = pl.BlockSpec(memory_space=pltpu.SMEM)
+    vmem = pl.BlockSpec(memory_space=pltpu.VMEM)
     return pl.pallas_call(
         _backward_kernel,
         out_shape=jax.ShapeDtypeStruct(volume.shape, jnp.float32),
-        scratch_shapes=[pltpu.VMEM((view_count, 2 * slab_rows, band), jnp.bfloat16)],
+        in_specs=[smem] + [vmem] * 6,
+        scratch_shapes=[pltpu.VMEM((view_count, 2 * slab_rows, B), jnp.bfloat16)],
         interpret=INTERPRET,
-    )(back_band, volume, amplitude, column_offset, column_width, row_weight[:, :, None])
+    )(band_start.reshape(-1), back_chunks, volume, amplitude, column_offset, column_width, row_weight[:, :, None])
 
 
 def _bit_count(count):
@@ -160,7 +169,7 @@
         low = jnp.where(bit == 0, y, other)
         high = jnp.where(bit == 0, other, y)
         y = jnp.stack([low, high], axis=step)
-    return jnp.transpose(y.reshape(count, rows, width), (1, 0, 2)).reshape(rows, count * width)
+    return y.reshape(count, rows, width)
 
 
 def local(volume, measured, band_start, column_offset, column_width, amplitude, axial_weight):
@@ -229,14 +238,7 @@
         + axial_weight[1][:, :, None] * residual
         + axial_weight[2][:, :, None] * residual_ext[:, 2 : slab_rows + 2]
     )
-    back_full = all_gather_xy(back_rows.reshape(view_count * slab_rows, shard_width), xy_count)
-    back_full = back_full.reshape(view_count, slab_rows, detector_width)
-    back_band = jnp.stack(
-        [
-            lax.dynamic_slice(back_full[v], (jnp.int32(0), band_start[v, 0]), (slab_rows, B))
-            for v in range(view_count)
-        ]
-    )
+    back_chunks = all_gather_xy(back_rows.reshape(view_count * slab_rows, shard_width), xy_count)
 
     own_rows = first_row + jnp.arange(slab_rows, dtype=jnp.int32)
     row_weight = (
@@ -244,7 +246,7 @@
         + axial_weight[1]
         + jnp.where(own_rows[None, :] < total_rows - 1, axial_weight[2], 0.0)
     )
-    volume_next = backward_update(back_band, volume, amplitude, column_offset, column_width, row_weight)
+    volume_next = backward_update(back_chunks, band_start, volume, amplitude, column_offset, column_width, row_weight)
     return (volume_next, residual)
 
 

time: 69.3 us -> 67 us (0.967)
  between operations: 4.75 us -> 0.93 us
  waiting for transfers between devices: 18.6 us -> 20.5 us
  starting transfers between devices: 16.5 us -> 15.8 us
    ppermute x4, waiting for transfers between devices: 7.71 us -> 8.88 us  [all_gather_xy(): other = lax.ppermute(y, 'xy', [(i, i ^ 1 << j) for i in range(count)])]
    another operation x1, local copies, waits for them, and re-layouts: 0.04 us -> 0.86 us  [all_gather_xy(): y = jnp.stack([low, high], axis=step)]
  transfers between devices with their start and end apart: 10 -> 10, of which waited for: 7 -> 8; matrix products, arithmetic and copies ran while one was open for 4% -> 3% of each run, Pallas kernels for 0% -> 0%
where the time goes in v16:
time: 67 us; the launch traced here: 66.7 us
  Pallas kernels  23.4 us (35%)
  waiting for transfers between devices  20.5 us (31%)
  starting transfers between devices  15.8 us (24%)
  local copies, waits for them, and re-layouts  3.89 us (6%)
  other arithmetic  2.08 us (3%)
  between operations  0.93 us (1%)
    pallas_call x1, Pallas kernels, forward_band(): pl.pallas_call(_forward_kernel, out_shape=jax.ShapeDtypeStruct((chunks, v...  13.4 us
    pallas_call x1, Pallas kernels, backward_update(): pl.pallas_call(_backward_kernel, out_shape=jax.ShapeDtypeStruct(volume.sh...  10 us
    ppermute x4, waiting for transfers between devices, all_gather_xy(): other = lax.ppermute(y, 'xy', [(i, i ^ 1 << j) for i in range(count)])  8.88 us
    ppermute x4, waiting for transfers between devices, reduce_scatter_xy(): y = keep + lax.ppermute(send, 'xy', [(i, i ^ 1 << j) for i in range(count)])  8.66 us
    ppermute x4, starting transfers between devices, reduce_scatter_xy(): y = keep + lax.ppermute(send, 'xy', [(i, i ^ 1 << j) for i in range(count)])  6.4 us
    ppermute x4, starting transfers between devices, all_gather_xy(): other = lax.ppermute(y, 'xy', [(i, i ^ 1 << j) for i in range(count)])  5.92 us
    ppermute x2, starting transfers between devices, exchange(): lax.ppermute(jnp.where(gz_index == 0, upward, downward), 'gz', [(0, 1), (...  3.5 us
    ppermute x2, waiting for transfers between devices, exchange(): lax.ppermute(jnp.where(gz_index == 0, upward, downward), 'gz', [(0, 1), (...  3.01 us
  transfers between devices with their start and end apart: 10, of which 8 were waited for; matrix products, arithmetic and copies ran while one was open for 3% of the time, Pallas kernels for 0%

profile of v16, /device:TPU:0, one launch (start us, length us, event | category | flops | bytes accessed | tf_op | source)
XLA Modules:
  0.0 66.7 jit_solution(12712343629223904517)
XLA Ops:
  0.6 13.4 %shard_map.86 = f32[16,34,256]{2,1,0:T(8,128)} custom-call(s32[2]{0:T(128)} %bitcast.84, f32[16,16384]{1,0:T(8,128)} %vol_ref.3, f32[2,16384]{1,0:T(2,128)} %amp_ref.3, s32[2,16384]{1,0:T(2,128)} %off_ref.3, s32[2,16384]{1,0:T(2,128)} %wid_ref.3), custom_call_target="tpu_custom_call" | custom-call | flops 1610612736 | bytes 1441792 | tf_op jit(solution)/shard_map/pallas_call | solution.py:80
  14.0 1.1 %constant_dynamic-slice_fusion.5 = (f32[2,2,2,1,34,256]{5,4,3,2,1,0:T(8,128)S(1)}, f32[2,2,2,1,34,256]{5,4,3,2,1,0:T(8,128)S(1)}) fusion(f32[2,2,2,2,34,256]{5,4,3,2,1,0:T(8,128)} %bitcast.76, s32[]{:T(128)S(6)} %select_n.142, s32[]{:T(128)S(6)} %select_n.143), kind=kLoop, calls=%fused_computation.52 | loop fusion | bytes 1114120 | tf_op jit(solution)/shard_map/jit(dynamic_index_in_dim)/dynamic_slice | solution.py:155
  15.1 0.0 copy-start.2
  15.1 0.2 copy.114
  15.4 0.5 collective-permute-start.1
  15.9 0.0 copy-done.2
  15.9 0.7 copy-done.1
  16.6 0.1 slice_bitcast_fusion.1
  16.7 0.1 reshape.121
  16.8 0.1 reshape.122
  16.8 3.0 %collective-permute-start = (f32[2,2,256]{2,0,1:T(2,128)S(1)}, f32[2,2,256]{2,0,1:T(2,128)S(1)}, u32[]{:S(2)}, u32[]{:S(2)}) collective-permute-start(f32[2,2,256]{2,0,1:T(2,128)S(1)} %fusion.8), channel_id=1, source_target_pairs={{0,1},{1,0},{2,3},{3,2},{4,5},{5,4},{6,7},{7,6},{8,9},{9,8},{10,11... | collective-permute-start | bytes 12296 | tf_op jit(solution)/shard_map/ppermute | solution.py:201
  19.8 0.0 collective-permute-done.1
  19.8 0.3 bitcast_add_fusion
  20.1 1.6 %collective-permute-start.2 = (f32[2,2,34,256]{3,1,2,0:T(2,128)S(1)}, f32[2,2,34,256]{3,1,2,0:T(2,128)S(1)}, u32[]{:S(2)}, u32[]{:S(2)}) collective-permute-start(f32[2,2,34,256]{3,1,2,0:T(2,128)S(1)} %dynamic-slice_bitcast_fusion), channel_id=1, source_target_pairs={{0,4},{2,6},{4,0},{6,2},{8,12},{10,14},{12,8},{14,10},{16,20},{18,... | collective-permute-start | bytes 417800 | tf_op jit(solution)/shard_map/ppermute | solution.py:157
  21.7 3.8 %collective-permute-done.2 = f32[2,2,34,256]{3,1,2,0:T(2,128)S(1)} collective-permute-done((f32[2,2,34,256]{3,1,2,0:T(2,128)S(1)}, f32[2,2,34,256]{3,1,2,0:T(2,128)S(1)}, u32[]{:S(2)}, u32[]{:S(2)}) %collective-permute-start.2) | collective-permute-done | bytes 139296 | tf_op jit(solution)/shard_map/ppermute | solution.py:157
  25.6 0.1 bitcast_add_fusion.1
  25.6 0.1 constant_dynamic-slice_fusion.3
  25.8 1.6 %collective-permute-start.3 = (f32[2,34,256]{2,0,1:T(2,128)S(1)}, f32[2,34,256]{2,0,1:T(2,128)S(1)}, u32[]{:S(2)}, u32[]{:S(2)}) collective-permute-start(f32[2,34,256]{2,0,1:T(2,128)S(1)} %bitcast.79), channel_id=1, source_target_pairs={{0,8},{2,10},{4,12},{6,14},{8,0},{10,2},{12,4},{14,6},{16,24},{18,... | collective-permute-start | bytes 208904 | tf_op jit(solution)/shard_map/ppermute | solution.py:157
  27.5 2.7 %collective-permute-done.3 = f32[2,34,256]{2,0,1:T(2,128)S(1)} collective-permute-done((f32[2,34,256]{2,0,1:T(2,128)S(1)}, f32[2,34,256]{2,0,1:T(2,128)S(1)}, u32[]{:S(2)}, u32[]{:S(2)}) %collective-permute-start.3) | collective-permute-done | bytes 69664 | tf_op jit(solution)/shard_map/ppermute | solution.py:157
  30.2 0.1 bitcast_add_fusion.2
  30.3 0.1 constant_dynamic-slice_fusion.1
  30.3 2.7 %collective-permute-start.4 = (f32[34,256]{1,0:T(8,128)S(1)}, f32[34,256]{1,0:T(8,128)S(1)}, u32[]{:S(2)}, u32[]{:S(2)}) collective-permute-start(f32[34,256]{1,0:T(8,128)S(1)} %bitcast.80), channel_id=1, source_target_pairs={{0,16},{2,18},{4,20},{6,22},{8,24},{10,26},{12,28},{14,30},{16,0},... | collective-permute-start | bytes 104456 | tf_op jit(solution)/shard_map/ppermute | solution.py:157
  33.0 0.0 collective-permute-done
  33.0 0.1 reshape_squeeze.7
  33.1 0.1 reshape_squeeze.6
  33.2 2.1 %collective-permute-done.4 = f32[34,256]{1,0:T(8,128)S(1)} collective-permute-done((f32[34,256]{1,0:T(8,128)S(1)}, f32[34,256]{1,0:T(8,128)S(1)}, u32[]{:S(2)}, u32[]{:S(2)}) %collective-permute-start.4) | collective-permute-done | bytes 34848 | tf_op jit(solution)/shard_map/ppermute | solution.py:157
  35.3 0.0 copy-start
  35.4 0.5 collective-permute-start.5
  35.9 0.1 add_add_fusion
  36.0 0.0 slice-start
  36.0 3.0 %collective-permute-done.5 = f32[2,2,256]{2,0,1:T(2,128)S(1)} collective-permute-done((f32[2,2,256]{2,0,1:T(2,128)S(1)}, f32[2,2,256]{2,0,1:T(2,128)S(1)}, u32[]{:S(2)}, u32[]{:S(2)}) %collective-permute-start.5) | collective-permute-done | bytes 4128 | tf_op jit(solution)/shard_map/ppermute | solution.py:201
  39.1 0.0 slice-done
  39.1 0.1 fusion.5
  39.2 0.6 fusion.6
  39.8 2.6 %collective-permute-start.6 = (f32[32,256]{1,0:T(8,128)S(1)}, f32[32,256]{1,0:T(8,128)S(1)}, u32[]{:S(2)}, u32[]{:S(2)}) collective-permute-start(f32[32,256]{1,0:T(8,128)S(1)} %bitcast.78), channel_id=1, source_target_pairs={{0,16},{2,18},{4,20},{6,22},{8,24},{10,26},{12,28},{14,30},{16,0},... | collective-permute-start | bytes 98312 | tf_op jit(solution)/shard_map/ppermute | solution.py:168
  42.4 2.2 %collective-permute-done.6 = f32[32,256]{1,0:T(8,128)S(1)} collective-permute-done((f32[32,256]{1,0:T(8,128)S(1)}, f32[32,256]{1,0:T(8,128)S(1)}, u32[]{:S(2)}, u32[]{:S(2)}) %collective-permute-start.6) | collective-permute-done | bytes 32800 | tf_op jit(solution)/shard_map/ppermute | solution.py:168
  44.6 1.6 %collective-permute-start.7 = (f32[2,32,256]{2,1,0:T(8,128)S(1)}, f32[2,32,256]{2,1,0:T(8,128)S(1)}, u32[]{:S(2)}, u32[]{:S(2)}) collective-permute-start(f32[2,32,256]{2,1,0:T(8,128)S(1)} %pad_maximum_fusion.3), channel_id=1, source_target_pairs={{0,8},{2,10},{4,12},{6,14},{8,0},{10,2},{12,4},{14,6},{16,24},{18,... | collective-permute-start | bytes 196616 | tf_op jit(solution)/shard_map/ppermute | solution.py:168
  46.3 2.7 %collective-permute-done.7 = f32[2,32,256]{2,1,0:T(8,128)S(1)} collective-permute-done((f32[2,32,256]{2,1,0:T(8,128)S(1)}, f32[2,32,256]{2,1,0:T(8,128)S(1)}, u32[]{:S(2)}, u32[]{:S(2)}) %collective-permute-start.7) | collective-permute-done | bytes 65568 | tf_op jit(solution)/shard_map/ppermute | solution.py:168
  49.0 1.6 %collective-permute-start.8 = (f32[2,2,32,256]{3,2,0,1:T(8,128)S(1)}, f32[2,2,32,256]{3,2,0,1:T(8,128)S(1)}, u32[]{:S(2)}, u32[]{:S(2)}) collective-permute-start(f32[2,2,32,256]{3,2,0,1:T(8,128)S(1)} %pad_maximum_fusion.2), channel_id=1, source_target_pairs={{0,4},{2,6},{4,0},{6,2},{8,12},{10,14},{12,8},{14,10},{16,20},{18,... | collective-permute-start | bytes 393224 | tf_op jit(solution)/shard_map/ppermute | solution.py:168
  50.6 3.4 %collective-permute-done.8 = f32[2,2,32,256]{3,2,0,1:T(8,128)S(1)} collective-permute-done((f32[2,2,32,256]{3,2,0,1:T(8,128)S(1)}, f32[2,2,32,256]{3,2,0,1:T(8,128)S(1)}, u32[]{:S(2)}, u32[]{:S(2)}) %collective-permute-start.8) | collective-permute-done | bytes 131104 | tf_op jit(solution)/shard_map/ppermute | solution.py:168
  54.1 0.1 collective-permute-start.9
  54.2 0.1 copy.95
  54.3 0.1 copy.97
  54.4 0.1 copy.96
  54.5 0.7 %select_add_fusion.rw_ref = f32[2,16,1]{2,1,0:T(8,128)} fusion(f32[2,16,1]{2,1,0:T(8,128)S(1)} %copy.97, f32[2,16,1]{2,1,0:T(8,128)S(1)} %copy.96, f32[2,16,1]{2,1,0:T(8,128)S(1)} %copy.95, pred[16]{0:T(512)(128)(4,1)S(1)} %get-tuple-element.40, pred[16]{0:T(512)(128)(4,1)S(1)} %get-tuple-element.41), kind=kLoop, calls=%fused_computation.35 | loop fusion | flops 128 | bytes 544 | tf_op jit(solution)/shard_map/add | solution.py:245
  55.1 0.6 collective-permute-done.9
  55.8 0.9 %copy.94 = f32[2,2,2,2,32,256]{5,4,3,2,1,0:T(8,128)} copy(f32[2,2,2,2,32,256]{5,4,0,1,2,3:T(8,128)S(1)} %pad_maximum_fusion) | data formatting | bytes 1048576 | tf_op jit(solution)/shard_map/stack | solution.py:171
  56.7 10.0 %shard_map.87 = f32[16,16384]{1,0:T(8,128)} custom-call(s32[2]{0:T(128)} %bitcast.85, f32[16,32,256]{2,1,0:T(8,128)} %bitcast.75, f32[16,16384]{1,0:T(8,128)} %vol_ref.3, f32[2,16384]{1,0:T(2,128)} %amp_ref.3, s32[2,16384]{1,0:T(2,128)} %off_ref.3, s32[2,16384]{1,0:T(2,128)} %wid_ref.3, f32[2,16,1]{2,1,0:T(8,128)} %select_add_fusion.rw_ref), custom_call_target="tpu_custom_call" | custom-call | tf_op jit(solution)/shard_map/pallas_call | solution.py:132
  (40 shorter events, 0.3 us)
Async XLA Ops:
  15.1 0.8 %copy-start.2 = (f32[2,16,256]{2,1,0:T(8,128)S(1)}, f32[2,16,256]{2,1,0:T(8,128)}, u32[]{:S(2)}) copy-start(f32[2,16,256]{2,1,0:T(8,128)} %param.8) | copy-start | bytes 98308
  15.4 4.5 %collective-permute-start.1 = (f32[2,2,2,34,256]{4,1,3,0,2:T(2,128)S(1)}, f32[2,2,2,34,256]{4,1,3,0,2:T(2,128)S(1)}, u32[]{:S(2)}, u32[]{:S(2)}) collective-permute-start(f32[2,2,2,34,256]{4,1,3,0,2:T(2,128)S(1)} %bitcast.77), channel_id=1, source_target_pairs={{0,2},{2,0},{4,6},{6,4},{8,10},{10,8},{12,14},{14,12},{16,18},{18,... | collective-permute-start | bytes 835592 | tf_op jit(solution)/shard_map/ppermute | solution.py:157
  15.9 0.7 %copy-start.1 = (f32[3,2,16]{2,1,0:T(2,128)S(1)}, f32[3,2,16]{2,1,0:T(2,128)}, u32[]{:S(2)}) copy-start(f32[3,2,16]{2,1,0:T(2,128)} %param.13) | copy-start | bytes 1156
  16.8 16.2 %collective-permute-start = (f32[2,2,256]{2,0,1:T(2,128)S(1)}, f32[2,2,256]{2,0,1:T(2,128)S(1)}, u32[]{:S(2)}, u32[]{:S(2)}) collective-permute-start(f32[2,2,256]{2,0,1:T(2,128)S(1)} %fusion.8), channel_id=1, source_target_pairs={{0,1},{1,0},{2,3},{3,2},{4,5},{5,4},{6,7},{7,6},{8,9},{9,8},{10,11... | collective-permute-start | bytes 12296 | tf_op jit(solution)/shard_map/ppermute | solution.py:201
  20.1 5.4 %collective-permute-start.2 = (f32[2,2,34,256]{3,1,2,0:T(2,128)S(1)}, f32[2,2,34,256]{3,1,2,0:T(2,128)S(1)}, u32[]{:S(2)}, u32[]{:S(2)}) collective-permute-start(f32[2,2,34,256]{3,1,2,0:T(2,128)S(1)} %dynamic-slice_bitcast_fusion), channel_id=1, source_target_pairs={{0,4},{2,6},{4,0},{6,2},{8,12},{10,14},{12,8},{14,10},{16,20},{18,... | collective-permute-start | bytes 417800 | tf_op jit(solution)/shard_map/ppermute | solution.py:157
  25.8 4.4 %collective-permute-start.3 = (f32[2,34,256]{2,0,1:T(2,128)S(1)}, f32[2,34,256]{2,0,1:T(2,128)S(1)}, u32[]{:S(2)}, u32[]{:S(2)}) collective-permute-start(f32[2,34,256]{2,0,1:T(2,128)S(1)} %bitcast.79), channel_id=1, source_target_pairs={{0,8},{2,10},{4,12},{6,14},{8,0},{10,2},{12,4},{14,6},{16,24},{18,... | collective-permute-start | bytes 208904 | tf_op jit(solution)/shard_map/ppermute | solution.py:157
  30.3 5.0 %collective-permute-start.4 = (f32[34,256]{1,0:T(8,128)S(1)}, f32[34,256]{1,0:T(8,128)S(1)}, u32[]{:S(2)}, u32[]{:S(2)}) collective-permute-start(f32[34,256]{1,0:T(8,128)S(1)} %bitcast.80), channel_id=1, source_target_pairs={{0,16},{2,18},{4,20},{6,22},{8,24},{10,26},{12,28},{14,30},{16,0},... | collective-permute-start | bytes 104456 | tf_op jit(solution)/shard_map/ppermute | solution.py:157
  35.3 0.7 %copy-start = (f32[2,17,256]{2,1,0:T(8,128)}, f32[2,17,256]{2,1,0:T(8,128)S(1)}, u32[]{:S(2)}) copy-start(f32[2,17,256]{2,1,0:T(8,128)S(1)} %reshape.124) | copy-start | bytes 104452
  35.4 3.7 %collective-permute-start.5 = (f32[2,2,256]{2,0,1:T(2,128)S(1)}, f32[2,2,256]{2,0,1:T(2,128)S(1)}, u32[]{:S(2)}, u32[]{:S(2)}) collective-permute-start(f32[2,2,256]{2,0,1:T(2,128)S(1)} %copy_select_fusion), channel_id=1, source_target_pairs={{0,1},{1,0},{2,3},{3,2},{4,5},{5,4},{6,7},{7,6},{8,9},{9,8},{10,11... | collective-permute-start | bytes 12296 | tf_op jit(solution)/shard_map/ppermute | solution.py:201
  36.0 3.1 %slice-start = ((f32[2,17,256]{2,1,0:T(8,128)}), f32[2,16,256]{2,1,0:T(8,128)S(1)}, s32[]{:S(2)}) async-start(f32[2,17,256]{2,1,0:T(8,128)} %copy-done), calls=%async_computation | async-start | bytes 65536 | tf_op jit(solution)/shard_map/slice | solution.py:216
  39.8 4.8 %collective-permute-start.6 = (f32[32,256]{1,0:T(8,128)S(1)}, f32[32,256]{1,0:T(8,128)S(1)}, u32[]{:S(2)}, u32[]{:S(2)}) collective-permute-start(f32[32,256]{1,0:T(8,128)S(1)} %bitcast.78), channel_id=1, source_target_pairs={{0,16},{2,18},{4,20},{6,22},{8,24},{10,26},{12,28},{14,30},{16,0},... | collective-permute-start | bytes 98312 | tf_op jit(solution)/shard_map/ppermute | solution.py:168
  44.6 4.3 %collective-permute-start.7 = (f32[2,32,256]{2,1,0:T(8,128)S(1)}, f32[2,32,256]{2,1,0:T(8,128)S(1)}, u32[]{:S(2)}, u32[]{:S(2)}) collective-permute-start(f32[2,32,256]{2,1,0:T(8,128)S(1)} %pad_maximum_fusion.3), channel_id=1, source_target_pairs={{0,8},{2,10},{4,12},{6,14},{8,0},{10,2},{12,4},{14,6},{16,24},{18,... | collective-permute-start | bytes 196616 | tf_op jit(solution)/shard_map/ppermute | solution.py:168
  49.0 5.0 %collective-permute-start.8 = (f32[2,2,32,256]{3,2,0,1:T(8,128)S(1)}, f32[2,2,32,256]{3,2,0,1:T(8,128)S(1)}, u32[]{:S(2)}, u32[]{:S(2)}) collective-permute-start(f32[2,2,32,256]{3,2,0,1:T(8,128)S(1)} %pad_maximum_fusion.2), channel_id=1, source_target_pairs={{0,4},{2,6},{4,0},{6,2},{8,12},{10,14},{12,8},{14,10},{16,20},{18,... | collective-permute-start | bytes 393224 | tf_op jit(solution)/shard_map/ppermute | solution.py:168
  54.1 1.6 %collective-permute-start.9 = (f32[2,2,2,32,256]{4,3,0,1,2:T(8,128)S(1)}, f32[2,2,2,32,256]{4,3,0,1,2:T(8,128)S(1)}, u32[]{:S(2)}, u32[]{:S(2)}) collective-permute-start(f32[2,2,2,32,256]{4,3,0,1,2:T(8,128)S(1)} %pad_maximum_fusion.1), channel_id=1, source_target_pairs={{0,2},{2,0},{4,6},{6,4},{8,10},{10,8},{12,14},{14,12},{16,18},{18,... | collective-permute-start | bytes 786440 | tf_op jit(solution)/shard_map/ppermute | solution.py:168

commit v17 on v16

--- a/solution.py
+++ b/solution.py
@@ -91,14 +91,21 @@
     )(band_start.reshape(-1), volume, amplitude, column_offset, column_width)
 
 
-def _backward_kernel(start_ref, back_ref, vol_ref, amp_ref, off_ref, wid_ref, rw_ref, out_ref, split_ref):
+def _backward_kernel(start_ref, own_ref, got_ref, vol_ref, amp_ref, off_ref, wid_ref, rw_ref, out_ref, split_ref):
     slab_rows, columns = vol_ref.shape
     view_count, _, band = split_ref.shape
-    chunks = back_ref.shape[0]
-    detector_width = chunks * back_ref.shape[2]
+    chunks = 2 * own_ref.shape[0]
+    detector_width = chunks * own_ref.shape[2]
+    parity = lax.axis_index("xy") & 1
     for v in range(view_count):
         rows = slice(v * slab_rows, (v + 1) * slab_rows)
-        full = jnp.concatenate([back_ref[k, rows, :] for k in range(chunks)], axis=1)
+        full = jnp.concatenate(
+            [
+                jnp.where((k & 1) == parity, own_ref[k // 2, rows, :], got_ref[k // 2, rows, :])
+                for k in range(chunks)
+            ],
+            axis=1,
+        )
         rolled = pltpu.roll(full, (detector_width - start_ref[v]) % detector_width, 1)
         hi, lo = _split(rolled[:, :band])
         split_ref[v] = jnp.concatenate([hi, lo], axis=0)
@@ -124,7 +131,7 @@
     lax.fori_loop(0, columns // CHUNK, body, 0)
 
 
-def backward_update(back_chunks, band_start, volume, amplitude, column_offset, column_width, row_weight):
+def backward_update(back_halves, band_start, volume, amplitude, column_offset, column_width, row_weight):
     view_count = amplitude.shape[0]
     slab_rows = volume.shape[0]
     smem = pl.BlockSpec(memory_space=pltpu.SMEM)
@@ -132,10 +139,10 @@
     return pl.pallas_call(
         _backward_kernel,
         out_shape=jax.ShapeDtypeStruct(volume.shape, jnp.float32),
-        in_specs=[smem] + [vmem] * 6,
+        in_specs=[smem] + [vmem] * 7,
         scratch_shapes=[pltpu.VMEM((view_count, 2 * slab_rows, B), jnp.bfloat16)],
         interpret=INTERPRET,
-    )(band_start.reshape(-1), back_chunks, volume, amplitude, column_offset, column_width, row_weight[:, :, None])
+    )(band_start.reshape(-1), *back_halves, volume, amplitude, column_offset, column_width, row_weight[:, :, None])
 
 
 def _bit_count(count):
@@ -163,13 +170,14 @@
     bits = _bit_count(count)
     idx = lax.axis_index("xy")
     y = x
-    for step, j in enumerate(reversed(range(bits))):
+    for step, j in enumerate(reversed(range(1, bits))):
         bit = (idx >> j) & 1
         other = lax.ppermute(y, "xy", [(i, i ^ (1 << j)) for i in range(count)])
         low = jnp.where(bit == 0, y, other)
         high = jnp.where(bit == 0, other, y)
         y = jnp.stack([low, high], axis=step)
-    return y.reshape(count, rows, width)
+    y = y.reshape(count // 2, rows, width)
+    return y, lax.ppermute(y, "xy", [(i, i ^ 1) for i in range(count)])
 
 
 def local(volume, measured, band_start, column_offset, column_width, amplitude, axial_weight):
@@ -238,7 +246,7 @@
         + axial_weight[1][:, :, None] * residual
         + axial_weight[2][:, :, None] * residual_ext[:, 2 : slab_rows + 2]
     )
-    back_chunks = all_gather_xy(back_rows.reshape(view_count * slab_rows, shard_width), xy_count)
+    back_halves = all_gather_xy(back_rows.reshape(view_count * slab_rows, shard_width), xy_count)
 
     own_rows = first_row + jnp.arange(slab_rows, dtype=jnp.int32)
     row_weight = (
@@ -246,7 +254,7 @@
         + axial_weight[1]
         + jnp.where(own_rows[None, :] < total_rows - 1, axial_weight[2], 0.0)
     )
-    volume_next = backward_update(back_chunks, band_start, volume, amplitude, column_offset, column_width, row_weight)
+    volume_next = backward_update(back_halves, band_start, volume, amplitude, column_offset, column_width, row_weight)
     return (volume_next, residual)
 
 

time: 67 us -> 66.9 us (level)
    another operation x1, local copies, waits for them, and re-layouts: 0.86 us -> 0.02 us  [all_gather_xy(): y = jnp.stack([low, high], axis=step)]
    unnamed x10 -> x14, local copies, waits for them, and re-layouts: 0.7 us -> 1.42 us
    ppermute x4 -> x3, waiting for transfers between devices: 8.88 us -> 8.32 us  [all_gather_xy(): other = lax.ppermute(y, 'xy', [(i, i ^ 1 << j) for i in range(count)])]
    ppermute x4 -> x3, starting transfers between devices: 5.92 us -> 5.85 us  [all_gather_xy(): other = lax.ppermute(y, 'xy', [(i, i ^ 1 << j) for i in range(count)])]
where the time goes in v17:
time: 66.9 us; the launch traced here: 66.6 us
  Pallas kernels  23.5 us (35%)
  waiting for transfers between devices  20.6 us (31%)
  starting transfers between devices  15.8 us (24%)
  local copies, waits for them, and re-layouts  3.76 us (6%)
  other arithmetic  2.01 us (3%)
  between operations  0.92 us (1%)
    pallas_call x1, Pallas kernels, forward_band(): pl.pallas_call(_forward_kernel, out_shape=jax.ShapeDtypeStruct((chunks, v...  13.4 us
    pallas_call x1, Pallas kernels, backward_update(): pl.pallas_call(_backward_kernel, out_shape=jax.ShapeDtypeStruct(volume.sh...  10.1 us
    ppermute x4, waiting for transfers between devices, reduce_scatter_xy(): y = keep + lax.ppermute(send, 'xy', [(i, i ^ 1 << j) for i in range(count)])  8.66 us
    ppermute x3, waiting for transfers between devices, all_gather_xy(): other = lax.ppermute(y, 'xy', [(i, i ^ 1 << j) for i in range(count)])  8.32 us
    ppermute x4, starting transfers between devices, reduce_scatter_xy(): y = keep + lax.ppermute(send, 'xy', [(i, i ^ 1 << j) for i in range(count)])  6.4 us
    ppermute x3, starting transfers between devices, all_gather_xy(): other = lax.ppermute(y, 'xy', [(i, i ^ 1 << j) for i in range(count)])  5.85 us
    ppermute x2, starting transfers between devices, exchange(): lax.ppermute(jnp.where(gz_index == 0, upward, downward), 'gz', [(0, 1), (...  3.5 us
    ppermute x2, waiting for transfers between devices, exchange(): lax.ppermute(jnp.where(gz_index == 0, upward, downward), 'gz', [(0, 1), (...  3.01 us
  transfers between devices with their start and end apart: 10, of which 8 were waited for; matrix products, arithmetic and copies ran while one was open for 3% of the time, Pallas kernels for 0%

profile of v17, /device:TPU:0, one launch (start us, length us, event | category | flops | bytes accessed | tf_op | source)
XLA Modules:
  0.0 66.6 jit_solution(14293494733678675576)
XLA Ops:
  0.6 13.4 %shard_map.86 = f32[16,34,256]{2,1,0:T(8,128)} custom-call(s32[2]{0:T(128)} %bitcast.81, f32[16,16384]{1,0:T(8,128)} %vol_ref.3, f32[2,16384]{1,0:T(2,128)} %amp_ref.3, s32[2,16384]{1,0:T(2,128)} %off_ref.3, s32[2,16384]{1,0:T(2,128)} %wid_ref.3), custom_call_target="tpu_custom_call" | custom-call | flops 1610612736 | bytes 1441792 | tf_op jit(solution)/shard_map/pallas_call | solution.py:80
  14.0 1.1 %constant_dynamic-slice_fusion.5 = (f32[2,2,2,1,34,256]{5,4,3,2,1,0:T(8,128)S(1)}, f32[2,2,2,1,34,256]{5,4,3,2,1,0:T(8,128)S(1)}) fusion(f32[2,2,2,2,34,256]{5,4,3,2,1,0:T(8,128)} %bitcast.73, s32[]{:T(128)S(6)} %select_n.129, s32[]{:T(128)S(6)} %select_n.130), kind=kLoop, calls=%fused_computation.49 | loop fusion | bytes 1114120 | tf_op jit(solution)/shard_map/jit(dynamic_index_in_dim)/dynamic_slice | solution.py:162
  15.1 0.0 copy-start.4
  15.1 0.2 copy.113
  15.4 0.5 collective-permute-start.1
  15.9 0.0 copy-done.4
  15.9 0.7 %copy-done.3 = f32[3,2,16]{2,1,0:T(2,128)S(1)} copy-done((f32[3,2,16]{2,1,0:T(2,128)S(1)}, f32[3,2,16]{2,1,0:T(2,128)}, u32[]{:S(2)}) %copy-start.3) | copy-done | bytes 408
  16.6 0.1 slice_bitcast_fusion.1
  16.7 0.1 reshape.121
  16.8 0.1 reshape.122
  16.8 3.0 %collective-permute-start = (f32[2,2,256]{2,0,1:T(2,128)S(1)}, f32[2,2,256]{2,0,1:T(2,128)S(1)}, u32[]{:S(2)}, u32[]{:S(2)}) collective-permute-start(f32[2,2,256]{2,0,1:T(2,128)S(1)} %fusion.8), channel_id=1, source_target_pairs={{0,1},{1,0},{2,3},{3,2},{4,5},{5,4},{6,7},{7,6},{8,9},{9,8},{10,11... | collective-permute-start | bytes 12296 | tf_op jit(solution)/shard_map/ppermute | solution.py:209
  19.8 0.0 collective-permute-done.1
  19.8 0.3 bitcast_add_fusion
  20.1 1.6 %collective-permute-start.2 = (f32[2,2,34,256]{3,1,2,0:T(2,128)S(1)}, f32[2,2,34,256]{3,1,2,0:T(2,128)S(1)}, u32[]{:S(2)}, u32[]{:S(2)}) collective-permute-start(f32[2,2,34,256]{3,1,2,0:T(2,128)S(1)} %dynamic-slice_bitcast_fusion), channel_id=1, source_target_pairs={{0,4},{2,6},{4,0},{6,2},{8,12},{10,14},{12,8},{14,10},{16,20},{18,... | collective-permute-start | bytes 417800 | tf_op jit(solution)/shard_map/ppermute | solution.py:164
  21.7 3.8 %collective-permute-done.2 = f32[2,2,34,256]{3,1,2,0:T(2,128)S(1)} collective-permute-done((f32[2,2,34,256]{3,1,2,0:T(2,128)S(1)}, f32[2,2,34,256]{3,1,2,0:T(2,128)S(1)}, u32[]{:S(2)}, u32[]{:S(2)}) %collective-permute-start.2) | collective-permute-done | bytes 139296 | tf_op jit(solution)/shard_map/ppermute | solution.py:164
  25.6 0.1 bitcast_add_fusion.1
  25.6 0.1 constant_dynamic-slice_fusion.3
  25.8 1.6 %collective-permute-start.3 = (f32[2,34,256]{2,0,1:T(2,128)S(1)}, f32[2,34,256]{2,0,1:T(2,128)S(1)}, u32[]{:S(2)}, u32[]{:S(2)}) collective-permute-start(f32[2,34,256]{2,0,1:T(2,128)S(1)} %bitcast.76), channel_id=1, source_target_pairs={{0,8},{2,10},{4,12},{6,14},{8,0},{10,2},{12,4},{14,6},{16,24},{18,... | collective-permute-start | bytes 208904 | tf_op jit(solution)/shard_map/ppermute | solution.py:164
  27.5 2.7 %collective-permute-done.3 = f32[2,34,256]{2,0,1:T(2,128)S(1)} collective-permute-done((f32[2,34,256]{2,0,1:T(2,128)S(1)}, f32[2,34,256]{2,0,1:T(2,128)S(1)}, u32[]{:S(2)}, u32[]{:S(2)}) %collective-permute-start.3) | collective-permute-done | bytes 69664 | tf_op jit(solution)/shard_map/ppermute | solution.py:164
  30.2 0.1 bitcast_add_fusion.2
  30.3 0.1 constant_dynamic-slice_fusion.1
  30.3 2.7 %collective-permute-start.4 = (f32[34,256]{1,0:T(8,128)S(1)}, f32[34,256]{1,0:T(8,128)S(1)}, u32[]{:S(2)}, u32[]{:S(2)}) collective-permute-start(f32[34,256]{1,0:T(8,128)S(1)} %bitcast.77), channel_id=1, source_target_pairs={{0,16},{2,18},{4,20},{6,22},{8,24},{10,26},{12,28},{14,30},{16,0},... | collective-permute-start | bytes 104456 | tf_op jit(solution)/shard_map/ppermute | solution.py:164
  33.0 0.0 collective-permute-done
  33.0 0.1 reshape_squeeze.7
  33.1 0.1 reshape_squeeze.6
  33.2 2.1 %collective-permute-done.4 = f32[34,256]{1,0:T(8,128)S(1)} collective-permute-done((f32[34,256]{1,0:T(8,128)S(1)}, f32[34,256]{1,0:T(8,128)S(1)}, u32[]{:S(2)}, u32[]{:S(2)}) %collective-permute-start.4) | collective-permute-done | bytes 34848 | tf_op jit(solution)/shard_map/ppermute | solution.py:164
  35.3 0.0 copy-start.2
  35.4 0.5 collective-permute-start.5
  35.9 0.1 add_add_fusion
  36.0 0.0 slice-start
  36.0 3.0 %collective-permute-done.5 = f32[2,2,256]{2,0,1:T(2,128)S(1)} collective-permute-done((f32[2,2,256]{2,0,1:T(2,128)S(1)}, f32[2,2,256]{2,0,1:T(2,128)S(1)}, u32[]{:S(2)}, u32[]{:S(2)}) %collective-permute-start.5) | collective-permute-done | bytes 4128 | tf_op jit(solution)/shard_map/ppermute | solution.py:209
  39.1 0.0 slice-done
  39.1 0.1 fusion.5
  39.2 0.6 fusion.6
  39.8 2.6 %collective-permute-start.6 = (f32[32,256]{1,0:T(8,128)S(1)}, f32[32,256]{1,0:T(8,128)S(1)}, u32[]{:S(2)}, u32[]{:S(2)}) collective-permute-start(f32[32,256]{1,0:T(8,128)S(1)} %bitcast.75), channel_id=1, source_target_pairs={{0,16},{2,18},{4,20},{6,22},{8,24},{10,26},{12,28},{14,30},{16,0},... | collective-permute-start | bytes 98312 | tf_op jit(solution)/shard_map/ppermute | solution.py:175
  42.4 2.2 %collective-permute-done.6 = f32[32,256]{1,0:T(8,128)S(1)} collective-permute-done((f32[32,256]{1,0:T(8,128)S(1)}, f32[32,256]{1,0:T(8,128)S(1)}, u32[]{:S(2)}, u32[]{:S(2)}) %collective-permute-start.6) | collective-permute-done | bytes 32800 | tf_op jit(solution)/shard_map/ppermute | solution.py:175
  44.6 1.6 %collective-permute-start.7 = (f32[2,32,256]{2,1,0:T(8,128)S(1)}, f32[2,32,256]{2,1,0:T(8,128)S(1)}, u32[]{:S(2)}, u32[]{:S(2)}) collective-permute-start(f32[2,32,256]{2,1,0:T(8,128)S(1)} %pad_maximum_fusion.2), channel_id=1, source_target_pairs={{0,8},{2,10},{4,12},{6,14},{8,0},{10,2},{12,4},{14,6},{16,24},{18,... | collective-permute-start | bytes 196616 | tf_op jit(solution)/shard_map/ppermute | solution.py:175
  46.3 2.7 %collective-permute-done.7 = f32[2,32,256]{2,1,0:T(8,128)S(1)} collective-permute-done((f32[2,32,256]{2,1,0:T(8,128)S(1)}, f32[2,32,256]{2,1,0:T(8,128)S(1)}, u32[]{:S(2)}, u32[]{:S(2)}) %collective-permute-start.7) | collective-permute-done | bytes 65568 | tf_op jit(solution)/shard_map/ppermute | solution.py:175
  49.0 1.6 %collective-permute-start.8 = (f32[2,2,32,256]{3,2,0,1:T(8,128)S(1)}, f32[2,2,32,256]{3,2,0,1:T(8,128)S(1)}, u32[]{:S(2)}, u32[]{:S(2)}) collective-permute-start(f32[2,2,32,256]{3,2,0,1:T(8,128)S(1)} %pad_maximum_fusion.1), channel_id=1, source_target_pairs={{0,4},{2,6},{4,0},{6,2},{8,12},{10,14},{12,8},{14,10},{16,20},{18,... | collective-permute-start | bytes 393224 | tf_op jit(solution)/shard_map/ppermute | solution.py:175
  50.6 3.4 %collective-permute-done.8 = f32[2,2,32,256]{3,2,0,1:T(8,128)S(1)} collective-permute-done((f32[2,2,32,256]{3,2,0,1:T(8,128)S(1)}, f32[2,2,32,256]{3,2,0,1:T(8,128)S(1)}, u32[]{:S(2)}, u32[]{:S(2)}) %collective-permute-start.8) | collective-permute-done | bytes 131104 | tf_op jit(solution)/shard_map/ppermute | solution.py:175
  54.1 0.1 collective-permute-start.9
  54.2 0.1 copy.94
  54.3 0.1 copy.96
  54.4 0.1 copy.95
  54.5 0.7 %select_add_fusion.rw_ref = f32[2,16,1]{2,1,0:T(8,128)} fusion(f32[2,16,1]{2,1,0:T(8,128)S(1)} %copy.96, f32[2,16,1]{2,1,0:T(8,128)S(1)} %copy.95, f32[2,16,1]{2,1,0:T(8,128)S(1)} %copy.94, pred[16]{0:T(512)(128)(4,1)S(1)} %get-tuple-element.38, pred[16]{0:T(512)(128)(4,1)S(1)} %get-tuple-element.39), kind=kLoop, calls=%fused_computation.32 | loop fusion | flops 128 | bytes 544 | tf_op jit(solution)/shard_map/add | solution.py:253
  55.2 0.6 collective-permute-done.9.got_ref
  55.7 0.7 %copy-done.1 = f32[8,32,256]{2,1,0:T(8,128)} copy-done((f32[8,32,256]{2,1,0:T(8,128)}, f32[8,32,256]{2,1,0:T(8,128)S(1)}, u32[]{:S(2)}) %copy-start.1) | copy-done | bytes 262168
  56.4 10.1 %shard_map.87 = f32[16,16384]{1,0:T(8,128)} custom-call(s32[2]{0:T(128)} %bitcast.82, f32[8,32,256]{2,1,0:T(8,128)} %bitcast.72, f32[8,32,256]{2,1,0:T(8,128)} %copy-done.1, f32[16,16384]{1,0:T(8,128)} %vol_ref.3, f32[2,16384]{1,0:T(2,128)} %amp_ref.3, s32[2,16384]{1,0:T(2,128)} %off_ref.3, s32[2,16384]{1,0:T(2,128)} %wid_ref.3, ...), custom_call_target="tpu_custom_call" | custom-call | tf_op jit(solution)/shard_map/pallas_call | solution.py:139
  (42 shorter events, 0.3 us)
Async XLA Ops:
  15.1 0.8 %copy-start.4 = (f32[2,16,256]{2,1,0:T(8,128)S(1)}, f32[2,16,256]{2,1,0:T(8,128)}, u32[]{:S(2)}) copy-start(f32[2,16,256]{2,1,0:T(8,128)} %param.8) | copy-start | bytes 98308
  15.4 4.5 %collective-permute-start.1 = (f32[2,2,2,34,256]{4,1,3,0,2:T(2,128)S(1)}, f32[2,2,2,34,256]{4,1,3,0,2:T(2,128)S(1)}, u32[]{:S(2)}, u32[]{:S(2)}) collective-permute-start(f32[2,2,2,34,256]{4,1,3,0,2:T(2,128)S(1)} %bitcast.74), channel_id=1, source_target_pairs={{0,2},{2,0},{4,6},{6,4},{8,10},{10,8},{12,14},{14,12},{16,18},{18,... | collective-permute-start | bytes 835592 | tf_op jit(solution)/shard_map/ppermute | solution.py:164
  15.9 0.7 %copy-start.3 = (f32[3,2,16]{2,1,0:T(2,128)S(1)}, f32[3,2,16]{2,1,0:T(2,128)}, u32[]{:S(2)}) copy-start(f32[3,2,16]{2,1,0:T(2,128)} %param.13) | copy-start | bytes 1156
  16.8 16.2 %collective-permute-start = (f32[2,2,256]{2,0,1:T(2,128)S(1)}, f32[2,2,256]{2,0,1:T(2,128)S(1)}, u32[]{:S(2)}, u32[]{:S(2)}) collective-permute-start(f32[2,2,256]{2,0,1:T(2,128)S(1)} %fusion.8), channel_id=1, source_target_pairs={{0,1},{1,0},{2,3},{3,2},{4,5},{5,4},{6,7},{7,6},{8,9},{9,8},{10,11... | collective-permute-start | bytes 12296 | tf_op jit(solution)/shard_map/ppermute | solution.py:209
  20.1 5.4 %collective-permute-start.2 = (f32[2,2,34,256]{3,1,2,0:T(2,128)S(1)}, f32[2,2,34,256]{3,1,2,0:T(2,128)S(1)}, u32[]{:S(2)}, u32[]{:S(2)}) collective-permute-start(f32[2,2,34,256]{3,1,2,0:T(2,128)S(1)} %dynamic-slice_bitcast_fusion), channel_id=1, source_target_pairs={{0,4},{2,6},{4,0},{6,2},{8,12},{10,14},{12,8},{14,10},{16,20},{18,... | collective-permute-start | bytes 417800 | tf_op jit(solution)/shard_map/ppermute | solution.py:164
  25.8 4.4 %collective-permute-start.3 = (f32[2,34,256]{2,0,1:T(2,128)S(1)}, f32[2,34,256]{2,0,1:T(2,128)S(1)}, u32[]{:S(2)}, u32[]{:S(2)}) collective-permute-start(f32[2,34,256]{2,0,1:T(2,128)S(1)} %bitcast.76), channel_id=1, source_target_pairs={{0,8},{2,10},{4,12},{6,14},{8,0},{10,2},{12,4},{14,6},{16,24},{18,... | collective-permute-start | bytes 208904 | tf_op jit(solution)/shard_map/ppermute | solution.py:164
  30.3 5.0 %collective-permute-start.4 = (f32[34,256]{1,0:T(8,128)S(1)}, f32[34,256]{1,0:T(8,128)S(1)}, u32[]{:S(2)}, u32[]{:S(2)}) collective-permute-start(f32[34,256]{1,0:T(8,128)S(1)} %bitcast.77), channel_id=1, source_target_pairs={{0,16},{2,18},{4,20},{6,22},{8,24},{10,26},{12,28},{14,30},{16,0},... | collective-permute-start | bytes 104456 | tf_op jit(solution)/shard_map/ppermute | solution.py:164
  35.3 0.7 %copy-start.2 = (f32[2,17,256]{2,1,0:T(8,128)}, f32[2,17,256]{2,1,0:T(8,128)S(1)}, u32[]{:S(2)}) copy-start(f32[2,17,256]{2,1,0:T(8,128)S(1)} %reshape.124) | copy-start | bytes 104452
  35.4 3.7 %collective-permute-start.5 = (f32[2,2,256]{2,0,1:T(2,128)S(1)}, f32[2,2,256]{2,0,1:T(2,128)S(1)}, u32[]{:S(2)}, u32[]{:S(2)}) collective-permute-start(f32[2,2,256]{2,0,1:T(2,128)S(1)} %copy_select_fusion), channel_id=1, source_target_pairs={{0,1},{1,0},{2,3},{3,2},{4,5},{5,4},{6,7},{7,6},{8,9},{9,8},{10,11... | collective-permute-start | bytes 12296 | tf_op jit(solution)/shard_map/ppermute | solution.py:209
  36.0 3.1 %slice-start = ((f32[2,17,256]{2,1,0:T(8,128)}), f32[2,16,256]{2,1,0:T(8,128)S(1)}, s32[]{:S(2)}) async-start(f32[2,17,256]{2,1,0:T(8,128)} %copy-done.2), calls=%async_computation | async-start | bytes 65536 | tf_op jit(solution)/shard_map/slice | solution.py:224
  39.8 4.8 %collective-permute-start.6 = (f32[32,256]{1,0:T(8,128)S(1)}, f32[32,256]{1,0:T(8,128)S(1)}, u32[]{:S(2)}, u32[]{:S(2)}) collective-permute-start(f32[32,256]{1,0:T(8,128)S(1)} %bitcast.75), channel_id=1, source_target_pairs={{0,16},{2,18},{4,20},{6,22},{8,24},{10,26},{12,28},{14,30},{16,0},... | collective-permute-start | bytes 98312 | tf_op jit(solution)/shard_map/ppermute | solution.py:175
  44.6 4.3 %collective-permute-start.7 = (f32[2,32,256]{2,1,0:T(8,128)S(1)}, f32[2,32,256]{2,1,0:T(8,128)S(1)}, u32[]{:S(2)}, u32[]{:S(2)}) collective-permute-start(f32[2,32,256]{2,1,0:T(8,128)S(1)} %pad_maximum_fusion.2), channel_id=1, source_target_pairs={{0,8},{2,10},{4,12},{6,14},{8,0},{10,2},{12,4},{14,6},{16,24},{18,... | collective-permute-start | bytes 196616 | tf_op jit(solution)/shard_map/ppermute | solution.py:175
  49.0 5.0 %collective-permute-start.8 = (f32[2,2,32,256]{3,2,0,1:T(8,128)S(1)}, f32[2,2,32,256]{3,2,0,1:T(8,128)S(1)}, u32[]{:S(2)}, u32[]{:S(2)}) collective-permute-start(f32[2,2,32,256]{3,2,0,1:T(8,128)S(1)} %pad_maximum_fusion.1), channel_id=1, source_target_pairs={{0,4},{2,6},{4,0},{6,2},{8,12},{10,14},{12,8},{14,10},{16,20},{18,... | collective-permute-start | bytes 393224 | tf_op jit(solution)/shard_map/ppermute | solution.py:175
  54.1 1.6 %copy-start = (f32[2,2,2,32,256]{4,3,2,1,0:T(8,128)}, f32[2,2,2,32,256]{4,3,2,1,0:T(8,128)S(1)}, u32[]{:S(2)}) copy-start(f32[2,2,2,32,256]{4,3,2,1,0:T(8,128)S(1)} %copy.93) | copy-start | bytes 786436
  54.1 1.6 %collective-permute-start.9 = (f32[8,32,256]{2,1,0:T(8,128)S(1)}, f32[8,32,256]{2,1,0:T(8,128)S(1)}, u32[]{:S(2)}, u32[]{:S(2)}) collective-permute-start(f32[8,32,256]{2,1,0:T(8,128)S(1)} %bitcast.71), channel_id=1, source_target_pairs={{0,2},{2,0},{4,6},{6,4},{8,10},{10,8},{12,14},{14,12},{16,18},{18,... | collective-permute-start | bytes 786440 | tf_op jit(solution)/shard_map/ppermute | solution.py:180
  55.7 0.7 %copy-start.1 = (f32[8,32,256]{2,1,0:T(8,128)}, f32[8,32,256]{2,1,0:T(8,128)S(1)}, u32[]{:S(2)}) copy-start(f32[8,32,256]{2,1,0:T(8,128)S(1)} %collective-permute-done.9.got_ref) | copy-start | bytes 786436

commit v18 on v17

--- a/solution.py
+++ b/solution.py
@@ -8,6 +8,7 @@
 B = 512
 RELAX = 0.9
 CHUNK = 2048
+FORWARD_CHUNK = 4096
 INTERPRET = False
 
 
@@ -30,15 +31,15 @@
     chunks, _, shard_width = out_ref.shape
     detector_width = chunks * shard_width
     acc_ref[...] = jnp.zeros(acc_ref.shape, jnp.float32)
-    row = lax.broadcasted_iota(jnp.int32, (slab_rows, CHUNK), 0)
+    row = lax.broadcasted_iota(jnp.int32, (slab_rows, FORWARD_CHUNK), 0)
 
     def body(j, carry):
-        c0 = pl.multiple_of(j * CHUNK, CHUNK)
-        cells = vol_ref[:, pl.ds(c0, CHUNK)]
+        c0 = pl.multiple_of(j * FORWARD_CHUNK, FORWARD_CHUNK)
+        cells = vol_ref[:, pl.ds(c0, FORWARD_CHUNK)]
         for v in range(view_count):
-            amp = amp_ref[pl.ds(v, 1), pl.ds(c0, CHUNK)]
-            off = off_ref[pl.ds(v, 1), pl.ds(c0, CHUNK)]
-            wid = wid_ref[pl.ds(v, 1), pl.ds(c0, CHUNK)]
+            amp = amp_ref[pl.ds(v, 1), pl.ds(c0, FORWARD_CHUNK)]
+            off = off_ref[pl.ds(v, 1), pl.ds(c0, FORWARD_CHUNK)]
+            wid = wid_ref[pl.ds(v, 1), pl.ds(c0, FORWARD_CHUNK)]
             cells_hi, cells_lo = _split(cells * amp)
             amp_hi, amp_lo = _split(amp)
             amp_rows = jnp.where(
@@ -47,13 +48,13 @@
                 jnp.where(row == 1, amp_lo.astype(jnp.float32), 0.0),
             ).astype(jnp.bfloat16)
             lhs = jnp.concatenate([cells_hi, cells_lo, amp_rows], axis=0)
-            mask = _band_mask(off, wid, band, CHUNK)
+            mask = _band_mask(off, wid, band, FORWARD_CHUNK)
             acc_ref[v] += lax.dot_general(
                 lhs, mask, (((1,), (1,)), ((), ())), preferred_element_type=jnp.float32
             )
         return carry
 
-    lax.fori_loop(0, columns // CHUNK, body, 0)
+    lax.fori_loop(0, columns // FORWARD_CHUNK, body, 0)
     height = slab_rows + 1
     placed = []
     for v in range(view_count):

time: 66.9 us -> 66.4 us (level)
  no operation moved by 1% of the time
where the time goes in v18:
time: 66.4 us; the launch traced here: 66.1 us
  Pallas kernels  23 us (35%)
  waiting for transfers between devices  20.5 us (31%)
  starting transfers between devices  15.8 us (24%)
  local copies, waits for them, and re-layouts  3.76 us (6%)
  other arithmetic  2.01 us (3%)
  between operations  0.92 us (1%)
    pallas_call x1, Pallas kernels, forward_band(): pl.pallas_call(_forward_kernel, out_shape=jax.ShapeDtypeStruct((chunks, v...  12.9 us
    pallas_call x1, Pallas kernels, backward_update(): pl.pallas_call(_backward_kernel, out_shape=jax.ShapeDtypeStruct(volume.sh...  10.1 us
    ppermute x4, waiting for transfers between devices, reduce_scatter_xy(): y = keep + lax.ppermute(send, 'xy', [(i, i ^ 1 << j) for i in range(count)])  8.66 us
    ppermute x3, waiting for transfers between devices, all_gather_xy(): other = lax.ppermute(y, 'xy', [(i, i ^ 1 << j) for i in range(count)])  8.32 us
    ppermute x4, starting transfers between devices, reduce_scatter_xy(): y = keep + lax.ppermute(send, 'xy', [(i, i ^ 1 << j) for i in range(count)])  6.4 us
    ppermute x3, starting transfers between devices, all_gather_xy(): other = lax.ppermute(y, 'xy', [(i, i ^ 1 << j) for i in range(count)])  5.86 us
    ppermute x2, starting transfers between devices, exchange(): lax.ppermute(jnp.where(gz_index == 0, upward, downward), 'gz', [(0, 1), (...  3.5 us
    ppermute x2, waiting for transfers between devices, exchange(): lax.ppermute(jnp.where(gz_index == 0, upward, downward), 'gz', [(0, 1), (...  3.01 us
  transfers between devices with their start and end apart: 10, of which 8 were waited for; matrix products, arithmetic and copies ran while one was open for 3% of the time, Pallas kernels for 0%

profile of v18, /device:TPU:0, one launch (start us, length us, event | category | flops | bytes accessed | tf_op | source)
XLA Modules:
  0.0 66.1 jit_solution(8421975283894552678)
XLA Ops:
  0.6 12.9 %shard_map.86 = f32[16,34,256]{2,1,0:T(8,128)} custom-call(s32[2]{0:T(128)} %bitcast.81, f32[16,16384]{1,0:T(8,128)} %vol_ref.3, f32[2,16384]{1,0:T(2,128)} %amp_ref.3, s32[2,16384]{1,0:T(2,128)} %off_ref.3, s32[2,16384]{1,0:T(2,128)} %wid_ref.3), custom_call_target="tpu_custom_call" | custom-call | flops 1610612736 | bytes 1441792 | tf_op jit(solution)/shard_map/pallas_call | solution.py:81
  13.5 1.1 %constant_dynamic-slice_fusion.5 = (f32[2,2,2,1,34,256]{5,4,3,2,1,0:T(8,128)S(1)}, f32[2,2,2,1,34,256]{5,4,3,2,1,0:T(8,128)S(1)}) fusion(f32[2,2,2,2,34,256]{5,4,3,2,1,0:T(8,128)} %bitcast.73, s32[]{:T(128)S(6)} %select_n.129, s32[]{:T(128)S(6)} %select_n.130), kind=kLoop, calls=%fused_computation.49 | loop fusion | bytes 1114120 | tf_op jit(solution)/shard_map/jit(dynamic_index_in_dim)/dynamic_slice | solution.py:163
  14.6 0.0 copy-start.4
  14.7 0.2 copy.113
  14.9 0.5 collective-permute-start.1
  15.4 0.0 copy-done.4
  15.4 0.7 %copy-done.3 = f32[3,2,16]{2,1,0:T(2,128)S(1)} copy-done((f32[3,2,16]{2,1,0:T(2,128)S(1)}, f32[3,2,16]{2,1,0:T(2,128)}, u32[]{:S(2)}) %copy-start.3) | copy-done | bytes 408
  16.1 0.1 slice_bitcast_fusion.1
  16.2 0.1 reshape.121
  16.3 0.1 reshape.122
  16.4 3.0 %collective-permute-start = (f32[2,2,256]{2,0,1:T(2,128)S(1)}, f32[2,2,256]{2,0,1:T(2,128)S(1)}, u32[]{:S(2)}, u32[]{:S(2)}) collective-permute-start(f32[2,2,256]{2,0,1:T(2,128)S(1)} %fusion.8), channel_id=1, source_target_pairs={{0,1},{1,0},{2,3},{3,2},{4,5},{5,4},{6,7},{7,6},{8,9},{9,8},{10,11... | collective-permute-start | bytes 12296 | tf_op jit(solution)/shard_map/ppermute | solution.py:210
  19.3 0.0 collective-permute-done.1
  19.3 0.3 bitcast_add_fusion
  19.7 1.6 %collective-permute-start.2 = (f32[2,2,34,256]{3,1,2,0:T(2,128)S(1)}, f32[2,2,34,256]{3,1,2,0:T(2,128)S(1)}, u32[]{:S(2)}, u32[]{:S(2)}) collective-permute-start(f32[2,2,34,256]{3,1,2,0:T(2,128)S(1)} %dynamic-slice_bitcast_fusion), channel_id=1, source_target_pairs={{0,4},{2,6},{4,0},{6,2},{8,12},{10,14},{12,8},{14,10},{16,20},{18,... | collective-permute-start | bytes 417800 | tf_op jit(solution)/shard_map/ppermute | solution.py:165
  21.3 3.8 %collective-permute-done.2 = f32[2,2,34,256]{3,1,2,0:T(2,128)S(1)} collective-permute-done((f32[2,2,34,256]{3,1,2,0:T(2,128)S(1)}, f32[2,2,34,256]{3,1,2,0:T(2,128)S(1)}, u32[]{:S(2)}, u32[]{:S(2)}) %collective-permute-start.2) | collective-permute-done | bytes 139296 | tf_op jit(solution)/shard_map/ppermute | solution.py:165
  25.1 0.1 bitcast_add_fusion.1
  25.2 0.1 constant_dynamic-slice_fusion.3
  25.3 1.6 %collective-permute-start.3 = (f32[2,34,256]{2,0,1:T(2,128)S(1)}, f32[2,34,256]{2,0,1:T(2,128)S(1)}, u32[]{:S(2)}, u32[]{:S(2)}) collective-permute-start(f32[2,34,256]{2,0,1:T(2,128)S(1)} %bitcast.76), channel_id=1, source_target_pairs={{0,8},{2,10},{4,12},{6,14},{8,0},{10,2},{12,4},{14,6},{16,24},{18,... | collective-permute-start | bytes 208904 | tf_op jit(solution)/shard_map/ppermute | solution.py:165
  27.0 2.7 %collective-permute-done.3 = f32[2,34,256]{2,0,1:T(2,128)S(1)} collective-permute-done((f32[2,34,256]{2,0,1:T(2,128)S(1)}, f32[2,34,256]{2,0,1:T(2,128)S(1)}, u32[]{:S(2)}, u32[]{:S(2)}) %collective-permute-start.3) | collective-permute-done | bytes 69664 | tf_op jit(solution)/shard_map/ppermute | solution.py:165
  29.7 0.1 bitcast_add_fusion.2
  29.8 0.1 constant_dynamic-slice_fusion.1
  29.9 2.7 %collective-permute-start.4 = (f32[34,256]{1,0:T(8,128)S(1)}, f32[34,256]{1,0:T(8,128)S(1)}, u32[]{:S(2)}, u32[]{:S(2)}) collective-permute-start(f32[34,256]{1,0:T(8,128)S(1)} %bitcast.77), channel_id=1, source_target_pairs={{0,16},{2,18},{4,20},{6,22},{8,24},{10,26},{12,28},{14,30},{16,0},... | collective-permute-start | bytes 104456 | tf_op jit(solution)/shard_map/ppermute | solution.py:165
  32.5 0.0 collective-permute-done
  32.5 0.1 reshape_squeeze.7
  32.6 0.1 reshape_squeeze.6
  32.7 2.1 %collective-permute-done.4 = f32[34,256]{1,0:T(8,128)S(1)} collective-permute-done((f32[34,256]{1,0:T(8,128)S(1)}, f32[34,256]{1,0:T(8,128)S(1)}, u32[]{:S(2)}, u32[]{:S(2)}) %collective-permute-start.4) | collective-permute-done | bytes 34848 | tf_op jit(solution)/shard_map/ppermute | solution.py:165
  34.8 0.0 copy-start.2
  34.9 0.5 collective-permute-start.5
  35.4 0.1 add_add_fusion
  35.5 0.0 copy-done.2
  35.5 0.0 slice-start
  35.6 3.0 %collective-permute-done.5 = f32[2,2,256]{2,0,1:T(2,128)S(1)} collective-permute-done((f32[2,2,256]{2,0,1:T(2,128)S(1)}, f32[2,2,256]{2,0,1:T(2,128)S(1)}, u32[]{:S(2)}, u32[]{:S(2)}) %collective-permute-start.5) | collective-permute-done | bytes 4128 | tf_op jit(solution)/shard_map/ppermute | solution.py:210
  38.6 0.1 fusion.5
  38.7 0.6 fusion.6
  39.3 2.6 %collective-permute-start.6 = (f32[32,256]{1,0:T(8,128)S(1)}, f32[32,256]{1,0:T(8,128)S(1)}, u32[]{:S(2)}, u32[]{:S(2)}) collective-permute-start(f32[32,256]{1,0:T(8,128)S(1)} %bitcast.75), channel_id=1, source_target_pairs={{0,16},{2,18},{4,20},{6,22},{8,24},{10,26},{12,28},{14,30},{16,0},... | collective-permute-start | bytes 98312 | tf_op jit(solution)/shard_map/ppermute | solution.py:176
  41.9 2.2 %collective-permute-done.6 = f32[32,256]{1,0:T(8,128)S(1)} collective-permute-done((f32[32,256]{1,0:T(8,128)S(1)}, f32[32,256]{1,0:T(8,128)S(1)}, u32[]{:S(2)}, u32[]{:S(2)}) %collective-permute-start.6) | collective-permute-done | bytes 32800 | tf_op jit(solution)/shard_map/ppermute | solution.py:176
  44.2 1.6 %collective-permute-start.7 = (f32[2,32,256]{2,1,0:T(8,128)S(1)}, f32[2,32,256]{2,1,0:T(8,128)S(1)}, u32[]{:S(2)}, u32[]{:S(2)}) collective-permute-start(f32[2,32,256]{2,1,0:T(8,128)S(1)} %pad_maximum_fusion.2), channel_id=1, source_target_pairs={{0,8},{2,10},{4,12},{6,14},{8,0},{10,2},{12,4},{14,6},{16,24},{18,... | collective-permute-start | bytes 196616 | tf_op jit(solution)/shard_map/ppermute | solution.py:176
  45.8 2.7 %collective-permute-done.7 = f32[2,32,256]{2,1,0:T(8,128)S(1)} collective-permute-done((f32[2,32,256]{2,1,0:T(8,128)S(1)}, f32[2,32,256]{2,1,0:T(8,128)S(1)}, u32[]{:S(2)}, u32[]{:S(2)}) %collective-permute-start.7) | collective-permute-done | bytes 65568 | tf_op jit(solution)/shard_map/ppermute | solution.py:176
  48.5 1.6 %collective-permute-start.8 = (f32[2,2,32,256]{3,2,0,1:T(8,128)S(1)}, f32[2,2,32,256]{3,2,0,1:T(8,128)S(1)}, u32[]{:S(2)}, u32[]{:S(2)}) collective-permute-start(f32[2,2,32,256]{3,2,0,1:T(8,128)S(1)} %pad_maximum_fusion.1), channel_id=1, source_target_pairs={{0,4},{2,6},{4,0},{6,2},{8,12},{10,14},{12,8},{14,10},{16,20},{18,... | collective-permute-start | bytes 393224 | tf_op jit(solution)/shard_map/ppermute | solution.py:176
  50.1 3.4 %collective-permute-done.8 = f32[2,2,32,256]{3,2,0,1:T(8,128)S(1)} collective-permute-done((f32[2,2,32,256]{3,2,0,1:T(8,128)S(1)}, f32[2,2,32,256]{3,2,0,1:T(8,128)S(1)}, u32[]{:S(2)}, u32[]{:S(2)}) %collective-permute-start.8) | collective-permute-done | bytes 131104 | tf_op jit(solution)/shard_map/ppermute | solution.py:176
  53.6 0.1 collective-permute-start.9
  53.7 0.1 copy.94
  53.8 0.1 copy.96
  53.9 0.1 copy.95
  54.0 0.7 %select_add_fusion.rw_ref = f32[2,16,1]{2,1,0:T(8,128)} fusion(f32[2,16,1]{2,1,0:T(8,128)S(1)} %copy.96, f32[2,16,1]{2,1,0:T(8,128)S(1)} %copy.95, f32[2,16,1]{2,1,0:T(8,128)S(1)} %copy.94, pred[16]{0:T(512)(128)(4,1)S(1)} %get-tuple-element.38, pred[16]{0:T(512)(128)(4,1)S(1)} %get-tuple-element.39), kind=kLoop, calls=%fused_computation.32 | loop fusion | flops 128 | bytes 544 | tf_op jit(solution)/shard_map/add | solution.py:254
  54.7 0.6 collective-permute-done.9.got_ref
  55.3 0.7 %copy-done.1 = f32[8,32,256]{2,1,0:T(8,128)} copy-done((f32[8,32,256]{2,1,0:T(8,128)}, f32[8,32,256]{2,1,0:T(8,128)S(1)}, u32[]{:S(2)}) %copy-start.1) | copy-done | bytes 262168
  56.0 10.1 %shard_map.87 = f32[16,16384]{1,0:T(8,128)} custom-call(s32[2]{0:T(128)} %bitcast.82, f32[8,32,256]{2,1,0:T(8,128)} %bitcast.72, f32[8,32,256]{2,1,0:T(8,128)} %copy-done.1, f32[16,16384]{1,0:T(8,128)} %vol_ref.3, f32[2,16384]{1,0:T(2,128)} %amp_ref.3, s32[2,16384]{1,0:T(2,128)} %off_ref.3, s32[2,16384]{1,0:T(2,128)} %wid_ref.3, ...), custom_call_target="tpu_custom_call" | custom-call | tf_op jit(solution)/shard_map/pallas_call | solution.py:140
  (42 shorter events, 0.3 us)
Async XLA Ops:
  14.6 0.8 %copy-start.4 = (f32[2,16,256]{2,1,0:T(8,128)S(1)}, f32[2,16,256]{2,1,0:T(8,128)}, u32[]{:S(2)}) copy-start(f32[2,16,256]{2,1,0:T(8,128)} %param.8) | copy-start | bytes 98308
  14.9 4.5 %collective-permute-start.1 = (f32[2,2,2,34,256]{4,1,3,0,2:T(2,128)S(1)}, f32[2,2,2,34,256]{4,1,3,0,2:T(2,128)S(1)}, u32[]{:S(2)}, u32[]{:S(2)}) collective-permute-start(f32[2,2,2,34,256]{4,1,3,0,2:T(2,128)S(1)} %bitcast.74), channel_id=1, source_target_pairs={{0,2},{2,0},{4,6},{6,4},{8,10},{10,8},{12,14},{14,12},{16,18},{18,... | collective-permute-start | bytes 835592 | tf_op jit(solution)/shard_map/ppermute | solution.py:165
  15.4 0.7 %copy-start.3 = (f32[3,2,16]{2,1,0:T(2,128)S(1)}, f32[3,2,16]{2,1,0:T(2,128)}, u32[]{:S(2)}) copy-start(f32[3,2,16]{2,1,0:T(2,128)} %param.13) | copy-start | bytes 1156
  16.4 16.2 %collective-permute-start = (f32[2,2,256]{2,0,1:T(2,128)S(1)}, f32[2,2,256]{2,0,1:T(2,128)S(1)}, u32[]{:S(2)}, u32[]{:S(2)}) collective-permute-start(f32[2,2,256]{2,0,1:T(2,128)S(1)} %fusion.8), channel_id=1, source_target_pairs={{0,1},{1,0},{2,3},{3,2},{4,5},{5,4},{6,7},{7,6},{8,9},{9,8},{10,11... | collective-permute-start | bytes 12296 | tf_op jit(solution)/shard_map/ppermute | solution.py:210
  19.7 5.4 %collective-permute-start.2 = (f32[2,2,34,256]{3,1,2,0:T(2,128)S(1)}, f32[2,2,34,256]{3,1,2,0:T(2,128)S(1)}, u32[]{:S(2)}, u32[]{:S(2)}) collective-permute-start(f32[2,2,34,256]{3,1,2,0:T(2,128)S(1)} %dynamic-slice_bitcast_fusion), channel_id=1, source_target_pairs={{0,4},{2,6},{4,0},{6,2},{8,12},{10,14},{12,8},{14,10},{16,20},{18,... | collective-permute-start | bytes 417800 | tf_op jit(solution)/shard_map/ppermute | solution.py:165
  25.3 4.4 %collective-permute-start.3 = (f32[2,34,256]{2,0,1:T(2,128)S(1)}, f32[2,34,256]{2,0,1:T(2,128)S(1)}, u32[]{:S(2)}, u32[]{:S(2)}) collective-permute-start(f32[2,34,256]{2,0,1:T(2,128)S(1)} %bitcast.76), channel_id=1, source_target_pairs={{0,8},{2,10},{4,12},{6,14},{8,0},{10,2},{12,4},{14,6},{16,24},{18,... | collective-permute-start | bytes 208904 | tf_op jit(solution)/shard_map/ppermute | solution.py:165
  29.9 5.0 %collective-permute-start.4 = (f32[34,256]{1,0:T(8,128)S(1)}, f32[34,256]{1,0:T(8,128)S(1)}, u32[]{:S(2)}, u32[]{:S(2)}) collective-permute-start(f32[34,256]{1,0:T(8,128)S(1)} %bitcast.77), channel_id=1, source_target_pairs={{0,16},{2,18},{4,20},{6,22},{8,24},{10,26},{12,28},{14,30},{16,0},... | collective-permute-start | bytes 104456 | tf_op jit(solution)/shard_map/ppermute | solution.py:165
  34.8 0.7 %copy-start.2 = (f32[2,17,256]{2,1,0:T(8,128)}, f32[2,17,256]{2,1,0:T(8,128)S(1)}, u32[]{:S(2)}) copy-start(f32[2,17,256]{2,1,0:T(8,128)S(1)} %reshape.124) | copy-start | bytes 104452
  34.9 3.7 %collective-permute-start.5 = (f32[2,2,256]{2,0,1:T(2,128)S(1)}, f32[2,2,256]{2,0,1:T(2,128)S(1)}, u32[]{:S(2)}, u32[]{:S(2)}) collective-permute-start(f32[2,2,256]{2,0,1:T(2,128)S(1)} %copy_select_fusion), channel_id=1, source_target_pairs={{0,1},{1,0},{2,3},{3,2},{4,5},{5,4},{6,7},{7,6},{8,9},{9,8},{10,11... | collective-permute-start | bytes 12296 | tf_op jit(solution)/shard_map/ppermute | solution.py:210
  35.5 3.1 %slice-start = ((f32[2,17,256]{2,1,0:T(8,128)}), f32[2,16,256]{2,1,0:T(8,128)S(1)}, s32[]{:S(2)}) async-start(f32[2,17,256]{2,1,0:T(8,128)} %copy-done.2), calls=%async_computation | async-start | bytes 65536 | tf_op jit(solution)/shard_map/slice | solution.py:225
  39.3 4.8 %collective-permute-start.6 = (f32[32,256]{1,0:T(8,128)S(1)}, f32[32,256]{1,0:T(8,128)S(1)}, u32[]{:S(2)}, u32[]{:S(2)}) collective-permute-start(f32[32,256]{1,0:T(8,128)S(1)} %bitcast.75), channel_id=1, source_target_pairs={{0,16},{2,18},{4,20},{6,22},{8,24},{10,26},{12,28},{14,30},{16,0},... | collective-permute-start | bytes 98312 | tf_op jit(solution)/shard_map/ppermute | solution.py:176
  44.2 4.3 %collective-permute-start.7 = (f32[2,32,256]{2,1,0:T(8,128)S(1)}, f32[2,32,256]{2,1,0:T(8,128)S(1)}, u32[]{:S(2)}, u32[]{:S(2)}) collective-permute-start(f32[2,32,256]{2,1,0:T(8,128)S(1)} %pad_maximum_fusion.2), channel_id=1, source_target_pairs={{0,8},{2,10},{4,12},{6,14},{8,0},{10,2},{12,4},{14,6},{16,24},{18,... | collective-permute-start | bytes 196616 | tf_op jit(solution)/shard_map/ppermute | solution.py:176
  48.5 5.0 %collective-permute-start.8 = (f32[2,2,32,256]{3,2,0,1:T(8,128)S(1)}, f32[2,2,32,256]{3,2,0,1:T(8,128)S(1)}, u32[]{:S(2)}, u32[]{:S(2)}) collective-permute-start(f32[2,2,32,256]{3,2,0,1:T(8,128)S(1)} %pad_maximum_fusion.1), channel_id=1, source_target_pairs={{0,4},{2,6},{4,0},{6,2},{8,12},{10,14},{12,8},{14,10},{16,20},{18,... | collective-permute-start | bytes 393224 | tf_op jit(solution)/shard_map/ppermute | solution.py:176
  53.6 1.6 %copy-start = (f32[2,2,2,32,256]{4,3,2,1,0:T(8,128)}, f32[2,2,2,32,256]{4,3,2,1,0:T(8,128)S(1)}, u32[]{:S(2)}) copy-start(f32[2,2,2,32,256]{4,3,2,1,0:T(8,128)S(1)} %copy.93) | copy-start | bytes 786436
  53.6 1.6 %collective-permute-start.9 = (f32[8,32,256]{2,1,0:T(8,128)S(1)}, f32[8,32,256]{2,1,0:T(8,128)S(1)}, u32[]{:S(2)}, u32[]{:S(2)}) collective-permute-start(f32[8,32,256]{2,1,0:T(8,128)S(1)} %bitcast.71), channel_id=1, source_target_pairs={{0,2},{2,0},{4,6},{6,4},{8,10},{10,8},{12,14},{14,12},{16,18},{18,... | collective-permute-start | bytes 786440 | tf_op jit(solution)/shard_map/ppermute | solution.py:181
  55.2 0.7 %copy-start.1 = (f32[8,32,256]{2,1,0:T(8,128)}, f32[8,32,256]{2,1,0:T(8,128)S(1)}, u32[]{:S(2)}) copy-start(f32[8,32,256]{2,1,0:T(8,128)S(1)} %collective-permute-done.9.got_ref) | copy-start | bytes 786436
